TPU v7x, 32 devices: a whole 2x2x4 slice. The times are simulated.
32 devices in a mesh: section: 2 (over x), fsdp: 16 (over z, y, core).
Axes of the slice: x: 2, y: 2, z: 4, core: 2. Of those that a mesh axis runs over, the one named last changes fastest.
Arguments:
- history: bfloat16 [4, 16, 32, 2048], P(None, 'fsdp'), may hold values from -6 to 6
- keymask: int32 [4, 16, 32], P(None, 'fsdp'), may hold values from 0 to 1, as said below
- codes: int32 [4, 16, 16, 2], P(None, 'fsdp'), may hold values from 0 to 15
- plan_table: bfloat16 [16, 2048], replicated, may hold values from -6 to 6
- query_weights: bfloat16 [2, 2048, 1024], P('section', 'fsdp'), may hold values from -0.125 to 0.125
- output_weights: bfloat16 [2, 1024, 2048], P('section', 'fsdp'), may hold values from -0.75 to 0.75
- gains: float32 [2, 2048], P('section'), may hold values from 0.5 to 1.5
- cotangent: bfloat16 [4, 16, 32, 2048], P(None, 'fsdp'), may hold values from -6 to 6
Outputs:
- section_grads: bfloat16 [2, 4, 16, 32, 2048], P('section', None, 'fsdp')
- gain_grads: float32 [2, 2048], P('section')
Inputs may be any that keep to these rules, and one draw needn't show every extreme that they name: `keymask`: in each series the ones form one run that ends at the last position and covers at least a quarter of the 32 positions.
All inputs are finite; a program needn't handle non-finite values.
Results may differ from a plain program's by a relative error of at most 0.014.
Values may be sent and summed in bfloat16 or wider, within the bound.
No kernel may reach another device: no remote copies, remote signals or barrier semaphores. Data moves between devices by JAX's collectives and lax.ppermute only.
A program may use at most 64 MiB of HBM per device.

v0:
```python
import math

import jax
import jax.numpy as jnp
from jax import lax
from jax.sharding import PartitionSpec as P

HEADS = 8


EPSILON = 1e-05


def shifted(array, axis, by):
    size = lax.axis_size(axis)
    pairs = [(i, i + by) for i in range(size) if 0 <= i + by < size]
    return lax.ppermute(array, axis, pairs)


def rms_scale(inputs, gain_vector):
    return (
        inputs
        * lax.rsqrt(jnp.mean(inputs * inputs, axis=-1, keepdims=True) + EPSILON)
        * gain_vector
    )


def attend_layer(section_input, source, key_mask, query_weight, output_weight, gain_vector):
    series_count, seq_length, model_width = section_input.shape
    half_width = model_width // 2
    head_dim = half_width // HEADS
    head_shape = (series_count, seq_length, HEADS, head_dim)
    input_wide = section_input.astype(jnp.float32)
    normed = rms_scale(input_wide, gain_vector)
    normed_source = rms_scale(source.astype(jnp.float32), gain_vector)
    normed_rows = normed.astype(jnp.bfloat16).reshape(series_count * seq_length, model_width)
    query_flat = jnp.dot(normed_rows, query_weight, preferred_element_type=jnp.float32)
    queries = query_flat.astype(jnp.bfloat16).reshape(head_shape)
    key_rows = normed_source[..., :half_width].astype(jnp.bfloat16).reshape(head_shape)
    value_rows = normed_source[..., half_width:].astype(jnp.bfloat16).reshape(head_shape)
    scores = jnp.einsum(
        "bqhd,bkhd->bhqk", queries, key_rows, preferred_element_type=jnp.float32
    ) / math.sqrt(head_dim)
    raised = jnp.exp(scores) * key_mask.astype(jnp.float32)[:, None, None, :]
    probs = (raised / jnp.sum(raised, axis=-1, keepdims=True)).astype(jnp.bfloat16)
    mixed = jnp.einsum("bhqk,bkhd->bqhd", probs, value_rows, preferred_element_type=jnp.float32)
    mixed = mixed.astype(jnp.bfloat16).reshape(series_count * seq_length, half_width)
    update = jnp.dot(mixed, output_weight, preferred_element_type=jnp.float32)
    return (input_wide + update.reshape(series_count, seq_length, model_width)).astype(jnp.bfloat16)


def pick_slot(stack, slot):
    return lax.dynamic_index_in_dim(stack, slot, 0, False)


def place_slot(stack, slot, update, keep):
    previous = pick_slot(stack, slot)
    return lax.dynamic_update_index_in_dim(stack, jnp.where(keep, update, previous), slot, 0)


def on_device(history, keymask, codes, plan_table, query_weights, output_weights, gains, cotangent):
    section_index = lax.axis_index("section")
    section_count = lax.axis_size("section")
    half_sections = section_count // 2
    micro_count, series_count, seq_length, model_width = history.shape
    gathered_query, gathered_output = (
        lax.all_gather(query_weights, "fsdp", axis=1, tiled=True),
        lax.all_gather(output_weights, "fsdp", axis=1, tiled=True),
    )
    query_weight = gathered_query[0]
    output_weight = gathered_output[0]
    gain_vector = gains[0]
    code_rows = codes.reshape(micro_count, series_count, seq_length)
    code_count = plan_table.shape[0]
    one_hot = (code_rows[..., None] == jnp.arange(code_count, dtype=jnp.int32)).astype(jnp.bfloat16)
    plan_tokens = jnp.einsum(
        "msln,nd->msld", one_hot, plan_table, preferred_element_type=jnp.float32
    ).astype(jnp.bfloat16)
    is_decoder = section_index >= half_sections
    zero_act = jnp.zeros((series_count, seq_length, model_width), jnp.bfloat16)
    zero_stack = jnp.zeros(history.shape, jnp.bfloat16)
    tick_count = micro_count + section_count - 1

    def forward_tick(tick_index, state_tuple):
        got_input, got_memory, inputs_buf, memory_buf = state_tuple
        micro_index = tick_index - section_index
        is_active = (micro_index >= 0) & (micro_index < micro_count)
        slot = jnp.clip(micro_index, 0, micro_count - 1)
        key_mask = pick_slot(keymask, slot)
        section_input = jnp.where(
            section_index == 0,
            pick_slot(history, slot),
            jnp.where(section_index == half_sections, pick_slot(plan_tokens, slot), got_input),
        )
        memory = got_memory
        source = jnp.where(is_decoder, memory, section_input)

        def run_layer():
            return attend_layer(
                section_input, source, key_mask, query_weight, output_weight, gain_vector
            )

        def skip_layer():
            return zero_act

        output = lax.cond(is_active, run_layer, skip_layer)
        inputs_buf = place_slot(inputs_buf, slot, section_input, is_active)
        memory_buf = place_slot(memory_buf, slot, memory, is_active & is_decoder)
        outgoing = jnp.where(
            section_index == half_sections - 1, output, jnp.where(is_decoder, memory, zero_act)
        )
        got_input, got_memory = shifted((output, outgoing), "section", 1)
        return (got_input, got_memory, inputs_buf, memory_buf)

    start_state = (zero_act, zero_act, zero_stack, zero_stack)
    _, _, inputs_buf, memory_buf = lax.fori_loop(0, tick_count, forward_tick, start_state)

    def backward_tick(tick_index, state_tuple):
        got_grad, got_memory_grad, grads_buf, gain_total = state_tuple
        micro_index = tick_index - (section_count - 1 - section_index)
        is_active = (micro_index >= 0) & (micro_index < micro_count)
        slot = jnp.clip(micro_index, 0, micro_count - 1)
        key_mask = pick_slot(keymask, slot)
        out_grad = jnp.where(
            section_index == section_count - 1, pick_slot(cotangent, slot), got_grad
        )
        section_input = pick_slot(inputs_buf, slot)
        memory = pick_slot(memory_buf, slot)

        def section_map(layer_input, layer_memory, layer_gain):
            layer_source = jnp.where(is_decoder, layer_memory, layer_input)
            return attend_layer(
                layer_input, layer_source, key_mask, query_weight, output_weight, layer_gain
            )

        def run_grads():
            _, pull = jax.vjp(section_map, section_input, memory, gain_vector)
            return pull(out_grad)

        def skip_grads():
            return (zero_act, zero_act, jnp.zeros_like(gain_vector))

        input_grad, memory_grad, gain_grad = lax.cond(is_active, run_grads, skip_grads)
        memory_sum = jnp.where(is_decoder, got_memory_grad + memory_grad, zero_act)
        send_main = jnp.where(section_index == half_sections, memory_sum, input_grad)
        send_side = jnp.where(is_decoder & (section_index != half_sections), memory_sum, zero_act)
        got_grad, got_memory_grad = shifted((send_main, send_side), "section", -1)
        grads_buf = place_slot(grads_buf, slot, input_grad, is_active)
        gain_total = gain_total + lax.psum(gain_grad, "fsdp")
        return (got_grad, got_memory_grad, grads_buf, gain_total)

    back_state = (zero_act, zero_act, zero_stack, jnp.zeros_like(gain_vector))
    _, _, grads_buf, gain_total = lax.fori_loop(0, tick_count, backward_tick, back_state)
    return (grads_buf[None], gain_total[None])


def solution(mesh):
    return jax.shard_map(
        on_device,
        mesh=mesh,
        in_specs=(
            P(None, "fsdp", None, None),
            P(None, "fsdp", None),
            P(None, "fsdp", None, None),
            P(),
            P("section", "fsdp", None),
            P("section", "fsdp", None),
            P("section", None),
            P(None, "fsdp", None, None),
        ),
        out_specs=(P("section", None, "fsdp", None, None), P("section", None)),
        check_vma=False,
    )
```

profile of v0, /device:TPU:0, one launch (start us, length us, event | category | flops | bytes accessed | tf_op | source)
XLA Modules:
  0.0 415.8 jit_solution(3246150808287306456)
XLA Ops:
  9.9 53.6 %all-gather.3.cloned.1.call-done = bf16[1,1024,2048]{2,1,0:T(8,128)(2,1)} async-done(((bf16[1,64,2048]{2,1,0:T(8,128)(2,1)}), bf16[1,1024,2048]{2,1,0:T(8,128)(2,1)}) %all-gather.3.cloned.1.call-update) | async-done | bytes 4194320 | tf_op jit(solution)/shard_map/all_gather | solution.py:68
  63.5 51.2 %all-gather.5.cloned.1.call-done = bf16[1,2048,1024]{2,1,0:T(8,128)(2,1)} async-done(((bf16[1,128,1024]{2,1,0:T(8,128)(2,1)}), bf16[1,2048,1024]{2,1,0:T(8,128)(2,1)}) %all-gather.5.cloned.1.call-update) | async-done | bytes 4194320 | tf_op jit(solution)/shard_map/all_gather | solution.py:67
  114.9 89.8 %while.42 = (s32[]{:T(128)}, bf16[1,32,2048]{2,1,0:T(8,128)(2,1)S(1)}, bf16[1,32,2048]{2,1,0:T(8,128)(2,1)S(1)}, bf16[4,1,32,2048]{3,2,1,0:T(8,128)(2,1)S(1)}, b...) while((s32[]{:T(128)}, ...), condition=%wide.region_6.7_spmd, body=%wide.region_0.6_spmd.sunk | while | flops 274366848 | bytes 14173985 | solution.py:116
  116.0 8.3 %conditional.5 = (bf16[1,32,2048]{2,1,0:T(8,128)(2,1)S(1)}) conditional(s32[]{:T(128)} %convert_element_type.398, () %tuple.120, (bf16[1,32,2048]{2,1,0:T(8,128)(2,1)S(1)}, pred[1,32,2048]{2,1,0:T(8,128)(4,1)S(1)}, bf16[1,32,2048]{2,1,0:T(8,128)(2,1)S(1)}, f32[1,2048]{1,0:T(1,128)}, bf16[2048,1024]{1,0:T(8,128)(2,1)}, ...), branch_computations={%region_1.1_spmd, %region_2.5_spmd} | conditional | flops 273973632 | bytes 10700172 | solution.py:106
  117.0 3.1 fusion.5
  121.2 3.0 fusion.1
  125.6 1.3 collective-permute-start.1
  127.0 4.8 %collective-permute-done.1 = bf16[1,32,2048]{2,1,0:T(8,128)(2,1)S(1)} collective-permute-done((bf16[1,32,2048]{2,1,0:T(8,128)(2,1)S(1)}, bf16[1,32,2048]{2,1,0:T(8,128)(2,1)S(1)}, u32[]{:S(2)}, u32[]{:S(2)}) %collective-permute-start.1) | collective-permute-done | bytes 131104 | tf_op jit(solution)/shard_map/while/body/eval_jaxpr/ppermute | solution.py:17
  132.9 8.3 %conditional.5 = (bf16[1,32,2048]{2,1,0:T(8,128)(2,1)S(1)}) conditional(s32[]{:T(128)} %convert_element_type.398, () %tuple.120, (bf16[1,32,2048]{2,1,0:T(8,128)(2,1)S(1)}, pred[1,32,2048]{2,1,0:T(8,128)(4,1)S(1)}, bf16[1,32,2048]{2,1,0:T(8,128)(2,1)S(1)}, f32[1,2048]{1,0:T(1,128)}, bf16[2048,1024]{1,0:T(8,128)(2,1)}, ...), branch_computations={%region_1.1_spmd, %region_2.5_spmd} | conditional | flops 273973632 | bytes 10700172 | solution.py:106
  134.0 3.1 fusion.5
  138.2 3.0 fusion.1
  141.2 4.4 %collective-permute-start = (bf16[1,32,2048]{2,1,0:T(8,128)(2,1)S(1)}, bf16[1,32,2048]{2,1,0:T(8,128)(2,1)S(1)}, u32[]{:S(2)}, u32[]{:S(2)}) collective-permute-start(bf16[1,32,2048]{2,1,0:T(8,128)(2,1)S(1)} %get-tuple-element.1286), channel_id=1, source_target_pairs={{0,16},{1,17},{2,18},{3,19},{4,20},{5,21},{6,22},{7,23},{8,24},{9,... | collective-permute-start | bytes 393224 | tf_op jit(solution)/shard_map/while/body/eval_jaxpr/ppermute | solution.py:17
  145.6 1.3 collective-permute-start.1
  147.0 4.0 collective-permute-done.1
  152.1 8.3 %conditional.5 = (bf16[1,32,2048]{2,1,0:T(8,128)(2,1)S(1)}) conditional(s32[]{:T(128)} %convert_element_type.398, () %tuple.120, (bf16[1,32,2048]{2,1,0:T(8,128)(2,1)S(1)}, pred[1,32,2048]{2,1,0:T(8,128)(4,1)S(1)}, bf16[1,32,2048]{2,1,0:T(8,128)(2,1)S(1)}, f32[1,2048]{1,0:T(1,128)}, bf16[2048,1024]{1,0:T(8,128)(2,1)}, ...), branch_computations={%region_1.1_spmd, %region_2.5_spmd} | conditional | flops 273973632 | bytes 10700172 | solution.py:106
  153.2 3.1 fusion.5
  157.4 3.0 fusion.1
  160.4 4.4 %collective-permute-start = (bf16[1,32,2048]{2,1,0:T(8,128)(2,1)S(1)}, bf16[1,32,2048]{2,1,0:T(8,128)(2,1)S(1)}, u32[]{:S(2)}, u32[]{:S(2)}) collective-permute-start(bf16[1,32,2048]{2,1,0:T(8,128)(2,1)S(1)} %get-tuple-element.1286), channel_id=1, source_target_pairs={{0,16},{1,17},{2,18},{3,19},{4,20},{5,21},{6,22},{7,23},{8,24},{9,... | collective-permute-start | bytes 393224 | tf_op jit(solution)/shard_map/while/body/eval_jaxpr/ppermute | solution.py:17
  166.2 3.2 collective-permute-done.1
  170.5 8.3 %conditional.5 = (bf16[1,32,2048]{2,1,0:T(8,128)(2,1)S(1)}) conditional(s32[]{:T(128)} %convert_element_type.398, () %tuple.120, (bf16[1,32,2048]{2,1,0:T(8,128)(2,1)S(1)}, pred[1,32,2048]{2,1,0:T(8,128)(4,1)S(1)}, bf16[1,32,2048]{2,1,0:T(8,128)(2,1)S(1)}, f32[1,2048]{1,0:T(1,128)}, bf16[2048,1024]{1,0:T(8,128)(2,1)}, ...), branch_computations={%region_1.1_spmd, %region_2.5_spmd} | conditional | flops 273973632 | bytes 10700172 | solution.py:106
  171.5 3.1 fusion.5
  175.7 3.0 fusion.1
  178.8 4.4 %collective-permute-start = (bf16[1,32,2048]{2,1,0:T(8,128)(2,1)S(1)}, bf16[1,32,2048]{2,1,0:T(8,128)(2,1)S(1)}, u32[]{:S(2)}, u32[]{:S(2)}) collective-permute-start(bf16[1,32,2048]{2,1,0:T(8,128)(2,1)S(1)} %get-tuple-element.1286), channel_id=1, source_target_pairs={{0,16},{1,17},{2,18},{3,19},{4,20},{5,21},{6,22},{7,23},{8,24},{9,... | collective-permute-start | bytes 393224 | tf_op jit(solution)/shard_map/while/body/eval_jaxpr/ppermute | solution.py:17
  184.6 2.5 collective-permute-done.1
  188.2 12.6 %collective-permute-start = (bf16[1,32,2048]{2,1,0:T(8,128)(2,1)S(1)}, bf16[1,32,2048]{2,1,0:T(8,128)(2,1)S(1)}, u32[]{:S(2)}, u32[]{:S(2)}) collective-permute-start(bf16[1,32,2048]{2,1,0:T(8,128)(2,1)S(1)} %get-tuple-element.1286), channel_id=1, source_target_pairs={{0,16},{1,17},{2,18},{3,19},{4,20},{5,21},{6,22},{7,23},{8,24},{9,... | collective-permute-start | bytes 393224 | tf_op jit(solution)/shard_map/while/body/eval_jaxpr/ppermute | solution.py:17
  202.2 2.5 collective-permute-done.1
  204.8 203.3 %while.43 = (s32[]{:T(128)}, bf16[1,32,2048]{2,1,0:T(8,128)(2,1)S(1)}, bf16[1,32,2048]{2,1,0:T(8,128)(2,1)S(1)}, bf16[4,1,32,2048]{3,2,1,0:T(8,128)(2,1)S(1)}, f...) while((s32[]{:T(128)}, ...), condition=%wide.region_19.20_spmd.clone, body=%wide.region_7.19_spmd.clone.sunk | while | flops 417616544 | bytes 54182452 | solution.py:153
  207.6 30.0 %psum.15 = f32[2048]{0:T(1024)S(1)} all-reduce(f32[2048]{0:T(1024)S(1)} %get-tuple-element.1162), channel_id=1, replica_groups=mesh['section'=2,'fsdp'=16] {'fsdp'}, use_global_device_ids=true, to_apply=%region_18.18 | all-reduce | flops 2048 | bytes 16384 | tf_op jit(solution)/shard_map/while/body/eval_jaxpr/psum | solution.py:149
  237.8 9.8 %conditional.6 = (bf16[1,32,2048]{2,1,0:T(8,128)(2,1)S(1)}, bf16[1,32,2048]{2,1,0:T(8,128)(2,1)S(1)}, f32[2048]{0:T(1024)S(1)}) conditional(s32[]{:T(128)} %convert_element_type.399, () %tuple.124, (bf16[4,1,32,2048]{3,2,1,0:T(8,128)(2,1)S(1)}, s32[]{:T(128)}, pred[1,32,2048]{2,1,0:T(32,128)(4,1)S(1)}, bf16[1,32,2048]{2,1,0:T(8,128)(2,1)S(1)}, ...), branch_computations={%region_8.8_spmd, %region_9.17_spmd} | conditional | flops 417282720 | bytes 51716228 | solution.py:143
  239.0 3.1 fusion.38
  243.2 1.3 fusion.37
  245.7 1.5 fusion.50
  250.3 30.0 %psum.15 = f32[2048]{0:T(1024)S(1)} all-reduce(f32[2048]{0:T(1024)S(1)} %get-tuple-element.1162), channel_id=1, replica_groups=mesh['section'=2,'fsdp'=16] {'fsdp'}, use_global_device_ids=true, to_apply=%region_18.18 | all-reduce | flops 2048 | bytes 16384 | tf_op jit(solution)/shard_map/while/body/eval_jaxpr/psum | solution.py:149
  280.4 9.8 %conditional.6 = (bf16[1,32,2048]{2,1,0:T(8,128)(2,1)S(1)}, bf16[1,32,2048]{2,1,0:T(8,128)(2,1)S(1)}, f32[2048]{0:T(1024)S(1)}) conditional(s32[]{:T(128)} %convert_element_type.399, () %tuple.124, (bf16[4,1,32,2048]{3,2,1,0:T(8,128)(2,1)S(1)}, s32[]{:T(128)}, pred[1,32,2048]{2,1,0:T(32,128)(4,1)S(1)}, bf16[1,32,2048]{2,1,0:T(8,128)(2,1)S(1)}, ...), branch_computations={%region_8.8_spmd, %region_9.17_spmd} | conditional | flops 417282720 | bytes 51716228 | solution.py:143
  281.6 3.1 fusion.38
  285.8 1.3 fusion.37
  288.4 1.5 fusion.50
  292.9 30.0 %psum.15 = f32[2048]{0:T(1024)S(1)} all-reduce(f32[2048]{0:T(1024)S(1)} %get-tuple-element.1162), channel_id=1, replica_groups=mesh['section'=2,'fsdp'=16] {'fsdp'}, use_global_device_ids=true, to_apply=%region_18.18 | all-reduce | flops 2048 | bytes 16384 | tf_op jit(solution)/shard_map/while/body/eval_jaxpr/psum | solution.py:149
  323.0 9.8 %conditional.6 = (bf16[1,32,2048]{2,1,0:T(8,128)(2,1)S(1)}, bf16[1,32,2048]{2,1,0:T(8,128)(2,1)S(1)}, f32[2048]{0:T(1024)S(1)}) conditional(s32[]{:T(128)} %convert_element_type.399, () %tuple.124, (bf16[4,1,32,2048]{3,2,1,0:T(8,128)(2,1)S(1)}, s32[]{:T(128)}, pred[1,32,2048]{2,1,0:T(32,128)(4,1)S(1)}, bf16[1,32,2048]{2,1,0:T(8,128)(2,1)S(1)}, ...), branch_computations={%region_8.8_spmd, %region_9.17_spmd} | conditional | flops 417282720 | bytes 51716228 | solution.py:143
  324.2 3.1 fusion.38
  328.4 1.3 fusion.37
  331.0 1.5 fusion.50
  335.5 30.0 %psum.15 = f32[2048]{0:T(1024)S(1)} all-reduce(f32[2048]{0:T(1024)S(1)} %get-tuple-element.1162), channel_id=1, replica_groups=mesh['section'=2,'fsdp'=16] {'fsdp'}, use_global_device_ids=true, to_apply=%region_18.18 | all-reduce | flops 2048 | bytes 16384 | tf_op jit(solution)/shard_map/while/body/eval_jaxpr/psum | solution.py:149
  365.6 9.8 %conditional.6 = (bf16[1,32,2048]{2,1,0:T(8,128)(2,1)S(1)}, bf16[1,32,2048]{2,1,0:T(8,128)(2,1)S(1)}, f32[2048]{0:T(1024)S(1)}) conditional(s32[]{:T(128)} %convert_element_type.399, () %tuple.124, (bf16[4,1,32,2048]{3,2,1,0:T(8,128)(2,1)S(1)}, s32[]{:T(128)}, pred[1,32,2048]{2,1,0:T(32,128)(4,1)S(1)}, bf16[1,32,2048]{2,1,0:T(8,128)(2,1)S(1)}, ...), branch_computations={%region_8.8_spmd, %region_9.17_spmd} | conditional | flops 417282720 | bytes 51716228 | solution.py:143
  366.8 3.1 fusion.38
  371.0 1.3 fusion.37
  373.6 1.5 fusion.50
  378.1 30.0 %psum.15 = f32[2048]{0:T(1024)S(1)} all-reduce(f32[2048]{0:T(1024)S(1)} %get-tuple-element.1162), channel_id=1, replica_groups=mesh['section'=2,'fsdp'=16] {'fsdp'}, use_global_device_ids=true, to_apply=%region_18.18 | all-reduce | flops 2048 | bytes 16384 | tf_op jit(solution)/shard_map/while/body/eval_jaxpr/psum | solution.py:149
  (278 shorter events, 51.1 us)
Async XLA Ops:
  7.2 2.4 copy-start
  7.2 56.3 %all-gather.3.cloned.1.call-start = ((), (), s32[]{:S(2)}) async-start(), calls=%async_computation | async-start | bytes 4456448 | tf_op jit(solution)/shard_map/all_gather | solution.py:68
  7.9 106.8 %all-gather.5.cloned.1.call-start = ((), (), s32[]{:S(2)}) async-start(), calls=%async_computation.1 | async-start | bytes 4456448 | tf_op jit(solution)/shard_map/all_gather | solution.py:67
  114.9 89.9 %copy-start.4 = (bf16[4,1,32,2048]{3,2,1,0:T(8,128)(2,1)S(1)}, bf16[4,1,32,2048]{3,2,1,0:T(8,128)(2,1)}, u32[]{:S(2)}) copy-start(bf16[4,1,32,2048]{3,2,1,0:T(8,128)(2,1)} %param.23) | copy-start | bytes 1572868
  124.3 7.6 %collective-permute-start = (bf16[1,32,2048]{2,1,0:T(8,128)(2,1)S(1)}, bf16[1,32,2048]{2,1,0:T(8,128)(2,1)S(1)}, u32[]{:S(2)}, u32[]{:S(2)}) collective-permute-start(bf16[1,32,2048]{2,1,0:T(8,128)(2,1)S(1)} %get-tuple-element.1286), channel_id=1, source_target_pairs={{0,16},{1,17},{2,18},{3,19},{4,20},{5,21},{6,22},{7,23},{8,24},{9,... | collective-permute-start | bytes 393224 | tf_op jit(solution)/shard_map/while/body/eval_jaxpr/ppermute | solution.py:17
  125.6 6.2 %collective-permute-start.1 = (bf16[1,32,2048]{2,1,0:T(8,128)(2,1)S(1)}, bf16[1,32,2048]{2,1,0:T(8,128)(2,1)S(1)}, u32[]{:S(2)}, u32[]{:S(2)}) collective-permute-start(bf16[1,32,2048]{2,1,0:T(8,128)(2,1)S(1)} %select_select_fusion.2), channel_id=1, source_target_pairs={{0,16},{1,17},{2,18},{3,19},{4,20},{5,21},{6,22},{7,23},{8,24},{9,... | collective-permute-start | bytes 393224 | tf_op jit(solution)/shard_map/while/body/eval_jaxpr/ppermute | solution.py:17
  141.2 9.9 %collective-permute-start = (bf16[1,32,2048]{2,1,0:T(8,128)(2,1)S(1)}, bf16[1,32,2048]{2,1,0:T(8,128)(2,1)S(1)}, u32[]{:S(2)}, u32[]{:S(2)}) collective-permute-start(bf16[1,32,2048]{2,1,0:T(8,128)(2,1)S(1)} %get-tuple-element.1286), channel_id=1, source_target_pairs={{0,16},{1,17},{2,18},{3,19},{4,20},{5,21},{6,22},{7,23},{8,24},{9,... | collective-permute-start | bytes 393224 | tf_op jit(solution)/shard_map/while/body/eval_jaxpr/ppermute | solution.py:17
  145.6 5.4 %collective-permute-start.1 = (bf16[1,32,2048]{2,1,0:T(8,128)(2,1)S(1)}, bf16[1,32,2048]{2,1,0:T(8,128)(2,1)S(1)}, u32[]{:S(2)}, u32[]{:S(2)}) collective-permute-start(bf16[1,32,2048]{2,1,0:T(8,128)(2,1)S(1)} %select_select_fusion.2), channel_id=1, source_target_pairs={{0,16},{1,17},{2,18},{3,19},{4,20},{5,21},{6,22},{7,23},{8,24},{9,... | collective-permute-start | bytes 393224 | tf_op jit(solution)/shard_map/while/body/eval_jaxpr/ppermute | solution.py:17
  160.4 9.0 %collective-permute-start = (bf16[1,32,2048]{2,1,0:T(8,128)(2,1)S(1)}, bf16[1,32,2048]{2,1,0:T(8,128)(2,1)S(1)}, u32[]{:S(2)}, u32[]{:S(2)}) collective-permute-start(bf16[1,32,2048]{2,1,0:T(8,128)(2,1)S(1)} %get-tuple-element.1286), channel_id=1, source_target_pairs={{0,16},{1,17},{2,18},{3,19},{4,20},{5,21},{6,22},{7,23},{8,24},{9,... | collective-permute-start | bytes 393224 | tf_op jit(solution)/shard_map/while/body/eval_jaxpr/ppermute | solution.py:17
  164.8 4.5 %collective-permute-start.1 = (bf16[1,32,2048]{2,1,0:T(8,128)(2,1)S(1)}, bf16[1,32,2048]{2,1,0:T(8,128)(2,1)S(1)}, u32[]{:S(2)}, u32[]{:S(2)}) collective-permute-start(bf16[1,32,2048]{2,1,0:T(8,128)(2,1)S(1)} %select_select_fusion.2), channel_id=1, source_target_pairs={{0,16},{1,17},{2,18},{3,19},{4,20},{5,21},{6,22},{7,23},{8,24},{9,... | collective-permute-start | bytes 393224 | tf_op jit(solution)/shard_map/while/body/eval_jaxpr/ppermute | solution.py:17
  178.8 8.3 %collective-permute-start = (bf16[1,32,2048]{2,1,0:T(8,128)(2,1)S(1)}, bf16[1,32,2048]{2,1,0:T(8,128)(2,1)S(1)}, u32[]{:S(2)}, u32[]{:S(2)}) collective-permute-start(bf16[1,32,2048]{2,1,0:T(8,128)(2,1)S(1)} %get-tuple-element.1286), channel_id=1, source_target_pairs={{0,16},{1,17},{2,18},{3,19},{4,20},{5,21},{6,22},{7,23},{8,24},{9,... | collective-permute-start | bytes 393224 | tf_op jit(solution)/shard_map/while/body/eval_jaxpr/ppermute | solution.py:17
  183.2 3.8 collective-permute-start.1
  188.2 16.5 %collective-permute-start = (bf16[1,32,2048]{2,1,0:T(8,128)(2,1)S(1)}, bf16[1,32,2048]{2,1,0:T(8,128)(2,1)S(1)}, u32[]{:S(2)}, u32[]{:S(2)}) collective-permute-start(bf16[1,32,2048]{2,1,0:T(8,128)(2,1)S(1)} %get-tuple-element.1286), channel_id=1, source_target_pairs={{0,16},{1,17},{2,18},{3,19},{4,20},{5,21},{6,22},{7,23},{8,24},{9,... | collective-permute-start | bytes 393224 | tf_op jit(solution)/shard_map/while/body/eval_jaxpr/ppermute | solution.py:17
  200.8 3.8 collective-permute-start.1
  205.0 32.7 %collective-permute-start.2 = (bf16[1,32,2048]{2,1,0:T(8,128)(2,1)S(1)}, bf16[1,32,2048]{2,1,0:T(8,128)(2,1)S(1)}, u32[]{:S(2)}, u32[]{:S(2)}) collective-permute-start(bf16[1,32,2048]{2,1,0:T(8,128)(2,1)S(1)} %get-tuple-element.1160), channel_id=1, source_target_pairs={{16,0},{17,1},{18,2},{19,3},{20,4},{21,5},{22,6},{23,7},{24,8},{25... | collective-permute-start | bytes 393224 | tf_op jit(solution)/shard_map/while/body/eval_jaxpr/ppermute | solution.py:17
  206.3 31.4 %collective-permute-start.3 = (bf16[1,32,2048]{2,1,0:T(8,128)(2,1)S(1)}, bf16[1,32,2048]{2,1,0:T(8,128)(2,1)S(1)}, u32[]{:S(2)}, u32[]{:S(2)}) collective-permute-start(bf16[1,32,2048]{2,1,0:T(8,128)(2,1)S(1)} %get-tuple-element.1161), channel_id=1, source_target_pairs={{16,0},{17,1},{18,2},{19,3},{20,4},{21,5},{22,6},{23,7},{24,8},{25... | collective-permute-start | bytes 393224 | tf_op jit(solution)/shard_map/while/body/eval_jaxpr/ppermute | solution.py:17
  237.8 5.4 %copy-start.2 = (bf16[1024,2048]{1,0:T(8,128)(2,1)S(1)}, bf16[1024,2048]{1,0:T(8,128)(2,1)}, u32[]{:S(2)}) copy-start(bf16[1024,2048]{1,0:T(8,128)(2,1)} %get-tuple-element.750) | copy-start | bytes 12582916 | tf_op jit(solution)/shard_map/while/body/eval_jaxpr/cond
  242.1 3.1 copy-start.3
  242.1 3.6 copy-start.1
  247.6 32.7 %collective-permute-start.2 = (bf16[1,32,2048]{2,1,0:T(8,128)(2,1)S(1)}, bf16[1,32,2048]{2,1,0:T(8,128)(2,1)S(1)}, u32[]{:S(2)}, u32[]{:S(2)}) collective-permute-start(bf16[1,32,2048]{2,1,0:T(8,128)(2,1)S(1)} %get-tuple-element.1160), channel_id=1, source_target_pairs={{16,0},{17,1},{18,2},{19,3},{20,4},{21,5},{22,6},{23,7},{24,8},{25... | collective-permute-start | bytes 393224 | tf_op jit(solution)/shard_map/while/body/eval_jaxpr/ppermute | solution.py:17
  248.9 31.4 %collective-permute-start.3 = (bf16[1,32,2048]{2,1,0:T(8,128)(2,1)S(1)}, bf16[1,32,2048]{2,1,0:T(8,128)(2,1)S(1)}, u32[]{:S(2)}, u32[]{:S(2)}) collective-permute-start(bf16[1,32,2048]{2,1,0:T(8,128)(2,1)S(1)} %get-tuple-element.1161), channel_id=1, source_target_pairs={{16,0},{17,1},{18,2},{19,3},{20,4},{21,5},{22,6},{23,7},{24,8},{25... | collective-permute-start | bytes 393224 | tf_op jit(solution)/shard_map/while/body/eval_jaxpr/ppermute | solution.py:17
  280.4 5.4 %copy-start.2 = (bf16[1024,2048]{1,0:T(8,128)(2,1)S(1)}, bf16[1024,2048]{1,0:T(8,128)(2,1)}, u32[]{:S(2)}) copy-start(bf16[1024,2048]{1,0:T(8,128)(2,1)} %get-tuple-element.750) | copy-start | bytes 12582916 | tf_op jit(solution)/shard_map/while/body/eval_jaxpr/cond
  284.7 3.1 copy-start.3
  284.8 3.6 copy-start.1
  290.2 32.7 %collective-permute-start.2 = (bf16[1,32,2048]{2,1,0:T(8,128)(2,1)S(1)}, bf16[1,32,2048]{2,1,0:T(8,128)(2,1)S(1)}, u32[]{:S(2)}, u32[]{:S(2)}) collective-permute-start(bf16[1,32,2048]{2,1,0:T(8,128)(2,1)S(1)} %get-tuple-element.1160), channel_id=1, source_target_pairs={{16,0},{17,1},{18,2},{19,3},{20,4},{21,5},{22,6},{23,7},{24,8},{25... | collective-permute-start | bytes 393224 | tf_op jit(solution)/shard_map/while/body/eval_jaxpr/ppermute | solution.py:17
  291.5 31.4 %collective-permute-start.3 = (bf16[1,32,2048]{2,1,0:T(8,128)(2,1)S(1)}, bf16[1,32,2048]{2,1,0:T(8,128)(2,1)S(1)}, u32[]{:S(2)}, u32[]{:S(2)}) collective-permute-start(bf16[1,32,2048]{2,1,0:T(8,128)(2,1)S(1)} %get-tuple-element.1161), channel_id=1, source_target_pairs={{16,0},{17,1},{18,2},{19,3},{20,4},{21,5},{22,6},{23,7},{24,8},{25... | collective-permute-start | bytes 393224 | tf_op jit(solution)/shard_map/while/body/eval_jaxpr/ppermute | solution.py:17
  323.0 5.4 %copy-start.2 = (bf16[1024,2048]{1,0:T(8,128)(2,1)S(1)}, bf16[1024,2048]{1,0:T(8,128)(2,1)}, u32[]{:S(2)}) copy-start(bf16[1024,2048]{1,0:T(8,128)(2,1)} %get-tuple-element.750) | copy-start | bytes 12582916 | tf_op jit(solution)/shard_map/while/body/eval_jaxpr/cond
  327.4 3.1 copy-start.3
  327.4 3.6 copy-start.1
  332.8 32.7 %collective-permute-start.2 = (bf16[1,32,2048]{2,1,0:T(8,128)(2,1)S(1)}, bf16[1,32,2048]{2,1,0:T(8,128)(2,1)S(1)}, u32[]{:S(2)}, u32[]{:S(2)}) collective-permute-start(bf16[1,32,2048]{2,1,0:T(8,128)(2,1)S(1)} %get-tuple-element.1160), channel_id=1, source_target_pairs={{16,0},{17,1},{18,2},{19,3},{20,4},{21,5},{22,6},{23,7},{24,8},{25... | collective-permute-start | bytes 393224 | tf_op jit(solution)/shard_map/while/body/eval_jaxpr/ppermute | solution.py:17
  334.1 31.4 %collective-permute-start.3 = (bf16[1,32,2048]{2,1,0:T(8,128)(2,1)S(1)}, bf16[1,32,2048]{2,1,0:T(8,128)(2,1)S(1)}, u32[]{:S(2)}, u32[]{:S(2)}) collective-permute-start(bf16[1,32,2048]{2,1,0:T(8,128)(2,1)S(1)} %get-tuple-element.1161), channel_id=1, source_target_pairs={{16,0},{17,1},{18,2},{19,3},{20,4},{21,5},{22,6},{23,7},{24,8},{25... | collective-permute-start | bytes 393224 | tf_op jit(solution)/shard_map/while/body/eval_jaxpr/ppermute | solution.py:17
  365.6 5.4 %copy-start.2 = (bf16[1024,2048]{1,0:T(8,128)(2,1)S(1)}, bf16[1024,2048]{1,0:T(8,128)(2,1)}, u32[]{:S(2)}) copy-start(bf16[1024,2048]{1,0:T(8,128)(2,1)} %get-tuple-element.750) | copy-start | bytes 12582916 | tf_op jit(solution)/shard_map/while/body/eval_jaxpr/cond
  370.0 3.1 copy-start.3
  370.0 3.6 copy-start.1
  375.4 32.7 %collective-permute-start.2 = (bf16[1,32,2048]{2,1,0:T(8,128)(2,1)S(1)}, bf16[1,32,2048]{2,1,0:T(8,128)(2,1)S(1)}, u32[]{:S(2)}, u32[]{:S(2)}) collective-permute-start(bf16[1,32,2048]{2,1,0:T(8,128)(2,1)S(1)} %get-tuple-element.1160), channel_id=1, source_target_pairs={{16,0},{17,1},{18,2},{19,3},{20,4},{21,5},{22,6},{23,7},{24,8},{25... | collective-permute-start | bytes 393224 | tf_op jit(solution)/shard_map/while/body/eval_jaxpr/ppermute | solution.py:17
  376.7 31.4 %collective-permute-start.3 = (bf16[1,32,2048]{2,1,0:T(8,128)(2,1)S(1)}, bf16[1,32,2048]{2,1,0:T(8,128)(2,1)S(1)}, u32[]{:S(2)}, u32[]{:S(2)}) collective-permute-start(bf16[1,32,2048]{2,1,0:T(8,128)(2,1)S(1)} %get-tuple-element.1161), channel_id=1, source_target_pairs={{16,0},{17,1},{18,2},{19,3},{20,4},{21,5},{22,6},{23,7},{24,8},{25... | collective-permute-start | bytes 393224 | tf_op jit(solution)/shard_map/while/body/eval_jaxpr/ppermute | solution.py:17
  408.2 0.8 copy-start.5
  408.2 0.8 copy-start.6
Sparse Core Ops, SparseCore 0:
  10.2 53.2 all-gather.2
  65.6 49.0 all-gather.4
where the time goes:
time: 417 us; the launch traced here: 416 us
  blocking collectives  150 us (36%)
  waiting for transfers between devices  123 us (29%)
  matrix products  54.3 us (13%)
  starting transfers between devices  46.6 us (11%)
  other arithmetic  22.1 us (5%)
  between operations  14.2 us (3%)
    psum x5, blocking collectives, backward_tick(): gain_total = gain_total + lax.psum(gain_grad, 'fsdp')  150 us
    all_gather x1, waiting for transfers between devices, on_device(): lax.all_gather(output_weights, 'fsdp', axis=1, tiled=True)  53.6 us
    all_gather x1, waiting for transfers between devices, on_device(): lax.all_gather(query_weights, 'fsdp', axis=1, tiled=True)  51.2 us
    ppermute x20, starting transfers between devices, shifted(): return lax.ppermute(array, axis, pairs)  46.5 us
    dot_general x12, matrix products, attend_layer(): jnp.dot(normed_rows, query_weight, preferred_element_type=jnp.float32)  30.8 us
    dot_general x8, matrix products, attend_layer(): update = jnp.dot(mixed, output_weight, preferred_element_type=jnp.float32)  17.4 us
    ppermute x20, waiting for transfers between devices, shifted(): return lax.ppermute(array, axis, pairs)  17 us
  transfers between devices with their start and end apart: 22, of which 7 were waited for; matrix products, arithmetic and copies ran while one was open for 0% of the time, Pallas kernels for 0%

commit v1 on v0

v1 whole, which is shorter than its diff:
```python
import math

import jax
import jax.numpy as jnp
from jax import lax
from jax.sharding import PartitionSpec as P

HEADS = 8


EPSILON = 1e-05


def send_to(arrays, axis, source, target):
    return lax.ppermute(arrays, axis, [(source, target)])


def rms_scale(inputs, gain_vector):
    return (
        inputs
        * lax.rsqrt(jnp.mean(inputs * inputs, axis=-1, keepdims=True) + EPSILON)
        * gain_vector
    )


def attend_layer(section_input, source, key_mask, query_weight, output_weight, gain_vector):
    series_count, seq_length, model_width = section_input.shape
    half_width = model_width // 2
    head_dim = half_width // HEADS
    head_shape = (series_count, seq_length, HEADS, head_dim)
    input_wide = section_input.astype(jnp.float32)
    normed = rms_scale(input_wide, gain_vector)
    normed_source = rms_scale(source.astype(jnp.float32), gain_vector)
    normed_rows = normed.astype(jnp.bfloat16).reshape(series_count * seq_length, model_width)
    query_flat = jnp.dot(normed_rows, query_weight, preferred_element_type=jnp.float32)
    queries = query_flat.astype(jnp.bfloat16).reshape(head_shape)
    key_rows = normed_source[..., :half_width].astype(jnp.bfloat16).reshape(head_shape)
    value_rows = normed_source[..., half_width:].astype(jnp.bfloat16).reshape(head_shape)
    scores = jnp.einsum(
        "bqhd,bkhd->bhqk", queries, key_rows, preferred_element_type=jnp.float32
    ) / math.sqrt(head_dim)
    raised = jnp.exp(scores) * key_mask.astype(jnp.float32)[:, None, None, :]
    probs = (raised / jnp.sum(raised, axis=-1, keepdims=True)).astype(jnp.bfloat16)
    mixed = jnp.einsum("bhqk,bkhd->bqhd", probs, value_rows, preferred_element_type=jnp.float32)
    mixed = mixed.astype(jnp.bfloat16).reshape(series_count * seq_length, half_width)
    update = jnp.dot(mixed, output_weight, preferred_element_type=jnp.float32)
    return (input_wide + update.reshape(series_count, seq_length, model_width)).astype(jnp.bfloat16)


def on_device(history, keymask, codes, plan_table, query_weights, output_weights, gains, cotangent):
    section_index = lax.axis_index("section")
    section_count = lax.axis_size("section")
    half_sections = section_count // 2
    micro_count, series_count, seq_length, model_width = history.shape
    rows = micro_count * series_count
    act_shape = (rows, seq_length, model_width)
    query_weight = lax.all_gather(query_weights, "fsdp", axis=1, tiled=True)[0]
    output_weight = lax.all_gather(output_weights, "fsdp", axis=1, tiled=True)[0]
    gain_vector = gains[0]
    code_rows = codes.reshape(micro_count, series_count, seq_length)
    code_count = plan_table.shape[0]
    one_hot = (code_rows[..., None] == jnp.arange(code_count, dtype=jnp.int32)).astype(jnp.bfloat16)
    plan_tokens = jnp.einsum(
        "msln,nd->msld", one_hot, plan_table, preferred_element_type=jnp.float32
    ).astype(jnp.bfloat16).reshape(act_shape)
    key_mask = keymask.reshape(rows, seq_length)
    history_rows = history.reshape(act_shape)

    def encoder_map(layer_input, layer_gain):
        return attend_layer(
            layer_input, layer_input, key_mask, query_weight, output_weight, layer_gain
        )

    def decoder_map(layer_input, layer_memory, layer_gain):
        return attend_layer(
            layer_input, layer_memory, key_mask, query_weight, output_weight, layer_gain
        )

    saved_inputs = {}
    got_input = None
    got_memory = None
    for tick in range(section_count - 1):
        if tick == 0:
            layer_input = history_rows
        elif tick == half_sections:
            layer_input = plan_tokens
        else:
            layer_input = got_input
        if tick < half_sections:
            output = encoder_map(layer_input, gain_vector)
            saved_inputs[tick] = (layer_input, None)
            if tick == half_sections - 1:
                got_memory = send_to(output, "section", tick, tick + 1)
            else:
                got_input = send_to(output, "section", tick, tick + 1)
        else:
            output = decoder_map(layer_input, got_memory, gain_vector)
            saved_inputs[tick] = (layer_input, got_memory)
            got_input, got_memory = send_to((output, got_memory), "section", tick, tick + 1)
    last = section_count - 1
    if last == half_sections:
        saved_inputs[last] = (plan_tokens, got_memory)
    else:
        saved_inputs[last] = (got_input, got_memory)

    zero_gain = jnp.zeros_like(gain_vector)
    grads_out = jnp.zeros(act_shape, jnp.bfloat16)
    gain_total = zero_gain
    got_grad = None
    got_memory_grad = None
    for tick in range(section_count):
        run = section_count - 1 - tick
        out_grad = cotangent.reshape(act_shape) if run == section_count - 1 else got_grad
        layer_input, layer_memory = saved_inputs[run]
        mine = section_index == run
        if run >= half_sections:
            _, pull = jax.vjp(decoder_map, layer_input, layer_memory, gain_vector)
            input_grad, memory_grad, gain_grad = pull(out_grad)
            if got_memory_grad is not None:
                memory_grad = got_memory_grad + memory_grad
            if run == half_sections:
                got_grad = send_to(memory_grad, "section", run, run - 1)
            else:
                got_grad, got_memory_grad = send_to(
                    (input_grad, memory_grad), "section", run, run - 1
                )
        else:
            _, pull = jax.vjp(encoder_map, layer_input, gain_vector)
            input_grad, gain_grad = pull(out_grad)
            if run > 0:
                got_grad = send_to(input_grad, "section", run, run - 1)
        grads_out = jnp.where(mine, input_grad, grads_out)
        gain_total = gain_total + jnp.where(mine, gain_grad, zero_gain)
    gain_total = lax.psum(gain_total, "fsdp")
    grads_out = grads_out.reshape(history.shape)
    return (grads_out[None], gain_total[None])


def solution(mesh):
    return jax.shard_map(
        on_device,
        mesh=mesh,
        in_specs=(
            P(None, "fsdp", None, None),
            P(None, "fsdp", None),
            P(None, "fsdp", None, None),
            P(),
            P("section", "fsdp", None),
            P("section", "fsdp", None),
            P("section", None),
            P(None, "fsdp", None, None),
        ),
        out_specs=(P("section", None, "fsdp", None, None), P("section", None)),
        check_vma=False,
    )
```

time: 417 us -> 198 us (0.47)
  blocking collectives: 150 us -> 30.6 us
  starting transfers between devices: 46.6 us -> 4.95 us
  matrix products: 54.3 us -> 17.3 us
  other arithmetic: 22.1 us -> 9.04 us
    psum x5 -> x1, blocking collectives: 150 us -> 30.6 us  [on_device(): gain_total = lax.psum(gain_total, 'fsdp')]
    ppermute x20 -> x2, starting transfers between devices: 46.5 us -> 4.88 us  [send_to(): return lax.ppermute(arrays, axis, [(source, target)])]
    dot_general x12 -> x4, matrix products: 30.8 us -> 6.66 us  [attend_layer(): jnp.dot(normed_rows, query_weight, preferred_element_type=jnp.float32)]
    dot_general x8 -> x3, matrix products: 17.4 us -> 6.16 us  [attend_layer(): update = jnp.dot(mixed, output_weight, preferred_element_type=jnp.float32)]
    all_gather x2, waiting for transfers between devices: 105 us -> 97 us  [the longest x1 50.1 us: on_device(): query_weight = lax.all_gather(query_weights, 'fsdp', axis=1, tiled=True)[0]]
    another operation x8 -> x2, other arithmetic: 6.99 us -> 1.53 us
    dynamic_update_slice x15 -> x0, other arithmetic: 5.35 us -> none  [place_slot(): lax.dynamic_update_index_in_dim(stack, jnp.where(keep, update, previous),...]
    convert_element_type x8 -> x1, other arithmetic: 5.91 us -> 0.69 us  [attend_layer(): raised = jnp.exp(scores) * key_mask.astype(jnp.float32)[:, None, None, :]]
  transfers between devices with their start and end apart: 22 -> 4, of which waited for: 7 -> 4; matrix products, arithmetic and copies ran while one was open for 0% -> 6% of each run, Pallas kernels for 0% -> 0%
where the time goes in v1:
time: 198 us
  waiting for transfers between devices  120 us (61%)
  blocking collectives  30.6 us (15%)
  matrix products  17.3 us (9%)
  between operations  14.4 us (7%)
  other arithmetic  9.04 us (5%)
  starting transfers between devices  4.95 us (2%)
    all_gather x1, waiting for transfers between devices, on_device(): query_weight = lax.all_gather(query_weights, 'fsdp', axis=1, tiled=True)[0]  50.1 us
    all_gather x1, waiting for transfers between devices, on_device(): lax.all_gather(output_weights, 'fsdp', axis=1, tiled=True)[0]  46.9 us
    psum x1, blocking collectives, on_device(): gain_total = lax.psum(gain_total, 'fsdp')  30.6 us
    ppermute x2, waiting for transfers between devices, send_to(): return lax.ppermute(arrays, axis, [(source, target)])  21.7 us
    dot_general x4, matrix products, attend_layer(): jnp.dot(normed_rows, query_weight, preferred_element_type=jnp.float32)  6.66 us
    dot_general x3, matrix products, attend_layer(): update = jnp.dot(mixed, output_weight, preferred_element_type=jnp.float32)  6.16 us
    ppermute x2, starting transfers between devices, send_to(): return lax.ppermute(arrays, axis, [(source, target)])  4.88 us
  transfers between devices with their start and end apart: 4, of which 4 were waited for; matrix products, arithmetic and copies ran while one was open for 6% of the time, Pallas kernels for 0%

profile of v1, /device:TPU:0, one launch (start us, length us, event | category | flops | bytes accessed | tf_op | source)
XLA Modules:
  0.0 198.0 jit_solution(13190037115055075257)
XLA Ops:
  7.2 0.0 copy-start
  7.2 0.0 all-gather.5.cloned.1.call-start
  7.2 0.7 all-gather.5.cloned.1.call-update
  7.9 0.0 all-gather.3.cloned.1.call-start
  8.0 0.7 all-gather.3.cloned.1.call-update
  8.7 0.7 convert_element_type.213
  9.4 0.8 copy.36
  10.2 0.1 copy.37
  10.2 1.2 fusion.82
  11.5 0.4 multiply_reduce_fusion
  11.9 1.2 fusion.80
  13.2 0.2 fusion.86
  13.4 50.1 %all-gather.5.cloned.1.call-done = bf16[1,2048,1024]{2,1,0:T(8,128)(2,1)} async-done(((bf16[1,128,1024]{2,1,0:T(8,128)(2,1)}), bf16[1,2048,1024]{2,1,0:T(8,128)(2,1)}) %all-gather.5.cloned.1.call-update) | async-done | bytes 4194320 | tf_op jit(solution)/shard_map/all_gather | solution.py:57
  63.5 2.9 %fusion.56 = bf16[16,8,8,128]{3,1,2,0:T(8,128)(2,1)S(1)} fusion(bf16[128,2048]{1,0:T(8,128)(2,1)S(1)} %bitcast.248, bf16[1,2048,1024]{2,1,0:T(8,128)(2,1)} %all-gather.5.cloned.1.call-done), kind=kOutput, calls=%fused_computation.66 | convolution fusion | flops 537001984 | bytes 4980736 | tf_op jit(solution)/shard_map/dot_general | solution.py:35
  66.5 0.3 multiply_reduce_fusion.4
  66.8 1.1 fusion.68
  67.8 46.9 %all-gather.3.cloned.1.call-done = bf16[1,1024,2048]{2,1,0:T(8,128)(2,1)} async-done(((bf16[1,64,2048]{2,1,0:T(8,128)(2,1)}), bf16[1,1024,2048]{2,1,0:T(8,128)(2,1)}) %all-gather.3.cloned.1.call-update) | async-done | bytes 4194320 | tf_op jit(solution)/shard_map/all_gather | solution.py:58
  114.7 3.1 %fusion.17 = bf16[4,32,2048]{2,1,0:T(8,128)(2,1)S(1)} fusion(bf16[1,1024,2048]{2,1,0:T(8,128)(2,1)} %all-gather.3.cloned.1.call-done, bf16[4,1,32,2048]{3,2,1,0:T(8,128)(2,1)S(1)} %copy-done.3, bf16[4,8,4,8,128]{4,3,2,1,0:T(8,128)(2,1)} %fusion.68), kind=kOutput, calls=%fused_computation.15 | convolution fusion | flops 537657344 | bytes 5505024 | tf_op jit(solution)/shard_map/dot_general | solution.py:46
  117.9 3.4 %collective-permute-start = (bf16[4,32,2048]{2,1,0:T(8,128)(2,1)S(1)}, bf16[4,32,2048]{2,1,0:T(8,128)(2,1)S(1)}, u32[]{:S(2)}, u32[]{:S(2)}) collective-permute-start(bf16[4,32,2048]{2,1,0:T(8,128)(2,1)S(1)} %fusion.17), channel_id=1, source_target_pairs={{0,16},{1,17},{2,18},{3,19},{4,20},{5,21},{6,22},{7,23},{8,24},{9,... | collective-permute-start | bytes 1572872 | tf_op jit(solution)/shard_map/ppermute | solution.py:15
  121.3 1.5 fusion.65
  122.9 9.9 %collective-permute-done = bf16[4,32,2048]{2,1,0:T(8,128)(2,1)S(1)} collective-permute-done((bf16[4,32,2048]{2,1,0:T(8,128)(2,1)S(1)}, bf16[4,32,2048]{2,1,0:T(8,128)(2,1)S(1)}, u32[]{:S(2)}, u32[]{:S(2)}) %collective-permute-start) | collective-permute-done | bytes 524320 | tf_op jit(solution)/shard_map/ppermute | solution.py:15
  132.8 0.2 fusion.93
  133.0 0.3 fusion.75
  133.4 0.7 fusion.59
  134.2 0.3 multiply_reduce_fusion.3
  134.5 0.3 fusion.73
  134.8 0.3 multiply_reduce_fusion.2
  135.1 0.3 fusion.69
  135.4 0.1 copy_bitcast_fusion.2
  135.4 0.6 fusion.76
  136.0 0.3 fusion.89
  136.3 1.5 collective-permute-start.1
  137.8 0.4 fusion.72
  138.1 0.1 copy.61
  138.3 1.5 fusion.23
  139.8 11.8 %collective-permute-done.1 = bf16[4,32,2048]{2,1,0:T(8,128)(2,1)S(1)} collective-permute-done((bf16[4,32,2048]{2,1,0:T(8,128)(2,1)S(1)}, bf16[4,32,2048]{2,1,0:T(8,128)(2,1)S(1)}, u32[]{:S(2)}, u32[]{:S(2)}) %collective-permute-start.1) | collective-permute-done | bytes 524320 | tf_op jit(solution)/shard_map/ppermute | solution.py:15
  151.6 1.5 fusion.62
  153.2 0.3 fusion.74
  153.5 0.3 multiply_reduce_fusion.1
  153.8 0.4 fusion.71
  154.1 0.3 fusion.70
  154.4 0.1 copy.57
  154.5 0.1 copy.166
  154.6 0.1 copy.165
  154.7 1.5 fusion.20
  156.2 1.3 fusion.81
  157.4 30.6 %psum.7 = f32[1,2048]{1,0:T(1,128)} all-reduce(f32[1,2048]{1,0:T(1,128)S(1)} %bitcast.267), channel_id=1, replica_groups=mesh['section'=2,'fsdp'=16] {'fsdp'}, use_global_device_ids=true, to_apply=%region_15.0 | all-reduce | flops 2048 | bytes 16384 | tf_op jit(solution)/shard_map/psum | solution.py:134
  188.1 3.0 %fusion.99 = bf16[1,4,1,32,2048]{4,3,2,1,0:T(8,128)(2,1)} fusion(f32[4,32,2048]{2,1,0:T(8,128)S(1)} %get-tuple-element.27, bf16[4,32,2048]{2,1,0:T(8,128)(2,1)} %copy-done.5, bf16[4,32,1024]{2,1,0:T(8,128)(2,1)S(1)} %bitcast.244, bf16[4,32,1024]{2,1,0:T(8,128)(2,1)S(1)} %bitcast.242, bf16[4,1,32,2048]{3,2,1,0:T(8,128)(2,1)} %param.15, ...), kind=kLoop, calls=%fused_computation.105 | loop fusion | flops 8912896 | bytes 4729346
  (30 shorter events, 0.4 us)
Async XLA Ops:
  7.2 4.3 %copy-start = (bf16[16,2048]{1,0:T(8,128)(2,1)S(1)}, bf16[16,2048]{1,0:T(8,128)(2,1)}, u32[]{:S(2)}) copy-start(bf16[16,2048]{1,0:T(8,128)(2,1)} %param.11) | copy-start | bytes 196612
  7.2 6.0 %copy-start.3 = (bf16[4,1,32,2048]{3,2,1,0:T(8,128)(2,1)S(1)}, bf16[4,1,32,2048]{3,2,1,0:T(8,128)(2,1)}, u32[]{:S(2)}) copy-start(bf16[4,1,32,2048]{3,2,1,0:T(8,128)(2,1)} %param.8) | copy-start | bytes 1572868
  7.2 6.0 %copy-start.6 = (f32[1,2048]{1,0:T(1,128)S(1)}, f32[1,2048]{1,0:T(1,128)}, u32[]{:S(2)}) copy-start(f32[1,2048]{1,0:T(1,128)} %param.14) | copy-start | bytes 24580
  7.2 56.3 %all-gather.5.cloned.1.call-start = ((), (), s32[]{:S(2)}) async-start(), calls=%async_computation.1 | async-start | bytes 4456448 | tf_op jit(solution)/shard_map/all_gather | solution.py:57
  7.9 106.8 %all-gather.3.cloned.1.call-start = ((), (), s32[]{:S(2)}) async-start(), calls=%async_computation | async-start | bytes 4456448 | tf_op jit(solution)/shard_map/all_gather | solution.py:58
  66.5 54.8 %copy-start.4 = (bf16[4,1,32,2048]{3,2,1,0:T(8,128)(2,1)S(1)}, bf16[4,1,32,2048]{3,2,1,0:T(8,128)(2,1)}, u32[]{:S(2)}) copy-start(bf16[4,1,32,2048]{3,2,1,0:T(8,128)(2,1)} %param.15) | copy-start | bytes 1572868
  114.7 6.6 %copy-start.2 = (bf16[1,1024,2048]{2,1,0:T(8,128)(2,1)S(1)}, bf16[1,1024,2048]{2,1,0:T(8,128)(2,1)}, u32[]{:S(2)}) copy-start(bf16[1,1024,2048]{2,1,0:T(8,128)(2,1)} %all-gather.3.cloned.1.call-done) | copy-start | bytes 12582916
  117.9 15.0 %collective-permute-start = (bf16[4,32,2048]{2,1,0:T(8,128)(2,1)S(1)}, bf16[4,32,2048]{2,1,0:T(8,128)(2,1)S(1)}, u32[]{:S(2)}, u32[]{:S(2)}) collective-permute-start(bf16[4,32,2048]{2,1,0:T(8,128)(2,1)S(1)} %fusion.17), channel_id=1, source_target_pairs={{0,16},{1,17},{2,18},{3,19},{4,20},{5,21},{6,22},{7,23},{8,24},{9,... | collective-permute-start | bytes 1572872 | tf_op jit(solution)/shard_map/ppermute | solution.py:15
  121.3 12.1 %copy-start.1 = (bf16[1,2048,1024]{2,1,0:T(8,128)(2,1)S(1)}, bf16[1,2048,1024]{2,1,0:T(8,128)(2,1)}, u32[]{:S(2)}) copy-start(bf16[1,2048,1024]{2,1,0:T(8,128)(2,1)} %all-gather.5.cloned.1.call-done) | copy-start | bytes 12582916
  136.3 15.3 %collective-permute-start.1 = (bf16[4,32,2048]{2,1,0:T(8,128)(2,1)S(1)}, bf16[4,32,2048]{2,1,0:T(8,128)(2,1)S(1)}, u32[]{:S(2)}, u32[]{:S(2)}) collective-permute-start(bf16[4,32,2048]{2,1,0:T(8,128)(2,1)S(1)} %fusion.89), channel_id=1, source_target_pairs={{16,0},{17,1},{18,2},{19,3},{20,4},{21,5},{22,6},{23,7},{24,8},{25... | collective-permute-start | bytes 1572872 | tf_op jit(solution)/shard_map/ppermute | solution.py:15
  151.6 2.2 %copy-start.5 = (bf16[4,32,2048]{2,1,0:T(8,128)(2,1)}, bf16[4,32,2048]{2,1,0:T(8,128)(2,1)S(1)}, u32[]{:S(2)}) copy-start(bf16[4,32,2048]{2,1,0:T(8,128)(2,1)S(1)} %collective-permute-done.1) | copy-start | bytes 1572868
Sparse Core Ops, SparseCore 0:
  10.2 53.2 all-gather.4
  65.7 49.0 all-gather.2

commit v2 on v1

--- a/solution.py
+++ b/solution.py
@@ -13,6 +13,41 @@
 
 def send_to(arrays, axis, source, target):
     return lax.ppermute(arrays, axis, [(source, target)])
+
+
+def butterfly_gather(shard, axis, size):
+    if size & (size - 1):
+        return lax.all_gather(shard, axis, axis=1, tiled=True)[0]
+    index = lax.axis_index(axis)
+    held = shard
+    step = size // 2
+    while step >= 1:
+        other = lax.ppermute(held, axis, [(j, j ^ step) for j in range(size)])
+        held = jnp.concatenate([held, other], axis=0)
+        step //= 2
+    bits = size.bit_length() - 1
+
+    def reversed_bits(value):
+        total = 0
+        for bit in range(bits):
+            total = total + ((value >> bit) & 1) * (1 << (bits - 1 - bit))
+        return total
+
+    flipped = reversed_bits(index)
+    blocks = [
+        lax.dynamic_index_in_dim(held, flipped ^ reversed_bits(j), 0, False) for j in range(size)
+    ]
+    return jnp.concatenate(blocks, axis=0)
+
+
+def butterfly_sum(value, axis, size):
+    if size & (size - 1):
+        return lax.psum(value, axis)
+    step = 1
+    while step < size:
+        value = value + lax.ppermute(value, axis, [(j, j ^ step) for j in range(size)])
+        step *= 2
+    return value
 
 
 def rms_scale(inputs, gain_vector):
@@ -55,7 +90,8 @@
     rows = micro_count * series_count
     act_shape = (rows, seq_length, model_width)
     query_weight = lax.all_gather(query_weights, "fsdp", axis=1, tiled=True)[0]
-    output_weight = lax.all_gather(output_weights, "fsdp", axis=1, tiled=True)[0]
+    fsdp_count = lax.axis_size("fsdp")
+    output_weight = butterfly_gather(output_weights, "fsdp", fsdp_count)
     gain_vector = gains[0]
     code_rows = codes.reshape(micro_count, series_count, seq_length)
     code_count = plan_table.shape[0]
@@ -131,7 +167,7 @@
                 got_grad = send_to(input_grad, "section", run, run - 1)
         grads_out = jnp.where(mine, input_grad, grads_out)
         gain_total = gain_total + jnp.where(mine, gain_grad, zero_gain)
-    gain_total = lax.psum(gain_total, "fsdp")
+    gain_total = butterfly_sum(gain_total, "fsdp", fsdp_count)
     grads_out = grads_out.reshape(history.shape)
     return (grads_out[None], gain_total[None])
 

time: 198 us -> 167 us (0.84)
  waiting for transfers between devices: 120 us -> 78.9 us
  blocking collectives: 30.6 us -> 0 us
  starting transfers between devices: 4.95 us -> 22.5 us
  local copies, waits for them, and re-layouts: 1.52 us -> 16 us
  matrix products: 17.3 us -> 22.2 us
  other arithmetic: 9.04 us -> 12.6 us
    ppermute x0 -> x8, waiting for transfers between devices: none -> 60.6 us  [the longest x4 56.2 us: butterfly_gather(): other = lax.ppermute(held, axis, [(j, j ^ step) for j in range(size)])]
    all_gather x1, waiting for transfers between devices: 50.1 us -> 0.01 us  [on_device(): query_weight = lax.all_gather(query_weights, 'fsdp', axis=1, tiled=True)[0]]
    all_gather x1 -> x0, waiting for transfers between devices: 46.9 us -> none  [on_device(): lax.all_gather(output_weights, 'fsdp', axis=1, tiled=True)[0]]
    psum x1 -> x0, blocking collectives: 30.6 us -> none  [on_device(): gain_total = lax.psum(gain_total, 'fsdp')]
    ppermute x0 -> x8, starting transfers between devices: none -> 17.8 us  [the longest x4 11.4 us: butterfly_sum(): lax.ppermute(value, axis, [(j, j ^ step) for j in range(size)])]
    unnamed x21 -> x54, local copies, waits for them, and re-layouts: 1.06 us -> 13.4 us
    dot_general x3, matrix products: 6.16 us -> 11.7 us  [attend_layer(): update = jnp.dot(mixed, output_weight, preferred_element_type=jnp.float32)]
    concatenate x0 -> x3, other arithmetic: none -> 4.28 us  [butterfly_gather(): held = jnp.concatenate([held, other], axis=0)]
  transfers between devices with their start and end apart: 4 -> 11, of which waited for: 4 -> 9; matrix products, arithmetic and copies ran while one was open for 6% -> 18% of each run, Pallas kernels for 0% -> 0%
where the time goes in v2:
time: 167 us
  waiting for transfers between devices  78.9 us (47%)
  starting transfers between devices  22.5 us (13%)
  matrix products  22.2 us (13%)
  local copies, waits for them, and re-layouts  16 us (10%)
  between operations  14.6 us (9%)
  other arithmetic  12.6 us (8%)
    ppermute x4, waiting for transfers between devices, butterfly_gather(): other = lax.ppermute(held, axis, [(j, j ^ step) for j in range(size)])  56.2 us
    ppermute x2, waiting for transfers between devices, send_to(): return lax.ppermute(arrays, axis, [(source, target)])  18.2 us
    unnamed x54, local copies, waits for them, and re-layouts  13.4 us
    dot_general x3, matrix products, attend_layer(): update = jnp.dot(mixed, output_weight, preferred_element_type=jnp.float32)  11.7 us
    ppermute x4, starting transfers between devices, butterfly_sum(): lax.ppermute(value, axis, [(j, j ^ step) for j in range(size)])  11.4 us
    dot_general x4, matrix products, attend_layer(): jnp.dot(normed_rows, query_weight, preferred_element_type=jnp.float32)  6.71 us
    ppermute x4, starting transfers between devices, butterfly_gather(): other = lax.ppermute(held, axis, [(j, j ^ step) for j in range(size)])  6.39 us
    ppermute x2, starting transfers between devices, send_to(): return lax.ppermute(arrays, axis, [(source, target)])  4.67 us
  transfers between devices with their start and end apart: 11, of which 9 were waited for; matrix products, arithmetic and copies ran while one was open for 18% of the time, Pallas kernels for 0%

profile of v2, /device:TPU:0, one launch (start us, length us, event | category | flops | bytes accessed | tf_op | source)
XLA Modules:
  0.0 166.7 jit_solution(793568422961075351)
XLA Ops:
  7.2 4.1 %collective-permute-start = (bf16[1,64,2048]{2,1,0:T(8,128)(2,1)}, bf16[1,64,2048]{2,1,0:T(8,128)(2,1)S(1)}, u32[]{:S(2)}, u32[]{:S(2)}) collective-permute-start(bf16[1,64,2048]{2,1,0:T(8,128)(2,1)} %param.13), channel_id=1, source_target_pairs={{0,8},{1,9},{2,10},{3,11},{4,12},{5,13},{6,14},{7,15},{8,0},{9,1},... | collective-permute-start | bytes 786440 | tf_op jit(solution)/shard_map/ppermute | solution.py:25
  11.3 12.1 %collective-permute-done = bf16[1,64,2048]{2,1,0:T(8,128)(2,1)S(1)} collective-permute-done((bf16[1,64,2048]{2,1,0:T(8,128)(2,1)}, bf16[1,64,2048]{2,1,0:T(8,128)(2,1)S(1)}, u32[]{:S(2)}, u32[]{:S(2)}) %collective-permute-start) | collective-permute-done | bytes 262176 | tf_op jit(solution)/shard_map/ppermute | solution.py:25
  23.5 1.1 pad_maximum_fusion.2
  24.6 0.9 collective-permute-start.1
  25.5 13.8 %collective-permute-done.1 = bf16[2,64,2048]{2,1,0:T(8,128)(2,1)S(1)} collective-permute-done((bf16[2,64,2048]{2,1,0:T(8,128)(2,1)S(1)}, bf16[2,64,2048]{2,1,0:T(8,128)(2,1)S(1)}, u32[]{:S(2)}, u32[]{:S(2)}) %collective-permute-start.1) | collective-permute-done | bytes 524320 | tf_op jit(solution)/shard_map/ppermute | solution.py:25
  39.3 2.0 %pad_maximum_fusion.1 = bf16[4,64,2048]{2,1,0:T(8,128)(2,1)} fusion(bf16[2,64,2048]{2,1,0:T(8,128)(2,1)S(1)} %collective-permute-done.1, bf16[1,64,2048]{2,1,0:T(8,128)(2,1)S(1)} %collective-permute-done, bf16[1,64,2048]{2,1,0:T(8,128)(2,1)} %param.13), kind=kLoop, calls=%fused_computation.94 | loop fusion | flops 1048576 | bytes 2097152 | tf_op jit(solution)/shard_map/concatenate | solution.py:26
  41.3 1.3 collective-permute-start.2
  43.3 0.8 copy.36
  44.2 1.2 fusion.68
  45.9 28.4 %collective-permute-done.2 = bf16[4,64,2048]{2,1,0:T(8,128)(2,1)S(1)} collective-permute-done((bf16[4,64,2048]{2,1,0:T(8,128)(2,1)}, bf16[4,64,2048]{2,1,0:T(8,128)(2,1)S(1)}, u32[]{:S(2)}, u32[]{:S(2)}) %collective-permute-start.2) | collective-permute-done | bytes 1048608 | tf_op jit(solution)/shard_map/ppermute | solution.py:25
  74.3 1.2 pad_maximum_fusion
  75.8 0.9 slice_bitcast_fusion.3
  76.7 1.0 fusion.72
  77.8 1.9 %collective-permute-done.3 = bf16[8,64,2048]{2,1,0:T(8,128)(2,1)S(1)} collective-permute-done((bf16[8,64,2048]{2,1,0:T(8,128)(2,1)S(1)}, bf16[8,64,2048]{2,1,0:T(8,128)(2,1)S(1)}, u32[]{:S(2)}, u32[]{:S(2)}) %collective-permute-start.3) | collective-permute-done | bytes 2097184 | tf_op jit(solution)/shard_map/ppermute | solution.py:25
  80.7 0.7 bitcast_dynamic-update-slice_fusion.14
  81.4 0.7 bitcast_dynamic-update-slice_fusion.13
  82.1 0.7 bitcast_dynamic-update-slice_fusion.12
  82.9 0.7 bitcast_dynamic-update-slice_fusion.11
  83.6 0.7 bitcast_dynamic-update-slice_fusion.10
  84.3 0.7 bitcast_dynamic-update-slice_fusion.9
  85.1 0.7 bitcast_dynamic-update-slice_fusion.8
  85.8 0.7 bitcast_dynamic-update-slice_fusion.7
  86.5 0.7 bitcast_dynamic-update-slice_fusion.6
  87.2 0.7 bitcast_dynamic-update-slice_fusion.5
  88.0 0.7 bitcast_dynamic-update-slice_fusion.4
  88.7 0.7 bitcast_dynamic-update-slice_fusion.3
  90.1 0.7 bitcast_dynamic-update-slice_fusion.1
  90.9 0.7 bitcast_dynamic-update-slice_fusion
  91.6 2.9 %fusion.48 = bf16[16,8,8,128]{3,1,2,0:T(8,128)(2,1)S(1)} fusion(bf16[128,2048]{1,0:T(8,128)(2,1)S(1)} %bitcast.266, bf16[1,2048,1024]{2,1,0:T(8,128)(2,1)} %all-gather.2.cloned.1.call-done), kind=kOutput, calls=%fused_computation.65 | convolution fusion | flops 537001984 | bytes 4980736 | tf_op jit(solution)/shard_map/dot_general | solution.py:70
  95.8 3.7 %fusion.13 = bf16[4,32,2048]{2,1,0:T(8,128)(2,1)} fusion(bf16[1024,2048]{1,0:T(8,128)(2,1)} %bitcast_dynamic-update-slice_fusion, bf16[4,1,32,2048]{3,2,1,0:T(8,128)(2,1)S(1)} %copy-done.2, bf16[4,8,4,8,128]{4,3,2,1,0:T(8,128)(2,1)S(1)} %fusion.54), kind=kOutput, calls=%fused_computation.11 | convolution fusion | flops 537657344 | bytes 5505024 | tf_op jit(solution)/shard_map/dot_general | solution.py:81
  99.5 3.2 %collective-permute-start.4 = (bf16[4,32,2048]{2,1,0:T(8,128)(2,1)}, bf16[4,32,2048]{2,1,0:T(8,128)(2,1)S(1)}, u32[]{:S(2)}, u32[]{:S(2)}) collective-permute-start(bf16[4,32,2048]{2,1,0:T(8,128)(2,1)} %fusion.13), channel_id=1, source_target_pairs={{0,16},{1,17},{2,18},{3,19},{4,20},{5,21},{6,22},{7,23},{8,24},{9,... | collective-permute-start | bytes 1572872 | tf_op jit(solution)/shard_map/ppermute | solution.py:15
  102.7 4.2 %fusion.46 = bf16[128,1024]{0,1:T(8,128)(2,1)} fusion(bf16[1024,2048]{1,0:T(8,128)(2,1)} %bitcast_dynamic-update-slice_fusion, bf16[128,2048]{1,0:T(8,128)(2,1)S(1)} %bitcast.273), kind=kOutput, calls=%fused_computation.63 | convolution fusion | flops 537001984 | bytes 4980736 | tf_op jit(solution)/shard_map/transpose(jvp())/dot_general | solution.py:81
  106.9 1.1 copy.35
  108.1 6.5 %collective-permute-done.4 = bf16[4,32,2048]{2,1,0:T(8,128)(2,1)S(1)} collective-permute-done((bf16[4,32,2048]{2,1,0:T(8,128)(2,1)}, bf16[4,32,2048]{2,1,0:T(8,128)(2,1)S(1)}, u32[]{:S(2)}, u32[]{:S(2)}) %collective-permute-start.4) | collective-permute-done | bytes 524320 | tf_op jit(solution)/shard_map/ppermute | solution.py:15
  115.1 0.8 fusion.51
  118.1 1.5 collective-permute-start.5
  120.1 1.5 fusion.19
  121.6 11.7 %collective-permute-done.5 = bf16[4,32,2048]{2,1,0:T(8,128)(2,1)S(1)} collective-permute-done((bf16[4,32,2048]{2,1,0:T(8,128)(2,1)S(1)}, bf16[4,32,2048]{2,1,0:T(8,128)(2,1)S(1)}, u32[]{:S(2)}, u32[]{:S(2)}) %collective-permute-start.5) | collective-permute-done | bytes 524320 | tf_op jit(solution)/shard_map/ppermute | solution.py:15
  133.3 3.8 %fusion.47 = bf16[16,8,8,128]{3,1,2,0:T(8,128)(2,1)S(1)} fusion(bf16[128,2048]{1,0:T(8,128)(2,1)S(1)} %bitcast.264, bf16[1024,2048]{1,0:T(8,128)(2,1)} %bitcast_dynamic-update-slice_fusion), kind=kOutput, calls=%fused_computation.64 | convolution fusion | flops 537001984 | bytes 4980736 | tf_op jit(solution)/shard_map/transpose(jvp())/dot_general | solution.py:81
  138.6 1.5 fusion.16
  140.2 1.3 fusion.67
  141.6 1.2 collective-permute-done.6
  142.8 2.0 %collective-permute-start.7 = (f32[2048]{0:T(1024)S(1)}, f32[2048]{0:T(1024)S(1)}, u32[]{:S(2)}, u32[]{:S(2)}) collective-permute-start(f32[2048]{0:T(1024)S(1)} %add.143), channel_id=1, source_target_pairs={{0,2},{1,3},{2,0},{3,1},{4,6},{5,7},{6,4},{7,5},{8,10},{9,11},{10,... | collective-permute-start | bytes 24584 | tf_op jit(solution)/shard_map/ppermute | solution.py:48
  144.8 1.6 collective-permute-done.7
  146.4 2.9 %collective-permute-start.8 = (f32[2048]{0:T(1024)S(1)}, f32[2048]{0:T(1024)S(1)}, u32[]{:S(2)}, u32[]{:S(2)}) collective-permute-start(f32[2048]{0:T(1024)S(1)} %add.144), channel_id=1, source_target_pairs={{0,4},{1,5},{2,6},{3,7},{4,0},{5,1},{6,2},{7,3},{8,12},{9,13},{10,... | collective-permute-start | bytes 24584 | tf_op jit(solution)/shard_map/ppermute | solution.py:48
  149.4 1.6 collective-permute-done.8
  151.0 6.4 %collective-permute-start.9 = (f32[2048]{0:T(1024)S(1)}, f32[2048]{0:T(1024)S(1)}, u32[]{:S(2)}, u32[]{:S(2)}) collective-permute-start(f32[2048]{0:T(1024)S(1)} %add.145), channel_id=1, source_target_pairs={{0,8},{1,9},{2,10},{3,11},{4,12},{5,13},{6,14},{7,15},{8,0},{9,1},... | collective-permute-start | bytes 24584 | tf_op jit(solution)/shard_map/ppermute | solution.py:48
  157.3 1.9 %fusion.85 = bf16[1,4,1,32,2048]{4,3,2,1,0:T(8,128)(2,1)} fusion(f32[4,32,2048]{2,1,0:T(8,128)S(1)} %get-tuple-element.27, bf16[4,32,2048]{2,1,0:T(8,128)(2,1)S(1)} %collective-permute-done.5, bf16[4,32,1024]{2,1,0:T(8,128)(2,1)S(1)} %bitcast.263, bf16[4,32,1024]{2,1,0:T(8,128)(2,1)S(1)} %bitcast.261, bf16[4,1,32,2048]{3,2,1,0:T(8,128)(2,1)S(1)} %copy-done.8, ...), kind=kLoop, calls=%fused_computation.103 | loop fusion | flops 8912896 | bytes 4729346
  (86 shorter events, 9.9 us)
Async XLA Ops:
  7.2 38.3 %copy-start = (bf16[16,2048]{1,0:T(8,128)(2,1)S(1)}, bf16[16,2048]{1,0:T(8,128)(2,1)}, u32[]{:S(2)}) copy-start(bf16[16,2048]{1,0:T(8,128)(2,1)} %param.11) | copy-start | bytes 196612
  7.2 38.3 %copy-start.3 = (bf16[1,64,2048]{2,1,0:T(8,128)(2,1)S(1)}, bf16[1,64,2048]{2,1,0:T(8,128)(2,1)}, u32[]{:S(2)}) copy-start(bf16[1,64,2048]{2,1,0:T(8,128)(2,1)} %param.13) | copy-start | bytes 786436
  7.2 84.4 %all-gather.2.cloned.1.call-start = ((), (), s32[]{:S(2)}) async-start(), calls=%async_computation | async-start | bytes 4456448 | tf_op jit(solution)/shard_map/all_gather | solution.py:92
  7.2 16.2 %collective-permute-start = (bf16[1,64,2048]{2,1,0:T(8,128)(2,1)}, bf16[1,64,2048]{2,1,0:T(8,128)(2,1)S(1)}, u32[]{:S(2)}, u32[]{:S(2)}) collective-permute-start(bf16[1,64,2048]{2,1,0:T(8,128)(2,1)} %param.13), channel_id=1, source_target_pairs={{0,8},{1,9},{2,10},{3,11},{4,12},{5,13},{6,14},{7,15},{8,0},{9,1},... | collective-permute-start | bytes 786440 | tf_op jit(solution)/shard_map/ppermute | solution.py:25
  23.5 22.0 %copy-start.4 = (bf16[1,64,2048]{2,1,0:T(8,128)(2,1)}, bf16[1,64,2048]{2,1,0:T(8,128)(2,1)S(1)}, u32[]{:S(2)}) copy-start(bf16[1,64,2048]{2,1,0:T(8,128)(2,1)S(1)} %collective-permute-done) | copy-start | bytes 786436
  24.6 14.7 %collective-permute-start.1 = (bf16[2,64,2048]{2,1,0:T(8,128)(2,1)S(1)}, bf16[2,64,2048]{2,1,0:T(8,128)(2,1)S(1)}, u32[]{:S(2)}, u32[]{:S(2)}) collective-permute-start(bf16[2,64,2048]{2,1,0:T(8,128)(2,1)S(1)} %pad_maximum_fusion.2), channel_id=1, source_target_pairs={{0,4},{1,5},{2,6},{3,7},{4,0},{5,1},{6,2},{7,3},{8,12},{9,13},{10,... | collective-permute-start | bytes 1572872 | tf_op jit(solution)/shard_map/ppermute | solution.py:25
  25.5 50.1 %copy-start.2 = (bf16[4,1,32,2048]{3,2,1,0:T(8,128)(2,1)S(1)}, bf16[4,1,32,2048]{3,2,1,0:T(8,128)(2,1)}, u32[]{:S(2)}) copy-start(bf16[4,1,32,2048]{3,2,1,0:T(8,128)(2,1)} %param.8) | copy-start | bytes 1572868
  25.5 50.1 %copy-start.11 = (f32[1,2048]{1,0:T(1,128)S(1)}, f32[1,2048]{1,0:T(1,128)}, u32[]{:S(2)}) copy-start(f32[1,2048]{1,0:T(1,128)} %param.14) | copy-start | bytes 24580
  41.3 33.0 %collective-permute-start.2 = (bf16[4,64,2048]{2,1,0:T(8,128)(2,1)}, bf16[4,64,2048]{2,1,0:T(8,128)(2,1)S(1)}, u32[]{:S(2)}, u32[]{:S(2)}) collective-permute-start(bf16[4,64,2048]{2,1,0:T(8,128)(2,1)} %pad_maximum_fusion.1), channel_id=1, source_target_pairs={{0,2},{1,3},{2,0},{3,1},{4,6},{5,7},{6,4},{7,5},{8,10},{9,11},{10,... | collective-permute-start | bytes 3145736 | tf_op jit(solution)/shard_map/ppermute | solution.py:25
  45.5 32.2 %copy-start.5 = (bf16[1,64,2048]{2,1,0:T(8,128)(2,1)S(1)}, bf16[1,64,2048]{2,1,0:T(8,128)(2,1)}, u32[]{:S(2)}) copy-start(bf16[1,64,2048]{2,1,0:T(8,128)(2,1)} %copy-done.4) | copy-start | bytes 786436
  75.5 4.2 %collective-permute-start.3 = (bf16[8,64,2048]{2,1,0:T(8,128)(2,1)S(1)}, bf16[8,64,2048]{2,1,0:T(8,128)(2,1)S(1)}, u32[]{:S(2)}, u32[]{:S(2)}) collective-permute-start(bf16[8,64,2048]{2,1,0:T(8,128)(2,1)S(1)} %pad_maximum_fusion), channel_id=1, source_target_pairs={{0,1},{1,0},{2,3},{3,2},{4,5},{5,4},{6,7},{7,6},{8,9},{9,8},{10,11... | collective-permute-start | bytes 6291464 | tf_op jit(solution)/shard_map/ppermute | solution.py:25
  80.0 11.6 %copy-start.6 = (bf16[4,1,32,2048]{3,2,0,1:T(8,128)(2,1)S(1)}, bf16[4,1,32,2048]{3,2,0,1:T(8,128)(2,1)}, u32[]{:S(2)}) copy-start(bf16[4,1,32,2048]{3,2,0,1:T(8,128)(2,1)} %fusion.72) | copy-start | bytes 1572868
  88.0 6.6 %copy-start.12 = (bf16[4,4,8,8,128]{4,3,2,1,0:T(8,128)(2,1)S(1)}, bf16[4,4,8,8,128]{4,3,2,1,0:T(8,128)(2,1)}, u32[]{:S(2)}) copy-start(bf16[4,4,8,8,128]{4,3,2,1,0:T(8,128)(2,1)} %get-tuple-element.16) | copy-start | bytes 786436
  89.4 5.5 %copy-start.7 = (bf16[4,4,8,8,128]{4,3,2,1,0:T(8,128)(2,1)S(1)}, bf16[4,4,8,8,128]{4,3,2,1,0:T(8,128)(2,1)}, u32[]{:S(2)}) copy-start(bf16[4,4,8,8,128]{4,3,2,1,0:T(8,128)(2,1)} %get-tuple-element.17) | copy-start | bytes 786436
  94.6 8.1 %copy-start.8 = (bf16[4,1,32,2048]{3,2,1,0:T(8,128)(2,1)S(1)}, bf16[4,1,32,2048]{3,2,1,0:T(8,128)(2,1)}, u32[]{:S(2)}) copy-start(bf16[4,1,32,2048]{3,2,1,0:T(8,128)(2,1)} %param.15) | copy-start | bytes 1572868
  94.9 0.8 copy-start.9
  99.5 15.1 %collective-permute-start.4 = (bf16[4,32,2048]{2,1,0:T(8,128)(2,1)}, bf16[4,32,2048]{2,1,0:T(8,128)(2,1)S(1)}, u32[]{:S(2)}, u32[]{:S(2)}) collective-permute-start(bf16[4,32,2048]{2,1,0:T(8,128)(2,1)} %fusion.13), channel_id=1, source_target_pairs={{0,16},{1,17},{2,18},{3,19},{4,20},{5,21},{6,22},{7,23},{8,24},{9,... | collective-permute-start | bytes 1572872 | tf_op jit(solution)/shard_map/ppermute | solution.py:15
  108.0 7.2 %copy-start.1 = (bf16[1,2048,1024]{2,1,0:T(8,128)(2,1)S(1)}, bf16[1,2048,1024]{2,1,0:T(8,128)(2,1)}, u32[]{:S(2)}) copy-start(bf16[1,2048,1024]{2,1,0:T(8,128)(2,1)} %all-gather.2.cloned.1.call-done) | copy-start | bytes 12582916
  118.1 15.2 %collective-permute-start.5 = (bf16[4,32,2048]{2,1,0:T(8,128)(2,1)S(1)}, bf16[4,32,2048]{2,1,0:T(8,128)(2,1)S(1)}, u32[]{:S(2)}, u32[]{:S(2)}) collective-permute-start(bf16[4,32,2048]{2,1,0:T(8,128)(2,1)S(1)} %fusion.75), channel_id=1, source_target_pairs={{16,0},{17,1},{18,2},{19,3},{20,4},{21,5},{22,6},{23,7},{24,8},{25... | collective-permute-start | bytes 1572872 | tf_op jit(solution)/shard_map/ppermute | solution.py:15
  120.0 17.1 %copy-start.10 = (f32[4,8,32,32]{2,3,1,0:T(8,128)S(1)}, f32[4,8,32,32]{2,3,1,0:T(8,128)}, u32[]{:S(2)}) copy-start(f32[4,8,32,32]{2,3,1,0:T(8,128)} %copy-done.9) | copy-start | bytes 393220
  133.3 4.4 %copy-start.13 = (bf16[4,4,8,8,128]{4,3,2,1,0:T(8,128)(2,1)S(1)}, bf16[4,4,8,8,128]{4,3,2,1,0:T(8,128)(2,1)}, u32[]{:S(2)}) copy-start(bf16[4,4,8,8,128]{4,3,2,1,0:T(8,128)(2,1)} %get-tuple-element.16) | copy-start | bytes 786436
  141.5 1.2 collective-permute-start.6
  142.8 3.7 %collective-permute-start.7 = (f32[2048]{0:T(1024)S(1)}, f32[2048]{0:T(1024)S(1)}, u32[]{:S(2)}, u32[]{:S(2)}) collective-permute-start(f32[2048]{0:T(1024)S(1)} %add.143), channel_id=1, source_target_pairs={{0,2},{1,3},{2,0},{3,1},{4,6},{5,7},{6,4},{7,5},{8,10},{9,11},{10,... | collective-permute-start | bytes 24584 | tf_op jit(solution)/shard_map/ppermute | solution.py:48
  146.4 4.6 %collective-permute-start.8 = (f32[2048]{0:T(1024)S(1)}, f32[2048]{0:T(1024)S(1)}, u32[]{:S(2)}, u32[]{:S(2)}) collective-permute-start(f32[2048]{0:T(1024)S(1)} %add.144), channel_id=1, source_target_pairs={{0,4},{1,5},{2,6},{3,7},{4,0},{5,1},{6,2},{7,3},{8,12},{9,13},{10,... | collective-permute-start | bytes 24584 | tf_op jit(solution)/shard_map/ppermute | solution.py:48
  151.0 8.2 %collective-permute-start.9 = (f32[2048]{0:T(1024)S(1)}, f32[2048]{0:T(1024)S(1)}, u32[]{:S(2)}, u32[]{:S(2)}) collective-permute-start(f32[2048]{0:T(1024)S(1)} %add.145), channel_id=1, source_target_pairs={{0,8},{1,9},{2,10},{3,11},{4,12},{5,13},{6,14},{7,15},{8,0},{9,1},... | collective-permute-start | bytes 24584 | tf_op jit(solution)/shard_map/ppermute | solution.py:48
Sparse Core Ops, SparseCore 0:
  25.6 61.6 all-gather.1

commit v3 on v1

--- a/solution.py
+++ b/solution.py
@@ -13,6 +13,53 @@
 
 def send_to(arrays, axis, source, target):
     return lax.ppermute(arrays, axis, [(source, target)])
+
+
+def exchange_orders(size):
+    steps = []
+    step = size // 2
+    while step >= 1:
+        steps.append(step)
+        step //= 2
+    other = list(steps)
+    if len(other) >= 3:
+        other[1], other[2] = other[2], other[1]
+    return steps, other
+
+
+def butterfly_gathers(shards, orders, axis, size):
+    index = lax.axis_index(axis)
+    held = [shard for shard in shards]
+    for level in range(len(orders[0])):
+        for which, order in enumerate(orders):
+            step = order[level]
+            other = lax.ppermute(held[which], axis, [(j, j ^ step) for j in range(size)])
+            upper = ((index // step) % 2) == 1
+            low = jnp.where(upper, other, held[which])
+            high = jnp.where(upper, held[which], other)
+            held[which] = jnp.stack([low, high], axis=1).reshape(
+                (-1,) + held[which].shape[1:]
+            )
+    results = []
+    for which, order in enumerate(orders):
+        block_rows, width = held[which].shape[1:]
+        wanted = sorted(order, reverse=True)
+        if order != wanted:
+            split = held[which].reshape(tuple(2 for _ in order) + (block_rows, width))
+            axes = tuple(order.index(value) for value in wanted) + (len(order), len(order) + 1)
+            held[which] = jnp.transpose(split, axes)
+        results.append(held[which].reshape(size * block_rows, width))
+    return results
+
+
+def butterfly_sum(value, axis, size):
+    if size & (size - 1):
+        return lax.psum(value, axis)
+    step = 1
+    while step < size:
+        value = value + lax.ppermute(value, axis, [(j, j ^ step) for j in range(size)])
+        step *= 2
+    return value
 
 
 def rms_scale(inputs, gain_vector):
@@ -54,8 +101,14 @@
     micro_count, series_count, seq_length, model_width = history.shape
     rows = micro_count * series_count
     act_shape = (rows, seq_length, model_width)
-    query_weight = lax.all_gather(query_weights, "fsdp", axis=1, tiled=True)[0]
-    output_weight = lax.all_gather(output_weights, "fsdp", axis=1, tiled=True)[0]
+    fsdp_count = lax.axis_size("fsdp")
+    if fsdp_count & (fsdp_count - 1):
+        query_weight = lax.all_gather(query_weights, "fsdp", axis=1, tiled=True)[0]
+        output_weight = lax.all_gather(output_weights, "fsdp", axis=1, tiled=True)[0]
+    else:
+        query_weight, output_weight = butterfly_gathers(
+            [query_weights, output_weights], exchange_orders(fsdp_count), "fsdp", fsdp_count
+        )
     gain_vector = gains[0]
     code_rows = codes.reshape(micro_count, series_count, seq_length)
     code_count = plan_table.shape[0]
@@ -131,7 +184,7 @@
                 got_grad = send_to(input_grad, "section", run, run - 1)
         grads_out = jnp.where(mine, input_grad, grads_out)
         gain_total = gain_total + jnp.where(mine, gain_grad, zero_gain)
-    gain_total = lax.psum(gain_total, "fsdp")
+    gain_total = butterfly_sum(gain_total, "fsdp", fsdp_count)
     grads_out = grads_out.reshape(history.shape)
     return (grads_out[None], gain_total[None])
 

time: 198 us -> 137 us (0.69)
  waiting for transfers between devices: 120 us -> 79.7 us
  blocking collectives: 30.6 us -> 0 us
  starting transfers between devices: 4.95 us -> 20.2 us
  between operations: 14.4 us -> 1.22 us
  other arithmetic: 9.04 us -> 16.3 us
  local copies, waits for them, and re-layouts: 1.52 us -> 5.99 us
  matrix products: 17.3 us -> 13.3 us
    all_gather x2 -> x0, waiting for transfers between devices: 97 us -> none  [the longest x1 50.1 us: on_device(): query_weight = lax.all_gather(query_weights, 'fsdp', axis=1, tiled=True)[0]]
    ppermute x0 -> x12, waiting for transfers between devices: none -> 59.4 us  [the longest x8 52.6 us: butterfly_gathers(): lax.ppermute(held[which], axis, [(j, j ^ step) for j in range(size)])]
    psum x1 -> x0, blocking collectives: 30.6 us -> none  [on_device(): gain_total = lax.psum(gain_total, 'fsdp')]
    ppermute x0 -> x12, starting transfers between devices: none -> 15.1 us  [the longest x8 10.7 us: butterfly_gathers(): lax.ppermute(held[which], axis, [(j, j ^ step) for j in range(size)])]
    another operation x2 -> x14, other arithmetic: 1.53 us -> 10.1 us  [the longest x12 9.6 us: butterfly_gathers(): jnp.stack([low, high], axis=1).reshape((-1,) + held[which].shape[1:])]
    another operation x0 -> x3, local copies, waits for them, and re-layouts: none -> 2.23 us  [butterfly_gathers(): jnp.stack([low, high], axis=1).reshape((-1,) + held[which].shape[1:])]
    dot_general x4, matrix products: 6.66 us -> 4.51 us  [attend_layer(): jnp.dot(normed_rows, query_weight, preferred_element_type=jnp.float32)]
  transfers between devices with their start and end apart: 4 -> 14, of which waited for: 4 -> 12; matrix products, arithmetic and copies ran while one was open for 6% -> 15% of each run, Pallas kernels for 0% -> 0%
where the time goes in v3:
time: 137 us
  waiting for transfers between devices  79.7 us (58%)
  starting transfers between devices  20.2 us (15%)
  other arithmetic  16.3 us (12%)
  matrix products  13.3 us (10%)
  local copies, waits for them, and re-layouts  5.99 us (4%)
    ppermute x8, waiting for transfers between devices, butterfly_gathers(): lax.ppermute(held[which], axis, [(j, j ^ step) for j in range(size)])  52.6 us
    ppermute x2, waiting for transfers between devices, send_to(): return lax.ppermute(arrays, axis, [(source, target)])  20.2 us
    ppermute x8, starting transfers between devices, butterfly_gathers(): lax.ppermute(held[which], axis, [(j, j ^ step) for j in range(size)])  10.7 us
    another operation x12, other arithmetic, butterfly_gathers(): jnp.stack([low, high], axis=1).reshape((-1,) + held[which].shape[1:])  9.6 us
    ppermute x4, waiting for transfers between devices, butterfly_sum(): lax.ppermute(value, axis, [(j, j ^ step) for j in range(size)])  6.84 us
    ppermute x2, starting transfers between devices, send_to(): return lax.ppermute(arrays, axis, [(source, target)])  5.11 us
    dot_general x3, matrix products, attend_layer(): update = jnp.dot(mixed, output_weight, preferred_element_type=jnp.float32)  5.09 us
    dot_general x4, matrix products, attend_layer(): jnp.dot(normed_rows, query_weight, preferred_element_type=jnp.float32)  4.51 us
  transfers between devices with their start and end apart: 14, of which 12 were waited for; matrix products, arithmetic and copies ran while one was open for 15% of the time, Pallas kernels for 0%

profile of v3, /device:TPU:0, one launch (start us, length us, event | category | flops | bytes accessed | tf_op | source)
XLA Modules:
  0.0 136.7 jit_solution(17222131320034390195)
XLA Ops:
  0.7 4.1 %collective-permute-start.4 = (bf16[1,128,1024]{2,1,0:T(8,128)(2,1)}, bf16[1,128,1024]{2,1,0:T(8,128)(2,1)S(1)}, u32[]{:S(2)}, u32[]{:S(2)}) collective-permute-start(bf16[1,128,1024]{2,1,0:T(8,128)(2,1)} %param.12), channel_id=1, source_target_pairs={{0,8},{1,9},{2,10},{3,11},{4,12},{5,13},{6,14},{7,15},{8,0},{9,1},... | collective-permute-start | bytes 786440 | tf_op jit(solution)/shard_map/ppermute | solution.py:36
  4.8 18.5 %collective-permute-done.4 = bf16[1,128,1024]{2,1,0:T(8,128)(2,1)S(1)} collective-permute-done((bf16[1,128,1024]{2,1,0:T(8,128)(2,1)}, bf16[1,128,1024]{2,1,0:T(8,128)(2,1)S(1)}, u32[]{:S(2)}, u32[]{:S(2)}) %collective-permute-start.4) | collective-permute-done | bytes 262176 | tf_op jit(solution)/shard_map/ppermute | solution.py:36
  23.3 1.0 select_bitcast_fusion.11
  24.5 3.7 %collective-permute-done = bf16[1,64,2048]{2,1,0:T(8,128)(2,1)S(1)} collective-permute-done((bf16[1,64,2048]{2,1,0:T(8,128)(2,1)}, bf16[1,64,2048]{2,1,0:T(8,128)(2,1)S(1)}, u32[]{:S(2)}, u32[]{:S(2)}) %collective-permute-start) | collective-permute-done | bytes 262176 | tf_op jit(solution)/shard_map/ppermute | solution.py:36
  28.2 1.0 select_bitcast_fusion.13
  29.3 1.6 %collective-permute-start.1 = (bf16[2,64,2048]{2,1,0:T(8,128)(2,1)S(1)}, bf16[2,64,2048]{2,1,0:T(8,128)(2,1)S(1)}, u32[]{:S(2)}, u32[]{:S(2)}) collective-permute-start(bf16[2,64,2048]{2,1,0:T(8,128)(2,1)S(1)} %maximum_bitcast_fusion.2), channel_id=1, source_target_pairs={{0,2},{1,3},{2,0},{3,1},{4,6},{5,7},{6,4},{7,5},{8,10},{9,11},{10,... | collective-permute-start | bytes 1572872 | tf_op jit(solution)/shard_map/ppermute | solution.py:36
  31.1 8.3 %collective-permute-done.5 = bf16[2,128,1024]{2,1,0:T(8,128)(2,1)S(1)} collective-permute-done((bf16[2,128,1024]{2,1,0:T(8,128)(2,1)S(1)}, bf16[2,128,1024]{2,1,0:T(8,128)(2,1)S(1)}, u32[]{:S(2)}, u32[]{:S(2)}) %collective-permute-start.5) | collective-permute-done | bytes 524320 | tf_op jit(solution)/shard_map/ppermute | solution.py:36
  39.4 1.1 pad_maximum_fusion.3
  40.5 1.6 %collective-permute-start.6 = (bf16[4,128,1024]{2,1,0:T(8,128)(2,1)}, bf16[4,128,1024]{2,1,0:T(8,128)(2,1)}, u32[]{:S(2)}, u32[]{:S(2)}) collective-permute-start(bf16[4,128,1024]{2,1,0:T(8,128)(2,1)} %bitcast.27), channel_id=1, source_target_pairs={{0,2},{1,3},{2,0},{3,1},{4,6},{5,7},{6,4},{7,5},{8,10},{9,11},{10,... | collective-permute-start | bytes 3145736 | tf_op jit(solution)/shard_map/ppermute | solution.py:36
  42.6 2.6 %collective-permute-start.2 = (bf16[4,64,2048]{2,1,0:T(8,128)(2,1)S(1)}, bf16[4,64,2048]{2,1,0:T(8,128)(2,1)}, u32[]{:S(2)}, u32[]{:S(2)}) collective-permute-start(bf16[4,64,2048]{2,1,0:T(8,128)(2,1)S(1)} %bitcast.279), channel_id=1, source_target_pairs={{0,4},{1,5},{2,6},{3,7},{4,0},{5,1},{6,2},{7,3},{8,12},{9,13},{10,... | collective-permute-start | bytes 3145736 | tf_op jit(solution)/shard_map/ppermute | solution.py:36
  45.3 0.4 multiply_reduce_fusion
  45.8 20.1 %collective-permute-done.6 = bf16[4,128,1024]{2,1,0:T(8,128)(2,1)} collective-permute-done((bf16[4,128,1024]{2,1,0:T(8,128)(2,1)}, bf16[4,128,1024]{2,1,0:T(8,128)(2,1)}, u32[]{:S(2)}, u32[]{:S(2)}) %collective-permute-start.6) | collective-permute-done | bytes 1048608 | tf_op jit(solution)/shard_map/ppermute | solution.py:36
  65.9 1.7 %select_bitcast_fusion.3 = (bf16[4,1,128,1024]{3,2,0,1:T(8,128)(2,1)S(1)}, bf16[4,1,128,1024]{3,2,0,1:T(8,128)(2,1)S(1)}) fusion(bf16[4,128,1024]{2,1,0:T(8,128)(2,1)} %collective-permute-done.6, pred[]{:T(512)S(6)} %eq.52, bf16[2,2,128,1024]{3,2,1,0:T(8,128)(2,1)} %pad_maximum_fusion.3), kind=kLoop, calls=%fused_computation.96 | loop fusion | flops 1048576 | bytes 4194305 | tf_op jit(solution)/shard_map/stack | solution.py:40
  67.8 1.5 %copy.78 = bf16[4,2,128,1024]{3,2,1,0:T(8,128)(2,1)} copy(bf16[4,2,128,1024]{3,2,0,1:T(8,128)(2,1)S(1)} %pad_maximum_fusion.1) | data formatting | bytes 4194304 | tf_op jit(solution)/shard_map/stack | solution.py:40
  69.3 1.4 %select_bitcast_fusion.5 = (bf16[4,1,64,2048]{3,2,0,1:T(8,128)(2,1)S(1)}, bf16[4,1,64,2048]{3,2,0,1:T(8,128)(2,1)S(1)}) fusion(bf16[4,64,2048]{2,1,0:T(8,128)(2,1)} %collective-permute-done.2, pred[]{:T(512)S(6)} %eq.51, bf16[2,2,64,2048]{3,2,1,0:T(8,128)(2,1)S(1)} %pad_maximum_fusion.4), kind=kLoop, calls=%fused_computation.100 | loop fusion | flops 1048576 | bytes 4194305 | tf_op jit(solution)/shard_map/stack | solution.py:40
  71.1 0.6 collective-permute-start.3
  72.1 1.7 %collective-permute-done.7 = bf16[8,128,1024]{2,1,0:T(8,128)(2,1)} collective-permute-done((bf16[8,128,1024]{2,1,0:T(8,128)(2,1)}, bf16[8,128,1024]{2,1,0:T(8,128)(2,1)}, u32[]{:S(2)}, u32[]{:S(2)}) %collective-permute-start.7) | collective-permute-done | bytes 2097184 | tf_op jit(solution)/shard_map/ppermute | solution.py:36
  73.8 2.5 %select_bitcast_fusion.1 = (bf16[8,1,128,1024]{3,2,0,1:T(8,128)(2,1)S(1)}, bf16[8,1,128,1024]{3,2,0,1:T(8,128)(2,1)S(1)}) fusion(bf16[8,128,1024]{2,1,0:T(8,128)(2,1)} %collective-permute-done.7, pred[]{:T(512)S(6)} %eq.50, bf16[4,2,128,1024]{3,2,1,0:T(8,128)(2,1)} %copy.78), kind=kLoop, calls=%fused_computation.11 | loop fusion | flops 2097152 | bytes 8388609 | tf_op jit(solution)/shard_map/stack | solution.py:40
  76.3 0.4 pad_maximum_fusion
  76.7 0.6 copy.79
  77.3 0.7 fusion.21
  78.1 0.4 broadcast_select_fusion.1
  78.5 0.7 copy-done.2
  79.2 0.4 maximum_bitcast_fusion
  79.6 0.6 copy.73
  80.9 0.5 copy-done.8
  81.4 1.6 %fusion = bf16[4,32,2048]{2,1,0:T(8,128)(2,1)} fusion(bf16[1024,2048,1]{1,0,2:T(8,128)(2,1)S(1)} %bitcast.271, bf16[4,1,32,2048]{3,2,1,0:T(8,128)(2,1)S(1)} %copy-done.6, bf16[4,8,4,8,128]{4,3,2,1,0:T(8,128)(2,1)S(1)} %fusion.23), kind=kOutput, calls=%fused_computation.3 | convolution fusion | flops 537657344 | bytes 5505024 | tf_op jit(solution)/shard_map/dot_general | solution.py:93
  83.0 3.6 %collective-permute-start.8 = (bf16[4,32,2048]{2,1,0:T(8,128)(2,1)}, bf16[4,32,2048]{2,1,0:T(8,128)(2,1)S(1)}, u32[]{:S(2)}, u32[]{:S(2)}) collective-permute-start(bf16[4,32,2048]{2,1,0:T(8,128)(2,1)} %fusion), channel_id=1, source_target_pairs={{0,16},{1,17},{2,18},{3,19},{4,20},{5,21},{6,22},{7,23},{8,24},{9,... | collective-permute-start | bytes 1572872 | tf_op jit(solution)/shard_map/ppermute | solution.py:15
  86.6 2.0 %fusion.19 = bf16[128,1024]{0,1:T(8,128)(2,1)} fusion(bf16[1024,2048]{1,0:T(8,128)(2,1)S(1)} %bitcast.272, bf16[128,2048]{1,0:T(8,128)(2,1)S(1)} %bitcast.293), kind=kOutput, calls=%fused_computation.60 | convolution fusion | flops 537001984 | bytes 4980736 | tf_op jit(solution)/shard_map/transpose(jvp())/dot_general | solution.py:93
  88.5 1.1 copy.74
  89.7 8.4 %collective-permute-done.8 = bf16[4,32,2048]{2,1,0:T(8,128)(2,1)S(1)} collective-permute-done((bf16[4,32,2048]{2,1,0:T(8,128)(2,1)}, bf16[4,32,2048]{2,1,0:T(8,128)(2,1)S(1)}, u32[]{:S(2)}, u32[]{:S(2)}) %collective-permute-start.8) | collective-permute-done | bytes 524320 | tf_op jit(solution)/shard_map/ppermute | solution.py:15
  98.7 0.8 fusion.20
  100.7 0.6 fusion.31
  101.6 1.6 %collective-permute-start.9 = (bf16[4,32,2048]{2,1,0:T(8,128)(2,1)S(1)}, bf16[4,32,2048]{2,1,0:T(8,128)(2,1)S(1)}, u32[]{:S(2)}, u32[]{:S(2)}) collective-permute-start(bf16[4,32,2048]{2,1,0:T(8,128)(2,1)S(1)} %fusion.44), channel_id=1, source_target_pairs={{16,0},{17,1},{18,2},{19,3},{20,4},{21,5},{22,6},{23,7},{24,8},{25... | collective-permute-start | bytes 1572872 | tf_op jit(solution)/shard_map/ppermute | solution.py:15
  103.7 1.5 %convolution_convert_fusion = bf16[128,2048]{1,0:T(8,128)(2,1)S(1)} fusion(bf16[2048,1024]{1,0:T(8,128)(2,1)S(1)} %bitcast.269, bf16[16,8,8,128]{3,2,1,0:T(8,128)(2,1)S(1)} %bitcast.290), kind=kOutput, calls=%fused_computation.4 | convolution fusion | flops 537133056 | bytes 4980736 | tf_op jit(solution)/shard_map/transpose(jvp())/dot_general | solution.py:82
  105.2 11.9 %collective-permute-done.9 = bf16[4,32,2048]{2,1,0:T(8,128)(2,1)S(1)} collective-permute-done((bf16[4,32,2048]{2,1,0:T(8,128)(2,1)S(1)}, bf16[4,32,2048]{2,1,0:T(8,128)(2,1)S(1)}, u32[]{:S(2)}, u32[]{:S(2)}) %collective-permute-start.9) | collective-permute-done | bytes 524320 | tf_op jit(solution)/shard_map/ppermute | solution.py:15
  117.0 1.5 %fusion.22 = bf16[16,8,8,128]{3,1,2,0:T(8,128)(2,1)S(1)} fusion(bf16[128,2048]{1,0:T(8,128)(2,1)S(1)} %bitcast.284, bf16[1024,2048]{1,0:T(8,128)(2,1)S(1)} %bitcast.273), kind=kOutput, calls=%fused_computation.63 | convolution fusion | flops 537001984 | bytes 4980736 | tf_op jit(solution)/shard_map/transpose(jvp())/dot_general | solution.py:93
  120.0 1.5 %convolution_convert_fusion.1 = bf16[128,2048]{1,0:T(8,128)(2,1)S(1)} fusion(bf16[2048,1024]{1,0:T(8,128)(2,1)S(1)} %bitcast.270, bf16[16,8,8,128]{3,2,1,0:T(8,128)(2,1)S(1)} %bitcast.289), kind=kOutput, calls=%fused_computation.5 | convolution fusion | flops 537133056 | bytes 4980736 | tf_op jit(solution)/shard_map/transpose(jvp())/dot_general | solution.py:82
  121.6 1.3 fusion.36
  123.1 1.2 collective-permute-done.10
  124.2 1.5 %collective-permute-start.11 = (f32[2048]{0:T(1024)S(1)}, f32[2048]{0:T(1024)S(1)}, u32[]{:S(2)}, u32[]{:S(2)}) collective-permute-start(f32[2048]{0:T(1024)S(1)} %add.91), channel_id=1, source_target_pairs={{0,2},{1,3},{2,0},{3,1},{4,6},{5,7},{6,4},{7,5},{8,10},{9,11},{10,... | collective-permute-start | bytes 24584 | tf_op jit(solution)/shard_map/ppermute | solution.py:60
  125.8 2.1 %collective-permute-done.11 = f32[2048]{0:T(1024)S(1)} collective-permute-done((f32[2048]{0:T(1024)S(1)}, f32[2048]{0:T(1024)S(1)}, u32[]{:S(2)}, u32[]{:S(2)}) %collective-permute-start.11) | collective-permute-done | bytes 8224 | tf_op jit(solution)/shard_map/ppermute | solution.py:60
  127.9 0.7 collective-permute-start.12
  128.6 3.0 %collective-permute-done.12 = f32[2048]{0:T(1024)S(1)} collective-permute-done((f32[2048]{0:T(1024)S(1)}, f32[2048]{0:T(1024)S(1)}, u32[]{:S(2)}, u32[]{:S(2)}) %collective-permute-start.12) | collective-permute-done | bytes 8224 | tf_op jit(solution)/shard_map/ppermute | solution.py:60
  131.5 2.1 %collective-permute-start.13 = (f32[2048]{0:T(1024)S(1)}, f32[2048]{0:T(1024)S(1)}, u32[]{:S(2)}, u32[]{:S(2)}) collective-permute-start(f32[2048]{0:T(1024)S(1)} %add.93), channel_id=1, source_target_pairs={{0,8},{1,9},{2,10},{3,11},{4,12},{5,13},{6,14},{7,15},{8,0},{9,1},... | collective-permute-start | bytes 24584 | tf_op jit(solution)/shard_map/ppermute | solution.py:60
  133.7 1.9 %fusion.54 = bf16[1,4,1,32,2048]{4,3,2,1,0:T(8,128)(2,1)} fusion(f32[4,32,2048]{2,1,0:T(8,128)S(1)} %get-tuple-element.45, bf16[4,32,2048]{2,1,0:T(8,128)(2,1)S(1)} %collective-permute-done.9, bf16[4,32,1024]{2,1,0:T(8,128)(2,1)S(1)} %bitcast.283, bf16[4,32,1024]{2,1,0:T(8,128)(2,1)S(1)} %bitcast.281, bf16[4,1,32,2048]{3,2,1,0:T(8,128)(2,1)S(1)} %copy-done.7, ...), kind=kLoop, calls=%fused_computation.105 | loop fusion | flops 8912896 | bytes 4729346
  135.5 0.6 collective-permute-done.13
  136.1 0.6 add.94
  (89 shorter events, 7.1 us)
Async XLA Ops:
  0.6 44.7 %copy-start = (bf16[16,2048]{1,0:T(8,128)(2,1)S(1)}, bf16[16,2048]{1,0:T(8,128)(2,1)}, u32[]{:S(2)}) copy-start(bf16[16,2048]{1,0:T(8,128)(2,1)} %param.11) | copy-start | bytes 196612
  0.6 30.3 %copy-start.6 = (bf16[4,1,32,2048]{3,2,1,0:T(8,128)(2,1)S(1)}, bf16[4,1,32,2048]{3,2,1,0:T(8,128)(2,1)}, u32[]{:S(2)}) copy-start(bf16[4,1,32,2048]{3,2,1,0:T(8,128)(2,1)} %param.8) | copy-start | bytes 1572868
  0.7 22.7 %collective-permute-start.4 = (bf16[1,128,1024]{2,1,0:T(8,128)(2,1)}, bf16[1,128,1024]{2,1,0:T(8,128)(2,1)S(1)}, u32[]{:S(2)}, u32[]{:S(2)}) collective-permute-start(bf16[1,128,1024]{2,1,0:T(8,128)(2,1)} %param.12), channel_id=1, source_target_pairs={{0,8},{1,9},{2,10},{3,11},{4,12},{5,13},{6,14},{7,15},{8,0},{9,1},... | collective-permute-start | bytes 786440 | tf_op jit(solution)/shard_map/ppermute | solution.py:36
  4.8 23.5 %collective-permute-start = (bf16[1,64,2048]{2,1,0:T(8,128)(2,1)}, bf16[1,64,2048]{2,1,0:T(8,128)(2,1)S(1)}, u32[]{:S(2)}, u32[]{:S(2)}) collective-permute-start(bf16[1,64,2048]{2,1,0:T(8,128)(2,1)} %param.13), channel_id=1, source_target_pairs={{0,8},{1,9},{2,10},{3,11},{4,12},{5,13},{6,14},{7,15},{8,0},{9,1},... | collective-permute-start | bytes 786440 | tf_op jit(solution)/shard_map/ppermute | solution.py:36
  24.4 15.0 %collective-permute-start.5 = (bf16[2,128,1024]{2,1,0:T(8,128)(2,1)S(1)}, bf16[2,128,1024]{2,1,0:T(8,128)(2,1)S(1)}, u32[]{:S(2)}, u32[]{:S(2)}) collective-permute-start(bf16[2,128,1024]{2,1,0:T(8,128)(2,1)S(1)} %maximum_bitcast_fusion.1), channel_id=1, source_target_pairs={{0,4},{1,5},{2,6},{3,7},{4,0},{5,1},{6,2},{7,3},{8,12},{9,13},{10,... | collective-permute-start | bytes 1572872 | tf_op jit(solution)/shard_map/ppermute | solution.py:36
  29.3 13.1 %collective-permute-start.1 = (bf16[2,64,2048]{2,1,0:T(8,128)(2,1)S(1)}, bf16[2,64,2048]{2,1,0:T(8,128)(2,1)S(1)}, u32[]{:S(2)}, u32[]{:S(2)}) collective-permute-start(bf16[2,64,2048]{2,1,0:T(8,128)(2,1)S(1)} %maximum_bitcast_fusion.2), channel_id=1, source_target_pairs={{0,2},{1,3},{2,0},{3,1},{4,6},{5,7},{6,4},{7,5},{8,10},{9,11},{10,... | collective-permute-start | bytes 1572872 | tf_op jit(solution)/shard_map/ppermute | solution.py:36
  31.1 14.1 %copy-start.13 = (s32[4,1,16,2]{2,3,1,0:T(2,128)S(1)}, s32[4,1,16,2]{2,3,1,0:T(2,128)}, u32[]{:S(2)}) copy-start(s32[4,1,16,2]{2,3,1,0:T(2,128)} %param.10) | copy-start | bytes 1540
  40.5 25.4 %collective-permute-start.6 = (bf16[4,128,1024]{2,1,0:T(8,128)(2,1)}, bf16[4,128,1024]{2,1,0:T(8,128)(2,1)}, u32[]{:S(2)}, u32[]{:S(2)}) collective-permute-start(bf16[4,128,1024]{2,1,0:T(8,128)(2,1)} %bitcast.27), channel_id=1, source_target_pairs={{0,2},{1,3},{2,0},{3,1},{4,6},{5,7},{6,4},{7,5},{8,10},{9,11},{10,... | collective-permute-start | bytes 3145736 | tf_op jit(solution)/shard_map/ppermute | solution.py:36
  42.6 26.7 %collective-permute-start.2 = (bf16[4,64,2048]{2,1,0:T(8,128)(2,1)S(1)}, bf16[4,64,2048]{2,1,0:T(8,128)(2,1)}, u32[]{:S(2)}, u32[]{:S(2)}) collective-permute-start(bf16[4,64,2048]{2,1,0:T(8,128)(2,1)S(1)} %bitcast.279), channel_id=1, source_target_pairs={{0,4},{1,5},{2,6},{3,7},{4,0},{5,1},{6,2},{7,3},{8,12},{9,13},{10,... | collective-permute-start | bytes 3145736 | tf_op jit(solution)/shard_map/ppermute | solution.py:36
  67.6 1.7 %copy-start.14 = (s32[4,1,32]{2,1,0:T(1,128)S(1)}, s32[4,1,32]{2,1,0:T(1,128)}, u32[]{:S(2)}) copy-start(s32[4,1,32]{2,1,0:T(1,128)} %param.9) | copy-start | bytes 1540
  69.3 4.5 %collective-permute-start.7 = (bf16[8,128,1024]{2,1,0:T(8,128)(2,1)}, bf16[8,128,1024]{2,1,0:T(8,128)(2,1)}, u32[]{:S(2)}, u32[]{:S(2)}) collective-permute-start(bf16[8,128,1024]{2,1,0:T(8,128)(2,1)} %bitcast.30), channel_id=1, source_target_pairs={{0,1},{1,0},{2,3},{3,2},{4,5},{5,4},{6,7},{7,6},{8,9},{9,8},{10,11... | collective-permute-start | bytes 6291464 | tf_op jit(solution)/shard_map/ppermute | solution.py:36
  70.7 0.9 copy-start.10
  71.1 7.0 %collective-permute-start.3 = (bf16[8,64,2048]{2,1,0:T(8,128)(2,1)S(1)}, bf16[8,64,2048]{2,1,0:T(8,128)(2,1)S(1)}, u32[]{:S(2)}, u32[]{:S(2)}) collective-permute-start(bf16[8,64,2048]{2,1,0:T(8,128)(2,1)S(1)} %bitcast.274), channel_id=1, source_target_pairs={{0,1},{1,0},{2,3},{3,2},{4,5},{5,4},{6,7},{7,6},{8,9},{9,8},{10,11... | collective-permute-start | bytes 6291464 | tf_op jit(solution)/shard_map/ppermute | solution.py:36
  71.9 8.4 %copy-start.11 = (bf16[4,4,8,8,128]{4,3,2,1,0:T(8,128)(2,1)}, bf16[4,4,8,8,128]{4,3,2,1,0:T(8,128)(2,1)S(1)}, u32[]{:S(2)}) copy-start(bf16[4,4,8,8,128]{4,3,2,1,0:T(8,128)(2,1)S(1)} %get-tuple-element.32) | copy-start | bytes 786436
  77.3 1.9 %copy-start.2 = (bf16[8,2,128,1024]{3,2,1,0:T(8,128)(2,1)}, bf16[8,2,128,1024]{3,2,1,0:T(8,128)(2,1)S(1)}, u32[]{:S(2)}) copy-start(bf16[8,2,128,1024]{3,2,1,0:T(8,128)(2,1)S(1)} %copy.79) | copy-start | bytes 12582916
  80.2 6.3 %copy-start.4 = (bf16[2,2,2,2,64,2048]{5,4,3,2,1,0:T(8,128)(2,1)}, bf16[2,2,2,2,64,2048]{5,4,3,2,1,0:T(8,128)(2,1)S(1)}, u32[]{:S(2)}) copy-start(bf16[2,2,2,2,64,2048]{5,4,3,2,1,0:T(8,128)(2,1)S(1)} %copy.73) | copy-start | bytes 12582916
  80.2 6.3 %copy-start.7 = (bf16[4,1,32,2048]{3,2,1,0:T(8,128)(2,1)S(1)}, bf16[4,1,32,2048]{3,2,1,0:T(8,128)(2,1)}, u32[]{:S(2)}) copy-start(bf16[4,1,32,2048]{3,2,1,0:T(8,128)(2,1)} %param.15) | copy-start | bytes 1572868
  80.5 0.8 copy-start.8
  83.0 15.1 %collective-permute-start.8 = (bf16[4,32,2048]{2,1,0:T(8,128)(2,1)}, bf16[4,32,2048]{2,1,0:T(8,128)(2,1)S(1)}, u32[]{:S(2)}, u32[]{:S(2)}) collective-permute-start(bf16[4,32,2048]{2,1,0:T(8,128)(2,1)} %fusion), channel_id=1, source_target_pairs={{0,16},{1,17},{2,18},{3,19},{4,20},{5,21},{6,22},{7,23},{8,24},{9,... | collective-permute-start | bytes 1572872 | tf_op jit(solution)/shard_map/ppermute | solution.py:15
  89.6 9.0 %copy-start.3 = (bf16[8,2,128,1024]{3,2,1,0:T(8,128)(2,1)S(1)}, bf16[8,2,128,1024]{3,2,1,0:T(8,128)(2,1)}, u32[]{:S(2)}) copy-start(bf16[8,2,128,1024]{3,2,1,0:T(8,128)(2,1)} %copy-done.2) | copy-start | bytes 12582916
  101.6 15.4 %copy-start.5 = (bf16[2,2,2,2,64,2048]{5,4,3,2,1,0:T(8,128)(2,1)S(1)}, bf16[2,2,2,2,64,2048]{5,4,3,2,1,0:T(8,128)(2,1)}, u32[]{:S(2)}) copy-start(bf16[2,2,2,2,64,2048]{5,4,3,2,1,0:T(8,128)(2,1)} %copy-done.4) | copy-start | bytes 12582916
  101.6 15.4 %collective-permute-start.9 = (bf16[4,32,2048]{2,1,0:T(8,128)(2,1)S(1)}, bf16[4,32,2048]{2,1,0:T(8,128)(2,1)S(1)}, u32[]{:S(2)}, u32[]{:S(2)}) collective-permute-start(bf16[4,32,2048]{2,1,0:T(8,128)(2,1)S(1)} %fusion.44), channel_id=1, source_target_pairs={{16,0},{17,1},{18,2},{19,3},{20,4},{21,5},{22,6},{23,7},{24,8},{25... | collective-permute-start | bytes 1572872 | tf_op jit(solution)/shard_map/ppermute | solution.py:15
  103.6 15.0 %copy-start.9 = (f32[4,8,32,32]{2,3,1,0:T(8,128)S(1)}, f32[4,8,32,32]{2,3,1,0:T(8,128)}, u32[]{:S(2)}) copy-start(f32[4,8,32,32]{2,3,1,0:T(8,128)} %copy-done.8) | copy-start | bytes 393220
  117.0 2.2 %copy-start.12 = (bf16[4,4,8,8,128]{4,3,2,1,0:T(8,128)(2,1)S(1)}, bf16[4,4,8,8,128]{4,3,2,1,0:T(8,128)(2,1)}, u32[]{:S(2)}) copy-start(bf16[4,4,8,8,128]{4,3,2,1,0:T(8,128)(2,1)} %copy-done.11) | copy-start | bytes 786436
  121.6 15.1 %copy-start.1 = (bf16[16,2048]{1,0:T(8,128)(2,1)S(1)}, bf16[16,2048]{1,0:T(8,128)(2,1)}, u32[]{:S(2)}) copy-start(bf16[16,2048]{1,0:T(8,128)(2,1)} %param.11) | copy-start | bytes 196612
  123.0 1.2 collective-permute-start.10
  124.2 3.7 %collective-permute-start.11 = (f32[2048]{0:T(1024)S(1)}, f32[2048]{0:T(1024)S(1)}, u32[]{:S(2)}, u32[]{:S(2)}) collective-permute-start(f32[2048]{0:T(1024)S(1)} %add.91), channel_id=1, source_target_pairs={{0,2},{1,3},{2,0},{3,1},{4,6},{5,7},{6,4},{7,5},{8,10},{9,11},{10,... | collective-permute-start | bytes 24584 | tf_op jit(solution)/shard_map/ppermute | solution.py:60
  127.9 3.7 %collective-permute-start.12 = (f32[2048]{0:T(1024)S(1)}, f32[2048]{0:T(1024)S(1)}, u32[]{:S(2)}, u32[]{:S(2)}) collective-permute-start(f32[2048]{0:T(1024)S(1)} %add.92), channel_id=1, source_target_pairs={{0,4},{1,5},{2,6},{3,7},{4,0},{5,1},{6,2},{7,3},{8,12},{9,13},{10,... | collective-permute-start | bytes 24584 | tf_op jit(solution)/shard_map/ppermute | solution.py:60
  131.5 4.5 %collective-permute-start.13 = (f32[2048]{0:T(1024)S(1)}, f32[2048]{0:T(1024)S(1)}, u32[]{:S(2)}, u32[]{:S(2)}) collective-permute-start(f32[2048]{0:T(1024)S(1)} %add.93), channel_id=1, source_target_pairs={{0,8},{1,9},{2,10},{3,11},{4,12},{5,13},{6,14},{7,15},{8,0},{9,1},... | collective-permute-start | bytes 24584 | tf_op jit(solution)/shard_map/ppermute | solution.py:60

commit v4 on v3

--- a/solution.py
+++ b/solution.py
@@ -52,14 +52,16 @@
     return results
 
 
-def butterfly_sum(value, axis, size):
+def spread_sum(value, axis, size):
     if size & (size - 1):
         return lax.psum(value, axis)
-    step = 1
-    while step < size:
-        value = value + lax.ppermute(value, axis, [(j, j ^ step) for j in range(size)])
-        step *= 2
-    return value
+    index = lax.axis_index(axis)
+    received = [value] + [
+        lax.ppermute(value, axis, [(j, j ^ shift) for j in range(size)]) for shift in range(1, size)
+    ]
+    by_shift = jnp.stack(received, axis=0)
+    by_source = jnp.take(by_shift, jnp.arange(size, dtype=jnp.int32) ^ index, axis=0)
+    return jnp.sum(by_source, axis=0)
 
 
 def rms_scale(inputs, gain_vector):
@@ -129,7 +131,7 @@
             layer_input, layer_memory, key_mask, query_weight, output_weight, layer_gain
         )
 
-    saved_inputs = {}
+    pullbacks = {}
     got_input = None
     got_memory = None
     for tick in range(section_count - 1):
@@ -140,21 +142,22 @@
         else:
             layer_input = got_input
         if tick < half_sections:
-            output = encoder_map(layer_input, gain_vector)
-            saved_inputs[tick] = (layer_input, None)
+            output, pull = jax.vjp(encoder_map, layer_input, gain_vector)
+            pullbacks[tick] = pull
             if tick == half_sections - 1:
                 got_memory = send_to(output, "section", tick, tick + 1)
             else:
                 got_input = send_to(output, "section", tick, tick + 1)
         else:
-            output = decoder_map(layer_input, got_memory, gain_vector)
-            saved_inputs[tick] = (layer_input, got_memory)
+            output, pull = jax.vjp(decoder_map, layer_input, got_memory, gain_vector)
+            pullbacks[tick] = pull
             got_input, got_memory = send_to((output, got_memory), "section", tick, tick + 1)
     last = section_count - 1
     if last == half_sections:
-        saved_inputs[last] = (plan_tokens, got_memory)
+        last_input = plan_tokens
     else:
-        saved_inputs[last] = (got_input, got_memory)
+        last_input = got_input
+    pullbacks[last] = jax.vjp(decoder_map, last_input, got_memory, gain_vector)[1]
 
     zero_gain = jnp.zeros_like(gain_vector)
     grads_out = jnp.zeros(act_shape, jnp.bfloat16)
@@ -164,10 +167,9 @@
     for tick in range(section_count):
         run = section_count - 1 - tick
         out_grad = cotangent.reshape(act_shape) if run == section_count - 1 else got_grad
-        layer_input, layer_memory = saved_inputs[run]
+        pull = pullbacks[run]
         mine = section_index == run
         if run >= half_sections:
-            _, pull = jax.vjp(decoder_map, layer_input, layer_memory, gain_vector)
             input_grad, memory_grad, gain_grad = pull(out_grad)
             if got_memory_grad is not None:
                 memory_grad = got_memory_grad + memory_grad
@@ -178,13 +180,12 @@
                     (input_grad, memory_grad), "section", run, run - 1
                 )
         else:
-            _, pull = jax.vjp(encoder_map, layer_input, gain_vector)
             input_grad, gain_grad = pull(out_grad)
             if run > 0:
                 got_grad = send_to(input_grad, "section", run, run - 1)
         grads_out = jnp.where(mine, input_grad, grads_out)
         gain_total = gain_total + jnp.where(mine, gain_grad, zero_gain)
-    gain_total = butterfly_sum(gain_total, "fsdp", fsdp_count)
+    gain_total = spread_sum(gain_total, "fsdp", fsdp_count)
     grads_out = grads_out.reshape(history.shape)
     return (grads_out[None], gain_total[None])
 

time: 137 us -> 147 us (1.073)
  starting transfers between devices: 20.2 us -> 35 us
  other arithmetic: 16.3 us -> 13.3 us
  waiting for transfers between devices: 79.7 us -> 77.5 us
    ppermute x4 -> x15, starting transfers between devices: 4.36 us -> 21.7 us  [spread_sum(): lax.ppermute(value, axis, [(j, j ^ shift) for j in range(size)])]
    another operation x12, other arithmetic: 9.6 us -> 3.91 us  [butterfly_gathers(): jnp.stack([low, high], axis=1).reshape((-1,) + held[which].shape[1:])]
    ppermute x4 -> x15, waiting for transfers between devices: 6.84 us -> 3.79 us  [spread_sum(): lax.ppermute(value, axis, [(j, j ^ shift) for j in range(size)])]
    ppermute x8, starting transfers between devices: 10.7 us -> 8.4 us  [butterfly_gathers(): lax.ppermute(held[which], axis, [(j, j ^ step) for j in range(size)])]
    reshape x2, other arithmetic: 0.1 us -> 1.68 us  [butterfly_gathers(): jnp.stack([low, high], axis=1).reshape((-1,) + held[which].shape[1:])]
  transfers between devices with their start and end apart: 14 -> 25, of which waited for: 12 -> 11; matrix products, arithmetic and copies ran while one was open for 15% -> 12% of each run, Pallas kernels for 0% -> 0%
where the time goes in v4:
time: 147 us
  waiting for transfers between devices  77.5 us (53%)
  starting transfers between devices  35 us (24%)
  other arithmetic  13.3 us (9%)
  matrix products  13.3 us (9%)
  local copies, waits for them, and re-layouts  6.08 us (4%)
    ppermute x8, waiting for transfers between devices, butterfly_gathers(): lax.ppermute(held[which], axis, [(j, j ^ step) for j in range(size)])  53.4 us
    ppermute x15, starting transfers between devices, spread_sum(): lax.ppermute(value, axis, [(j, j ^ shift) for j in range(size)])  21.7 us
    ppermute x2, waiting for transfers between devices, send_to(): return lax.ppermute(arrays, axis, [(source, target)])  20.2 us
    ppermute x8, starting transfers between devices, butterfly_gathers(): lax.ppermute(held[which], axis, [(j, j ^ step) for j in range(size)])  8.4 us
    dot_general x3, matrix products, attend_layer(): update = jnp.dot(mixed, output_weight, preferred_element_type=jnp.float32)  5.09 us
    ppermute x2, starting transfers between devices, send_to(): return lax.ppermute(arrays, axis, [(source, target)])  4.9 us
    dot_general x4, matrix products, attend_layer(): jnp.dot(normed_rows, query_weight, preferred_element_type=jnp.float32)  4.51 us
    another operation x12, other arithmetic, butterfly_gathers(): jnp.stack([low, high], axis=1).reshape((-1,) + held[which].shape[1:])  3.91 us
  transfers between devices with their start and end apart: 25, of which 11 were waited for; matrix products, arithmetic and copies ran while one was open for 12% of the time, Pallas kernels for 0%

profile of v4, /device:TPU:0, one launch (start us, length us, event | category | flops | bytes accessed | tf_op | source)
XLA Modules:
  0.0 146.6 jit_solution(12826277313518280364)
XLA Ops:
  0.7 4.1 %collective-permute-start.4 = (bf16[1,128,1024]{2,1,0:T(8,128)(2,1)}, bf16[1,128,1024]{2,1,0:T(8,128)(2,1)S(1)}, u32[]{:S(2)}, u32[]{:S(2)}) collective-permute-start(bf16[1,128,1024]{2,1,0:T(8,128)(2,1)} %param.12), channel_id=1, source_target_pairs={{0,8},{1,9},{2,10},{3,11},{4,12},{5,13},{6,14},{7,15},{8,0},{9,1},... | collective-permute-start | bytes 786440 | tf_op jit(solution)/shard_map/ppermute | solution.py:36
  4.8 1.2 fusion.37
  6.1 0.8 copy.75
  7.0 0.4 multiply_reduce_fusion
  7.4 16.0 %collective-permute-done.4 = bf16[1,128,1024]{2,1,0:T(8,128)(2,1)S(1)} collective-permute-done((bf16[1,128,1024]{2,1,0:T(8,128)(2,1)}, bf16[1,128,1024]{2,1,0:T(8,128)(2,1)S(1)}, u32[]{:S(2)}, u32[]{:S(2)}) %collective-permute-start.4) | collective-permute-done | bytes 262176 | tf_op jit(solution)/shard_map/ppermute | solution.py:36
  23.3 1.0 select_bitcast_fusion.11
  24.3 0.8 maximum_bitcast_fusion.1
  25.3 3.0 %collective-permute-done = bf16[1,64,2048]{2,1,0:T(8,128)(2,1)S(1)} collective-permute-done((bf16[1,64,2048]{2,1,0:T(8,128)(2,1)}, bf16[1,64,2048]{2,1,0:T(8,128)(2,1)S(1)}, u32[]{:S(2)}, u32[]{:S(2)}) %collective-permute-start) | collective-permute-done | bytes 262176 | tf_op jit(solution)/shard_map/ppermute | solution.py:36
  28.2 1.0 select_bitcast_fusion.13
  29.2 0.8 maximum_bitcast_fusion.2
  30.1 1.6 %collective-permute-start.1 = (bf16[2,64,2048]{2,1,0:T(8,128)(2,1)}, bf16[2,64,2048]{2,1,0:T(8,128)(2,1)S(1)}, u32[]{:S(2)}, u32[]{:S(2)}) collective-permute-start(bf16[2,64,2048]{2,1,0:T(8,128)(2,1)} %maximum_bitcast_fusion.2), channel_id=1, source_target_pairs={{0,2},{1,3},{2,0},{3,1},{4,6},{5,7},{6,4},{7,5},{8,10},{9,11},{10,... | collective-permute-start | bytes 1572872 | tf_op jit(solution)/shard_map/ppermute | solution.py:36
  31.7 7.7 %collective-permute-done.5 = bf16[2,128,1024]{2,1,0:T(8,128)(2,1)S(1)} collective-permute-done((bf16[2,128,1024]{2,1,0:T(8,128)(2,1)}, bf16[2,128,1024]{2,1,0:T(8,128)(2,1)S(1)}, u32[]{:S(2)}, u32[]{:S(2)}) %collective-permute-start.5) | collective-permute-done | bytes 524320 | tf_op jit(solution)/shard_map/ppermute | solution.py:36
  39.5 1.6 %collective-permute-start.6 = (bf16[4,128,1024]{2,1,0:T(8,128)(2,1)S(1)}, bf16[4,128,1024]{2,1,0:T(8,128)(2,1)S(1)}, u32[]{:S(2)}, u32[]{:S(2)}) collective-permute-start(bf16[4,128,1024]{2,1,0:T(8,128)(2,1)S(1)} %bitcast.299), channel_id=1, source_target_pairs={{0,2},{1,3},{2,0},{3,1},{4,6},{5,7},{6,4},{7,5},{8,10},{9,11},{10,... | collective-permute-start | bytes 3145736 | tf_op jit(solution)/shard_map/ppermute | solution.py:36
  41.2 3.9 %collective-permute-done.1 = bf16[2,64,2048]{2,1,0:T(8,128)(2,1)S(1)} collective-permute-done((bf16[2,64,2048]{2,1,0:T(8,128)(2,1)}, bf16[2,64,2048]{2,1,0:T(8,128)(2,1)S(1)}, u32[]{:S(2)}, u32[]{:S(2)}) %collective-permute-start.1) | collective-permute-done | bytes 524320 | tf_op jit(solution)/shard_map/ppermute | solution.py:36
  45.2 0.8 collective-permute-start.2
  46.0 19.7 %collective-permute-done.6 = bf16[4,128,1024]{2,1,0:T(8,128)(2,1)S(1)} collective-permute-done((bf16[4,128,1024]{2,1,0:T(8,128)(2,1)S(1)}, bf16[4,128,1024]{2,1,0:T(8,128)(2,1)S(1)}, u32[]{:S(2)}, u32[]{:S(2)}) %collective-permute-start.6) | collective-permute-done | bytes 1048608 | tf_op jit(solution)/shard_map/ppermute | solution.py:36
  66.5 1.1 collective-permute-done.2
  68.3 0.5 copy-done.6
  69.3 1.3 collective-permute-done.7
  71.4 0.6 copy.79
  72.1 0.7 fusion.21
  72.8 0.8 collective-permute-done.3
  74.5 0.6 copy.73
  75.7 0.5 copy-done.8
  76.2 1.6 %fusion = bf16[4,32,2048]{2,1,0:T(8,128)(2,1)} fusion(bf16[1024,2048,1]{1,0,2:T(8,128)(2,1)S(1)} %bitcast.289, bf16[4,1,32,2048]{3,2,1,0:T(8,128)(2,1)S(1)} %copy-done.6, bf16[4,8,4,8,128]{4,3,2,1,0:T(8,128)(2,1)S(1)} %fusion.23), kind=kOutput, calls=%fused_computation.4 | convolution fusion | flops 537657344 | bytes 5505024 | tf_op jit(solution)/shard_map/jvp()/dot_general | solution.py:95
  77.8 3.3 %collective-permute-start.8 = (bf16[4,32,2048]{2,1,0:T(8,128)(2,1)}, bf16[4,32,2048]{2,1,0:T(8,128)(2,1)S(1)}, u32[]{:S(2)}, u32[]{:S(2)}) collective-permute-start(bf16[4,32,2048]{2,1,0:T(8,128)(2,1)} %fusion), channel_id=1, source_target_pairs={{0,16},{1,17},{2,18},{3,19},{4,20},{5,21},{6,22},{7,23},{8,24},{9,... | collective-permute-start | bytes 1572872 | tf_op jit(solution)/shard_map/ppermute | solution.py:15
  81.2 2.0 %fusion.19 = bf16[128,1024]{0,1:T(8,128)(2,1)} fusion(bf16[1024,2048]{1,0:T(8,128)(2,1)S(1)} %bitcast.290, bf16[128,2048]{1,0:T(8,128)(2,1)S(1)} %bitcast.313), kind=kOutput, calls=%fused_computation.61 | convolution fusion | flops 537001984 | bytes 4980736 | tf_op jit(solution)/shard_map/transpose(jvp())/dot_general | solution.py:95
  83.1 1.1 copy.74
  84.3 8.4 %collective-permute-done.8 = bf16[4,32,2048]{2,1,0:T(8,128)(2,1)S(1)} collective-permute-done((bf16[4,32,2048]{2,1,0:T(8,128)(2,1)}, bf16[4,32,2048]{2,1,0:T(8,128)(2,1)S(1)}, u32[]{:S(2)}, u32[]{:S(2)}) %collective-permute-start.8) | collective-permute-done | bytes 524320 | tf_op jit(solution)/shard_map/ppermute | solution.py:15
  93.2 0.8 fusion.20
  95.3 0.6 fusion.31
  96.2 1.6 %collective-permute-start.9 = (bf16[4,32,2048]{2,1,0:T(8,128)(2,1)S(1)}, bf16[4,32,2048]{2,1,0:T(8,128)(2,1)S(1)}, u32[]{:S(2)}, u32[]{:S(2)}) collective-permute-start(bf16[4,32,2048]{2,1,0:T(8,128)(2,1)S(1)} %fusion.44), channel_id=1, source_target_pairs={{16,0},{17,1},{18,2},{19,3},{20,4},{21,5},{22,6},{23,7},{24,8},{25... | collective-permute-start | bytes 1572872 | tf_op jit(solution)/shard_map/ppermute | solution.py:15
  98.3 1.5 %convolution_convert_fusion = bf16[128,2048]{1,0:T(8,128)(2,1)S(1)} fusion(bf16[2048,1024]{1,0:T(8,128)(2,1)S(1)} %bitcast.287, bf16[16,8,8,128]{3,2,1,0:T(8,128)(2,1)S(1)} %bitcast.310), kind=kOutput, calls=%fused_computation.5 | convolution fusion | flops 537133056 | bytes 4980736 | tf_op jit(solution)/shard_map/transpose(jvp())/dot_general | solution.py:84
  99.8 11.8 %collective-permute-done.9 = bf16[4,32,2048]{2,1,0:T(8,128)(2,1)S(1)} collective-permute-done((bf16[4,32,2048]{2,1,0:T(8,128)(2,1)S(1)}, bf16[4,32,2048]{2,1,0:T(8,128)(2,1)S(1)}, u32[]{:S(2)}, u32[]{:S(2)}) %collective-permute-start.9) | collective-permute-done | bytes 524320 | tf_op jit(solution)/shard_map/ppermute | solution.py:15
  111.6 1.5 %fusion.22 = bf16[16,8,8,128]{3,1,2,0:T(8,128)(2,1)S(1)} fusion(bf16[128,2048]{1,0:T(8,128)(2,1)S(1)} %bitcast.304, bf16[1024,2048]{1,0:T(8,128)(2,1)S(1)} %bitcast.291), kind=kOutput, calls=%fused_computation.64 | convolution fusion | flops 537001984 | bytes 4980736 | tf_op jit(solution)/shard_map/transpose(jvp())/dot_general | solution.py:95
  114.6 1.5 %convolution_convert_fusion.1 = bf16[128,2048]{1,0:T(8,128)(2,1)S(1)} fusion(bf16[2048,1024]{1,0:T(8,128)(2,1)S(1)} %bitcast.288, bf16[16,8,8,128]{3,2,1,0:T(8,128)(2,1)S(1)} %bitcast.309), kind=kOutput, calls=%fused_computation.6 | convolution fusion | flops 537133056 | bytes 4980736 | tf_op jit(solution)/shard_map/transpose(jvp())/dot_general | solution.py:84
  116.2 1.3 fusion.36
  117.7 1.6 %collective-permute-start.11 = (f32[2048]{0:T(1024)S(1)}, f32[2048]{0:T(1024)S(1)}, u32[]{:S(2)}, u32[]{:S(2)}) collective-permute-start(f32[2048]{0:T(1024)S(1)} %select_add_fusion), channel_id=1, source_target_pairs={{0,2},{1,3},{2,0},{3,1},{4,6},{5,7},{6,4},{7,5},{8,10},{9,11},{10,... | collective-permute-start | bytes 24584 | tf_op jit(solution)/shard_map/ppermute | solution.py:60
  119.5 1.8 %collective-permute-start.13 = (f32[2048]{0:T(1024)S(1)}, f32[2048]{0:T(1024)S(1)}, u32[]{:S(2)}, u32[]{:S(2)}) collective-permute-start(f32[2048]{0:T(1024)S(1)} %select_add_fusion), channel_id=1, source_target_pairs={{0,4},{1,5},{2,6},{3,7},{4,0},{5,1},{6,2},{7,3},{8,12},{9,13},{10,... | collective-permute-start | bytes 24584 | tf_op jit(solution)/shard_map/ppermute | solution.py:60
  121.4 2.7 %collective-permute-start.15 = (f32[2048]{0:T(1024)S(1)}, f32[2048]{0:T(1024)S(1)}, u32[]{:S(2)}, u32[]{:S(2)}) collective-permute-start(f32[2048]{0:T(1024)S(1)} %select_add_fusion), channel_id=1, source_target_pairs={{0,6},{1,7},{2,4},{3,5},{4,2},{5,3},{6,0},{7,1},{8,14},{9,15},{10,... | collective-permute-start | bytes 24584 | tf_op jit(solution)/shard_map/ppermute | solution.py:60
  124.2 3.3 %collective-permute-start.17 = (f32[2048]{0:T(1024)S(1)}, f32[2048]{0:T(1024)S(1)}, u32[]{:S(2)}, u32[]{:S(2)}) collective-permute-start(f32[2048]{0:T(1024)S(1)} %select_add_fusion), channel_id=1, source_target_pairs={{0,8},{1,9},{2,10},{3,11},{4,12},{5,13},{6,14},{7,15},{8,0},{9,1},... | collective-permute-start | bytes 24584 | tf_op jit(solution)/shard_map/ppermute | solution.py:60
  127.5 3.5 %collective-permute-start.19 = (f32[2048]{0:T(1024)S(1)}, f32[2048]{0:T(1024)S(1)}, u32[]{:S(2)}, u32[]{:S(2)}) collective-permute-start(f32[2048]{0:T(1024)S(1)} %select_add_fusion), channel_id=1, source_target_pairs={{0,10},{1,11},{2,8},{3,9},{4,14},{5,15},{6,12},{7,13},{8,2},{9,3},... | collective-permute-start | bytes 24584 | tf_op jit(solution)/shard_map/ppermute | solution.py:60
  131.1 3.7 %collective-permute-start.21 = (f32[2048]{0:T(1024)S(1)}, f32[2048]{0:T(1024)S(1)}, u32[]{:S(2)}, u32[]{:S(2)}) collective-permute-start(f32[2048]{0:T(1024)S(1)} %select_add_fusion), channel_id=1, source_target_pairs={{0,12},{1,13},{2,14},{3,15},{4,8},{5,9},{6,10},{7,11},{8,4},{9,5},... | collective-permute-start | bytes 24584 | tf_op jit(solution)/shard_map/ppermute | solution.py:60
  134.9 4.4 %collective-permute-start.23 = (f32[2048]{0:T(1024)S(1)}, f32[2048]{0:T(1024)S(1)}, u32[]{:S(2)}, u32[]{:S(2)}) collective-permute-start(f32[2048]{0:T(1024)S(1)} %select_add_fusion), channel_id=1, source_target_pairs={{0,14},{1,15},{2,12},{3,13},{4,10},{5,11},{6,8},{7,9},{8,6},{9,7},... | collective-permute-start | bytes 24584 | tf_op jit(solution)/shard_map/ppermute | solution.py:60
  139.4 1.9 %fusion.54 = bf16[1,4,1,32,2048]{4,3,2,1,0:T(8,128)(2,1)} fusion(f32[4,32,2048]{2,1,0:T(8,128)S(1)} %get-tuple-element.45, bf16[4,32,2048]{2,1,0:T(8,128)(2,1)S(1)} %collective-permute-done.9, bf16[4,32,1024]{2,1,0:T(8,128)(2,1)S(1)} %bitcast.303, bf16[4,32,1024]{2,1,0:T(8,128)(2,1)S(1)} %bitcast.301, bf16[4,1,32,2048]{3,2,1,0:T(8,128)(2,1)S(1)} %copy-done.7, ...), kind=kLoop, calls=%fused_computation.106 | loop fusion | flops 8912896 | bytes 4729346
  141.3 3.8 %collective-permute-done.24 = f32[2048]{0:T(1024)S(1)} collective-permute-done((f32[2048]{0:T(1024)S(1)}, f32[2048]{0:T(1024)S(1)}, u32[]{:S(2)}, u32[]{:S(2)}) %collective-permute-start.24) | collective-permute-done | bytes 8224 | tf_op jit(solution)/shard_map/ppermute | solution.py:60
  145.3 0.6 gather_fusion
  145.9 0.7 select_reduce_fusion
  (111 shorter events, 9.9 us)
Async XLA Ops:
  0.6 6.3 %copy-start = (bf16[16,2048]{1,0:T(8,128)(2,1)S(1)}, bf16[16,2048]{1,0:T(8,128)(2,1)}, u32[]{:S(2)}) copy-start(bf16[16,2048]{1,0:T(8,128)(2,1)} %param.11) | copy-start | bytes 196612
  0.6 31.0 %copy-start.13 = (s32[4,1,32]{2,1,0:T(1,128)S(1)}, s32[4,1,32]{2,1,0:T(1,128)}, u32[]{:S(2)}) copy-start(s32[4,1,32]{2,1,0:T(1,128)} %param.9) | copy-start | bytes 1540
  0.7 22.7 %collective-permute-start.4 = (bf16[1,128,1024]{2,1,0:T(8,128)(2,1)}, bf16[1,128,1024]{2,1,0:T(8,128)(2,1)S(1)}, u32[]{:S(2)}, u32[]{:S(2)}) collective-permute-start(bf16[1,128,1024]{2,1,0:T(8,128)(2,1)} %param.12), channel_id=1, source_target_pairs={{0,8},{1,9},{2,10},{3,11},{4,12},{5,13},{6,14},{7,15},{8,0},{9,1},... | collective-permute-start | bytes 786440 | tf_op jit(solution)/shard_map/ppermute | solution.py:36
  4.8 23.5 %collective-permute-start = (bf16[1,64,2048]{2,1,0:T(8,128)(2,1)}, bf16[1,64,2048]{2,1,0:T(8,128)(2,1)S(1)}, u32[]{:S(2)}, u32[]{:S(2)}) collective-permute-start(bf16[1,64,2048]{2,1,0:T(8,128)(2,1)} %param.13), channel_id=1, source_target_pairs={{0,8},{1,9},{2,10},{3,11},{4,12},{5,13},{6,14},{7,15},{8,0},{9,1},... | collective-permute-start | bytes 786440 | tf_op jit(solution)/shard_map/ppermute | solution.py:36
  25.2 14.2 %collective-permute-start.5 = (bf16[2,128,1024]{2,1,0:T(8,128)(2,1)}, bf16[2,128,1024]{2,1,0:T(8,128)(2,1)S(1)}, u32[]{:S(2)}, u32[]{:S(2)}) collective-permute-start(bf16[2,128,1024]{2,1,0:T(8,128)(2,1)} %maximum_bitcast_fusion.1), channel_id=1, source_target_pairs={{0,4},{1,5},{2,6},{3,7},{4,0},{5,1},{6,2},{7,3},{8,12},{9,13},{10,... | collective-permute-start | bytes 1572872 | tf_op jit(solution)/shard_map/ppermute | solution.py:36
  30.1 15.0 %collective-permute-start.1 = (bf16[2,64,2048]{2,1,0:T(8,128)(2,1)}, bf16[2,64,2048]{2,1,0:T(8,128)(2,1)S(1)}, u32[]{:S(2)}, u32[]{:S(2)}) collective-permute-start(bf16[2,64,2048]{2,1,0:T(8,128)(2,1)} %maximum_bitcast_fusion.2), channel_id=1, source_target_pairs={{0,2},{1,3},{2,0},{3,1},{4,6},{5,7},{6,4},{7,5},{8,10},{9,11},{10,... | collective-permute-start | bytes 1572872 | tf_op jit(solution)/shard_map/ppermute | solution.py:36
  39.5 26.2 %collective-permute-start.6 = (bf16[4,128,1024]{2,1,0:T(8,128)(2,1)S(1)}, bf16[4,128,1024]{2,1,0:T(8,128)(2,1)S(1)}, u32[]{:S(2)}, u32[]{:S(2)}) collective-permute-start(bf16[4,128,1024]{2,1,0:T(8,128)(2,1)S(1)} %bitcast.299), channel_id=1, source_target_pairs={{0,2},{1,3},{2,0},{3,1},{4,6},{5,7},{6,4},{7,5},{8,10},{9,11},{10,... | collective-permute-start | bytes 3145736 | tf_op jit(solution)/shard_map/ppermute | solution.py:36
  45.2 22.3 %collective-permute-start.2 = (bf16[4,64,2048]{2,1,0:T(8,128)(2,1)S(1)}, bf16[4,64,2048]{2,1,0:T(8,128)(2,1)S(1)}, u32[]{:S(2)}, u32[]{:S(2)}) collective-permute-start(bf16[4,64,2048]{2,1,0:T(8,128)(2,1)S(1)} %bitcast.298), channel_id=1, source_target_pairs={{0,4},{1,5},{2,6},{3,7},{4,0},{5,1},{6,2},{7,3},{8,12},{9,13},{10,... | collective-permute-start | bytes 3145736 | tf_op jit(solution)/shard_map/ppermute | solution.py:36
  66.4 4.2 %collective-permute-start.7 = (bf16[8,128,1024]{2,1,0:T(8,128)(2,1)S(1)}, bf16[8,128,1024]{2,1,0:T(8,128)(2,1)S(1)}, u32[]{:S(2)}, u32[]{:S(2)}) collective-permute-start(bf16[8,128,1024]{2,1,0:T(8,128)(2,1)S(1)} %bitcast.292), channel_id=1, source_target_pairs={{0,1},{1,0},{2,3},{3,2},{4,5},{5,4},{6,7},{7,6},{8,9},{9,8},{10,11... | collective-permute-start | bytes 6291464 | tf_op jit(solution)/shard_map/ppermute | solution.py:36
  67.8 1.0 copy-start.6
  67.8 1.0 copy-start.10
  68.3 5.4 %collective-permute-start.3 = (bf16[8,64,2048]{2,1,0:T(8,128)(2,1)S(1)}, bf16[8,64,2048]{2,1,0:T(8,128)(2,1)S(1)}, u32[]{:S(2)}, u32[]{:S(2)}) collective-permute-start(bf16[8,64,2048]{2,1,0:T(8,128)(2,1)S(1)} %bitcast.293), channel_id=1, source_target_pairs={{0,1},{1,0},{2,3},{3,2},{4,5},{5,4},{6,7},{7,6},{8,9},{9,8},{10,11... | collective-permute-start | bytes 6291464 | tf_op jit(solution)/shard_map/ppermute | solution.py:36
  69.1 6.0 %copy-start.11 = (bf16[4,4,8,8,128]{4,3,2,1,0:T(8,128)(2,1)}, bf16[4,4,8,8,128]{4,3,2,1,0:T(8,128)(2,1)S(1)}, u32[]{:S(2)}) copy-start(bf16[4,4,8,8,128]{4,3,2,1,0:T(8,128)(2,1)S(1)} %get-tuple-element.32) | copy-start | bytes 786436
  72.0 2.0 %copy-start.2 = (bf16[8,2,128,1024]{3,2,1,0:T(8,128)(2,1)}, bf16[8,2,128,1024]{3,2,1,0:T(8,128)(2,1)S(1)}, u32[]{:S(2)}) copy-start(bf16[8,2,128,1024]{3,2,1,0:T(8,128)(2,1)S(1)} %copy.79) | copy-start | bytes 12582916
  75.0 6.1 %copy-start.4 = (bf16[2,2,2,2,64,2048]{5,4,3,2,1,0:T(8,128)(2,1)}, bf16[2,2,2,2,64,2048]{5,4,3,2,1,0:T(8,128)(2,1)S(1)}, u32[]{:S(2)}) copy-start(bf16[2,2,2,2,64,2048]{5,4,3,2,1,0:T(8,128)(2,1)S(1)} %copy.73) | copy-start | bytes 12582916
  75.1 6.1 %copy-start.7 = (bf16[4,1,32,2048]{3,2,1,0:T(8,128)(2,1)S(1)}, bf16[4,1,32,2048]{3,2,1,0:T(8,128)(2,1)}, u32[]{:S(2)}) copy-start(bf16[4,1,32,2048]{3,2,1,0:T(8,128)(2,1)} %param.15) | copy-start | bytes 1572868
  75.4 0.8 copy-start.8
  77.8 14.9 %collective-permute-start.8 = (bf16[4,32,2048]{2,1,0:T(8,128)(2,1)}, bf16[4,32,2048]{2,1,0:T(8,128)(2,1)S(1)}, u32[]{:S(2)}, u32[]{:S(2)}) collective-permute-start(bf16[4,32,2048]{2,1,0:T(8,128)(2,1)} %fusion), channel_id=1, source_target_pairs={{0,16},{1,17},{2,18},{3,19},{4,20},{5,21},{6,22},{7,23},{8,24},{9,... | collective-permute-start | bytes 1572872 | tf_op jit(solution)/shard_map/ppermute | solution.py:15
  84.2 9.0 %copy-start.3 = (bf16[8,2,128,1024]{3,2,1,0:T(8,128)(2,1)S(1)}, bf16[8,2,128,1024]{3,2,1,0:T(8,128)(2,1)}, u32[]{:S(2)}) copy-start(bf16[8,2,128,1024]{3,2,1,0:T(8,128)(2,1)} %copy-done.2) | copy-start | bytes 12582916
  96.2 15.4 %copy-start.5 = (bf16[2,2,2,2,64,2048]{5,4,3,2,1,0:T(8,128)(2,1)S(1)}, bf16[2,2,2,2,64,2048]{5,4,3,2,1,0:T(8,128)(2,1)}, u32[]{:S(2)}) copy-start(bf16[2,2,2,2,64,2048]{5,4,3,2,1,0:T(8,128)(2,1)} %copy-done.4) | copy-start | bytes 12582916
  96.2 15.4 %collective-permute-start.9 = (bf16[4,32,2048]{2,1,0:T(8,128)(2,1)S(1)}, bf16[4,32,2048]{2,1,0:T(8,128)(2,1)S(1)}, u32[]{:S(2)}, u32[]{:S(2)}) collective-permute-start(bf16[4,32,2048]{2,1,0:T(8,128)(2,1)S(1)} %fusion.44), channel_id=1, source_target_pairs={{16,0},{17,1},{18,2},{19,3},{20,4},{21,5},{22,6},{23,7},{24,8},{25... | collective-permute-start | bytes 1572872 | tf_op jit(solution)/shard_map/ppermute | solution.py:15
  98.2 15.0 %copy-start.9 = (f32[4,8,32,32]{2,3,1,0:T(8,128)S(1)}, f32[4,8,32,32]{2,3,1,0:T(8,128)}, u32[]{:S(2)}) copy-start(f32[4,8,32,32]{2,3,1,0:T(8,128)} %copy-done.8) | copy-start | bytes 393220
  111.6 2.2 %copy-start.12 = (bf16[4,4,8,8,128]{4,3,2,1,0:T(8,128)(2,1)S(1)}, bf16[4,4,8,8,128]{4,3,2,1,0:T(8,128)(2,1)}, u32[]{:S(2)}) copy-start(bf16[4,4,8,8,128]{4,3,2,1,0:T(8,128)(2,1)} %copy-done.11) | copy-start | bytes 786436
  116.2 30.3 %copy-start.1 = (bf16[16,2048]{1,0:T(8,128)(2,1)S(1)}, bf16[16,2048]{1,0:T(8,128)(2,1)}, u32[]{:S(2)}) copy-start(bf16[16,2048]{1,0:T(8,128)(2,1)} %param.11) | copy-start | bytes 196612
  117.6 3.8 %collective-permute-start.10 = (f32[2048]{0:T(1024)S(1)}, f32[2048]{0:T(1024)S(1)}, u32[]{:S(2)}, u32[]{:S(2)}) collective-permute-start(f32[2048]{0:T(1024)S(1)} %select_add_fusion), channel_id=1, source_target_pairs={{0,1},{1,0},{2,3},{3,2},{4,5},{5,4},{6,7},{7,6},{8,9},{9,8},{10,11... | collective-permute-start | bytes 24584 | tf_op jit(solution)/shard_map/ppermute | solution.py:60
  117.7 6.4 %collective-permute-start.11 = (f32[2048]{0:T(1024)S(1)}, f32[2048]{0:T(1024)S(1)}, u32[]{:S(2)}, u32[]{:S(2)}) collective-permute-start(f32[2048]{0:T(1024)S(1)} %select_add_fusion), channel_id=1, source_target_pairs={{0,2},{1,3},{2,0},{3,1},{4,6},{5,7},{6,4},{7,5},{8,10},{9,11},{10,... | collective-permute-start | bytes 24584 | tf_op jit(solution)/shard_map/ppermute | solution.py:60
  119.3 5.0 %collective-permute-start.12 = (f32[2048]{0:T(1024)S(1)}, f32[2048]{0:T(1024)S(1)}, u32[]{:S(2)}, u32[]{:S(2)}) collective-permute-start(f32[2048]{0:T(1024)S(1)} %select_add_fusion), channel_id=1, source_target_pairs={{0,3},{1,2},{2,1},{3,0},{4,7},{5,6},{6,5},{7,4},{8,11},{9,10},{10,... | collective-permute-start | bytes 24584 | tf_op jit(solution)/shard_map/ppermute | solution.py:60
  119.5 8.0 %collective-permute-start.13 = (f32[2048]{0:T(1024)S(1)}, f32[2048]{0:T(1024)S(1)}, u32[]{:S(2)}, u32[]{:S(2)}) collective-permute-start(f32[2048]{0:T(1024)S(1)} %select_add_fusion), channel_id=1, source_target_pairs={{0,4},{1,5},{2,6},{3,7},{4,0},{5,1},{6,2},{7,3},{8,12},{9,13},{10,... | collective-permute-start | bytes 24584 | tf_op jit(solution)/shard_map/ppermute | solution.py:60
  121.4 6.2 %collective-permute-start.14 = (f32[2048]{0:T(1024)S(1)}, f32[2048]{0:T(1024)S(1)}, u32[]{:S(2)}, u32[]{:S(2)}) collective-permute-start(f32[2048]{0:T(1024)S(1)} %select_add_fusion), channel_id=1, source_target_pairs={{0,5},{1,4},{2,7},{3,6},{4,1},{5,0},{6,3},{7,2},{8,13},{9,12},{10,... | collective-permute-start | bytes 24584 | tf_op jit(solution)/shard_map/ppermute | solution.py:60
  121.4 9.6 %collective-permute-start.15 = (f32[2048]{0:T(1024)S(1)}, f32[2048]{0:T(1024)S(1)}, u32[]{:S(2)}, u32[]{:S(2)}) collective-permute-start(f32[2048]{0:T(1024)S(1)} %select_add_fusion), channel_id=1, source_target_pairs={{0,6},{1,7},{2,4},{3,5},{4,2},{5,3},{6,0},{7,1},{8,14},{9,15},{10,... | collective-permute-start | bytes 24584 | tf_op jit(solution)/shard_map/ppermute | solution.py:60
  124.1 7.0 %collective-permute-start.16 = (f32[2048]{0:T(1024)S(1)}, f32[2048]{0:T(1024)S(1)}, u32[]{:S(2)}, u32[]{:S(2)}) collective-permute-start(f32[2048]{0:T(1024)S(1)} %select_add_fusion), channel_id=1, source_target_pairs={{0,7},{1,6},{2,5},{3,4},{4,3},{5,2},{6,1},{7,0},{8,15},{9,14},{10,... | collective-permute-start | bytes 24584 | tf_op jit(solution)/shard_map/ppermute | solution.py:60
  124.2 10.6 %collective-permute-start.17 = (f32[2048]{0:T(1024)S(1)}, f32[2048]{0:T(1024)S(1)}, u32[]{:S(2)}, u32[]{:S(2)}) collective-permute-start(f32[2048]{0:T(1024)S(1)} %select_add_fusion), channel_id=1, source_target_pairs={{0,8},{1,9},{2,10},{3,11},{4,12},{5,13},{6,14},{7,15},{8,0},{9,1},... | collective-permute-start | bytes 24584 | tf_op jit(solution)/shard_map/ppermute | solution.py:60
  127.5 7.4 %collective-permute-start.18 = (f32[2048]{0:T(1024)S(1)}, f32[2048]{0:T(1024)S(1)}, u32[]{:S(2)}, u32[]{:S(2)}) collective-permute-start(f32[2048]{0:T(1024)S(1)} %select_add_fusion), channel_id=1, source_target_pairs={{0,9},{1,8},{2,11},{3,10},{4,13},{5,12},{6,15},{7,14},{8,1},{9,0},... | collective-permute-start | bytes 24584 | tf_op jit(solution)/shard_map/ppermute | solution.py:60
  127.5 11.8 %collective-permute-start.19 = (f32[2048]{0:T(1024)S(1)}, f32[2048]{0:T(1024)S(1)}, u32[]{:S(2)}, u32[]{:S(2)}) collective-permute-start(f32[2048]{0:T(1024)S(1)} %select_add_fusion), channel_id=1, source_target_pairs={{0,10},{1,11},{2,8},{3,9},{4,14},{5,15},{6,12},{7,13},{8,2},{9,3},... | collective-permute-start | bytes 24584 | tf_op jit(solution)/shard_map/ppermute | solution.py:60
  131.0 10.3 %collective-permute-start.20 = (f32[2048]{0:T(1024)S(1)}, f32[2048]{0:T(1024)S(1)}, u32[]{:S(2)}, u32[]{:S(2)}) collective-permute-start(f32[2048]{0:T(1024)S(1)} %select_add_fusion), channel_id=1, source_target_pairs={{0,11},{1,10},{2,9},{3,8},{4,15},{5,14},{6,13},{7,12},{8,3},{9,2},... | collective-permute-start | bytes 24584 | tf_op jit(solution)/shard_map/ppermute | solution.py:60
  131.1 10.2 %collective-permute-start.21 = (f32[2048]{0:T(1024)S(1)}, f32[2048]{0:T(1024)S(1)}, u32[]{:S(2)}, u32[]{:S(2)}) collective-permute-start(f32[2048]{0:T(1024)S(1)} %select_add_fusion), channel_id=1, source_target_pairs={{0,12},{1,13},{2,14},{3,15},{4,8},{5,9},{6,10},{7,11},{8,4},{9,5},... | collective-permute-start | bytes 24584 | tf_op jit(solution)/shard_map/ppermute | solution.py:60
  134.8 6.4 %collective-permute-start.22 = (f32[2048]{0:T(1024)S(1)}, f32[2048]{0:T(1024)S(1)}, u32[]{:S(2)}, u32[]{:S(2)}) collective-permute-start(f32[2048]{0:T(1024)S(1)} %select_add_fusion), channel_id=1, source_target_pairs={{0,13},{1,12},{2,15},{3,14},{4,9},{5,8},{6,11},{7,10},{8,5},{9,4},... | collective-permute-start | bytes 24584 | tf_op jit(solution)/shard_map/ppermute | solution.py:60
  134.9 6.4 %collective-permute-start.23 = (f32[2048]{0:T(1024)S(1)}, f32[2048]{0:T(1024)S(1)}, u32[]{:S(2)}, u32[]{:S(2)}) collective-permute-start(f32[2048]{0:T(1024)S(1)} %select_add_fusion), channel_id=1, source_target_pairs={{0,14},{1,15},{2,12},{3,13},{4,10},{5,11},{6,8},{7,9},{8,6},{9,7},... | collective-permute-start | bytes 24584 | tf_op jit(solution)/shard_map/ppermute | solution.py:60
  139.3 5.8 %collective-permute-start.24 = (f32[2048]{0:T(1024)S(1)}, f32[2048]{0:T(1024)S(1)}, u32[]{:S(2)}, u32[]{:S(2)}) collective-permute-start(f32[2048]{0:T(1024)S(1)} %select_add_fusion), channel_id=1, source_target_pairs={{0,15},{1,14},{2,13},{3,12},{4,11},{5,10},{6,9},{7,8},{8,7},{9,6},... | collective-permute-start | bytes 24584 | tf_op jit(solution)/shard_map/ppermute | solution.py:60

commit v5 on v4

--- a/solution.py
+++ b/solution.py
@@ -28,40 +28,49 @@
 
 
 def butterfly_gathers(shards, orders, axis, size):
-    index = lax.axis_index(axis)
-    held = [shard for shard in shards]
+    slots = [{0: shard[0]} for shard in shards]
     for level in range(len(orders[0])):
         for which, order in enumerate(orders):
             step = order[level]
-            other = lax.ppermute(held[which], axis, [(j, j ^ step) for j in range(size)])
-            upper = ((index // step) % 2) == 1
-            low = jnp.where(upper, other, held[which])
-            high = jnp.where(upper, held[which], other)
-            held[which] = jnp.stack([low, high], axis=1).reshape(
-                (-1,) + held[which].shape[1:]
+            offsets = sorted(slots[which])
+            got = lax.ppermute(
+                tuple(slots[which][offset] for offset in offsets),
+                axis,
+                [(j, j ^ step) for j in range(size)],
             )
-    results = []
-    for which, order in enumerate(orders):
-        block_rows, width = held[which].shape[1:]
-        wanted = sorted(order, reverse=True)
-        if order != wanted:
-            split = held[which].reshape(tuple(2 for _ in order) + (block_rows, width))
-            axes = tuple(order.index(value) for value in wanted) + (len(order), len(order) + 1)
-            held[which] = jnp.transpose(split, axes)
-        results.append(held[which].reshape(size * block_rows, width))
-    return results
-
-
-def spread_sum(value, axis, size):
+            for offset, block in zip(offsets, got):
+                slots[which][offset ^ step] = block
+    return [
+        jnp.concatenate([held[offset] for offset in range(size)], axis=0) for held in slots
+    ]
+
+
+def butterfly_sum(value, axis, size):
     if size & (size - 1):
         return lax.psum(value, axis)
-    index = lax.axis_index(axis)
-    received = [value] + [
-        lax.ppermute(value, axis, [(j, j ^ shift) for j in range(size)]) for shift in range(1, size)
-    ]
-    by_shift = jnp.stack(received, axis=0)
-    by_source = jnp.take(by_shift, jnp.arange(size, dtype=jnp.int32) ^ index, axis=0)
-    return jnp.sum(by_source, axis=0)
+    step = 1
+    while step < size:
+        value = value + lax.ppermute(value, axis, [(j, j ^ step) for j in range(size)])
+        step *= 2
+    return value
+
+
+@jax.custom_vjp
+def xor_blocks(matrix, index):
+    count = index.shape[0]
+    blocks = matrix.reshape(matrix.shape[0], count, matrix.shape[1] // count)
+    return jnp.take(blocks, index, axis=1).reshape(matrix.shape)
+
+
+def xor_blocks_fwd(matrix, index):
+    return xor_blocks(matrix, index), index
+
+
+def xor_blocks_bwd(index, grad):
+    return xor_blocks(grad, index), None
+
+
+xor_blocks.defvjp(xor_blocks_fwd, xor_blocks_bwd)
 
 
 def rms_scale(inputs, gain_vector):
@@ -72,7 +81,9 @@
     )
 
 
-def attend_layer(section_input, source, key_mask, query_weight, output_weight, gain_vector):
+def attend_layer(
+    section_input, source, key_mask, query_weight, output_weight, gain_vector, block_index
+):
     series_count, seq_length, model_width = section_input.shape
     half_width = model_width // 2
     head_dim = half_width // HEADS
@@ -81,6 +92,8 @@
     normed = rms_scale(input_wide, gain_vector)
     normed_source = rms_scale(source.astype(jnp.float32), gain_vector)
     normed_rows = normed.astype(jnp.bfloat16).reshape(series_count * seq_length, model_width)
+    if block_index is not None:
+        normed_rows = xor_blocks(normed_rows, block_index)
     query_flat = jnp.dot(normed_rows, query_weight, preferred_element_type=jnp.float32)
     queries = query_flat.astype(jnp.bfloat16).reshape(head_shape)
     key_rows = normed_source[..., :half_width].astype(jnp.bfloat16).reshape(head_shape)
@@ -92,6 +105,8 @@
     probs = (raised / jnp.sum(raised, axis=-1, keepdims=True)).astype(jnp.bfloat16)
     mixed = jnp.einsum("bhqk,bkhd->bqhd", probs, value_rows, preferred_element_type=jnp.float32)
     mixed = mixed.astype(jnp.bfloat16).reshape(series_count * seq_length, half_width)
+    if block_index is not None:
+        mixed = xor_blocks(mixed, block_index)
     update = jnp.dot(mixed, output_weight, preferred_element_type=jnp.float32)
     return (input_wide + update.reshape(series_count, seq_length, model_width)).astype(jnp.bfloat16)
 
@@ -105,9 +120,11 @@
     act_shape = (rows, seq_length, model_width)
     fsdp_count = lax.axis_size("fsdp")
     if fsdp_count & (fsdp_count - 1):
+        block_index = None
         query_weight = lax.all_gather(query_weights, "fsdp", axis=1, tiled=True)[0]
         output_weight = lax.all_gather(output_weights, "fsdp", axis=1, tiled=True)[0]
     else:
+        block_index = jnp.arange(fsdp_count, dtype=jnp.int32) ^ lax.axis_index("fsdp")
         query_weight, output_weight = butterfly_gathers(
             [query_weights, output_weights], exchange_orders(fsdp_count), "fsdp", fsdp_count
         )
@@ -123,12 +140,14 @@
 
     def encoder_map(layer_input, layer_gain):
         return attend_layer(
-            layer_input, layer_input, key_mask, query_weight, output_weight, layer_gain
+            layer_input, layer_input, key_mask, query_weight, output_weight, layer_gain,
+            block_index,
         )
 
     def decoder_map(layer_input, layer_memory, layer_gain):
         return attend_layer(
-            layer_input, layer_memory, key_mask, query_weight, output_weight, layer_gain
+            layer_input, layer_memory, key_mask, query_weight, output_weight, layer_gain,
+            block_index,
         )
 
     pullbacks = {}
@@ -185,7 +204,7 @@
                 got_grad = send_to(input_grad, "section", run, run - 1)
         grads_out = jnp.where(mine, input_grad, grads_out)
         gain_total = gain_total + jnp.where(mine, gain_grad, zero_gain)
-    gain_total = spread_sum(gain_total, "fsdp", fsdp_count)
+    gain_total = butterfly_sum(gain_total, "fsdp", fsdp_count)
     grads_out = grads_out.reshape(history.shape)
     return (grads_out[None], gain_total[None])
 

time: 147 us -> 155 us (1.054)
  local copies, waits for them, and re-layouts: 6.08 us -> 37.1 us
  waiting for transfers between devices: 77.5 us -> 54.6 us
  starting transfers between devices: 35 us -> 25.2 us
  matrix products: 13.3 us -> 20.9 us
  other arithmetic: 13.3 us -> 15.5 us
    ppermute x23 -> x34, waiting for transfers between devices: 57.2 us -> 34.7 us  [the longest x30 27 us: butterfly_gathers(): lax.ppermute(tuple((slots[which][offset] for offset in offsets)), axis, [...]
    unnamed x35 -> x81, local copies, waits for them, and re-layouts: 2.05 us -> 17 us
    ppermute x23 -> x34, starting transfers between devices: 30.1 us -> 20 us  [the longest x30 16.5 us: butterfly_gathers(): lax.ppermute(tuple((slots[which][offset] for offset in offsets)), axis, [...]
    convert_element_type x0 -> x5, local copies, waits for them, and re-layouts: none -> 8.25 us  [the longest x4 8.14 us: attend_layer(): normed.astype(jnp.bfloat16).reshape(series_count * seq_length, model_width)]
    gather x1 -> x7, local copies, waits for them, and re-layouts: 0.6 us -> 6.31 us  [the longest x3 2.98 us: xor_blocks(): return jnp.take(blocks, index, axis=1).reshape(matrix.shape)]
    dot_general x3, matrix products: 5.09 us -> 8.92 us  [attend_layer(): update = jnp.dot(mixed, output_weight, preferred_element_type=jnp.float32)]
    convert_element_type x1 -> x2, other arithmetic: 0.19 us -> 3.83 us  [attend_layer(): normed.astype(jnp.bfloat16).reshape(series_count * seq_length, model_width)]
    another operation x14 -> x2, other arithmetic: 4.39 us -> 2.24 us  [the longest x12 3.91 us: butterfly_gathers(): jnp.stack([low, high], axis=1).reshape((-1,) + held[which].shape[1:])]
  transfers between devices with their start and end apart: 25 -> 36, of which waited for: 11 -> 17; matrix products, arithmetic and copies ran while one was open for 12% -> 21% of each run, Pallas kernels for 0% -> 0%
where the time goes in v5:
time: 155 us
  waiting for transfers between devices  54.6 us (35%)
  local copies, waits for them, and re-layouts  37.1 us (24%)
  starting transfers between devices  25.2 us (16%)
  matrix products  20.9 us (13%)
  other arithmetic  15.5 us (10%)
  between operations  1.58 us (1%)
    ppermute x30, waiting for transfers between devices, butterfly_gathers(): lax.ppermute(tuple((slots[which][offset] for offset in offsets)), axis, [...  27 us
    ppermute x2, waiting for transfers between devices, send_to(): return lax.ppermute(arrays, axis, [(source, target)])  19.9 us
    unnamed x81, local copies, waits for them, and re-layouts  17 us
    ppermute x30, starting transfers between devices, butterfly_gathers(): lax.ppermute(tuple((slots[which][offset] for offset in offsets)), axis, [...  16.5 us
    dot_general x3, matrix products, attend_layer(): update = jnp.dot(mixed, output_weight, preferred_element_type=jnp.float32)  8.92 us
    convert_element_type x4, local copies, waits for them, and re-layouts, attend_layer(): normed.astype(jnp.bfloat16).reshape(series_count * seq_length, model_width)  8.14 us
    ppermute x4, waiting for transfers between devices, butterfly_sum(): lax.ppermute(value, axis, [(j, j ^ step) for j in range(size)])  7.72 us
    ppermute x2, starting transfers between devices, send_to(): return lax.ppermute(arrays, axis, [(source, target)])  5.18 us
  transfers between devices with their start and end apart: 36, of which 17 were waited for; matrix products, arithmetic and copies ran while one was open for 21% of the time, Pallas kernels for 0%

profile of v5, /device:TPU:0, one launch (start us, length us, event | category | flops | bytes accessed | tf_op | source)
XLA Modules:
  0.0 154.8 jit_solution(6966256254564648788)
XLA Ops:
  1.2 2.6 %collective-permute-start.16 = (bf16[128,1024]{1,0:T(8,128)(2,1)}, bf16[128,1024]{1,0:T(8,128)(2,1)}, u32[]{:S(2)}, u32[]{:S(2)}) collective-permute-start(bf16[128,1024]{1,0:T(8,128)(2,1)} %bitcast.241), channel_id=1, source_target_pairs={{0,2},{1,3},{2,0},{3,1},{4,6},{5,7},{6,4},{7,5},{8,10},{9,11},{10,... | collective-permute-start | bytes 786440 | tf_op jit(solution)/shard_map/ppermute | solution.py:36
  3.8 1.6 %collective-permute-start.18 = (bf16[128,1024]{1,0:T(8,128)(2,1)}, bf16[128,1024]{1,0:T(8,128)(2,1)}, u32[]{:S(2)}, u32[]{:S(2)}) collective-permute-start(bf16[128,1024]{1,0:T(8,128)(2,1)} %bitcast.242), channel_id=1, source_target_pairs={{0,4},{1,5},{2,6},{3,7},{4,0},{5,1},{6,2},{7,3},{8,12},{9,13},{10,... | collective-permute-start | bytes 786440 | tf_op jit(solution)/shard_map/ppermute | solution.py:36
  5.3 2.6 %collective-permute-start.22 = (bf16[128,1024]{1,0:T(8,128)(2,1)}, bf16[128,1024]{1,0:T(8,128)(2,1)}, u32[]{:S(2)}, u32[]{:S(2)}) collective-permute-start(bf16[128,1024]{1,0:T(8,128)(2,1)} %bitcast.243), channel_id=1, source_target_pairs={{0,8},{1,9},{2,10},{3,11},{4,12},{5,13},{6,14},{7,15},{8,0},{9,1},... | collective-permute-start | bytes 786440 | tf_op jit(solution)/shard_map/ppermute | solution.py:36
  7.9 1.2 fusion.40
  9.2 1.1 bitcast_convert_fusion.2
  10.3 1.7 %constant_dynamic-update-slice_fusion.31 = bf16[1024,2048]{1,0:T(8,128)(2,1)} fusion(bf16[1,64,2048]{2,1,0:T(8,128)(2,1)} %param.17), kind=kLoop, calls=%fused_computation.181 | loop fusion | bytes 524288
  13.0 2.0 %fusion.37 = bf16[4,32,2048]{2,1,0:T(8,128)(2,1)} fusion(bf16[4,1,32,2048]{3,2,1,0:T(8,128)(2,1)} %param.12, f32[2048]{0:T(1024)} %bitcast.233, f32[4,32]{1,0:T(4,128)S(1)} %fusion.84), kind=kLoop, calls=%fused_computation.73 | loop fusion | flops 1048576 | bytes 1057280 | tf_op jit(solution)/shard_map/convert.25
  16.0 1.6 %fusion.46 = (bf16[128,16,128]{2,0,1:T(8,128)(2,1)}, bf16[128,16,128]{2,0,1:T(8,128)(2,1)S(1)}) fusion(f32[128,16,128]{2,1,0:T(8,128)S(1)} %bitcast.213, f32[16,128]{1,0:T(8,128)S(1)} %bitcast.234, f32[128]{0:T(128)S(1)} %rsqrt.42, f32[128]{0:T(128)S(1)} %rsqrt.44, f32[128,16,128]{2,1,0:T(8,128)S(1)} %bitcast.214), kind=kLoop, calls=%fused_computation.84 | loop fusion | flops 1572864 | bytes 3154944 | tf_op jit(solution)/shard_map/jvp()/convert_element_type | solution.py:94
  17.5 1.7 %gather_fusion.1 = bf16[16,128,128]{2,1,0:T(8,128)(2,1)S(1)} fusion(bf16[128,16,128]{2,0,1:T(8,128)(2,1)} %get-tuple-element.26, s32[1024]{0:T(1024)S(1)} %pad_clamp_fusion), kind=kCustom, calls=%fused_computation.1.clone | custom fusion | bytes 1048640 | tf_op jit(solution)/shard_map/jvp(jit(_take))/gather | solution.py:62
  20.1 1.8 %slice_bitcast_fusion.3 = (bf16[4,4,8,8,128]{4,3,2,1,0:T(8,128)(2,1)}, bf16[4,4,8,8,128]{4,3,2,1,0:T(8,128)(2,1)S(1)}) fusion(bf16[4,32,2048]{2,1,0:T(8,128)(2,1)} %fusion.37), kind=kLoop, calls=%fused_computation.130 | loop fusion | bytes 1048576
  24.6 1.7 %constant_dynamic-update-slice_fusion.30 = bf16[1024,2048]{1,0:T(8,128)(2,1)} fusion(bf16[1024,2048]{1,0:T(8,128)(2,1)} %constant_dynamic-update-slice_fusion.31, bf16[64,2048]{1,0:T(8,128)(2,1)} %collective-permute-done), kind=kLoop, calls=%fused_computation.180 | loop fusion | bytes 524288
  26.3 5.3 %collective-permute-done.1 = bf16[64,2048]{1,0:T(8,128)(2,1)S(1)} collective-permute-done((bf16[64,2048]{1,0:T(8,128)(2,1)}, bf16[64,2048]{1,0:T(8,128)(2,1)S(1)}, u32[]{:S(2)}, u32[]{:S(2)}) %collective-permute-start.1) | collective-permute-done | bytes 262176 | tf_op jit(solution)/shard_map/ppermute | solution.py:36
  33.2 2.3 %collective-permute-done.3 = bf16[64,2048]{1,0:T(8,128)(2,1)S(1)} collective-permute-done((bf16[64,2048]{1,0:T(8,128)(2,1)}, bf16[64,2048]{1,0:T(8,128)(2,1)S(1)}, u32[]{:S(2)}, u32[]{:S(2)}) %collective-permute-start.3) | collective-permute-done | bytes 262176 | tf_op jit(solution)/shard_map/ppermute | solution.py:36
  37.5 1.5 collective-permute-start.20
  39.7 6.3 %collective-permute-done.5 = bf16[64,2048]{1,0:T(8,128)(2,1)S(1)} collective-permute-done((bf16[64,2048]{1,0:T(8,128)(2,1)S(1)}, bf16[64,2048]{1,0:T(8,128)(2,1)S(1)}, u32[]{:S(2)}, u32[]{:S(2)}) %collective-permute-start.5) | collective-permute-done | bytes 262176 | tf_op jit(solution)/shard_map/ppermute | solution.py:36
  46.0 1.6 %collective-permute-start.24 = (bf16[128,1024]{1,0:T(8,128)(2,1)}, bf16[128,1024]{1,0:T(8,128)(2,1)S(1)}, u32[]{:S(2)}, u32[]{:S(2)}) collective-permute-start(bf16[128,1024]{1,0:T(8,128)(2,1)} %collective-permute-done.22), channel_id=1, source_target_pairs={{0,2},{1,3},{2,0},{3,1},{4,6},{5,7},{6,4},{7,5},{8,10},{9,11},{10,... | collective-permute-start | bytes 786440 | tf_op jit(solution)/shard_map/ppermute | solution.py:36
  48.4 1.1 constant_dynamic-update-slice_fusion.11
  50.5 4.1 %collective-permute-done.24 = bf16[128,1024]{1,0:T(8,128)(2,1)S(1)} collective-permute-done((bf16[128,1024]{1,0:T(8,128)(2,1)}, bf16[128,1024]{1,0:T(8,128)(2,1)S(1)}, u32[]{:S(2)}, u32[]{:S(2)}) %collective-permute-start.24) | collective-permute-done | bytes 262176 | tf_op jit(solution)/shard_map/ppermute | solution.py:36
  54.6 2.2 %collective-permute-done.26 = bf16[128,1024]{1,0:T(8,128)(2,1)S(1)} collective-permute-done((bf16[128,1024]{1,0:T(8,128)(2,1)}, bf16[128,1024]{1,0:T(8,128)(2,1)S(1)}, u32[]{:S(2)}, u32[]{:S(2)}) %collective-permute-start.26) | collective-permute-done | bytes 262176 | tf_op jit(solution)/shard_map/ppermute | solution.py:36
  59.2 1.6 %collective-permute-start.13 = (bf16[64,2048]{1,0:T(8,128)(2,1)S(1)}, bf16[64,2048]{1,0:T(8,128)(2,1)S(1)}, u32[]{:S(2)}, u32[]{:S(2)}) collective-permute-start(bf16[64,2048]{1,0:T(8,128)(2,1)S(1)} %collective-permute-done.9), channel_id=1, source_target_pairs={{0,4},{1,5},{2,6},{3,7},{4,0},{5,1},{6,2},{7,3},{8,12},{9,13},{10,... | collective-permute-start | bytes 786440 | tf_op jit(solution)/shard_map/ppermute | solution.py:36
  61.6 5.0 %collective-permute-done.28 = bf16[128,1024]{1,0:T(8,128)(2,1)S(1)} collective-permute-done((bf16[128,1024]{1,0:T(8,128)(2,1)S(1)}, bf16[128,1024]{1,0:T(8,128)(2,1)S(1)}, u32[]{:S(2)}, u32[]{:S(2)}) %collective-permute-start.28) | collective-permute-done | bytes 262176 | tf_op jit(solution)/shard_map/ppermute | solution.py:36
  69.5 2.0 %copy-done.7 = bf16[1024,2048]{1,0:T(8,128)(2,1)} copy-done((bf16[1024,2048]{1,0:T(8,128)(2,1)}, bf16[1024,2048]{1,0:T(8,128)(2,1)S(1)}, u32[]{:S(2)}) %copy-start.7) | copy-done | bytes 4194328
  71.5 1.2 convolution_convert_fusion.15
  76.8 3.9 %fusion.5 = bf16[4,32,2048]{2,1,0:T(8,128)(2,1)} fusion(bf16[4,32,1024]{2,1,0:T(8,128)(2,1)S(1)} %dot_general.65, bf16[1024,2048]{1,0:T(8,128)(2,1)} %copy-done.7, bf16[4,1,32,2048]{3,2,1,0:T(8,128)(2,1)S(1)} %copy-done.5), kind=kOutput, calls=%fused_computation.10 | convolution fusion | flops 537657344 | bytes 5505024 | tf_op jit(solution)/shard_map/jvp()/dot_general | solution.py:110
  80.8 3.9 %collective-permute-start.30 = (bf16[4,32,2048]{2,1,0:T(8,128)(2,1)}, bf16[4,32,2048]{2,1,0:T(8,128)(2,1)S(1)}, u32[]{:S(2)}, u32[]{:S(2)}) collective-permute-start(bf16[4,32,2048]{2,1,0:T(8,128)(2,1)} %fusion.5), channel_id=1, source_target_pairs={{0,16},{1,17},{2,18},{3,19},{4,20},{5,21},{6,22},{7,23},{8,24},{9,... | collective-permute-start | bytes 1572872 | tf_op jit(solution)/shard_map/ppermute | solution.py:15
  86.2 9.8 %collective-permute-done.30 = bf16[4,32,2048]{2,1,0:T(8,128)(2,1)S(1)} collective-permute-done((bf16[4,32,2048]{2,1,0:T(8,128)(2,1)}, bf16[4,32,2048]{2,1,0:T(8,128)(2,1)S(1)}, u32[]{:S(2)}, u32[]{:S(2)}) %collective-permute-start.30) | collective-permute-done | bytes 524320 | tf_op jit(solution)/shard_map/ppermute | solution.py:15
  99.4 1.3 collective-permute-start.31
  101.1 1.5 fusion.12
  102.8 1.5 gather_fusion.6
  104.3 10.1 %collective-permute-done.31 = bf16[4,32,2048]{2,1,0:T(8,128)(2,1)S(1)} collective-permute-done((bf16[4,32,2048]{2,1,0:T(8,128)(2,1)}, bf16[4,32,2048]{2,1,0:T(8,128)(2,1)S(1)}, u32[]{:S(2)}, u32[]{:S(2)}) %collective-permute-start.31) | collective-permute-done | bytes 524320 | tf_op jit(solution)/shard_map/ppermute | solution.py:15
  114.4 3.7 %convolution_convert_fusion.12 = bf16[128,1024]{1,0:T(8,128)(2,1)S(1)} fusion(bf16[128,2048]{1,0:T(8,128)(2,1)S(1)} %bitcast.220, bf16[1024,2048]{1,0:T(8,128)(2,1)} %copy-done.7), kind=kOutput, calls=%fused_computation.42 | convolution fusion | flops 537001984 | bytes 4980736 | tf_op jit(solution)/shard_map/transpose(jvp())/dot_general | solution.py:110
  119.7 1.4 multiply_reduce_fusion.3
  121.1 1.6 %fusion.22 = bf16[4,32,8,128]{3,1,2,0:T(8,128)(2,1)S(1)} fusion(bf16[4,4,8,8,128]{4,3,2,1,0:T(8,128)(2,1)} %get-tuple-element.22, f32[4,8,32,32]{2,3,1,0:T(8,128)} %copy-done.13, f32[4,8,32,32]{2,3,1,0:T(8,128)S(1)} %get-tuple-element.45, f32[4,8,32]{2,1,0:T(8,128)S(1)} %neg.13, f32[4,8,32]{2,1,0:T(8,128)S(1)} %get-tuple-element.38, f32[4,32]{1,0:T(4,128)S(1)} %bitcast.261), kind=kOutput, calls=%fused_computation.51 | convolution fusion | flops 8683520 | bytes 795136 | tf_op jit(solution)/shard_map/transpose(jvp(bqhd,bkhd->bhqk))/dot_general | solution.py:101
  124.8 1.5 fusion.11
  127.2 2.3 %bitcast_convert_fusion.1 = (f32[128,16,128]{2,0,1:T(8,128)}, f32[128,16,128]{2,0,1:T(8,128)S(1)}) fusion(bf16[16,128,128]{2,1,0:T(8,128)(2,1)S(1)} %gather_fusion.5, pred[16]{0:T(512)(128)(4,1)S(1)} %compare_and_fusion, bf16[16,128,128]{2,1,0:T(8,128)(2,1)} %gather_fusion.6), kind=kLoop, calls=%fused_computation.99 | loop fusion | flops 1048576 | bytes 3145744 | tf_op jit(solution)/shard_map/transpose(jvp())/convert_element_type | solution.py:94
  129.4 1.6 %copy.114 = f32[128,16,128]{2,1,0:T(8,128)} copy(f32[128,16,128]{2,0,1:T(8,128)S(1)} %get-tuple-element.31) | data formatting | bytes 2097152 | tf_op jit(solution)/shard_map/transpose(jvp())/convert_element_type | solution.py:94
  131.0 1.4 reshape.259
  132.4 2.8 %copy.108 = f32[128,16,128]{2,1,0:T(8,128)} copy(f32[128,16,128]{2,0,1:T(8,128)} %get-tuple-element.30) | data formatting | bytes 2097152 | tf_op jit(solution)/shard_map/transpose(jvp())/convert_element_type | solution.py:94
  135.2 2.4 %reshape.257 = f32[4,32,2048]{2,1,0:T(8,128)} reshape(f32[128,16,128]{2,1,0:T(8,128)} %copy.108) | data formatting | bytes 2097152 | tf_op jit(solution)/shard_map/transpose(jvp())/convert_element_type | solution.py:94
  137.6 1.1 copy.222
  138.7 2.3 %fusion.38 = (f32[2048]{0:T(1024)S(1)}, f32[4,32]{1,0:T(4,128)S(1)}, f32[4,32]{1,0:T(4,128)S(1)}, f32[2048]{0:T(1024)S(1)}, f32[4,32]{1,0:T(4,128)S(1)}, /*index=5*/f32[2048]{0:T(1024)S(1)}) fusion(bf16[4,32,1024]{2,1,0:T(8,128)(2,1)S(1)} %bitcast.216, bf16[4,32,1024]{2,1,0:T(8,128)(2,1)S(1)} %bitcast.218, bf16[4,1,32,2048]{3,2,1,0:T(8,128)(2,1)S(1)} %copy-done.5, ...), kind=kLoop, calls=%fused_computation.74 | loop fusion | flops 5498496 | bytes 4229632 | tf_op jit(solution)/shard_map/transpose(jvp())/reduce_sum | solution.py:78
  141.1 1.2 collective-permute-done.32
  142.3 1.7 %collective-permute-start.33 = (f32[2048]{0:T(1024)S(1)}, f32[2048]{0:T(1024)S(1)}, u32[]{:S(2)}, u32[]{:S(2)}) collective-permute-start(f32[2048]{0:T(1024)S(1)} %add.74), channel_id=1, source_target_pairs={{0,2},{1,3},{2,0},{3,1},{4,6},{5,7},{6,4},{7,5},{8,10},{9,11},{10,... | collective-permute-start | bytes 24584 | tf_op jit(solution)/shard_map/ppermute | solution.py:53
  144.0 1.9 %collective-permute-done.33 = f32[2048]{0:T(1024)S(1)} collective-permute-done((f32[2048]{0:T(1024)S(1)}, f32[2048]{0:T(1024)S(1)}, u32[]{:S(2)}, u32[]{:S(2)}) %collective-permute-start.33) | collective-permute-done | bytes 8224 | tf_op jit(solution)/shard_map/ppermute | solution.py:53
  146.0 1.7 %collective-permute-start.34 = (f32[2048]{0:T(1024)S(1)}, f32[2048]{0:T(1024)S(1)}, u32[]{:S(2)}, u32[]{:S(2)}) collective-permute-start(f32[2048]{0:T(1024)S(1)} %add.75), channel_id=1, source_target_pairs={{0,4},{1,5},{2,6},{3,7},{4,0},{5,1},{6,2},{7,3},{8,12},{9,13},{10,... | collective-permute-start | bytes 24584 | tf_op jit(solution)/shard_map/ppermute | solution.py:53
  147.7 2.0 %collective-permute-done.34 = f32[2048]{0:T(1024)S(1)} collective-permute-done((f32[2048]{0:T(1024)S(1)}, f32[2048]{0:T(1024)S(1)}, u32[]{:S(2)}, u32[]{:S(2)}) %collective-permute-start.34) | collective-permute-done | bytes 8224 | tf_op jit(solution)/shard_map/ppermute | solution.py:53
  149.7 1.8 %fusion.51 = bf16[1,4,1,32,2048]{4,3,2,1,0:T(8,128)(2,1)} fusion(f32[4,32,2048]{2,1,0:T(8,128)S(1)} %get-tuple-element.37, f32[4,32,2048]{2,1,0:T(8,128)S(1)} %reshape.259, f32[4,32,2048]{2,1,0:T(8,128)S(1)} %copy-done.8, bf16[4,32,2048]{2,1,0:T(8,128)(2,1)S(1)} %collective-permute-done.31, bf16[4,32,1024]{2,1,0:T(8,128)(2,1)S(1)} %bitcast.217, ...), kind=kLoop, calls=%fused_computation.94 | loop fusion | flops 8388608 | bytes 5777922
  151.5 2.7 %collective-permute-done.35 = f32[2048]{0:T(1024)S(1)} collective-permute-done((f32[2048]{0:T(1024)S(1)}, f32[2048]{0:T(1024)S(1)}, u32[]{:S(2)}, u32[]{:S(2)}) %collective-permute-start.35) | collective-permute-done | bytes 8224 | tf_op jit(solution)/shard_map/ppermute | solution.py:53
  (192 shorter events, 32.4 us)
Async XLA Ops:
  0.6 14.4 %copy-start = (bf16[16,2048]{1,0:T(8,128)(2,1)S(1)}, bf16[16,2048]{1,0:T(8,128)(2,1)}, u32[]{:S(2)}) copy-start(bf16[16,2048]{1,0:T(8,128)(2,1)} %param.15) | copy-start | bytes 196612
  0.6 21.9 %collective-permute-start.15 = (bf16[128,1024]{1,0:T(8,128)(2,1)}, bf16[128,1024]{1,0:T(8,128)(2,1)}, u32[]{:S(2)}, u32[]{:S(2)}) collective-permute-start(bf16[128,1024]{1,0:T(8,128)(2,1)} %bitcast.240), channel_id=1, source_target_pairs={{0,1},{1,0},{2,3},{3,2},{4,5},{5,4},{6,7},{7,6},{8,9},{9,8},{10,11... | collective-permute-start | bytes 786440 | tf_op jit(solution)/shard_map/ppermute | solution.py:36
  1.2 25.1 %collective-permute-start.16 = (bf16[128,1024]{1,0:T(8,128)(2,1)}, bf16[128,1024]{1,0:T(8,128)(2,1)}, u32[]{:S(2)}, u32[]{:S(2)}) collective-permute-start(bf16[128,1024]{1,0:T(8,128)(2,1)} %bitcast.241), channel_id=1, source_target_pairs={{0,2},{1,3},{2,0},{3,1},{4,6},{5,7},{6,4},{7,5},{8,10},{9,11},{10,... | collective-permute-start | bytes 786440 | tf_op jit(solution)/shard_map/ppermute | solution.py:36
  3.8 33.2 %collective-permute-start.18 = (bf16[128,1024]{1,0:T(8,128)(2,1)}, bf16[128,1024]{1,0:T(8,128)(2,1)}, u32[]{:S(2)}, u32[]{:S(2)}) collective-permute-start(bf16[128,1024]{1,0:T(8,128)(2,1)} %bitcast.242), channel_id=1, source_target_pairs={{0,4},{1,5},{2,6},{3,7},{4,0},{5,1},{6,2},{7,3},{8,12},{9,13},{10,... | collective-permute-start | bytes 786440 | tf_op jit(solution)/shard_map/ppermute | solution.py:36
  5.3 34.4 %collective-permute-start.22 = (bf16[128,1024]{1,0:T(8,128)(2,1)}, bf16[128,1024]{1,0:T(8,128)(2,1)}, u32[]{:S(2)}, u32[]{:S(2)}) collective-permute-start(bf16[128,1024]{1,0:T(8,128)(2,1)} %bitcast.243), channel_id=1, source_target_pairs={{0,8},{1,9},{2,10},{3,11},{4,12},{5,13},{6,14},{7,15},{8,0},{9,1},... | collective-permute-start | bytes 786440 | tf_op jit(solution)/shard_map/ppermute | solution.py:36
  7.9 16.1 %collective-permute-start = (bf16[64,2048]{1,0:T(8,128)(2,1)}, bf16[64,2048]{1,0:T(8,128)(2,1)}, u32[]{:S(2)}, u32[]{:S(2)}) collective-permute-start(bf16[64,2048]{1,0:T(8,128)(2,1)} %bitcast.244), channel_id=1, source_target_pairs={{0,1},{1,0},{2,3},{3,2},{4,5},{5,4},{6,7},{7,6},{8,9},{9,8},{10,11... | collective-permute-start | bytes 786440 | tf_op jit(solution)/shard_map/ppermute | solution.py:36
  9.2 6.8 %copy-start.15 = (f32[1,2048]{1,0:T(1,128)S(1)}, f32[1,2048]{1,0:T(1,128)}, u32[]{:S(2)}) copy-start(f32[1,2048]{1,0:T(1,128)} %param.18) | copy-start | bytes 24580
  15.9 5.9 %copy-start.21 = (s32[4,1,32]{2,1,0:T(1,128)S(1)}, s32[4,1,32]{2,1,0:T(1,128)}, u32[]{:S(2)}) copy-start(s32[4,1,32]{2,1,0:T(1,128)} %param.13) | copy-start | bytes 1540
  17.5 5.0 %copy-start.16 = (bf16[1,128,1024]{2,1,0:T(8,128)(2,1)S(1)}, bf16[1,128,1024]{2,1,0:T(8,128)(2,1)}, u32[]{:S(2)}) copy-start(bf16[1,128,1024]{2,1,0:T(8,128)(2,1)} %param.16) | copy-start | bytes 786436
  21.9 51.8 %copy-start.9 = (bf16[4,4,8,8,128]{4,3,2,1,0:T(8,128)(2,1)}, bf16[4,4,8,8,128]{4,3,2,1,0:T(8,128)(2,1)S(1)}, u32[]{:S(2)}) copy-start(bf16[4,4,8,8,128]{4,3,2,1,0:T(8,128)(2,1)S(1)} %get-tuple-element.23) | copy-start | bytes 786436
  22.5 9.0 %collective-permute-start.1 = (bf16[64,2048]{1,0:T(8,128)(2,1)}, bf16[64,2048]{1,0:T(8,128)(2,1)S(1)}, u32[]{:S(2)}, u32[]{:S(2)}) collective-permute-start(bf16[64,2048]{1,0:T(8,128)(2,1)} %bitcast.245), channel_id=1, source_target_pairs={{0,2},{1,3},{2,0},{3,1},{4,6},{5,7},{6,4},{7,5},{8,10},{9,11},{10,... | collective-permute-start | bytes 786440 | tf_op jit(solution)/shard_map/ppermute | solution.py:36
  24.1 11.4 %collective-permute-start.3 = (bf16[64,2048]{1,0:T(8,128)(2,1)}, bf16[64,2048]{1,0:T(8,128)(2,1)S(1)}, u32[]{:S(2)}, u32[]{:S(2)}) collective-permute-start(bf16[64,2048]{1,0:T(8,128)(2,1)} %bitcast.246), channel_id=1, source_target_pairs={{0,4},{1,5},{2,6},{3,7},{4,0},{5,1},{6,2},{7,3},{8,12},{9,13},{10,... | collective-permute-start | bytes 786440 | tf_op jit(solution)/shard_map/ppermute | solution.py:36
  26.3 23.3 %collective-permute-start.7 = (bf16[64,2048]{1,0:T(8,128)(2,1)}, bf16[64,2048]{1,0:T(8,128)(2,1)S(1)}, u32[]{:S(2)}, u32[]{:S(2)}) collective-permute-start(bf16[64,2048]{1,0:T(8,128)(2,1)} %bitcast.247), channel_id=1, source_target_pairs={{0,8},{1,9},{2,10},{3,11},{4,12},{5,13},{6,14},{7,15},{8,0},{9,1},... | collective-permute-start | bytes 786440 | tf_op jit(solution)/shard_map/ppermute | solution.py:36
  31.5 4.0 %collective-permute-start.2 = (bf16[64,2048]{1,0:T(8,128)(2,1)S(1)}, bf16[64,2048]{1,0:T(8,128)(2,1)S(1)}, u32[]{:S(2)}, u32[]{:S(2)}) collective-permute-start(bf16[64,2048]{1,0:T(8,128)(2,1)S(1)} %collective-permute-done.1), channel_id=1, source_target_pairs={{0,1},{1,0},{2,3},{3,2},{4,5},{5,4},{6,7},{7,6},{8,9},{9,8},{10,11... | collective-permute-start | bytes 786440 | tf_op jit(solution)/shard_map/ppermute | solution.py:36
  35.5 10.5 %collective-permute-start.5 = (bf16[64,2048]{1,0:T(8,128)(2,1)S(1)}, bf16[64,2048]{1,0:T(8,128)(2,1)S(1)}, u32[]{:S(2)}, u32[]{:S(2)}) collective-permute-start(bf16[64,2048]{1,0:T(8,128)(2,1)S(1)} %collective-permute-done.1), channel_id=1, source_target_pairs={{0,4},{1,5},{2,6},{3,7},{4,0},{5,1},{6,2},{7,3},{8,12},{9,13},{10,... | collective-permute-start | bytes 786440 | tf_op jit(solution)/shard_map/ppermute | solution.py:36
  35.5 2.0 %collective-permute-start.4 = (bf16[64,2048]{1,0:T(8,128)(2,1)S(1)}, bf16[64,2048]{1,0:T(8,128)(2,1)S(1)}, u32[]{:S(2)}, u32[]{:S(2)}) collective-permute-start(bf16[64,2048]{1,0:T(8,128)(2,1)S(1)} %collective-permute-done.3), channel_id=1, source_target_pairs={{0,1},{1,0},{2,3},{3,2},{4,5},{5,4},{6,7},{7,6},{8,9},{9,8},{10,11... | collective-permute-start | bytes 786440 | tf_op jit(solution)/shard_map/ppermute | solution.py:36
  37.0 11.3 %collective-permute-start.17 = (bf16[128,1024]{1,0:T(8,128)(2,1)}, bf16[128,1024]{1,0:T(8,128)(2,1)S(1)}, u32[]{:S(2)}, u32[]{:S(2)}) collective-permute-start(bf16[128,1024]{1,0:T(8,128)(2,1)} %collective-permute-done.16), channel_id=1, source_target_pairs={{0,1},{1,0},{2,3},{3,2},{4,5},{5,4},{6,7},{7,6},{8,9},{9,8},{10,11... | collective-permute-start | bytes 786440 | tf_op jit(solution)/shard_map/ppermute | solution.py:36
  37.5 10.8 %collective-permute-start.20 = (bf16[128,1024]{1,0:T(8,128)(2,1)}, bf16[128,1024]{1,0:T(8,128)(2,1)S(1)}, u32[]{:S(2)}, u32[]{:S(2)}) collective-permute-start(bf16[128,1024]{1,0:T(8,128)(2,1)} %collective-permute-done.18), channel_id=1, source_target_pairs={{0,2},{1,3},{2,0},{3,1},{4,6},{5,7},{6,4},{7,5},{8,10},{9,11},{10,... | collective-permute-start | bytes 786440 | tf_op jit(solution)/shard_map/ppermute | solution.py:36
  39.7 10.2 %collective-permute-start.19 = (bf16[128,1024]{1,0:T(8,128)(2,1)}, bf16[128,1024]{1,0:T(8,128)(2,1)S(1)}, u32[]{:S(2)}, u32[]{:S(2)}) collective-permute-start(bf16[128,1024]{1,0:T(8,128)(2,1)} %collective-permute-done.18), channel_id=1, source_target_pairs={{0,1},{1,0},{2,3},{3,2},{4,5},{5,4},{6,7},{7,6},{8,9},{9,8},{10,11... | collective-permute-start | bytes 786440 | tf_op jit(solution)/shard_map/ppermute | solution.py:36
  46.0 8.6 %collective-permute-start.24 = (bf16[128,1024]{1,0:T(8,128)(2,1)}, bf16[128,1024]{1,0:T(8,128)(2,1)S(1)}, u32[]{:S(2)}, u32[]{:S(2)}) collective-permute-start(bf16[128,1024]{1,0:T(8,128)(2,1)} %collective-permute-done.22), channel_id=1, source_target_pairs={{0,2},{1,3},{2,0},{3,1},{4,6},{5,7},{6,4},{7,5},{8,10},{9,11},{10,... | collective-permute-start | bytes 786440 | tf_op jit(solution)/shard_map/ppermute | solution.py:36
  48.3 19.6 %copy-start.6 = (bf16[1024,2048]{1,0:T(8,128)(2,1)S(1)}, bf16[1024,2048]{1,0:T(8,128)(2,1)}, u32[]{:S(2)}) copy-start(bf16[1024,2048]{1,0:T(8,128)(2,1)} %constant_dynamic-update-slice_fusion.25) | copy-start | bytes 12582916
  48.3 8.5 %collective-permute-start.26 = (bf16[128,1024]{1,0:T(8,128)(2,1)}, bf16[128,1024]{1,0:T(8,128)(2,1)S(1)}, u32[]{:S(2)}, u32[]{:S(2)}) collective-permute-start(bf16[128,1024]{1,0:T(8,128)(2,1)} %collective-permute-done.22), channel_id=1, source_target_pairs={{0,4},{1,5},{2,6},{3,7},{4,0},{5,1},{6,2},{7,3},{8,12},{9,13},{10,... | collective-permute-start | bytes 786440 | tf_op jit(solution)/shard_map/ppermute | solution.py:36
  48.3 8.5 %collective-permute-start.21 = (bf16[128,1024]{1,0:T(8,128)(2,1)S(1)}, bf16[128,1024]{1,0:T(8,128)(2,1)S(1)}, u32[]{:S(2)}, u32[]{:S(2)}) collective-permute-start(bf16[128,1024]{1,0:T(8,128)(2,1)S(1)} %collective-permute-done.20), channel_id=1, source_target_pairs={{0,1},{1,0},{2,3},{3,2},{4,5},{5,4},{6,7},{7,6},{8,9},{9,8},{10,11... | collective-permute-start | bytes 786440 | tf_op jit(solution)/shard_map/ppermute | solution.py:36
  49.6 8.7 %collective-permute-start.23 = (bf16[128,1024]{1,0:T(8,128)(2,1)}, bf16[128,1024]{1,0:T(8,128)(2,1)S(1)}, u32[]{:S(2)}, u32[]{:S(2)}) collective-permute-start(bf16[128,1024]{1,0:T(8,128)(2,1)} %collective-permute-done.22), channel_id=1, source_target_pairs={{0,1},{1,0},{2,3},{3,2},{4,5},{5,4},{6,7},{7,6},{8,9},{9,8},{10,11... | collective-permute-start | bytes 786440 | tf_op jit(solution)/shard_map/ppermute | solution.py:36
  50.0 9.2 %collective-permute-start.9 = (bf16[64,2048]{1,0:T(8,128)(2,1)S(1)}, bf16[64,2048]{1,0:T(8,128)(2,1)S(1)}, u32[]{:S(2)}, u32[]{:S(2)}) collective-permute-start(bf16[64,2048]{1,0:T(8,128)(2,1)S(1)} %collective-permute-done.7), channel_id=1, source_target_pairs={{0,2},{1,3},{2,0},{3,1},{4,6},{5,7},{6,4},{7,5},{8,10},{9,11},{10,... | collective-permute-start | bytes 786440 | tf_op jit(solution)/shard_map/ppermute | solution.py:36
  54.6 6.6 %collective-permute-start.11 = (bf16[64,2048]{1,0:T(8,128)(2,1)S(1)}, bf16[64,2048]{1,0:T(8,128)(2,1)S(1)}, u32[]{:S(2)}, u32[]{:S(2)}) collective-permute-start(bf16[64,2048]{1,0:T(8,128)(2,1)S(1)} %collective-permute-done.7), channel_id=1, source_target_pairs={{0,4},{1,5},{2,6},{3,7},{4,0},{5,1},{6,2},{7,3},{8,12},{9,13},{10,... | collective-permute-start | bytes 786440 | tf_op jit(solution)/shard_map/ppermute | solution.py:36
  56.8 2.4 %collective-permute-start.25 = (bf16[128,1024]{1,0:T(8,128)(2,1)S(1)}, bf16[128,1024]{1,0:T(8,128)(2,1)S(1)}, u32[]{:S(2)}, u32[]{:S(2)}) collective-permute-start(bf16[128,1024]{1,0:T(8,128)(2,1)S(1)} %collective-permute-done.24), channel_id=1, source_target_pairs={{0,1},{1,0},{2,3},{3,2},{4,5},{5,4},{6,7},{7,6},{8,9},{9,8},{10,11... | collective-permute-start | bytes 786440 | tf_op jit(solution)/shard_map/ppermute | solution.py:36
  56.8 4.1 %collective-permute-start.27 = (bf16[128,1024]{1,0:T(8,128)(2,1)S(1)}, bf16[128,1024]{1,0:T(8,128)(2,1)S(1)}, u32[]{:S(2)}, u32[]{:S(2)}) collective-permute-start(bf16[128,1024]{1,0:T(8,128)(2,1)S(1)} %collective-permute-done.26), channel_id=1, source_target_pairs={{0,1},{1,0},{2,3},{3,2},{4,5},{5,4},{6,7},{7,6},{8,9},{9,8},{10,11... | collective-permute-start | bytes 786440 | tf_op jit(solution)/shard_map/ppermute | solution.py:36
  58.3 8.3 %collective-permute-start.28 = (bf16[128,1024]{1,0:T(8,128)(2,1)S(1)}, bf16[128,1024]{1,0:T(8,128)(2,1)S(1)}, u32[]{:S(2)}, u32[]{:S(2)}) collective-permute-start(bf16[128,1024]{1,0:T(8,128)(2,1)S(1)} %collective-permute-done.26), channel_id=1, source_target_pairs={{0,2},{1,3},{2,0},{3,1},{4,6},{5,7},{6,4},{7,5},{8,10},{9,11},{10,... | collective-permute-start | bytes 786440 | tf_op jit(solution)/shard_map/ppermute | solution.py:36
  59.2 7.4 %collective-permute-start.6 = (bf16[64,2048]{1,0:T(8,128)(2,1)S(1)}, bf16[64,2048]{1,0:T(8,128)(2,1)S(1)}, u32[]{:S(2)}, u32[]{:S(2)}) collective-permute-start(bf16[64,2048]{1,0:T(8,128)(2,1)S(1)} %collective-permute-done.5), channel_id=1, source_target_pairs={{0,1},{1,0},{2,3},{3,2},{4,5},{5,4},{6,7},{7,6},{8,9},{9,8},{10,11... | collective-permute-start | bytes 786440 | tf_op jit(solution)/shard_map/ppermute | solution.py:36
  59.2 8.7 %collective-permute-start.13 = (bf16[64,2048]{1,0:T(8,128)(2,1)S(1)}, bf16[64,2048]{1,0:T(8,128)(2,1)S(1)}, u32[]{:S(2)}, u32[]{:S(2)}) collective-permute-start(bf16[64,2048]{1,0:T(8,128)(2,1)S(1)} %collective-permute-done.9), channel_id=1, source_target_pairs={{0,4},{1,5},{2,6},{3,7},{4,0},{5,1},{6,2},{7,3},{8,12},{9,13},{10,... | collective-permute-start | bytes 786440 | tf_op jit(solution)/shard_map/ppermute | solution.py:36
  60.9 7.1 %collective-permute-start.8 = (bf16[64,2048]{1,0:T(8,128)(2,1)S(1)}, bf16[64,2048]{1,0:T(8,128)(2,1)S(1)}, u32[]{:S(2)}, u32[]{:S(2)}) collective-permute-start(bf16[64,2048]{1,0:T(8,128)(2,1)S(1)} %collective-permute-done.7), channel_id=1, source_target_pairs={{0,1},{1,0},{2,3},{3,2},{4,5},{5,4},{6,7},{7,6},{8,9},{9,8},{10,11... | collective-permute-start | bytes 786440 | tf_op jit(solution)/shard_map/ppermute | solution.py:36
  61.3 6.8 %collective-permute-start.10 = (bf16[64,2048]{1,0:T(8,128)(2,1)S(1)}, bf16[64,2048]{1,0:T(8,128)(2,1)S(1)}, u32[]{:S(2)}, u32[]{:S(2)}) collective-permute-start(bf16[64,2048]{1,0:T(8,128)(2,1)S(1)} %collective-permute-done.9), channel_id=1, source_target_pairs={{0,1},{1,0},{2,3},{3,2},{4,5},{5,4},{6,7},{7,6},{8,9},{9,8},{10,11... | collective-permute-start | bytes 786440 | tf_op jit(solution)/shard_map/ppermute | solution.py:36
  66.6 1.5 collective-permute-start.12
  66.6 1.9 %collective-permute-start.29 = (bf16[128,1024]{1,0:T(8,128)(2,1)S(1)}, bf16[128,1024]{1,0:T(8,128)(2,1)S(1)}, u32[]{:S(2)}, u32[]{:S(2)}) collective-permute-start(bf16[128,1024]{1,0:T(8,128)(2,1)S(1)} %collective-permute-done.28), channel_id=1, source_target_pairs={{0,1},{1,0},{2,3},{3,2},{4,5},{5,4},{6,7},{7,6},{8,9},{9,8},{10,11... | collective-permute-start | bytes 786440 | tf_op jit(solution)/shard_map/ppermute | solution.py:36
  67.9 1.5 collective-permute-start.14
  76.8 7.8 %copy-start.2 = (bf16[2048,1024]{1,0:T(8,128)(2,1)S(1)}, bf16[2048,1024]{1,0:T(8,128)(2,1)}, u32[]{:S(2)}) copy-start(bf16[2048,1024]{1,0:T(8,128)(2,1)} %copy-done.1) | copy-start | bytes 12582916
  80.8 15.2 %collective-permute-start.30 = (bf16[4,32,2048]{2,1,0:T(8,128)(2,1)}, bf16[4,32,2048]{2,1,0:T(8,128)(2,1)S(1)}, u32[]{:S(2)}, u32[]{:S(2)}) collective-permute-start(bf16[4,32,2048]{2,1,0:T(8,128)(2,1)} %fusion.5), channel_id=1, source_target_pairs={{0,16},{1,17},{2,18},{3,19},{4,20},{5,21},{6,22},{7,23},{8,24},{9,... | collective-permute-start | bytes 1572872 | tf_op jit(solution)/shard_map/ppermute | solution.py:15
  99.4 15.0 %collective-permute-start.31 = (bf16[4,32,2048]{2,1,0:T(8,128)(2,1)}, bf16[4,32,2048]{2,1,0:T(8,128)(2,1)S(1)}, u32[]{:S(2)}, u32[]{:S(2)}) collective-permute-start(bf16[4,32,2048]{2,1,0:T(8,128)(2,1)} %fusion.28), channel_id=1, source_target_pairs={{16,0},{17,1},{18,2},{19,3},{20,4},{21,5},{22,6},{23,7},{24,8},{25... | collective-permute-start | bytes 1572872 | tf_op jit(solution)/shard_map/ppermute | solution.py:15
  114.3 5.3 %copy-start.10 = (bf16[4,4,8,8,128]{4,3,2,1,0:T(8,128)(2,1)S(1)}, bf16[4,4,8,8,128]{4,3,2,1,0:T(8,128)(2,1)}, u32[]{:S(2)}) copy-start(bf16[4,4,8,8,128]{4,3,2,1,0:T(8,128)(2,1)} %copy-done.9) | copy-start | bytes 786436
  118.1 4.6 %copy-start.18 = (bf16[16,8,8,128]{3,2,1,0:T(8,128)(2,1)S(1)}, bf16[16,8,8,128]{3,2,1,0:T(8,128)(2,1)}, u32[]{:S(2)}) copy-start(bf16[16,8,8,128]{3,2,1,0:T(8,128)(2,1)} %copy-done.17) | copy-start | bytes 786436
  129.4 8.2 %copy-start.19 = (bf16[4,8,4,8,128]{4,3,2,1,0:T(8,128)(2,1)S(1)}, bf16[4,8,4,8,128]{4,3,2,1,0:T(8,128)(2,1)}, u32[]{:S(2)}) copy-start(bf16[4,8,4,8,128]{4,3,2,1,0:T(8,128)(2,1)} %fusion.21) | copy-start | bytes 786436
  137.6 12.1 %copy-start.8 = (f32[4,32,2048]{2,1,0:T(8,128)S(1)}, f32[4,32,2048]{2,1,0:T(8,128)}, u32[]{:S(2)}) copy-start(f32[4,32,2048]{2,1,0:T(8,128)} %reshape.257) | copy-start | bytes 3145732
  137.6 12.1 %copy-start.12 = (bf16[4,1,32,2048]{3,2,1,0:T(8,128)(2,1)S(1)}, bf16[4,1,32,2048]{3,2,1,0:T(8,128)(2,1)}, u32[]{:S(2)}) copy-start(bf16[4,1,32,2048]{3,2,1,0:T(8,128)(2,1)} %param.19) | copy-start | bytes 1572868
  141.1 1.2 collective-permute-start.32
  142.3 3.7 %collective-permute-start.33 = (f32[2048]{0:T(1024)S(1)}, f32[2048]{0:T(1024)S(1)}, u32[]{:S(2)}, u32[]{:S(2)}) collective-permute-start(f32[2048]{0:T(1024)S(1)} %add.74), channel_id=1, source_target_pairs={{0,2},{1,3},{2,0},{3,1},{4,6},{5,7},{6,4},{7,5},{8,10},{9,11},{10,... | collective-permute-start | bytes 24584 | tf_op jit(solution)/shard_map/ppermute | solution.py:53
  146.0 3.7 %collective-permute-start.34 = (f32[2048]{0:T(1024)S(1)}, f32[2048]{0:T(1024)S(1)}, u32[]{:S(2)}, u32[]{:S(2)}) collective-permute-start(f32[2048]{0:T(1024)S(1)} %add.75), channel_id=1, source_target_pairs={{0,4},{1,5},{2,6},{3,7},{4,0},{5,1},{6,2},{7,3},{8,12},{9,13},{10,... | collective-permute-start | bytes 24584 | tf_op jit(solution)/shard_map/ppermute | solution.py:53
  149.6 4.5 %collective-permute-start.35 = (f32[2048]{0:T(1024)S(1)}, f32[2048]{0:T(1024)S(1)}, u32[]{:S(2)}, u32[]{:S(2)}) collective-permute-start(f32[2048]{0:T(1024)S(1)} %add.76), channel_id=1, source_target_pairs={{0,8},{1,9},{2,10},{3,11},{4,12},{5,13},{6,14},{7,15},{8,0},{9,1},... | collective-permute-start | bytes 24584 | tf_op jit(solution)/shard_map/ppermute | solution.py:53
  (10 other events, 32.6 us)

commit v6 on v3

--- a/solution.py
+++ b/solution.py
@@ -94,6 +94,58 @@
     return (input_wide + update.reshape(series_count, seq_length, model_width)).astype(jnp.bfloat16)
 
 
+def two_section_relay(
+    history_rows, plan_tokens, cotangent_rows, key_mask, query_weight, output_weight, gain_vector
+):
+    is_encoder = lax.axis_index("section") == 0
+    half = history_rows.shape[0] // 2
+
+    def part(array, which):
+        return array[which * half:(which + 1) * half]
+
+    def pick(encoder_value, decoder_value):
+        return jnp.where(is_encoder, encoder_value, decoder_value)
+
+    def layer_vjp(layer_input, layer_source, layer_mask, out_grad):
+        def apply(x, source, layer_gain):
+            return attend_layer(x, source, layer_mask, query_weight, output_weight, layer_gain)
+
+        output, pull = jax.vjp(apply, layer_input, layer_source, gain_vector)
+        return (output,) + pull(out_grad)
+
+    both_ways = [(0, 1), (1, 0)]
+    zero_gain = jnp.zeros_like(gain_vector)
+    hist_a, hist_b = part(history_rows, 0), part(history_rows, 1)
+    mask_a, mask_b = part(key_mask, 0), part(key_mask, 1)
+    plan_a, plan_b = part(plan_tokens, 0), part(plan_tokens, 1)
+    memory_a = attend_layer(hist_a, hist_a, mask_a, query_weight, output_weight, gain_vector)
+    memory_a = send_to(memory_a, "section", 0, 1)
+    memory_b, input_grad, memory_grad, gain_1 = layer_vjp(
+        pick(hist_b, plan_a),
+        pick(hist_b, memory_a),
+        pick(mask_b, mask_a),
+        pick(jnp.zeros_like(hist_b), part(cotangent_rows, 0)),
+    )
+    decoder_grad_a = input_grad
+    received = lax.ppermute(pick(memory_b, memory_grad), "section", both_ways)
+    _, input_grad, memory_grad, gain_2 = layer_vjp(
+        pick(hist_a, plan_b),
+        pick(hist_a, received),
+        pick(mask_a, mask_b),
+        pick(received, part(cotangent_rows, 1)),
+    )
+    encoder_grad_a = input_grad + memory_grad
+    decoder_grad_b = input_grad
+    memory_grad_b = send_to(memory_grad, "section", 1, 0)
+    _, input_grad, memory_grad, gain_3 = layer_vjp(hist_b, hist_b, mask_b, memory_grad_b)
+    encoder_grad_b = input_grad + memory_grad
+    grads = jnp.concatenate(
+        [pick(encoder_grad_a, decoder_grad_a), pick(encoder_grad_b, decoder_grad_b)], axis=0
+    )
+    gain_total = pick(zero_gain, gain_1) + gain_2 + pick(gain_3, zero_gain)
+    return grads, gain_total
+
+
 def on_device(history, keymask, codes, plan_table, query_weights, output_weights, gains, cotangent):
     section_index = lax.axis_index("section")
     section_count = lax.axis_size("section")
@@ -118,6 +170,13 @@
     ).astype(jnp.bfloat16).reshape(act_shape)
     key_mask = keymask.reshape(rows, seq_length)
     history_rows = history.reshape(act_shape)
+    if section_count == 2 and micro_count % 2 == 0:
+        grads_out, gain_total = two_section_relay(
+            history_rows, plan_tokens, cotangent.reshape(act_shape), key_mask,
+            query_weight, output_weight, gain_vector,
+        )
+        gain_total = butterfly_sum(gain_total, "fsdp", fsdp_count)
+        return (grads_out.reshape(history.shape)[None], gain_total[None])
 
     def encoder_map(layer_input, layer_gain):
         return attend_layer(

time: 137 us -> 139 us (1.015)
  waiting for transfers between devices: 79.7 us -> 67.5 us
  matrix products: 13.3 us -> 22.4 us
  starting transfers between devices: 20.2 us -> 24.5 us
  local copies, waits for them, and re-layouts: 5.99 us -> 7.56 us
    ppermute x2, waiting for transfers between devices: 20.2 us -> 8.54 us  [send_to(): return lax.ppermute(arrays, axis, [(source, target)])]
    ppermute x0 -> x1, waiting for transfers between devices: none -> 4.32 us  [two_section_relay(): received = lax.ppermute(pick(memory_b, memory_grad), 'section', both_ways)]
    another operation x12, other arithmetic: 9.6 us -> 6.12 us  [butterfly_gathers(): jnp.stack([low, high], axis=1).reshape((-1,) + held[which].shape[1:])]
    ppermute x8, waiting for transfers between devices: 52.6 us -> 49.2 us  [butterfly_gathers(): lax.ppermute(held[which], axis, [(j, j ^ step) for j in range(size)])]
    dot_general x3 -> x5, matrix products: 5.09 us -> 8.4 us  [attend_layer(): update = jnp.dot(mixed, output_weight, preferred_element_type=jnp.float32)]
    dot_general x4 -> x7, matrix products: 4.51 us -> 7.59 us  [attend_layer(): jnp.dot(normed_rows, query_weight, preferred_element_type=jnp.float32)]
    ppermute x0 -> x1, starting transfers between devices: none -> 2.54 us  [two_section_relay(): received = lax.ppermute(pick(memory_b, memory_grad), 'section', both_ways)]
    ppermute x4, starting transfers between devices: 4.36 us -> 6.67 us  [butterfly_sum(): lax.ppermute(value, axis, [(j, j ^ step) for j in range(size)])]
  transfers between devices with their start and end apart: 14 -> 15, of which waited for: 12 -> 13; matrix products, arithmetic and copies ran while one was open for 15% -> 15% of each run, Pallas kernels for 0% -> 0%
where the time goes in v6:
time: 139 us
  waiting for transfers between devices  67.5 us (49%)
  starting transfers between devices  24.5 us (18%)
  matrix products  22.4 us (16%)
  other arithmetic  15.4 us (11%)
  local copies, waits for them, and re-layouts  7.56 us (5%)
    ppermute x8, waiting for transfers between devices, butterfly_gathers(): lax.ppermute(held[which], axis, [(j, j ^ step) for j in range(size)])  49.2 us
    ppermute x8, starting transfers between devices, butterfly_gathers(): lax.ppermute(held[which], axis, [(j, j ^ step) for j in range(size)])  10.3 us
    ppermute x2, waiting for transfers between devices, send_to(): return lax.ppermute(arrays, axis, [(source, target)])  8.54 us
    dot_general x5, matrix products, attend_layer(): update = jnp.dot(mixed, output_weight, preferred_element_type=jnp.float32)  8.4 us
    dot_general x7, matrix products, attend_layer(): jnp.dot(normed_rows, query_weight, preferred_element_type=jnp.float32)  7.59 us
    ppermute x4, starting transfers between devices, butterfly_sum(): lax.ppermute(value, axis, [(j, j ^ step) for j in range(size)])  6.67 us
    another operation x12, other arithmetic, butterfly_gathers(): jnp.stack([low, high], axis=1).reshape((-1,) + held[which].shape[1:])  6.12 us
    ppermute x4, waiting for transfers between devices, butterfly_sum(): lax.ppermute(value, axis, [(j, j ^ step) for j in range(size)])  5.39 us
  transfers between devices with their start and end apart: 15, of which 13 were waited for; matrix products, arithmetic and copies ran while one was open for 15% of the time, Pallas kernels for 0%

profile of v6, /device:TPU:0, one launch (start us, length us, event | category | flops | bytes accessed | tf_op | source)
XLA Modules:
  0.0 138.6 jit_solution(10224056704634047505)
XLA Ops:
  0.6 4.1 %collective-permute-start.4 = (bf16[1,64,2048]{2,1,0:T(8,128)(2,1)}, bf16[1,64,2048]{2,1,0:T(8,128)(2,1)S(1)}, u32[]{:S(2)}, u32[]{:S(2)}) collective-permute-start(bf16[1,64,2048]{2,1,0:T(8,128)(2,1)} %param.13), channel_id=1, source_target_pairs={{0,8},{1,9},{2,10},{3,11},{4,12},{5,13},{6,14},{7,15},{8,0},{9,1},... | collective-permute-start | bytes 786440 | tf_op jit(solution)/shard_map/ppermute | solution.py:36
  4.8 0.8 copy.102
  6.0 17.3 %collective-permute-done.4 = bf16[1,64,2048]{2,1,0:T(8,128)(2,1)S(1)} collective-permute-done((bf16[1,64,2048]{2,1,0:T(8,128)(2,1)}, bf16[1,64,2048]{2,1,0:T(8,128)(2,1)S(1)}, u32[]{:S(2)}, u32[]{:S(2)}) %collective-permute-start.4) | collective-permute-done | bytes 262176 | tf_op jit(solution)/shard_map/ppermute | solution.py:36
  23.3 1.0 select_bitcast_fusion.11
  24.4 1.9 %collective-permute-start.5 = (bf16[2,64,2048]{2,1,0:T(8,128)(2,1)S(1)}, bf16[2,64,2048]{2,1,0:T(8,128)(2,1)S(1)}, u32[]{:S(2)}, u32[]{:S(2)}) collective-permute-start(bf16[2,64,2048]{2,1,0:T(8,128)(2,1)S(1)} %maximum_bitcast_fusion.2), channel_id=1, source_target_pairs={{0,2},{1,3},{2,0},{3,1},{4,6},{5,7},{6,4},{7,5},{8,10},{9,11},{10,... | collective-permute-start | bytes 1572872 | tf_op jit(solution)/shard_map/ppermute | solution.py:36
  26.3 0.7 slice_convert_fusion
  27.0 1.2 fusion.50
  28.3 1.0 select_bitcast_fusion.13
  29.3 0.8 maximum_bitcast_fusion.1
  30.8 6.0 %collective-permute-done.5 = bf16[2,64,2048]{2,1,0:T(8,128)(2,1)S(1)} collective-permute-done((bf16[2,64,2048]{2,1,0:T(8,128)(2,1)S(1)}, bf16[2,64,2048]{2,1,0:T(8,128)(2,1)S(1)}, u32[]{:S(2)}, u32[]{:S(2)}) %collective-permute-start.5) | collective-permute-done | bytes 524320 | tf_op jit(solution)/shard_map/ppermute | solution.py:36
  36.9 1.6 %collective-permute-start.6 = (bf16[4,64,2048]{2,1,0:T(8,128)(2,1)S(1)}, bf16[4,64,2048]{2,1,0:T(8,128)(2,1)}, u32[]{:S(2)}, u32[]{:S(2)}) collective-permute-start(bf16[4,64,2048]{2,1,0:T(8,128)(2,1)S(1)} %bitcast.368), channel_id=1, source_target_pairs={{0,4},{1,5},{2,6},{3,7},{4,0},{5,1},{6,2},{7,3},{8,12},{9,13},{10,... | collective-permute-start | bytes 3145736 | tf_op jit(solution)/shard_map/ppermute | solution.py:36
  39.7 5.6 %collective-permute-done.1 = bf16[2,128,1024]{2,1,0:T(8,128)(2,1)} collective-permute-done((bf16[2,128,1024]{2,1,0:T(8,128)(2,1)}, bf16[2,128,1024]{2,1,0:T(8,128)(2,1)}, u32[]{:S(2)}, u32[]{:S(2)}) %collective-permute-start.1) | collective-permute-done | bytes 524320 | tf_op jit(solution)/shard_map/ppermute | solution.py:36
  45.3 1.1 select_bitcast_fusion.9
  46.5 1.5 %collective-permute-start.2 = (bf16[4,128,1024]{2,1,0:T(8,128)(2,1)S(1)}, bf16[4,128,1024]{2,1,0:T(8,128)(2,1)S(1)}, u32[]{:S(2)}, u32[]{:S(2)}) collective-permute-start(bf16[4,128,1024]{2,1,0:T(8,128)(2,1)S(1)} %bitcast.369), channel_id=1, source_target_pairs={{0,2},{1,3},{2,0},{3,1},{4,6},{5,7},{6,4},{7,5},{8,10},{9,11},{10,... | collective-permute-start | bytes 3145736 | tf_op jit(solution)/shard_map/ppermute | solution.py:36
  48.0 17.9 %collective-permute-done.6 = bf16[4,64,2048]{2,1,0:T(8,128)(2,1)} collective-permute-done((bf16[4,64,2048]{2,1,0:T(8,128)(2,1)S(1)}, bf16[4,64,2048]{2,1,0:T(8,128)(2,1)}, u32[]{:S(2)}, u32[]{:S(2)}) %collective-permute-start.6) | collective-permute-done | bytes 1048608 | tf_op jit(solution)/shard_map/ppermute | solution.py:36
  65.9 1.4 select_bitcast_fusion.3
  69.6 2.2 %collective-permute-done.7 = bf16[8,64,2048]{2,1,0:T(8,128)(2,1)S(1)} collective-permute-done((bf16[8,64,2048]{2,1,0:T(8,128)(2,1)S(1)}, bf16[8,64,2048]{2,1,0:T(8,128)(2,1)S(1)}, u32[]{:S(2)}, u32[]{:S(2)}) %collective-permute-start.7) | collective-permute-done | bytes 2097184 | tf_op jit(solution)/shard_map/ppermute | solution.py:36
  72.6 2.2 %copy.115 = bf16[2,2,2,2,64,2048]{5,4,3,2,1,0:T(8,128)(2,1)} copy(bf16[2,2,2,2,64,2048]{5,4,1,2,0,3:T(8,128)(2,1)S(1)} %maximum_bitcast_fusion) | data formatting | bytes 8388608 | tf_op jit(solution)/shard_map/transpose | solution.py:50
  76.3 2.0 %copy-done.2 = bf16[8,2,128,1024]{3,2,1,0:T(8,128)(2,1)} copy-done((bf16[8,2,128,1024]{3,2,1,0:T(8,128)(2,1)}, bf16[8,2,128,1024]{3,2,1,0:T(8,128)(2,1)S(1)}, u32[]{:S(2)}) %copy-start.2) | copy-done | bytes 4194328
  78.2 0.8 fusion.10
  79.1 0.9 fusion.6
  80.0 1.3 fusion.23
  81.3 3.2 %fusion = bf16[2,32,2048]{2,1,0:T(8,128)(2,1)S(1)} fusion(bf16[1024,2048,1]{1,0,2:T(8,128)(2,1)} %bitcast.349, bf16[2,8,4,8,128]{4,3,2,1,0:T(8,128)(2,1)S(1)} %fusion.23, bf16[4,1,32,2048]{3,2,0,1:T(8,128)(2,1)S(1)} %bitcast.357), kind=kOutput, calls=%fused_computation.5 | convolution fusion | flops 268828672 | bytes 4849664 | tf_op jit(solution)/shard_map/dot_general | solution.py:93
  84.5 3.5 %collective-permute-start.8 = (bf16[2,32,2048]{2,1,0:T(8,128)(2,1)S(1)}, bf16[2,32,2048]{2,1,0:T(8,128)(2,1)S(1)}, u32[]{:S(2)}, u32[]{:S(2)}) collective-permute-start(bf16[2,32,2048]{2,1,0:T(8,128)(2,1)S(1)} %fusion), channel_id=1, source_target_pairs={{0,16},{1,17},{2,18},{3,19},{4,20},{5,21},{6,22},{7,23},{8,24},{9,... | collective-permute-start | bytes 786440 | tf_op jit(solution)/shard_map/ppermute | solution.py:15
  88.1 0.9 fusion.11
  89.0 1.4 %fusion.12 = bf16[8,8,8,128]{3,1,2,0:T(8,128)(2,1)S(1)} fusion(bf16[64,2048]{1,0:T(8,128)(2,1)S(1)} %bitcast.392, bf16[1024,2048]{1,0:T(8,128)(2,1)S(1)} %bitcast.350), kind=kOutput, calls=%fused_computation.57 | convolution fusion | flops 268500992 | bytes 4587520 | tf_op jit(solution)/shard_map/transpose(jvp())/dot_general | solution.py:93
  90.4 0.9 fusion.15
  91.3 0.9 fusion.20
  92.2 1.5 %collective-permute-done.8 = bf16[2,32,2048]{2,1,0:T(8,128)(2,1)S(1)} collective-permute-done((bf16[2,32,2048]{2,1,0:T(8,128)(2,1)S(1)}, bf16[2,32,2048]{2,1,0:T(8,128)(2,1)S(1)}, u32[]{:S(2)}, u32[]{:S(2)}) %collective-permute-start.8) | collective-permute-done | bytes 262176 | tf_op jit(solution)/shard_map/ppermute | solution.py:15
  95.9 1.0 fusion.76
  97.0 2.5 %collective-permute-start.9 = (bf16[2,32,2048]{2,1,0:T(8,128)(2,1)S(1)}, bf16[2,32,2048]{2,1,0:T(8,128)(2,1)S(1)}, u32[]{:S(2)}, u32[]{:S(2)}) collective-permute-start(bf16[2,32,2048]{2,1,0:T(8,128)(2,1)S(1)} %fusion.76), channel_id=1, source_target_pairs={{0,16},{16,0},{1,17},{17,1},{2,18},{18,2},{3,19},{19,3},{4,20},{20... | collective-permute-start | bytes 786440 | tf_op jit(solution)/shard_map/ppermute | solution.py:130
  99.6 1.4 %convolution_convert_fusion.2 = bf16[64,2048]{1,0:T(8,128)(2,1)S(1)} fusion(bf16[2048,1024]{1,0:T(8,128)(2,1)S(1)} %bitcast.346, bf16[8,8,8,128]{3,2,1,0:T(8,128)(2,1)S(1)} %bitcast.410), kind=kOutput, calls=%fused_computation.8 | convolution fusion | flops 268566528 | bytes 4587520 | tf_op jit(solution)/shard_map/transpose(jvp())/dot_general | solution.py:82
  101.0 4.3 %collective-permute-done.9 = bf16[2,32,2048]{2,1,0:T(8,128)(2,1)S(1)} collective-permute-done((bf16[2,32,2048]{2,1,0:T(8,128)(2,1)S(1)}, bf16[2,32,2048]{2,1,0:T(8,128)(2,1)S(1)}, u32[]{:S(2)}, u32[]{:S(2)}) %collective-permute-start.9) | collective-permute-done | bytes 262176 | tf_op jit(solution)/shard_map/ppermute | solution.py:130
  105.3 1.4 %fusion.14 = bf16[8,8,8,128]{3,1,2,0:T(8,128)(2,1)S(1)} fusion(bf16[64,2048]{1,0:T(8,128)(2,1)S(1)} %bitcast.371, bf16[1024,2048]{1,0:T(8,128)(2,1)S(1)} %bitcast.352), kind=kOutput, calls=%fused_computation.59 | convolution fusion | flops 268500992 | bytes 4587520 | tf_op jit(solution)/shard_map/transpose(jvp())/dot_general | solution.py:93
  108.4 1.4 %convolution_convert_fusion.3 = bf16[64,2048]{1,0:T(8,128)(2,1)S(1)} fusion(bf16[2048,1024]{1,0:T(8,128)(2,1)S(1)} %bitcast.347, bf16[8,8,8,128]{3,2,1,0:T(8,128)(2,1)S(1)} %bitcast.411), kind=kOutput, calls=%fused_computation.9 | convolution fusion | flops 268566528 | bytes 4587520 | tf_op jit(solution)/shard_map/transpose(jvp())/dot_general | solution.py:82
  109.9 0.8 fusion.39
  111.3 1.5 %collective-permute-start.10 = (bf16[2,32,2048]{2,1,0:T(8,128)(2,1)S(1)}, bf16[2,32,2048]{2,1,0:T(8,128)(2,1)S(1)}, u32[]{:S(2)}, u32[]{:S(2)}) collective-permute-start(bf16[2,32,2048]{2,1,0:T(8,128)(2,1)S(1)} %get-tuple-element.23), channel_id=1, source_target_pairs={{16,0},{17,1},{18,2},{19,3},{20,4},{21,5},{22,6},{23,7},{24,8},{25... | collective-permute-start | bytes 786440 | tf_op jit(solution)/shard_map/ppermute | solution.py:15
  113.0 7.0 %collective-permute-done.10 = bf16[2,32,2048]{2,1,0:T(8,128)(2,1)S(1)} collective-permute-done((bf16[2,32,2048]{2,1,0:T(8,128)(2,1)S(1)}, bf16[2,32,2048]{2,1,0:T(8,128)(2,1)S(1)}, u32[]{:S(2)}, u32[]{:S(2)}) %collective-permute-start.10) | collective-permute-done | bytes 262176 | tf_op jit(solution)/shard_map/ppermute | solution.py:15
  120.0 1.4 %fusion.19 = bf16[8,8,8,128]{3,1,2,0:T(8,128)(2,1)S(1)} fusion(bf16[64,2048]{1,0:T(8,128)(2,1)S(1)} %bitcast.387, bf16[1024,2048]{1,0:T(8,128)(2,1)S(1)} %bitcast.353), kind=kOutput, calls=%fused_computation.64 | convolution fusion | flops 268500992 | bytes 4587520 | tf_op jit(solution)/shard_map/transpose(jvp())/dot_general | solution.py:93
  122.5 1.4 %convolution_convert_fusion.1 = bf16[64,2048]{1,0:T(8,128)(2,1)S(1)} fusion(bf16[2048,1024]{1,0:T(8,128)(2,1)S(1)} %bitcast.348, bf16[8,8,8,128]{3,2,1,0:T(8,128)(2,1)S(1)} %bitcast.409), kind=kOutput, calls=%fused_computation.7 | convolution fusion | flops 268566528 | bytes 4587520 | tf_op jit(solution)/shard_map/transpose(jvp())/dot_general | solution.py:82
  124.7 1.1 collective-permute-done.11
  125.8 1.5 %collective-permute-start.12 = (f32[2048]{0:T(1024)S(1)}, f32[2048]{0:T(1024)S(1)}, u32[]{:S(2)}, u32[]{:S(2)}) collective-permute-start(f32[2048]{0:T(1024)S(1)} %add.141), channel_id=1, source_target_pairs={{0,2},{1,3},{2,0},{3,1},{4,6},{5,7},{6,4},{7,5},{8,10},{9,11},{10,... | collective-permute-start | bytes 24584 | tf_op jit(solution)/shard_map/ppermute | solution.py:60
  127.3 2.1 %collective-permute-done.12 = f32[2048]{0:T(1024)S(1)} collective-permute-done((f32[2048]{0:T(1024)S(1)}, f32[2048]{0:T(1024)S(1)}, u32[]{:S(2)}, u32[]{:S(2)}) %collective-permute-start.12) | collective-permute-done | bytes 8224 | tf_op jit(solution)/shard_map/ppermute | solution.py:60
  129.5 1.8 %collective-permute-start.13 = (f32[2048]{0:T(1024)S(1)}, f32[2048]{0:T(1024)S(1)}, u32[]{:S(2)}, u32[]{:S(2)}) collective-permute-start(f32[2048]{0:T(1024)S(1)} %add.142), channel_id=1, source_target_pairs={{0,4},{1,5},{2,6},{3,7},{4,0},{5,1},{6,2},{7,3},{8,12},{9,13},{10,... | collective-permute-start | bytes 24584 | tf_op jit(solution)/shard_map/ppermute | solution.py:60
  131.8 1.3 collective-permute-done.13
  133.1 3.3 %collective-permute-start.14 = (f32[2048]{0:T(1024)S(1)}, f32[2048]{0:T(1024)S(1)}, u32[]{:S(2)}, u32[]{:S(2)}) collective-permute-start(f32[2048]{0:T(1024)S(1)} %add.143), channel_id=1, source_target_pairs={{0,8},{1,9},{2,10},{3,11},{4,12},{5,13},{6,14},{7,15},{8,0},{9,1},... | collective-permute-start | bytes 24584 | tf_op jit(solution)/shard_map/ppermute | solution.py:60
  136.4 0.8 maximum_bitcast_fusion.3
  137.2 0.8 collective-permute-done.14
  (111 shorter events, 14.8 us)
Async XLA Ops:
  0.6 5.1 %copy-start = (bf16[16,2048]{1,0:T(8,128)(2,1)S(1)}, bf16[16,2048]{1,0:T(8,128)(2,1)}, u32[]{:S(2)}) copy-start(bf16[16,2048]{1,0:T(8,128)(2,1)} %param.11) | copy-start | bytes 196612
  0.6 22.7 %collective-permute-start.4 = (bf16[1,64,2048]{2,1,0:T(8,128)(2,1)}, bf16[1,64,2048]{2,1,0:T(8,128)(2,1)S(1)}, u32[]{:S(2)}, u32[]{:S(2)}) collective-permute-start(bf16[1,64,2048]{2,1,0:T(8,128)(2,1)} %param.13), channel_id=1, source_target_pairs={{0,8},{1,9},{2,10},{3,11},{4,12},{5,13},{6,14},{7,15},{8,0},{9,1},... | collective-permute-start | bytes 786440 | tf_op jit(solution)/shard_map/ppermute | solution.py:36
  4.7 23.5 %collective-permute-start = (bf16[1,128,1024]{2,1,0:T(8,128)(2,1)}, bf16[1,128,1024]{2,1,0:T(8,128)(2,1)S(1)}, u32[]{:S(2)}, u32[]{:S(2)}) collective-permute-start(bf16[1,128,1024]{2,1,0:T(8,128)(2,1)} %param.12), channel_id=1, source_target_pairs={{0,8},{1,9},{2,10},{3,11},{4,12},{5,13},{6,14},{7,15},{8,0},{9,1},... | collective-permute-start | bytes 786440 | tf_op jit(solution)/shard_map/ppermute | solution.py:36
  24.3 14.2 %copy-start.5 = (bf16[4,1,32,2048]{3,2,1,0:T(8,128)(2,1)S(1)}, bf16[4,1,32,2048]{3,2,1,0:T(8,128)(2,1)}, u32[]{:S(2)}) copy-start(bf16[4,1,32,2048]{3,2,1,0:T(8,128)(2,1)} %param.8) | copy-start | bytes 1572868
  24.3 14.2 %copy-start.7 = (f32[1,2048]{1,0:T(1,128)S(1)}, f32[1,2048]{1,0:T(1,128)}, u32[]{:S(2)}) copy-start(f32[1,2048]{1,0:T(1,128)} %param.14) | copy-start | bytes 24580
  24.4 12.3 %collective-permute-start.5 = (bf16[2,64,2048]{2,1,0:T(8,128)(2,1)S(1)}, bf16[2,64,2048]{2,1,0:T(8,128)(2,1)S(1)}, u32[]{:S(2)}, u32[]{:S(2)}) collective-permute-start(bf16[2,64,2048]{2,1,0:T(8,128)(2,1)S(1)} %maximum_bitcast_fusion.2), channel_id=1, source_target_pairs={{0,2},{1,3},{2,0},{3,1},{4,6},{5,7},{6,4},{7,5},{8,10},{9,11},{10,... | collective-permute-start | bytes 1572872 | tf_op jit(solution)/shard_map/ppermute | solution.py:36
  30.1 15.2 %collective-permute-start.1 = (bf16[2,128,1024]{2,1,0:T(8,128)(2,1)}, bf16[2,128,1024]{2,1,0:T(8,128)(2,1)}, u32[]{:S(2)}, u32[]{:S(2)}) collective-permute-start(bf16[2,128,1024]{2,1,0:T(8,128)(2,1)} %maximum_bitcast_fusion.1), channel_id=1, source_target_pairs={{0,4},{1,5},{2,6},{3,7},{4,0},{5,1},{6,2},{7,3},{8,12},{9,13},{10,... | collective-permute-start | bytes 1572872 | tf_op jit(solution)/shard_map/ppermute | solution.py:36
  36.9 28.9 %collective-permute-start.6 = (bf16[4,64,2048]{2,1,0:T(8,128)(2,1)S(1)}, bf16[4,64,2048]{2,1,0:T(8,128)(2,1)}, u32[]{:S(2)}, u32[]{:S(2)}) collective-permute-start(bf16[4,64,2048]{2,1,0:T(8,128)(2,1)S(1)} %bitcast.368), channel_id=1, source_target_pairs={{0,4},{1,5},{2,6},{3,7},{4,0},{5,1},{6,2},{7,3},{8,12},{9,13},{10,... | collective-permute-start | bytes 3145736 | tf_op jit(solution)/shard_map/ppermute | solution.py:36
  46.5 21.5 %collective-permute-start.2 = (bf16[4,128,1024]{2,1,0:T(8,128)(2,1)S(1)}, bf16[4,128,1024]{2,1,0:T(8,128)(2,1)S(1)}, u32[]{:S(2)}, u32[]{:S(2)}) collective-permute-start(bf16[4,128,1024]{2,1,0:T(8,128)(2,1)S(1)} %bitcast.369), channel_id=1, source_target_pairs={{0,2},{1,3},{2,0},{3,1},{4,6},{5,7},{6,4},{7,5},{8,10},{9,11},{10,... | collective-permute-start | bytes 3145736 | tf_op jit(solution)/shard_map/ppermute | solution.py:36
  67.6 4.2 %collective-permute-start.7 = (bf16[8,64,2048]{2,1,0:T(8,128)(2,1)S(1)}, bf16[8,64,2048]{2,1,0:T(8,128)(2,1)S(1)}, u32[]{:S(2)}, u32[]{:S(2)}) collective-permute-start(bf16[8,64,2048]{2,1,0:T(8,128)(2,1)S(1)} %bitcast.362), channel_id=1, source_target_pairs={{0,1},{1,0},{2,3},{3,2},{4,5},{5,4},{6,7},{7,6},{8,9},{9,8},{10,11... | collective-permute-start | bytes 6291464 | tf_op jit(solution)/shard_map/ppermute | solution.py:36
  68.2 1.0 copy-start.6
  68.7 6.1 %collective-permute-start.3 = (bf16[8,128,1024]{2,1,0:T(8,128)(2,1)S(1)}, bf16[8,128,1024]{2,1,0:T(8,128)(2,1)S(1)}, u32[]{:S(2)}, u32[]{:S(2)}) collective-permute-start(bf16[8,128,1024]{2,1,0:T(8,128)(2,1)S(1)} %bitcast.363), channel_id=1, source_target_pairs={{0,1},{1,0},{2,3},{3,2},{4,5},{5,4},{6,7},{7,6},{8,9},{9,8},{10,11... | collective-permute-start | bytes 6291464 | tf_op jit(solution)/shard_map/ppermute | solution.py:36
  76.2 2.0 %copy-start.2 = (bf16[8,2,128,1024]{3,2,1,0:T(8,128)(2,1)}, bf16[8,2,128,1024]{3,2,1,0:T(8,128)(2,1)S(1)}, u32[]{:S(2)}) copy-start(bf16[8,2,128,1024]{3,2,1,0:T(8,128)(2,1)S(1)} %copy.107) | copy-start | bytes 12582916
  76.3 3.8 %copy-start.8 = (bf16[2,4,8,8,128]{4,3,2,1,0:T(8,128)(2,1)S(1)}, bf16[2,4,8,8,128]{4,3,2,1,0:T(8,128)(2,1)}, u32[]{:S(2)}) copy-start(bf16[2,4,8,8,128]{4,3,2,1,0:T(8,128)(2,1)} %get-tuple-element.64) | copy-start | bytes 393220
  81.3 6.8 %copy-start.3 = (bf16[8,2,128,1024]{3,2,1,0:T(8,128)(2,1)S(1)}, bf16[8,2,128,1024]{3,2,1,0:T(8,128)(2,1)}, u32[]{:S(2)}) copy-start(bf16[8,2,128,1024]{3,2,1,0:T(8,128)(2,1)} %copy-done.2) | copy-start | bytes 12582916
  81.3 7.7 %copy-start.4 = (bf16[2,2,2,2,64,2048]{5,4,3,2,1,0:T(8,128)(2,1)S(1)}, bf16[2,2,2,2,64,2048]{5,4,3,2,1,0:T(8,128)(2,1)}, u32[]{:S(2)}) copy-start(bf16[2,2,2,2,64,2048]{5,4,3,2,1,0:T(8,128)(2,1)} %copy.115) | copy-start | bytes 12582916
  84.5 9.2 %collective-permute-start.8 = (bf16[2,32,2048]{2,1,0:T(8,128)(2,1)S(1)}, bf16[2,32,2048]{2,1,0:T(8,128)(2,1)S(1)}, u32[]{:S(2)}, u32[]{:S(2)}) collective-permute-start(bf16[2,32,2048]{2,1,0:T(8,128)(2,1)S(1)} %fusion), channel_id=1, source_target_pairs={{0,16},{1,17},{2,18},{3,19},{4,20},{5,21},{6,22},{7,23},{8,24},{9,... | collective-permute-start | bytes 786440 | tf_op jit(solution)/shard_map/ppermute | solution.py:15
  97.0 8.3 %collective-permute-start.9 = (bf16[2,32,2048]{2,1,0:T(8,128)(2,1)S(1)}, bf16[2,32,2048]{2,1,0:T(8,128)(2,1)S(1)}, u32[]{:S(2)}, u32[]{:S(2)}) collective-permute-start(bf16[2,32,2048]{2,1,0:T(8,128)(2,1)S(1)} %fusion.76), channel_id=1, source_target_pairs={{0,16},{16,0},{1,17},{17,1},{2,18},{18,2},{3,19},{19,3},{4,20},{20... | collective-permute-start | bytes 786440 | tf_op jit(solution)/shard_map/ppermute | solution.py:130
  111.3 8.8 %collective-permute-start.10 = (bf16[2,32,2048]{2,1,0:T(8,128)(2,1)S(1)}, bf16[2,32,2048]{2,1,0:T(8,128)(2,1)S(1)}, u32[]{:S(2)}, u32[]{:S(2)}) collective-permute-start(bf16[2,32,2048]{2,1,0:T(8,128)(2,1)S(1)} %get-tuple-element.23), channel_id=1, source_target_pairs={{16,0},{17,1},{18,2},{19,3},{20,4},{21,5},{22,6},{23,7},{24,8},{25... | collective-permute-start | bytes 786440 | tf_op jit(solution)/shard_map/ppermute | solution.py:15
  122.5 16.1 %copy-start.1 = (bf16[16,2048]{1,0:T(8,128)(2,1)S(1)}, bf16[16,2048]{1,0:T(8,128)(2,1)}, u32[]{:S(2)}) copy-start(bf16[16,2048]{1,0:T(8,128)(2,1)} %param.11) | copy-start | bytes 196612
  124.6 1.2 collective-permute-start.11
  125.8 3.7 %collective-permute-start.12 = (f32[2048]{0:T(1024)S(1)}, f32[2048]{0:T(1024)S(1)}, u32[]{:S(2)}, u32[]{:S(2)}) collective-permute-start(f32[2048]{0:T(1024)S(1)} %add.141), channel_id=1, source_target_pairs={{0,2},{1,3},{2,0},{3,1},{4,6},{5,7},{6,4},{7,5},{8,10},{9,11},{10,... | collective-permute-start | bytes 24584 | tf_op jit(solution)/shard_map/ppermute | solution.py:60
  129.5 3.7 %collective-permute-start.13 = (f32[2048]{0:T(1024)S(1)}, f32[2048]{0:T(1024)S(1)}, u32[]{:S(2)}, u32[]{:S(2)}) collective-permute-start(f32[2048]{0:T(1024)S(1)} %add.142), channel_id=1, source_target_pairs={{0,4},{1,5},{2,6},{3,7},{4,0},{5,1},{6,2},{7,3},{8,12},{9,13},{10,... | collective-permute-start | bytes 24584 | tf_op jit(solution)/shard_map/ppermute | solution.py:60
  133.1 4.9 %collective-permute-start.14 = (f32[2048]{0:T(1024)S(1)}, f32[2048]{0:T(1024)S(1)}, u32[]{:S(2)}, u32[]{:S(2)}) collective-permute-start(f32[2048]{0:T(1024)S(1)} %add.143), channel_id=1, source_target_pairs={{0,8},{1,9},{2,10},{3,11},{4,12},{5,13},{6,14},{7,15},{8,0},{9,1},... | collective-permute-start | bytes 24584 | tf_op jit(solution)/shard_map/ppermute | solution.py:60

commit v7 on v3

--- a/solution.py
+++ b/solution.py
@@ -29,27 +29,37 @@
 
 def butterfly_gathers(shards, orders, axis, size):
     index = lax.axis_index(axis)
-    held = [shard for shard in shards]
-    for level in range(len(orders[0])):
+    held = [shard[0][None] for shard in shards]
+    done = [[] for _ in shards]
+    for level in range(len(orders[0]) - 1):
         for which, order in enumerate(orders):
             step = order[level]
             other = lax.ppermute(held[which], axis, [(j, j ^ step) for j in range(size)])
             upper = ((index // step) % 2) == 1
             low = jnp.where(upper, other, held[which])
             high = jnp.where(upper, held[which], other)
-            held[which] = jnp.stack([low, high], axis=1).reshape(
-                (-1,) + held[which].shape[1:]
-            )
-    results = []
+            grid = (2,) * len(done[which]) + held[which].shape[1:]
+            place = sum(1 for value in done[which] if value > step)
+            held[which] = jnp.stack(
+                [low.reshape(grid), high.reshape(grid)], axis=place
+            ).reshape((-1,) + held[which].shape[1:])
+            done[which].append(step)
+    pairs = []
     for which, order in enumerate(orders):
+        other = lax.ppermute(held[which], axis, [(j, j ^ order[-1]) for j in range(size)])
         block_rows, width = held[which].shape[1:]
-        wanted = sorted(order, reverse=True)
-        if order != wanted:
-            split = held[which].reshape(tuple(2 for _ in order) + (block_rows, width))
-            axes = tuple(order.index(value) for value in wanted) + (len(order), len(order) + 1)
-            held[which] = jnp.transpose(split, axes)
-        results.append(held[which].reshape(size * block_rows, width))
-    return results
+        pairs.append((held[which].reshape(-1, width), other.reshape(-1, width), block_rows))
+    return pairs
+
+
+def split_product(rows, pair, own_bit):
+    mine, theirs, block_rows = pair
+    grid = rows.reshape(rows.shape[0], -1, 2, block_rows)
+    own_part = lax.dynamic_index_in_dim(grid, own_bit, 2, False).reshape(rows.shape[0], -1)
+    other_part = lax.dynamic_index_in_dim(grid, 1 - own_bit, 2, False).reshape(rows.shape[0], -1)
+    return jnp.dot(own_part, mine, preferred_element_type=jnp.float32) + jnp.dot(
+        other_part, theirs, preferred_element_type=jnp.float32
+    )
 
 
 def butterfly_sum(value, axis, size):
@@ -70,7 +80,7 @@
     )
 
 
-def attend_layer(section_input, source, key_mask, query_weight, output_weight, gain_vector):
+def attend_layer(section_input, source, key_mask, project_query, project_output, gain_vector):
     series_count, seq_length, model_width = section_input.shape
     half_width = model_width // 2
     head_dim = half_width // HEADS
@@ -79,7 +89,7 @@
     normed = rms_scale(input_wide, gain_vector)
     normed_source = rms_scale(source.astype(jnp.float32), gain_vector)
     normed_rows = normed.astype(jnp.bfloat16).reshape(series_count * seq_length, model_width)
-    query_flat = jnp.dot(normed_rows, query_weight, preferred_element_type=jnp.float32)
+    query_flat = project_query(normed_rows)
     queries = query_flat.astype(jnp.bfloat16).reshape(head_shape)
     key_rows = normed_source[..., :half_width].astype(jnp.bfloat16).reshape(head_shape)
     value_rows = normed_source[..., half_width:].astype(jnp.bfloat16).reshape(head_shape)
@@ -90,7 +100,7 @@
     probs = (raised / jnp.sum(raised, axis=-1, keepdims=True)).astype(jnp.bfloat16)
     mixed = jnp.einsum("bhqk,bkhd->bqhd", probs, value_rows, preferred_element_type=jnp.float32)
     mixed = mixed.astype(jnp.bfloat16).reshape(series_count * seq_length, half_width)
-    update = jnp.dot(mixed, output_weight, preferred_element_type=jnp.float32)
+    update = project_output(mixed)
     return (input_wide + update.reshape(series_count, seq_length, model_width)).astype(jnp.bfloat16)
 
 
@@ -102,13 +112,26 @@
     rows = micro_count * series_count
     act_shape = (rows, seq_length, model_width)
     fsdp_count = lax.axis_size("fsdp")
-    if fsdp_count & (fsdp_count - 1):
+    if fsdp_count < 2 or fsdp_count & (fsdp_count - 1):
         query_weight = lax.all_gather(query_weights, "fsdp", axis=1, tiled=True)[0]
         output_weight = lax.all_gather(output_weights, "fsdp", axis=1, tiled=True)[0]
+
+        def query_weight(rows, weight=query_weight):
+            return jnp.dot(rows, weight, preferred_element_type=jnp.float32)
+
+        def output_weight(rows, weight=output_weight):
+            return jnp.dot(rows, weight, preferred_element_type=jnp.float32)
     else:
-        query_weight, output_weight = butterfly_gathers(
+        own_bit = lax.axis_index("fsdp") % 2
+        query_pair, output_pair = butterfly_gathers(
             [query_weights, output_weights], exchange_orders(fsdp_count), "fsdp", fsdp_count
         )
+
+        def query_weight(rows):
+            return split_product(rows, query_pair, own_bit)
+
+        def output_weight(rows):
+            return split_product(rows, output_pair, own_bit)
     gain_vector = gains[0]
     code_rows = codes.reshape(micro_count, series_count, seq_length)
     code_count = plan_table.shape[0]

time: 137 us -> 216 us (1.58)
  the two profiles are of different devices: /device:TPU:0 before, /device:TPU:14 now
where the time goes in v7:
time: 216 us; the launch traced here: 212 us
  local copies, waits for them, and re-layouts  77.3 us (36%)
  waiting for transfers between devices  60.1 us (28%)
  matrix products  34.1 us (16%)
  other arithmetic  25.2 us (12%)
  starting transfers between devices  14.2 us (7%)
    ppermute x6, waiting for transfers between devices, butterfly_gathers(): lax.ppermute(held[which], axis, [(j, j ^ step) for j in range(size)])  42.6 us
    add_any x4, local copies, waits for them, and re-layouts, split_product(): lax.dynamic_index_in_dim(grid, own_bit, 2, False).reshape(rows.shape[0], -1)  26.6 us
    dynamic_update_slice x4, local copies, waits for them, and re-layouts, split_product(): lax.dynamic_index_in_dim(grid, 1 - own_bit, 2, False)  24.1 us
    dot_general x7, matrix products, split_product(): jnp.dot(other_part, theirs, preferred_element_type=jnp.float32)  17 us
    dot_general x7, matrix products, split_product(): jnp.dot(own_part, mine, preferred_element_type=jnp.float32)  12.2 us
    ppermute x2, waiting for transfers between devices, send_to(): return lax.ppermute(arrays, axis, [(source, target)])  9.82 us
    convert_element_type x4, local copies, waits for them, and re-layouts, attend_layer(): input_wide = section_input.astype(jnp.float32)  8.44 us
    ppermute x4, waiting for transfers between devices, butterfly_sum(): lax.ppermute(value, axis, [(j, j ^ step) for j in range(size)])  7.61 us
  transfers between devices with their start and end apart: 14, of which 10 were waited for; matrix products, arithmetic and copies ran while one was open for 34% of the time, Pallas kernels for 0%

profile of v7, /device:TPU:14, one launch (start us, length us, event | category | flops | bytes accessed | tf_op | source)
XLA Modules:
  0.0 212.3 jit_solution(72699838097496899)
XLA Ops:
  0.7 2.7 %collective-permute-start = (bf16[1,64,2048]{2,1,0:T(8,128)(2,1)}, bf16[1,64,2048]{2,1,0:T(8,128)(2,1)S(1)}, u32[]{:S(2)}, u32[]{:S(2)}) collective-permute-start(bf16[1,64,2048]{2,1,0:T(8,128)(2,1)} %param.13), channel_id=1, source_target_pairs={{0,8},{1,9},{2,10},{3,11},{4,12},{5,13},{6,14},{7,15},{8,0},{9,1},... | collective-permute-start | bytes 786440 | tf_op jit(solution)/shard_map/ppermute | solution.py:37
  4.9 15.5 %collective-permute-done = bf16[1,64,2048]{2,1,0:T(8,128)(2,1)S(1)} collective-permute-done((bf16[1,64,2048]{2,1,0:T(8,128)(2,1)}, bf16[1,64,2048]{2,1,0:T(8,128)(2,1)S(1)}, u32[]{:S(2)}, u32[]{:S(2)}) %collective-permute-start) | collective-permute-done | bytes 262176 | tf_op jit(solution)/shard_map/ppermute | solution.py:37
  22.3 3.6 %collective-permute-done.4 = bf16[1,128,1024]{2,1,0:T(8,128)(2,1)} collective-permute-done((bf16[1,128,1024]{2,1,0:T(8,128)(2,1)}, bf16[1,128,1024]{2,1,0:T(8,128)(2,1)}, u32[]{:S(2)}, u32[]{:S(2)}) %collective-permute-start.4) | collective-permute-done | bytes 262176 | tf_op jit(solution)/shard_map/ppermute | solution.py:37
  27.0 1.4 collective-permute-start.5
  28.4 6.9 %collective-permute-done.1 = bf16[2,64,2048]{2,1,0:T(8,128)(2,1)S(1)} collective-permute-done((bf16[2,64,2048]{2,1,0:T(8,128)(2,1)S(1)}, bf16[2,64,2048]{2,1,0:T(8,128)(2,1)S(1)}, u32[]{:S(2)}, u32[]{:S(2)}) %collective-permute-start.1) | collective-permute-done | bytes 524320 | tf_op jit(solution)/shard_map/ppermute | solution.py:37
  36.8 5.0 %collective-permute-done.5 = bf16[2,128,1024]{2,1,0:T(8,128)(2,1)S(1)} collective-permute-done((bf16[2,128,1024]{2,1,0:T(8,128)(2,1)S(1)}, bf16[2,128,1024]{2,1,0:T(8,128)(2,1)S(1)}, u32[]{:S(2)}, u32[]{:S(2)}) %collective-permute-start.5) | collective-permute-done | bytes 524320 | tf_op jit(solution)/shard_map/ppermute | solution.py:37
  43.6 1.9 reshape.291
  45.5 2.4 %copy.45 = f32[128,8,2,128]{0,3,1,2:T(8,128)} copy(f32[128,8,2,128]{3,2,1,0:T(2,128)} %reshape.291) | data formatting | bytes 2097152 | tf_op jit(solution)/shard_map/jvp()/convert_element_type | solution.py:88
  47.9 1.9 reshape.293
  49.7 2.3 %copy.51 = f32[128,8,2,128]{0,3,1,2:T(8,128)} copy(f32[128,8,2,128]{3,2,1,0:T(2,128)} %reshape.293) | data formatting | bytes 2097152 | tf_op jit(solution)/shard_map/convert_element_type | solution.py:88
  52.1 11.4 %collective-permute-done.2 = bf16[4,64,2048]{2,1,0:T(8,128)(2,1)} collective-permute-done((bf16[4,64,2048]{2,1,0:T(8,128)(2,1)S(1)}, bf16[4,64,2048]{2,1,0:T(8,128)(2,1)}, u32[]{:S(2)}, u32[]{:S(2)}) %collective-permute-start.2) | collective-permute-done | bytes 1048608 | tf_op jit(solution)/shard_map/ppermute | solution.py:37
  63.5 1.4 broadcast_select_fusion.3
  64.8 1.5 pad_maximum_fusion.1
  66.6 1.7 broadcast_select_fusion.1
  69.8 1.2 multiply_convert_fusion.1
  71.0 1.9 constant_dynamic-slice_fusion.2
  73.2 3.1 %convolution_convert_fusion.16 = bf16[512,128]{1,0:T(8,128)(2,1)} fusion(bf16[512,2048]{1,0:T(8,128)(2,1)} %bitcast.13, bf16[128,2048]{1,0:T(8,128)(2,1)S(1)} %bitcast.243), kind=kOutput, calls=%fused_computation.43 | convolution fusion | flops 268500992 | bytes 2752512 | tf_op jit(solution)/shard_map/transpose(jvp())/dot_general | solution.py:60
  76.3 1.3 fusion.77
  78.1 3.0 %convolution_convert_fusion.17 = bf16[512,128]{1,0:T(8,128)(2,1)} fusion(bf16[512,2048]{1,0:T(8,128)(2,1)} %bitcast.9, bf16[128,2048]{1,0:T(8,128)(2,1)S(1)} %bitcast.244), kind=kOutput, calls=%fused_computation.44 | convolution fusion | flops 268500992 | bytes 2752512 | tf_op jit(solution)/shard_map/transpose(jvp())/dot_general | solution.py:60
  81.1 2.1 fusion.39
  84.7 2.1 constant_dynamic-slice_fusion
  86.7 1.3 copy.57
  88.1 3.1 %fusion.79 = f32[128,2048]{1,0:T(8,128)} fusion(bf16[128,512]{0,1:T(8,128)(2,1)S(1)} %bitcast.272, bf16[512,2048]{1,0:T(8,128)(2,1)} %bitcast.13), kind=kOutput, calls=%fused_computation.184 | convolution fusion | flops 268435456 | bytes 3276800 | tf_op jit(solution)/shard_map/dot_general | solution.py:60
  91.5 2.3 %convolution_add_fusion = f32[128,2048]{1,0:T(8,128)S(1)} fusion(f32[128,2048]{1,0:T(8,128)} %fusion.79, bf16[128,512]{0,1:T(8,128)(2,1)S(1)} %bitcast.271, bf16[512,2048]{1,0:T(8,128)(2,1)} %bitcast.9), kind=kOutput, calls=%fused_computation | convolution fusion | flops 268697600 | bytes 4325376 | tf_op jit(solution)/shard_map/dot_general | solution.py:60
  94.8 1.5 collective-permute-start.8
  97.5 1.3 reshape.270
  98.8 2.2 %fusion.38 = bf16[16,8,8,128]{3,1,2,0:T(8,128)(2,1)S(1)} fusion(f32[128,1024]{1,0:T(8,128)} %fusion.77, bf16[128,1024]{0,1:T(8,128)(2,1)} %bitcast.267, bf16[1024,1024]{1,0:T(8,128)(2,1)} %bitcast.32), kind=kOutput, calls=%fused_computation.109 | convolution fusion | flops 268697600 | bytes 3145728 | tf_op jit(solution)/shard_map/jvp()/dot_general | solution.py:60
  101.1 9.8 %collective-permute-done.8 = bf16[4,32,2048]{2,1,0:T(8,128)(2,1)S(1)} collective-permute-done((bf16[4,32,2048]{2,1,0:T(8,128)(2,1)}, bf16[4,32,2048]{2,1,0:T(8,128)(2,1)S(1)}, u32[]{:S(2)}, u32[]{:S(2)}) %collective-permute-start.8) | collective-permute-done | bytes 524320 | tf_op jit(solution)/shard_map/ppermute | solution.py:15
  114.7 2.4 %collective-permute-start.9 = (bf16[4,32,2048]{2,1,0:T(8,128)(2,1)}, bf16[4,32,2048]{2,1,0:T(8,128)(2,1)}, u32[]{:S(2)}, u32[]{:S(2)}) collective-permute-start(bf16[4,32,2048]{2,1,0:T(8,128)(2,1)} %fusion.16), channel_id=1, source_target_pairs={{16,0},{17,1},{18,2},{19,3},{20,4},{21,5},{22,6},{23,7},{24,8},{25... | collective-permute-start | bytes 1572872 | tf_op jit(solution)/shard_map/ppermute | solution.py:15
  119.0 2.4 %convolution_convert_fusion.4 = bf16[128,1024]{1,0:T(8,128)(2,1)S(1)} fusion(bf16[1024,1024]{1,0:T(8,128)(2,1)} %bitcast.32, bf16[16,8,8,128]{3,2,1,0:T(8,128)(2,1)S(1)} %bitcast.252), kind=kOutput, calls=%fused_computation.22 | convolution fusion | flops 268566528 | bytes 2621440 | tf_op jit(solution)/shard_map/transpose(jvp())/dot_general | solution.py:60
  122.6 12.4 %dynamic_update_slice.43 = bf16[128,8,2,128]{3,2,1,0:T(2,128)(2,1)S(1)} dynamic-update-slice(bf16[128,8,2,128]{3,2,1,0:T(2,128)(2,1)S(1)} %broadcast_in_dim.89.clone, bf16[128,8,1,128]{3,2,1,0:T(2,128)(2,1)} %broadcast_in_dim.101, s32[]{:T(128)} %constant.145.clone.1, s32[]{:T(128)} %constant.145.clone.1, s32[]{:T(128)S(6)} %select_n.175, s32[]{:T(128)} %constant.145.clone.1) | dynamic-update-slice | bytes 524292 | tf_op jit(solution)/shard_map/transpose(jvp(jit(dynamic_index_in_dim)))/dynamic_update_slice | solution.py:59
  135.0 2.6 %dynamic-slice_add_fusion = bf16[128,8,1,128]{3,2,1,0:T(2,128)(2,1)} fusion(bf16[128,8,1,128]{3,2,1,0:T(2,128)(2,1)} %broadcast_in_dim.102, bf16[128,8,2,128]{3,2,1,0:T(2,128)(2,1)S(1)} %dynamic_update_slice.43, s32[]{:T(128)S(6)} %select_n.176), kind=kLoop, calls=%fused_computation.93 | loop fusion | flops 524288 | bytes 786436 | tf_op jit(solution)/shard_map/transpose(jvp(jit(dynamic_index_in_dim)))/dynamic_update_slice | solution.py:58
  137.6 12.4 %add_any.78 = bf16[128,8,2,128]{3,2,1,0:T(2,128)(2,1)S(1)} dynamic-update-slice(bf16[128,8,2,128]{3,2,1,0:T(2,128)(2,1)S(1)} %dynamic_update_slice.43, bf16[128,8,1,128]{3,2,1,0:T(2,128)(2,1)} %dynamic-slice_add_fusion, s32[]{:T(128)} %constant.145.clone.1, s32[]{:T(128)} %constant.145.clone.1, s32[]{:T(128)S(6)} %select_n.176, s32[]{:T(128)} %constant.145.clone.1) | dynamic-update-slice | bytes 524292 | tf_op jit(solution)/shard_map/transpose(jvp())/add_any | solution.py:58
  150.0 1.3 reshape.296
  151.3 2.6 %convolution_convert_fusion.14 = bf16[128,512]{1,0:T(8,128)(2,1)S(1)} fusion(bf16[128,2048]{1,0:T(8,128)(2,1)} %bitcast.45, bf16[512,2048]{1,0:T(8,128)(2,1)} %bitcast.13), kind=kOutput, calls=%fused_computation.41 | convolution fusion | flops 268500992 | bytes 2752512 | tf_op jit(solution)/shard_map/transpose(jvp())/dot_general | solution.py:60
  153.9 2.6 %convolution_convert_fusion.15 = bf16[128,512]{1,0:T(8,128)(2,1)S(1)} fusion(bf16[128,2048]{1,0:T(8,128)(2,1)} %bitcast.45, bf16[512,2048]{1,0:T(8,128)(2,1)} %bitcast.9), kind=kOutput, calls=%fused_computation.42 | convolution fusion | flops 268500992 | bytes 2752512 | tf_op jit(solution)/shard_map/transpose(jvp())/dot_general | solution.py:60
  157.7 1.4 fusion.13
  161.4 2.4 %convolution_convert_fusion.7 = bf16[128,1024]{1,0:T(8,128)(2,1)S(1)} fusion(bf16[1024,1024]{1,0:T(8,128)(2,1)} %bitcast.32, bf16[16,8,8,128]{3,2,1,0:T(8,128)(2,1)S(1)} %bitcast.254), kind=kOutput, calls=%fused_computation.25 | convolution fusion | flops 268566528 | bytes 2621440 | tf_op jit(solution)/shard_map/transpose(jvp())/dot_general | solution.py:60
  166.0 11.7 %dynamic_update_slice.40 = bf16[128,8,2,128]{3,2,1,0:T(2,128)(2,1)S(1)} dynamic-update-slice(bf16[128,8,2,128]{3,2,1,0:T(2,128)(2,1)S(1)} %broadcast_in_dim.89.clone.1, bf16[128,8,1,128]{3,2,1,0:T(2,128)(2,1)S(1)} %broadcast_in_dim.99, s32[]{:T(128)} %constant.145.clone.1, s32[]{:T(128)} %constant.145.clone.1, s32[]{:T(128)S(6)} %select_n.175, s32[]{:T(128)} %constant.145.clone.1) | dynamic-update-slice | bytes 524292 | tf_op jit(solution)/shard_map/transpose(jvp(jit(dynamic_index_in_dim)))/dynamic_update_slice | solution.py:59
  177.7 2.7 %dynamic-slice_add_fusion.1 = bf16[128,8,1,128]{3,2,1,0:T(2,128)(2,1)} fusion(bf16[128,8,1,128]{3,2,1,0:T(2,128)(2,1)} %broadcast_in_dim.100, bf16[128,8,2,128]{3,2,1,0:T(2,128)(2,1)S(1)} %dynamic_update_slice.40, s32[]{:T(128)S(6)} %select_n.176), kind=kLoop, calls=%fused_computation.94 | loop fusion | flops 524288 | bytes 786436 | tf_op jit(solution)/shard_map/transpose(jvp(jit(dynamic_index_in_dim)))/dynamic_update_slice | solution.py:58
  180.5 12.6 %add_any.73 = bf16[128,8,2,128]{3,2,1,0:T(2,128)(2,1)S(1)} dynamic-update-slice(bf16[128,8,2,128]{3,2,1,0:T(2,128)(2,1)S(1)} %dynamic_update_slice.40, bf16[128,8,1,128]{3,2,1,0:T(2,128)(2,1)} %dynamic-slice_add_fusion.1, s32[]{:T(128)} %constant.145.clone.1, s32[]{:T(128)} %constant.145.clone.1, s32[]{:T(128)S(6)} %select_n.176, s32[]{:T(128)} %constant.145.clone.1) | dynamic-update-slice | bytes 524292 | tf_op jit(solution)/shard_map/transpose(jvp())/add_any | solution.py:58
  193.1 1.2 reshape.294
  194.3 2.5 %fusion.26 = (f32[2048]{0:T(1024)S(1)}, f32[4,32]{1,0:T(4,128)S(1)}, f32[4,32]{1,0:T(4,128)S(1)}, f32[2048]{0:T(1024)S(1)}, f32[4,32]{1,0:T(4,128)S(1)}, /*index=5*/f32[2048]{0:T(1024)S(1)}) fusion(bf16[4,32,1024]{2,1,0:T(8,128)(2,1)} %bitcast.261, bf16[4,32,1024]{2,1,0:T(8,128)(2,1)S(1)} %bitcast.259, bf16[4,1,32,2048]{3,2,1,0:T(8,128)(2,1)S(1)} %copy-done.1, ...), kind=kLoop, calls=%fused_computation.67 | loop fusion | flops 5498496 | bytes 4229632 | tf_op jit(solution)/shard_map/transpose(jvp())/reduce_sum | solution.py:77
  196.9 1.2 collective-permute-done.10
  198.6 3.1 %collective-permute-done.11 = f32[2048]{0:T(1024)S(1)} collective-permute-done((f32[2048]{0:T(1024)S(1)}, f32[2048]{0:T(1024)S(1)}, u32[]{:S(2)}, u32[]{:S(2)}) %collective-permute-start.11) | collective-permute-done | bytes 8224 | tf_op jit(solution)/shard_map/ppermute | solution.py:70
  202.1 3.3 %collective-permute-done.12 = f32[2048]{0:T(1024)S(1)} collective-permute-done((f32[2048]{0:T(1024)S(1)}, f32[2048]{0:T(1024)S(1)}, u32[]{:S(2)}, u32[]{:S(2)}) %collective-permute-start.12) | collective-permute-done | bytes 8224 | tf_op jit(solution)/shard_map/ppermute | solution.py:70
  205.4 3.4 %collective-permute-start.13 = (f32[2048]{0:T(1024)S(1)}, f32[2048]{0:T(1024)S(1)}, u32[]{:S(2)}, u32[]{:S(2)}) collective-permute-start(f32[2048]{0:T(1024)S(1)} %add.135), channel_id=1, source_target_pairs={{0,8},{1,9},{2,10},{3,11},{4,12},{5,13},{6,14},{7,15},{8,0},{9,1},... | collective-permute-start | bytes 24584 | tf_op jit(solution)/shard_map/ppermute | solution.py:70
  208.8 2.9 %fusion.36 = bf16[1,4,1,32,2048]{4,3,2,1,0:T(8,128)(2,1)} fusion(f32[4,32,2048]{2,1,0:T(8,128)S(1)} %copy-done.3, f32[4,32,2048]{2,1,0:T(8,128)S(1)} %copy-done.4, f32[4,32,2048]{2,1,0:T(8,128)S(1)} %copy-done.5, bf16[4,32,2048]{2,1,0:T(8,128)(2,1)} %collective-permute-done.9, bf16[4,32,1024]{2,1,0:T(8,128)(2,1)S(1)} %bitcast.262, ...), kind=kLoop, calls=%fused_computation.88 | loop fusion | flops 8388608 | bytes 5777922
  (148 shorter events, 28.2 us)
Async XLA Ops:
  0.6 3.9 %copy-start = (bf16[16,2048]{1,0:T(8,128)(2,1)S(1)}, bf16[16,2048]{1,0:T(8,128)(2,1)}, u32[]{:S(2)}) copy-start(bf16[16,2048]{1,0:T(8,128)(2,1)} %param.11) | copy-start | bytes 196612
  0.6 25.3 %copy-start.22 = (bf16[1,128,1024]{2,1,0:T(8,128)(2,1)S(1)}, bf16[1,128,1024]{2,1,0:T(8,128)(2,1)}, u32[]{:S(2)}) copy-start(bf16[1,128,1024]{2,1,0:T(8,128)(2,1)} %param.12) | copy-start | bytes 786436
  0.7 21.5 %copy-start.1 = (bf16[4,1,32,2048]{3,2,1,0:T(8,128)(2,1)S(1)}, bf16[4,1,32,2048]{3,2,1,0:T(8,128)(2,1)}, u32[]{:S(2)}) copy-start(bf16[4,1,32,2048]{3,2,1,0:T(8,128)(2,1)} %param.8) | copy-start | bytes 1572868
  0.7 19.8 %collective-permute-start = (bf16[1,64,2048]{2,1,0:T(8,128)(2,1)}, bf16[1,64,2048]{2,1,0:T(8,128)(2,1)S(1)}, u32[]{:S(2)}, u32[]{:S(2)}) collective-permute-start(bf16[1,64,2048]{2,1,0:T(8,128)(2,1)} %param.13), channel_id=1, source_target_pairs={{0,8},{1,9},{2,10},{3,11},{4,12},{5,13},{6,14},{7,15},{8,0},{9,1},... | collective-permute-start | bytes 786440 | tf_op jit(solution)/shard_map/ppermute | solution.py:37
  3.3 22.6 %collective-permute-start.4 = (bf16[1,128,1024]{2,1,0:T(8,128)(2,1)}, bf16[1,128,1024]{2,1,0:T(8,128)(2,1)}, u32[]{:S(2)}, u32[]{:S(2)}) collective-permute-start(bf16[1,128,1024]{2,1,0:T(8,128)(2,1)} %param.12), channel_id=1, source_target_pairs={{0,8},{1,9},{2,10},{3,11},{4,12},{5,13},{6,14},{7,15},{8,0},{9,1},... | collective-permute-start | bytes 786440 | tf_op jit(solution)/shard_map/ppermute | solution.py:37
  4.9 38.7 %copy-start.2 = (f32[4,32,2048]{2,1,0:T(8,128)}, f32[4,32,2048]{2,1,0:T(8,128)S(1)}, u32[]{:S(2)}) copy-start(f32[4,32,2048]{2,1,0:T(8,128)S(1)} %get-tuple-element.45) | copy-start | bytes 3145732
  21.5 13.8 %collective-permute-start.1 = (bf16[2,64,2048]{2,1,0:T(8,128)(2,1)S(1)}, bf16[2,64,2048]{2,1,0:T(8,128)(2,1)S(1)}, u32[]{:S(2)}, u32[]{:S(2)}) collective-permute-start(bf16[2,64,2048]{2,1,0:T(8,128)(2,1)S(1)} %pad_maximum_fusion.5), channel_id=1, source_target_pairs={{0,2},{1,3},{2,0},{3,1},{4,6},{5,7},{6,4},{7,5},{8,10},{9,11},{10,... | collective-permute-start | bytes 1572872 | tf_op jit(solution)/shard_map/ppermute | solution.py:37
  27.0 14.8 %collective-permute-start.5 = (bf16[2,128,1024]{2,1,0:T(8,128)(2,1)S(1)}, bf16[2,128,1024]{2,1,0:T(8,128)(2,1)S(1)}, u32[]{:S(2)}, u32[]{:S(2)}) collective-permute-start(bf16[2,128,1024]{2,1,0:T(8,128)(2,1)S(1)} %pad_maximum_fusion.4), channel_id=1, source_target_pairs={{0,4},{1,5},{2,6},{3,7},{4,0},{5,1},{6,2},{7,3},{8,12},{9,13},{10,... | collective-permute-start | bytes 1572872 | tf_op jit(solution)/shard_map/ppermute | solution.py:37
  35.5 28.0 %collective-permute-start.2 = (bf16[4,64,2048]{2,1,0:T(8,128)(2,1)S(1)}, bf16[4,64,2048]{2,1,0:T(8,128)(2,1)}, u32[]{:S(2)}, u32[]{:S(2)}) collective-permute-start(bf16[4,64,2048]{2,1,0:T(8,128)(2,1)S(1)} %bitcast.245), channel_id=1, source_target_pairs={{0,4},{1,5},{2,6},{3,7},{4,0},{5,1},{6,2},{7,3},{8,12},{9,13},{10,... | collective-permute-start | bytes 3145736 | tf_op jit(solution)/shard_map/ppermute | solution.py:37
  43.0 23.6 %collective-permute-start.6 = (bf16[4,128,1024]{2,1,0:T(8,128)(2,1)}, bf16[4,128,1024]{2,1,0:T(8,128)(2,1)}, u32[]{:S(2)}, u32[]{:S(2)}) collective-permute-start(bf16[4,128,1024]{2,1,0:T(8,128)(2,1)} %bitcast.24), channel_id=1, source_target_pairs={{0,2},{1,3},{2,0},{3,1},{4,6},{5,7},{6,4},{7,5},{8,10},{9,11},{10,... | collective-permute-start | bytes 3145736 | tf_op jit(solution)/shard_map/ppermute | solution.py:37
  45.5 2.4 %copy-start.10 = (f32[4,1,32,2048]{3,2,0,1:T(8,128)S(1)}, f32[4,1,32,2048]{3,2,0,1:T(8,128)}, u32[]{:S(2)}) copy-start(f32[4,1,32,2048]{3,2,0,1:T(8,128)} %bitcast_convert_fusion) | copy-start | bytes 3145732
  47.9 4.2 %copy-start.19 = (f32[1,2048]{1,0:T(1,128)S(1)}, f32[1,2048]{1,0:T(1,128)}, u32[]{:S(2)}) copy-start(f32[1,2048]{1,0:T(1,128)} %param.14) | copy-start | bytes 24580
  66.4 11.8 %collective-permute-start.3 = (bf16[8,64,2048]{2,1,0:T(8,128)(2,1)}, bf16[8,64,2048]{2,1,0:T(8,128)(2,1)}, u32[]{:S(2)}, u32[]{:S(2)}) collective-permute-start(bf16[8,64,2048]{2,1,0:T(8,128)(2,1)} %bitcast.8), channel_id=1, source_target_pairs={{0,1},{1,0},{2,3},{3,2},{4,5},{5,4},{6,7},{7,6},{8,9},{9,8},{10,11... | collective-permute-start | bytes 6291464 | tf_op jit(solution)/shard_map/ppermute | solution.py:49
  68.3 1.2 copy-start.8
  68.3 1.5 copy-start.9
  68.5 2.5 %copy-start.25 = (s32[4,1,32]{2,1,0:T(1,128)S(1)}, s32[4,1,32]{2,1,0:T(1,128)}, u32[]{:S(2)}) copy-start(s32[4,1,32]{2,1,0:T(1,128)} %param.9) | copy-start | bytes 1540
  68.5 12.5 %collective-permute-start.7 = (bf16[8,128,1024]{2,1,0:T(8,128)(2,1)S(1)}, bf16[8,128,1024]{2,1,0:T(8,128)(2,1)}, u32[]{:S(2)}, u32[]{:S(2)}) collective-permute-start(bf16[8,128,1024]{2,1,0:T(8,128)(2,1)S(1)} %bitcast.238), channel_id=1, source_target_pairs={{0,1},{1,0},{2,3},{3,2},{4,5},{5,4},{6,7},{7,6},{8,9},{9,8},{10,11... | collective-permute-start | bytes 6291464 | tf_op jit(solution)/shard_map/ppermute | solution.py:49
  71.0 2.1 %copy-start.6 = (bf16[4,1,32,2048]{3,2,1,0:T(8,128)(2,1)S(1)}, bf16[4,1,32,2048]{3,2,1,0:T(8,128)(2,1)}, u32[]{:S(2)}) copy-start(bf16[4,1,32,2048]{3,2,1,0:T(8,128)(2,1)} %param.15) | copy-start | bytes 1572868
  73.2 10.1 %copy-start.23 = (bf16[4,4,8,8,128]{4,3,2,1,0:T(8,128)(2,1)}, bf16[4,4,8,8,128]{4,3,2,1,0:T(8,128)(2,1)S(1)}, u32[]{:S(2)}) copy-start(bf16[4,4,8,8,128]{4,3,2,1,0:T(8,128)(2,1)S(1)} %get-tuple-element.34) | copy-start | bytes 786436
  73.2 10.4 %copy-start.13 = (bf16[4,4,8,8,128]{4,3,2,1,0:T(8,128)(2,1)}, bf16[4,4,8,8,128]{4,3,2,1,0:T(8,128)(2,1)S(1)}, u32[]{:S(2)}) copy-start(bf16[4,4,8,8,128]{4,3,2,1,0:T(8,128)(2,1)S(1)} %get-tuple-element.35) | copy-start | bytes 786436
  83.2 0.7 copy-start.20
  83.5 0.8 copy-start.15
  86.7 4.4 %copy-start.12 = (bf16[128,8,1,64]{3,2,1,0:T(2,128)(2,1)S(1)}, bf16[128,8,1,64]{3,2,1,0:T(2,128)(2,1)}, u32[]{:S(2)}) copy-start(bf16[128,8,1,64]{3,2,1,0:T(2,128)(2,1)} %get-tuple-element.28) | copy-start | bytes 393220
  93.9 2.4 %copy-start.18 = (bf16[512,128]{1,0:T(8,128)(2,1)S(1)}, bf16[512,128]{1,0:T(8,128)(2,1)}, u32[]{:S(2)}) copy-start(bf16[512,128]{1,0:T(8,128)(2,1)} %convolution_convert_fusion.17) | copy-start | bytes 393220
  93.9 2.5 %copy-start.17 = (bf16[512,128]{1,0:T(8,128)(2,1)S(1)}, bf16[512,128]{1,0:T(8,128)(2,1)}, u32[]{:S(2)}) copy-start(bf16[512,128]{1,0:T(8,128)(2,1)} %convolution_convert_fusion.16) | copy-start | bytes 393220
  94.8 16.2 %collective-permute-start.8 = (bf16[4,32,2048]{2,1,0:T(8,128)(2,1)}, bf16[4,32,2048]{2,1,0:T(8,128)(2,1)S(1)}, u32[]{:S(2)}, u32[]{:S(2)}) collective-permute-start(bf16[4,32,2048]{2,1,0:T(8,128)(2,1)} %fusion.29), channel_id=1, source_target_pairs={{0,16},{1,17},{2,18},{3,19},{4,20},{5,21},{6,22},{7,23},{8,24},{9,... | collective-permute-start | bytes 1572872 | tf_op jit(solution)/shard_map/ppermute | solution.py:15
  114.7 36.6 %collective-permute-start.9 = (bf16[4,32,2048]{2,1,0:T(8,128)(2,1)}, bf16[4,32,2048]{2,1,0:T(8,128)(2,1)}, u32[]{:S(2)}, u32[]{:S(2)}) collective-permute-start(bf16[4,32,2048]{2,1,0:T(8,128)(2,1)} %fusion.16), channel_id=1, source_target_pairs={{16,0},{17,1},{18,2},{19,3},{20,4},{21,5},{22,6},{23,7},{24,8},{25... | collective-permute-start | bytes 1572872 | tf_op jit(solution)/shard_map/ppermute | solution.py:15
  157.7 1.4 copy-start.14
  157.7 1.4 copy-start.16
  157.7 1.7 copy-start.21
  159.1 1.0 copy-start.24
  177.7 16.6 %copy-start.3 = (f32[4,32,2048]{2,1,0:T(8,128)S(1)}, f32[4,32,2048]{2,1,0:T(8,128)}, u32[]{:S(2)}) copy-start(f32[4,32,2048]{2,1,0:T(8,128)} %copy-done.2) | copy-start | bytes 3145732
  177.7 16.6 %copy-start.4 = (f32[4,32,2048]{2,1,0:T(8,128)S(1)}, f32[4,32,2048]{2,1,0:T(8,128)}, u32[]{:S(2)}) copy-start(f32[4,32,2048]{2,1,0:T(8,128)} %reshape.296) | copy-start | bytes 3145732
  194.3 14.5 %copy-start.5 = (f32[4,32,2048]{2,1,0:T(8,128)S(1)}, f32[4,32,2048]{2,1,0:T(8,128)}, u32[]{:S(2)}) copy-start(f32[4,32,2048]{2,1,0:T(8,128)} %reshape.294) | copy-start | bytes 3145732
  194.3 14.5 %copy-start.7 = (bf16[4,1,32,2048]{3,2,1,0:T(8,128)(2,1)S(1)}, bf16[4,1,32,2048]{3,2,1,0:T(8,128)(2,1)}, u32[]{:S(2)}) copy-start(bf16[4,1,32,2048]{3,2,1,0:T(8,128)(2,1)} %param.15) | copy-start | bytes 1572868
  194.3 14.5 %copy-start.11 = (bf16[4,8,4,8,128]{4,3,1,2,0:T(8,128)(2,1)S(1)}, bf16[4,8,4,8,128]{4,3,1,2,0:T(8,128)(2,1)}, u32[]{:S(2)}) copy-start(bf16[4,8,4,8,128]{4,3,1,2,0:T(8,128)(2,1)} %copy.183) | copy-start | bytes 786436
  196.8 1.2 collective-permute-start.10
  198.1 3.7 %collective-permute-start.11 = (f32[2048]{0:T(1024)S(1)}, f32[2048]{0:T(1024)S(1)}, u32[]{:S(2)}, u32[]{:S(2)}) collective-permute-start(f32[2048]{0:T(1024)S(1)} %add.133), channel_id=1, source_target_pairs={{0,2},{1,3},{2,0},{3,1},{4,6},{5,7},{6,4},{7,5},{8,10},{9,11},{10,... | collective-permute-start | bytes 24584 | tf_op jit(solution)/shard_map/ppermute | solution.py:70
  201.7 3.7 %collective-permute-start.12 = (f32[2048]{0:T(1024)S(1)}, f32[2048]{0:T(1024)S(1)}, u32[]{:S(2)}, u32[]{:S(2)}) collective-permute-start(f32[2048]{0:T(1024)S(1)} %add.134), channel_id=1, source_target_pairs={{0,4},{1,5},{2,6},{3,7},{4,0},{5,1},{6,2},{7,3},{8,12},{9,13},{10,... | collective-permute-start | bytes 24584 | tf_op jit(solution)/shard_map/ppermute | solution.py:70
  205.4 6.2 %collective-permute-start.13 = (f32[2048]{0:T(1024)S(1)}, f32[2048]{0:T(1024)S(1)}, u32[]{:S(2)}, u32[]{:S(2)}) collective-permute-start(f32[2048]{0:T(1024)S(1)} %add.135), channel_id=1, source_target_pairs={{0,8},{1,9},{2,10},{3,11},{4,12},{5,13},{6,14},{7,15},{8,0},{9,1},... | collective-permute-start | bytes 24584 | tf_op jit(solution)/shard_map/ppermute | solution.py:70

commit v8 on v7

--- a/solution.py
+++ b/solution.py
@@ -55,8 +55,10 @@
 def split_product(rows, pair, own_bit):
     mine, theirs, block_rows = pair
     grid = rows.reshape(rows.shape[0], -1, 2, block_rows)
-    own_part = lax.dynamic_index_in_dim(grid, own_bit, 2, False).reshape(rows.shape[0], -1)
-    other_part = lax.dynamic_index_in_dim(grid, 1 - own_bit, 2, False).reshape(rows.shape[0], -1)
+    even = grid[:, :, 0].reshape(rows.shape[0], -1)
+    odd = grid[:, :, 1].reshape(rows.shape[0], -1)
+    own_part = jnp.where(own_bit == 0, even, odd)
+    other_part = jnp.where(own_bit == 0, odd, even)
     return jnp.dot(own_part, mine, preferred_element_type=jnp.float32) + jnp.dot(
         other_part, theirs, preferred_element_type=jnp.float32
     )

time: 216 us -> 183 us (0.85)
  the two profiles are of different devices: /device:TPU:14 before, /device:TPU:0 now
where the time goes in v8:
time: 183 us; the launch traced here: 182 us
  waiting for transfers between devices  57.9 us (32%)
  local copies, waits for them, and re-layouts  36.5 us (20%)
  matrix products  35 us (19%)
  other arithmetic  27.5 us (15%)
  starting transfers between devices  23.6 us (13%)
    ppermute x6, waiting for transfers between devices, butterfly_gathers(): lax.ppermute(held[which], axis, [(j, j ^ step) for j in range(size)])  47.6 us
    dot_general x7, matrix products, split_product(): jnp.dot(other_part, theirs, preferred_element_type=jnp.float32)  17.9 us
    dot_general x7, matrix products, split_product(): jnp.dot(own_part, mine, preferred_element_type=jnp.float32)  11.4 us
    convert_element_type x4, local copies, waits for them, and re-layouts, attend_layer(): input_wide = section_input.astype(jnp.float32)  10.8 us
    ppermute x6, starting transfers between devices, butterfly_gathers(): lax.ppermute(held[which], axis, [(j, j ^ step) for j in range(size)])  10.3 us
    convert_element_type x3, other arithmetic, attend_layer(): normed.astype(jnp.bfloat16).reshape(series_count * seq_length, model_width)  9.29 us
    ppermute x4, starting transfers between devices, butterfly_sum(): lax.ppermute(value, axis, [(j, j ^ step) for j in range(size)])  8.05 us
    convert_element_type x2, local copies, waits for them, and re-layouts, attend_layer(): normed.astype(jnp.bfloat16).reshape(series_count * seq_length, model_width)  6.15 us
  transfers between devices with their start and end apart: 14, of which 10 were waited for; matrix products, arithmetic and copies ran while one was open for 30% of the time, Pallas kernels for 0%

profile of v8, /device:TPU:0, one launch (start us, length us, event | category | flops | bytes accessed | tf_op | source)
XLA Modules:
  0.0 181.9 jit_solution(3366813669193602714)
XLA Ops:
  0.7 4.1 %collective-permute-start = (bf16[1,64,2048]{2,1,0:T(8,128)(2,1)}, bf16[1,64,2048]{2,1,0:T(8,128)(2,1)S(1)}, u32[]{:S(2)}, u32[]{:S(2)}) collective-permute-start(bf16[1,64,2048]{2,1,0:T(8,128)(2,1)} %param.13), channel_id=1, source_target_pairs={{0,8},{1,9},{2,10},{3,11},{4,12},{5,13},{6,14},{7,15},{8,0},{9,1},... | collective-permute-start | bytes 786440 | tf_op jit(solution)/shard_map/ppermute | solution.py:37
  4.9 2.2 %bitcast_convert_fusion = f32[4,1,32,2048]{3,2,0,1:T(8,128)} fusion(bf16[4,1,32,2048]{3,2,1,0:T(8,128)(2,1)} %param.8), kind=kLoop, calls=%fused_computation.94 | loop fusion | flops 262144 | bytes 1572864 | tf_op jit(solution)/shard_map/convert_element_type | solution.py:90
  8.1 15.3 %collective-permute-done = bf16[1,64,2048]{2,1,0:T(8,128)(2,1)S(1)} collective-permute-done((bf16[1,64,2048]{2,1,0:T(8,128)(2,1)}, bf16[1,64,2048]{2,1,0:T(8,128)(2,1)S(1)}, u32[]{:S(2)}, u32[]{:S(2)}) %collective-permute-start) | collective-permute-done | bytes 262176 | tf_op jit(solution)/shard_map/ppermute | solution.py:37
  23.5 1.9 %collective-permute-start.1 = (bf16[2,64,2048]{2,1,0:T(8,128)(2,1)S(1)}, bf16[2,64,2048]{2,1,0:T(8,128)(2,1)S(1)}, u32[]{:S(2)}, u32[]{:S(2)}) collective-permute-start(bf16[2,64,2048]{2,1,0:T(8,128)(2,1)S(1)} %pad_maximum_fusion.5), channel_id=1, source_target_pairs={{0,2},{1,3},{2,0},{3,1},{4,6},{5,7},{6,4},{7,5},{8,10},{9,11},{10,... | collective-permute-start | bytes 1572872 | tf_op jit(solution)/shard_map/ppermute | solution.py:37
  25.4 2.7 %collective-permute-done.4 = bf16[1,128,1024]{2,1,0:T(8,128)(2,1)S(1)} collective-permute-done((bf16[1,128,1024]{2,1,0:T(8,128)(2,1)}, bf16[1,128,1024]{2,1,0:T(8,128)(2,1)S(1)}, u32[]{:S(2)}, u32[]{:S(2)}) %collective-permute-start.4) | collective-permute-done | bytes 262176 | tf_op jit(solution)/shard_map/ppermute | solution.py:37
  29.2 6.7 %collective-permute-done.1 = bf16[2,64,2048]{2,1,0:T(8,128)(2,1)S(1)} collective-permute-done((bf16[2,64,2048]{2,1,0:T(8,128)(2,1)S(1)}, bf16[2,64,2048]{2,1,0:T(8,128)(2,1)S(1)}, u32[]{:S(2)}, u32[]{:S(2)}) %collective-permute-start.1) | collective-permute-done | bytes 524320 | tf_op jit(solution)/shard_map/ppermute | solution.py:37
  36.0 1.6 collective-permute-start.2
  37.8 5.4 %collective-permute-done.5 = bf16[2,128,1024]{2,1,0:T(8,128)(2,1)S(1)} collective-permute-done((bf16[2,128,1024]{2,1,0:T(8,128)(2,1)S(1)}, bf16[2,128,1024]{2,1,0:T(8,128)(2,1)S(1)}, u32[]{:S(2)}, u32[]{:S(2)}) %collective-permute-start.5) | collective-permute-done | bytes 524320 | tf_op jit(solution)/shard_map/ppermute | solution.py:37
  43.4 1.6 collective-permute-start.6
  45.0 1.3 multiply_reduce_fusion.2
  46.3 17.6 %collective-permute-done.2 = bf16[4,64,2048]{2,1,0:T(8,128)(2,1)S(1)} collective-permute-done((bf16[4,64,2048]{2,1,0:T(8,128)(2,1)S(1)}, bf16[4,64,2048]{2,1,0:T(8,128)(2,1)S(1)}, u32[]{:S(2)}, u32[]{:S(2)}) %collective-permute-start.2) | collective-permute-done | bytes 1048608 | tf_op jit(solution)/shard_map/ppermute | solution.py:37
  64.1 1.5 pad_maximum_fusion.1
  66.8 3.1 %reshape.281 = f32[128,8,2,128]{3,2,1,0:T(2,128)} reshape(f32[4,32,2048]{2,1,0:T(8,128)} %get-tuple-element.53) | data formatting | bytes 2097152 | tf_op jit(solution)/shard_map/jvp()/convert_element_type | solution.py:90
  69.9 2.3 %copy.44 = f32[128,8,2,128]{0,3,1,2:T(8,128)} copy(f32[128,8,2,128]{3,2,1,0:T(2,128)} %reshape.281) | data formatting | bytes 2097152 | tf_op jit(solution)/shard_map/jvp()/convert_element_type | solution.py:90
  72.2 3.1 %reshape.283 = f32[128,8,2,128]{3,2,1,0:T(2,128)} reshape(f32[4,1,32,2048]{3,2,0,1:T(8,128)} %bitcast_convert_fusion) | data formatting | bytes 2097152 | tf_op jit(solution)/shard_map/convert_element_type | solution.py:90
  75.3 2.3 %copy.50 = f32[128,8,2,128]{0,3,1,2:T(8,128)} copy(f32[128,8,2,128]{3,2,1,0:T(2,128)} %reshape.283) | data formatting | bytes 2097152 | tf_op jit(solution)/shard_map/convert_element_type | solution.py:90
  78.5 2.0 %multiply_convert_fusion.1 = (bf16[128,8,2,128]{0,3,1,2:T(8,128)(2,1)S(1)}, bf16[128,8,2,128]{0,3,1,2:T(8,128)(2,1)S(1)}) fusion(f32[128,8,2,128]{0,3,1,2:T(8,128)} %copy.44, f32[8,2,128]{2,0,1:T(8,128)S(1)} %copy.45, f32[128]{0:T(128)S(1)} %rsqrt.44, f32[128,8,2,128]{0,3,1,2:T(8,128)} %copy.50, f32[128]{0:T(128)S(1)} %rsqrt.46), kind=kLoop, calls=%fused_computation.78 | loop fusion | flops 1572864 | bytes 3154944 | tf_op jit(solution)/shard_map/jvp()/convert_element_type | solution.py:93
  81.2 2.3 %convolution_convert_fusion.16 = bf16[512,128]{1,0:T(8,128)(2,1)S(1)} fusion(bf16[512,2048]{1,0:T(8,128)(2,1)} %bitcast.11, bf16[128,2048]{1,0:T(8,128)(2,1)S(1)} %bitcast.262), kind=kOutput, calls=%fused_computation.43 | convolution fusion | flops 268500992 | bytes 2752512 | tf_op jit(solution)/shard_map/transpose(jvp())/dot_general | solution.py:62
  85.4 3.0 %select_add_fusion.7 = (bf16[512,128]{1,0:T(8,128)(2,1)}, bf16[512,128]{1,0:T(8,128)(2,1)}) fusion(bf16[512,128]{1,0:T(8,128)(2,1)S(1)} %convolution_convert_fusion.16, pred[]{:T(512)S(6)} %eq.59, bf16[512,2048]{1,0:T(8,128)(2,1)} %bitcast.9, bf16[128,2048]{1,0:T(8,128)(2,1)S(1)} %bitcast.263), kind=kOutput, calls=%fused_computation.170 | convolution fusion | flops 268894208 | bytes 3014657 | tf_op jit(solution)/shard_map/transpose(jvp())/dot_general | solution.py:62
  88.4 1.9 %copy.40 = bf16[128,8,1,64]{3,2,1,0:T(2,128)(2,1)} copy(bf16[128,8,1,64]{0,3,1,2:T(8,128)(2,1)} %bitcast.294) | data formatting | bytes 262144 | tf_op jit(solution)/shard_map/transpose(jvp())/broadcast_in_dim;transpose(jvp())/reshape | solution.py:59
  90.4 1.9 %copy.41 = bf16[128,8,1,64]{3,2,1,0:T(2,128)(2,1)} copy(bf16[128,8,1,64]{0,3,1,2:T(8,128)(2,1)} %bitcast.293) | data formatting | bytes 262144 | tf_op jit(solution)/shard_map/transpose(jvp())/broadcast_in_dim;transpose(jvp())/reshape | solution.py:58
  92.3 2.2 %fusion.39 = bf16[16,8,8,128]{3,1,2,0:T(8,128)(2,1)S(1)} fusion(f32[128,1024]{1,0:T(8,128)S(1)} %fusion.78, bf16[128,1024]{0,1:T(8,128)(2,1)} %bitcast.269, bf16[1024,1024]{1,0:T(8,128)(2,1)} %bitcast.32), kind=kOutput, calls=%fused_computation.113 | convolution fusion | flops 268697600 | bytes 3145728 | tf_op jit(solution)/shard_map/dot_general | solution.py:62
  97.7 2.2 %broadcast_select_fusion = (bf16[128,8,1,64]{3,2,1,0:T(2,128)(2,1)}, bf16[128,8,1,64]{3,2,1,0:T(2,128)(2,1)}) fusion(pred[]{:T(512)S(6)} %eq.59, bf16[128,8,2,64]{3,2,1,0:T(2,128)(2,1)S(1)} %reshape_reshape.12), kind=kLoop, calls=%fused_computation.80 | loop fusion | flops 131072 | bytes 524289 | tf_op jit(solution)/shard_map/jit(_where)/select_n | solution.py:61
  99.9 1.9 %copy.56 = bf16[128,8,1,64]{0,3,1,2:T(8,128)(2,1)} copy(bf16[128,8,1,64]{3,2,1,0:T(2,128)(2,1)} %get-tuple-element.33) | data formatting | bytes 262144 | tf_op jit(solution)/shard_map/jit(_where)/select_n | solution.py:60
  101.8 3.2 %fusion.79 = f32[128,2048]{1,0:T(8,128)} fusion(bf16[128,512]{0,1:T(8,128)(2,1)} %bitcast.279, bf16[512,2048]{1,0:T(8,128)(2,1)} %bitcast.11), kind=kOutput, calls=%fused_computation.190 | convolution fusion | flops 268435456 | bytes 3276800 | tf_op jit(solution)/shard_map/dot_general | solution.py:62
  105.9 2.4 %convolution_add_fusion = f32[128,2048]{1,0:T(8,128)S(1)} fusion(f32[128,2048]{1,0:T(8,128)} %fusion.79, bf16[128,512]{0,1:T(8,128)(2,1)} %bitcast.278, bf16[512,2048]{1,0:T(8,128)(2,1)} %bitcast.9), kind=kOutput, calls=%fused_computation | convolution fusion | flops 268697600 | bytes 4325376 | tf_op jit(solution)/shard_map/dot_general | solution.py:62
  109.2 3.4 %collective-permute-start.8 = (bf16[4,32,2048]{2,1,0:T(8,128)(2,1)}, bf16[4,32,2048]{2,1,0:T(8,128)(2,1)S(1)}, u32[]{:S(2)}, u32[]{:S(2)}) collective-permute-start(bf16[4,32,2048]{2,1,0:T(8,128)(2,1)} %fusion.29), channel_id=1, source_target_pairs={{0,16},{1,17},{2,18},{3,19},{4,20},{5,21},{6,22},{7,23},{8,24},{9,... | collective-permute-start | bytes 1572872 | tf_op jit(solution)/shard_map/ppermute | solution.py:15
  112.7 2.2 %pad_add_fusion = bf16[128,8,2,64]{3,2,1,0:T(2,128)(2,1)} fusion(bf16[128,8,1,64]{3,2,1,0:T(2,128)(2,1)S(1)} %copy-done.6, bf16[128,8,1,64]{3,2,1,0:T(2,128)(2,1)S(1)} %copy-done.5), kind=kLoop, calls=%fused_computation.107 | loop fusion | flops 524288 | bytes 524288 | tf_op jit(solution)/shard_map/transpose(jvp())/add_any | solution.py:58
  114.8 2.0 %reshape.260 = bf16[4,32,8,128]{3,2,1,0:T(8,128)(2,1)} reshape(bf16[128,8,2,64]{3,2,1,0:T(2,128)(2,1)} %pad_add_fusion) | data formatting | bytes 524288 | tf_op jit(solution)/shard_map/transpose(jvp())/reshape;transpose(jvp())/reshape | solution.py:104
  116.9 2.1 %fusion.38 = bf16[16,8,8,128]{3,1,2,0:T(8,128)(2,1)S(1)} fusion(f32[128,1024]{1,0:T(8,128)} %fusion.77, bf16[128,1024]{0,1:T(8,128)(2,1)S(1)} %bitcast.266, bf16[1024,1024]{1,0:T(8,128)(2,1)} %bitcast.32), kind=kOutput, calls=%fused_computation.112 | convolution fusion | flops 268697600 | bytes 3145728 | tf_op jit(solution)/shard_map/jvp()/dot_general | solution.py:62
  119.1 5.0 %collective-permute-done.8 = bf16[4,32,2048]{2,1,0:T(8,128)(2,1)S(1)} collective-permute-done((bf16[4,32,2048]{2,1,0:T(8,128)(2,1)}, bf16[4,32,2048]{2,1,0:T(8,128)(2,1)S(1)}, u32[]{:S(2)}, u32[]{:S(2)}) %collective-permute-start.8) | collective-permute-done | bytes 524320 | tf_op jit(solution)/shard_map/ppermute | solution.py:15
  130.1 3.1 %select_add_fusion.1 = (bf16[128,1024]{1,0:T(8,128)(2,1)}, bf16[128,1024]{1,0:T(8,128)(2,1)S(1)}) fusion(bf16[128,1024]{1,0:T(8,128)(2,1)S(1)} %convolution_convert_fusion.3, pred[]{:T(512)S(6)} %eq.59, bf16[1024,1024]{1,0:T(8,128)(2,1)} %bitcast.32, bf16[16,8,8,128]{3,2,1,0:T(8,128)(2,1)S(1)} %bitcast.275), kind=kOutput, calls=%fused_computation.135 | convolution fusion | flops 269352960 | bytes 3145729 | tf_op jit(solution)/shard_map/transpose(jvp())/dot_general | solution.py:62
  133.3 1.8 reshape.290
  136.0 3.6 %add_convert_fusion = f32[128,8,2,128]{3,2,1,0:T(2,128)} fusion(bf16[128,8,1,128]{3,2,1,0:T(2,128)(2,1)} %reshape.291, bf16[128,8,1,128]{3,2,1,0:T(2,128)(2,1)} %reshape.290), kind=kLoop, calls=%fused_computation.95 | loop fusion | flops 1048576 | bytes 1572864 | tf_op jit(solution)/shard_map/transpose(jvp())/convert_element_type | solution.py:93
  139.6 3.1 %reshape.286 = f32[4,32,2048]{2,1,0:T(8,128)} reshape(f32[128,8,2,128]{3,2,1,0:T(2,128)} %add_convert_fusion) | data formatting | bytes 2097152 | tf_op jit(solution)/shard_map/transpose(jvp())/convert_element_type | solution.py:93
  143.0 2.6 %convolution_convert_fusion.15 = bf16[128,512]{1,0:T(8,128)(2,1)S(1)} fusion(bf16[128,2048]{1,0:T(8,128)(2,1)S(1)} %bitcast.264, bf16[512,2048]{1,0:T(8,128)(2,1)} %bitcast.9), kind=kOutput, calls=%fused_computation.42 | convolution fusion | flops 268500992 | bytes 2752512 | tf_op jit(solution)/shard_map/transpose(jvp())/dot_general | solution.py:62
  145.6 2.4 %select_add_fusion.5 = (bf16[128,512]{1,0:T(8,128)(2,1)S(1)}, bf16[128,512]{1,0:T(8,128)(2,1)S(1)}) fusion(bf16[128,512]{1,0:T(8,128)(2,1)S(1)} %convolution_convert_fusion.15, pred[]{:T(512)S(6)} %eq.59, bf16[128,2048]{1,0:T(8,128)(2,1)S(1)} %bitcast.265, bf16[512,2048]{1,0:T(8,128)(2,1)} %bitcast.11), kind=kOutput, calls=%fused_computation.168 | convolution fusion | flops 268894208 | bytes 3014657 | tf_op jit(solution)/shard_map/transpose(jvp())/dot_general | solution.py:62
  149.1 1.4 fusion.13
  152.9 2.4 %select_add_fusion.3 = (bf16[128,1024]{1,0:T(8,128)(2,1)S(1)}, bf16[128,1024]{1,0:T(8,128)(2,1)S(1)}) fusion(bf16[128,1024]{1,0:T(8,128)(2,1)S(1)} %convolution_convert_fusion.6, pred[]{:T(512)S(6)} %eq.59, bf16[1024,1024]{1,0:T(8,128)(2,1)} %bitcast.32, bf16[16,8,8,128]{3,2,1,0:T(8,128)(2,1)S(1)} %bitcast.273), kind=kOutput, calls=%fused_computation.137 | convolution fusion | flops 269352960 | bytes 3145729 | tf_op jit(solution)/shard_map/transpose(jvp())/dot_general | solution.py:62
  157.2 3.7 %add_convert_fusion.1 = f32[128,8,2,128]{3,2,1,0:T(2,128)} fusion(bf16[128,8,1,128]{3,2,1,0:T(2,128)(2,1)} %reshape.289, bf16[128,8,1,128]{3,2,1,0:T(2,128)(2,1)} %reshape.288), kind=kLoop, calls=%fused_computation.96 | loop fusion | flops 1048576 | bytes 1572864 | tf_op jit(solution)/shard_map/transpose(jvp())/convert_element_type | solution.py:93
  160.9 3.0 %reshape.284 = f32[4,32,2048]{2,1,0:T(8,128)} reshape(f32[128,8,2,128]{3,2,1,0:T(2,128)} %add_convert_fusion.1) | data formatting | bytes 2097152 | tf_op jit(solution)/shard_map/transpose(jvp())/convert_element_type | solution.py:93
  164.0 2.4 %fusion.26 = (f32[2048]{0:T(1024)S(1)}, f32[4,32]{1,0:T(4,128)S(1)}, f32[4,32]{1,0:T(4,128)S(1)}, f32[2048]{0:T(1024)S(1)}, f32[4,32]{1,0:T(4,128)S(1)}, /*index=5*/f32[2048]{0:T(1024)S(1)}) fusion(bf16[4,32,1024]{2,1,0:T(8,128)(2,1)S(1)} %bitcast.260, bf16[4,32,1024]{2,1,0:T(8,128)(2,1)S(1)} %bitcast.258, bf16[4,1,32,2048]{3,2,1,0:T(8,128)(2,1)S(1)} %copy-done.1, ...), kind=kLoop, calls=%fused_computation.67 | loop fusion | flops 5498496 | bytes 4229632 | tf_op jit(solution)/shard_map/transpose(jvp())/reduce_sum | solution.py:79
  167.7 1.5 collective-permute-start.11
  169.2 2.1 %collective-permute-done.11 = f32[2048]{0:T(1024)S(1)} collective-permute-done((f32[2048]{0:T(1024)S(1)}, f32[2048]{0:T(1024)S(1)}, u32[]{:S(2)}, u32[]{:S(2)}) %collective-permute-start.11) | collective-permute-done | bytes 8224 | tf_op jit(solution)/shard_map/ppermute | solution.py:72
  171.3 2.3 %collective-permute-start.12 = (f32[2048]{0:T(1024)S(1)}, f32[2048]{0:T(1024)S(1)}, u32[]{:S(2)}, u32[]{:S(2)}) collective-permute-start(f32[2048]{0:T(1024)S(1)} %add.123), channel_id=1, source_target_pairs={{0,4},{1,5},{2,6},{3,7},{4,0},{5,1},{6,2},{7,3},{8,12},{9,13},{10,... | collective-permute-start | bytes 24584 | tf_op jit(solution)/shard_map/ppermute | solution.py:72
  173.7 1.6 collective-permute-done.12
  175.3 4.1 %collective-permute-start.13 = (f32[2048]{0:T(1024)S(1)}, f32[2048]{0:T(1024)S(1)}, u32[]{:S(2)}, u32[]{:S(2)}) collective-permute-start(f32[2048]{0:T(1024)S(1)} %add.124), channel_id=1, source_target_pairs={{0,8},{1,9},{2,10},{3,11},{4,12},{5,13},{6,14},{7,15},{8,0},{9,1},... | collective-permute-start | bytes 24584 | tf_op jit(solution)/shard_map/ppermute | solution.py:72
  179.4 1.8 fusion.36
  (137 shorter events, 26.8 us)
Async XLA Ops:
  0.6 44.4 %copy-start = (bf16[16,2048]{1,0:T(8,128)(2,1)S(1)}, bf16[16,2048]{1,0:T(8,128)(2,1)}, u32[]{:S(2)}) copy-start(bf16[16,2048]{1,0:T(8,128)(2,1)} %param.11) | copy-start | bytes 196612
  0.6 22.7 %copy-start.20 = (bf16[1,64,2048]{2,1,0:T(8,128)(2,1)S(1)}, bf16[1,64,2048]{2,1,0:T(8,128)(2,1)}, u32[]{:S(2)}) copy-start(bf16[1,64,2048]{2,1,0:T(8,128)(2,1)} %param.13) | copy-start | bytes 786436
  0.7 27.5 %copy-start.21 = (bf16[1,128,1024]{2,1,0:T(8,128)(2,1)S(1)}, bf16[1,128,1024]{2,1,0:T(8,128)(2,1)}, u32[]{:S(2)}) copy-start(bf16[1,128,1024]{2,1,0:T(8,128)(2,1)} %param.12) | copy-start | bytes 786436
  0.7 7.2 %copy-start.1 = (bf16[4,1,32,2048]{3,2,1,0:T(8,128)(2,1)S(1)}, bf16[4,1,32,2048]{3,2,1,0:T(8,128)(2,1)}, u32[]{:S(2)}) copy-start(bf16[4,1,32,2048]{3,2,1,0:T(8,128)(2,1)} %param.8) | copy-start | bytes 1572868
  0.7 22.7 %collective-permute-start = (bf16[1,64,2048]{2,1,0:T(8,128)(2,1)}, bf16[1,64,2048]{2,1,0:T(8,128)(2,1)S(1)}, u32[]{:S(2)}, u32[]{:S(2)}) collective-permute-start(bf16[1,64,2048]{2,1,0:T(8,128)(2,1)} %param.13), channel_id=1, source_target_pairs={{0,8},{1,9},{2,10},{3,11},{4,12},{5,13},{6,14},{7,15},{8,0},{9,1},... | collective-permute-start | bytes 786440 | tf_op jit(solution)/shard_map/ppermute | solution.py:37
  4.8 23.4 %collective-permute-start.4 = (bf16[1,128,1024]{2,1,0:T(8,128)(2,1)}, bf16[1,128,1024]{2,1,0:T(8,128)(2,1)S(1)}, u32[]{:S(2)}, u32[]{:S(2)}) collective-permute-start(bf16[1,128,1024]{2,1,0:T(8,128)(2,1)} %param.12), channel_id=1, source_target_pairs={{0,8},{1,9},{2,10},{3,11},{4,12},{5,13},{6,14},{7,15},{8,0},{9,1},... | collective-permute-start | bytes 786440 | tf_op jit(solution)/shard_map/ppermute | solution.py:37
  23.5 12.3 %collective-permute-start.1 = (bf16[2,64,2048]{2,1,0:T(8,128)(2,1)S(1)}, bf16[2,64,2048]{2,1,0:T(8,128)(2,1)S(1)}, u32[]{:S(2)}, u32[]{:S(2)}) collective-permute-start(bf16[2,64,2048]{2,1,0:T(8,128)(2,1)S(1)} %pad_maximum_fusion.5), channel_id=1, source_target_pairs={{0,2},{1,3},{2,0},{3,1},{4,6},{5,7},{6,4},{7,5},{8,10},{9,11},{10,... | collective-permute-start | bytes 1572872 | tf_op jit(solution)/shard_map/ppermute | solution.py:37
  28.3 9.4 %copy-start.17 = (f32[1,2048]{1,0:T(1,128)S(1)}, f32[1,2048]{1,0:T(1,128)}, u32[]{:S(2)}) copy-start(f32[1,2048]{1,0:T(1,128)} %param.14) | copy-start | bytes 24580
  28.3 14.9 %collective-permute-start.5 = (bf16[2,128,1024]{2,1,0:T(8,128)(2,1)S(1)}, bf16[2,128,1024]{2,1,0:T(8,128)(2,1)S(1)}, u32[]{:S(2)}, u32[]{:S(2)}) collective-permute-start(bf16[2,128,1024]{2,1,0:T(8,128)(2,1)S(1)} %pad_maximum_fusion.4), channel_id=1, source_target_pairs={{0,4},{1,5},{2,6},{3,7},{4,0},{5,1},{6,2},{7,3},{8,12},{9,13},{10,... | collective-permute-start | bytes 1572872 | tf_op jit(solution)/shard_map/ppermute | solution.py:37
  36.0 27.9 %collective-permute-start.2 = (bf16[4,64,2048]{2,1,0:T(8,128)(2,1)S(1)}, bf16[4,64,2048]{2,1,0:T(8,128)(2,1)S(1)}, u32[]{:S(2)}, u32[]{:S(2)}) collective-permute-start(bf16[4,64,2048]{2,1,0:T(8,128)(2,1)S(1)} %bitcast.247), channel_id=1, source_target_pairs={{0,4},{1,5},{2,6},{3,7},{4,0},{5,1},{6,2},{7,3},{8,12},{9,13},{10,... | collective-permute-start | bytes 3145736 | tf_op jit(solution)/shard_map/ppermute | solution.py:37
  43.4 22.3 %collective-permute-start.6 = (bf16[4,128,1024]{2,1,0:T(8,128)(2,1)S(1)}, bf16[4,128,1024]{2,1,0:T(8,128)(2,1)S(1)}, u32[]{:S(2)}, u32[]{:S(2)}) collective-permute-start(bf16[4,128,1024]{2,1,0:T(8,128)(2,1)S(1)} %bitcast.248), channel_id=1, source_target_pairs={{0,2},{1,3},{2,0},{3,1},{4,6},{5,7},{6,4},{7,5},{8,10},{9,11},{10,... | collective-permute-start | bytes 3145736 | tf_op jit(solution)/shard_map/ppermute | solution.py:37
  65.6 19.8 %collective-permute-start.3 = (bf16[8,64,2048]{2,1,0:T(8,128)(2,1)}, bf16[8,64,2048]{2,1,0:T(8,128)(2,1)}, u32[]{:S(2)}, u32[]{:S(2)}) collective-permute-start(bf16[8,64,2048]{2,1,0:T(8,128)(2,1)} %bitcast.8), channel_id=1, source_target_pairs={{0,1},{1,0},{2,3},{3,2},{4,5},{5,4},{6,7},{7,6},{8,9},{9,8},{10,11... | collective-permute-start | bytes 6291464 | tf_op jit(solution)/shard_map/ppermute | solution.py:49
  66.0 26.2 %collective-permute-start.7 = (bf16[8,128,1024]{2,1,0:T(8,128)(2,1)S(1)}, bf16[8,128,1024]{2,1,0:T(8,128)(2,1)}, u32[]{:S(2)}, u32[]{:S(2)}) collective-permute-start(bf16[8,128,1024]{2,1,0:T(8,128)(2,1)S(1)} %bitcast.242), channel_id=1, source_target_pairs={{0,1},{1,0},{2,3},{3,2},{4,5},{5,4},{6,7},{7,6},{8,9},{9,8},{10,11... | collective-permute-start | bytes 6291464 | tf_op jit(solution)/shard_map/ppermute | solution.py:49
  72.2 5.4 %copy-start.24 = (s32[4,1,32]{2,1,0:T(1,128)S(1)}, s32[4,1,32]{2,1,0:T(1,128)}, u32[]{:S(2)}) copy-start(s32[4,1,32]{2,1,0:T(1,128)} %param.9) | copy-start | bytes 1540
  78.5 2.8 %copy-start.8 = (bf16[4,1,32,2048]{3,2,1,0:T(8,128)(2,1)S(1)}, bf16[4,1,32,2048]{3,2,1,0:T(8,128)(2,1)}, u32[]{:S(2)}) copy-start(bf16[4,1,32,2048]{3,2,1,0:T(8,128)(2,1)} %param.15) | copy-start | bytes 1572868
  92.3 2.3 %copy-start.22 = (bf16[4,4,8,8,128]{4,3,2,1,0:T(8,128)(2,1)S(1)}, bf16[4,4,8,8,128]{4,3,2,1,0:T(8,128)(2,1)}, u32[]{:S(2)}) copy-start(bf16[4,4,8,8,128]{4,3,2,1,0:T(8,128)(2,1)} %get-tuple-element.38) | copy-start | bytes 786436
  92.3 2.6 %copy-start.13 = (bf16[4,4,8,8,128]{4,3,2,1,0:T(8,128)(2,1)S(1)}, bf16[4,4,8,8,128]{4,3,2,1,0:T(8,128)(2,1)}, u32[]{:S(2)}) copy-start(bf16[4,4,8,8,128]{4,3,2,1,0:T(8,128)(2,1)} %get-tuple-element.39) | copy-start | bytes 786436
  94.6 0.7 copy-start.18
  94.9 0.8 copy-start.15
  99.9 5.1 %copy-start.7 = (bf16[128,8,1,64]{3,2,1,0:T(2,128)(2,1)S(1)}, bf16[128,8,1,64]{3,2,1,0:T(2,128)(2,1)}, u32[]{:S(2)}) copy-start(bf16[128,8,1,64]{3,2,1,0:T(2,128)(2,1)} %get-tuple-element.32) | copy-start | bytes 393220
  108.3 4.3 %copy-start.5 = (bf16[128,8,1,64]{3,2,1,0:T(2,128)(2,1)S(1)}, bf16[128,8,1,64]{3,2,1,0:T(2,128)(2,1)}, u32[]{:S(2)}) copy-start(bf16[128,8,1,64]{3,2,1,0:T(2,128)(2,1)} %copy.40) | copy-start | bytes 393220
  108.3 4.3 %copy-start.6 = (bf16[128,8,1,64]{3,2,1,0:T(2,128)(2,1)S(1)}, bf16[128,8,1,64]{3,2,1,0:T(2,128)(2,1)}, u32[]{:S(2)}) copy-start(bf16[128,8,1,64]{3,2,1,0:T(2,128)(2,1)} %copy.41) | copy-start | bytes 393220
  109.2 14.9 %collective-permute-start.8 = (bf16[4,32,2048]{2,1,0:T(8,128)(2,1)}, bf16[4,32,2048]{2,1,0:T(8,128)(2,1)S(1)}, u32[]{:S(2)}, u32[]{:S(2)}) collective-permute-start(bf16[4,32,2048]{2,1,0:T(8,128)(2,1)} %fusion.29), channel_id=1, source_target_pairs={{0,16},{1,17},{2,18},{3,19},{4,20},{5,21},{6,22},{7,23},{8,24},{9,... | collective-permute-start | bytes 1572872 | tf_op jit(solution)/shard_map/ppermute | solution.py:15
  119.0 5.8 %copy-start.12 = (bf16[4,32,8,128]{3,2,1,0:T(8,128)(2,1)S(1)}, bf16[4,32,8,128]{3,2,1,0:T(8,128)(2,1)}, u32[]{:S(2)}) copy-start(bf16[4,32,8,128]{3,2,1,0:T(8,128)(2,1)} %reshape.260) | copy-start | bytes 786436
  127.9 15.1 %collective-permute-start.9 = (bf16[4,32,2048]{2,1,0:T(8,128)(2,1)}, bf16[4,32,2048]{2,1,0:T(8,128)(2,1)S(1)}, u32[]{:S(2)}, u32[]{:S(2)}) collective-permute-start(bf16[4,32,2048]{2,1,0:T(8,128)(2,1)} %fusion.16), channel_id=1, source_target_pairs={{16,0},{17,1},{18,2},{19,3},{20,4},{21,5},{22,6},{23,7},{24,8},{25... | collective-permute-start | bytes 1572872 | tf_op jit(solution)/shard_map/ppermute | solution.py:15
  143.0 5.1 %copy-start.10 = (bf16[4,32,2048]{2,1,0:T(8,128)(2,1)}, bf16[4,32,2048]{2,1,0:T(8,128)(2,1)S(1)}, u32[]{:S(2)}) copy-start(bf16[4,32,2048]{2,1,0:T(8,128)(2,1)S(1)} %collective-permute-done.9) | copy-start | bytes 1572868
  149.1 1.4 copy-start.14
  149.1 1.4 copy-start.16
  149.1 1.7 copy-start.19
  150.6 1.0 copy-start.23
  157.2 6.8 %copy-start.2 = (f32[4,32,2048]{2,1,0:T(8,128)S(1)}, f32[4,32,2048]{2,1,0:T(8,128)}, u32[]{:S(2)}) copy-start(f32[4,32,2048]{2,1,0:T(8,128)} %get-tuple-element.53) | copy-start | bytes 3145732
  157.2 6.8 %copy-start.3 = (f32[4,32,2048]{2,1,0:T(8,128)S(1)}, f32[4,32,2048]{2,1,0:T(8,128)}, u32[]{:S(2)}) copy-start(f32[4,32,2048]{2,1,0:T(8,128)} %reshape.286) | copy-start | bytes 3145732
  163.9 15.5 %copy-start.4 = (f32[4,32,2048]{2,1,0:T(8,128)S(1)}, f32[4,32,2048]{2,1,0:T(8,128)}, u32[]{:S(2)}) copy-start(f32[4,32,2048]{2,1,0:T(8,128)} %reshape.284) | copy-start | bytes 3145732
  164.0 15.5 %copy-start.9 = (bf16[4,1,32,2048]{3,2,1,0:T(8,128)(2,1)S(1)}, bf16[4,1,32,2048]{3,2,1,0:T(8,128)(2,1)}, u32[]{:S(2)}) copy-start(bf16[4,1,32,2048]{3,2,1,0:T(8,128)(2,1)} %param.15) | copy-start | bytes 1572868
  164.0 15.5 %copy-start.11 = (bf16[4,32,2048]{2,1,0:T(8,128)(2,1)S(1)}, bf16[4,32,2048]{2,1,0:T(8,128)(2,1)}, u32[]{:S(2)}) copy-start(bf16[4,32,2048]{2,1,0:T(8,128)(2,1)} %copy-done.10) | copy-start | bytes 1572868
  166.4 1.2 collective-permute-start.10
  167.7 3.7 %collective-permute-start.11 = (f32[2048]{0:T(1024)S(1)}, f32[2048]{0:T(1024)S(1)}, u32[]{:S(2)}, u32[]{:S(2)}) collective-permute-start(f32[2048]{0:T(1024)S(1)} %add.122), channel_id=1, source_target_pairs={{0,2},{1,3},{2,0},{3,1},{4,6},{5,7},{6,4},{7,5},{8,10},{9,11},{10,... | collective-permute-start | bytes 24584 | tf_op jit(solution)/shard_map/ppermute | solution.py:72
  171.3 4.0 %collective-permute-start.12 = (f32[2048]{0:T(1024)S(1)}, f32[2048]{0:T(1024)S(1)}, u32[]{:S(2)}, u32[]{:S(2)}) collective-permute-start(f32[2048]{0:T(1024)S(1)} %add.123), channel_id=1, source_target_pairs={{0,4},{1,5},{2,6},{3,7},{4,0},{5,1},{6,2},{7,3},{8,12},{9,13},{10,... | collective-permute-start | bytes 24584 | tf_op jit(solution)/shard_map/ppermute | solution.py:72
  175.3 6.0 %collective-permute-start.13 = (f32[2048]{0:T(1024)S(1)}, f32[2048]{0:T(1024)S(1)}, u32[]{:S(2)}, u32[]{:S(2)}) collective-permute-start(f32[2048]{0:T(1024)S(1)} %add.124), channel_id=1, source_target_pairs={{0,8},{1,9},{2,10},{3,11},{4,12},{5,13},{6,14},{7,15},{8,0},{9,1},... | collective-permute-start | bytes 24584 | tf_op jit(solution)/shard_map/ppermute | solution.py:72

commit v9 on v8

--- a/solution.py
+++ b/solution.py
@@ -54,9 +54,9 @@
 
 def split_product(rows, pair, own_bit):
     mine, theirs, block_rows = pair
-    grid = rows.reshape(rows.shape[0], -1, 2, block_rows)
-    even = grid[:, :, 0].reshape(rows.shape[0], -1)
-    odd = grid[:, :, 1].reshape(rows.shape[0], -1)
+    grid = rows.reshape(rows.shape[0], -1, 2 * block_rows)
+    even = grid[:, :, :block_rows].reshape(rows.shape[0], -1)
+    odd = grid[:, :, block_rows:].reshape(rows.shape[0], -1)
     own_part = jnp.where(own_bit == 0, even, odd)
     other_part = jnp.where(own_bit == 0, odd, even)
     return jnp.dot(own_part, mine, preferred_element_type=jnp.float32) + jnp.dot(

time: 183 us -> 164 us (0.90)
  local copies, waits for them, and re-layouts: 36.5 us -> 25.1 us
  starting transfers between devices: 23.6 us -> 18.9 us
  matrix products: 35 us -> 30.9 us
  waiting for transfers between devices: 57.9 us -> 61 us
    ppermute x2, waiting for transfers between devices: 5.34 us -> 15.7 us  [send_to(): return lax.ppermute(arrays, axis, [(source, target)])]
    ppermute x6, waiting for transfers between devices: 47.6 us -> 37.9 us  [butterfly_gathers(): lax.ppermute(held[which], axis, [(j, j ^ step) for j in range(size)])]
    reshape x8 -> x2, local copies, waits for them, and re-layouts: 10.6 us -> 2.89 us  [the longest x1 1.81 us: split_product(): odd = grid[:, :, block_rows:].reshape(rows.shape[0], -1)]
    convert_element_type x3, other arithmetic: 9.29 us -> 2.27 us  [attend_layer(): normed.astype(jnp.bfloat16).reshape(series_count * seq_length, model_width)]
    dot_general x7, matrix products: 17.9 us -> 11 us  [split_product(): jnp.dot(other_part, theirs, preferred_element_type=jnp.float32)]
    convert_element_type x4 -> x2, local copies, waits for them, and re-layouts: 10.8 us -> 4.26 us  [attend_layer(): input_wide = section_input.astype(jnp.float32)]
    unnamed x55 -> x86, local copies, waits for them, and re-layouts: 2.63 us -> 8.38 us
    ppermute x4, starting transfers between devices: 8.05 us -> 3.91 us  [butterfly_sum(): lax.ppermute(value, axis, [(j, j ^ step) for j in range(size)])]
  transfers between devices with their start and end apart: 14 -> 14, of which waited for: 10 -> 12; matrix products, arithmetic and copies ran while one was open for 30% -> 27% of each run, Pallas kernels for 0% -> 0%
where the time goes in v9:
time: 164 us; the launch traced here: 163 us
  waiting for transfers between devices  61 us (37%)
  matrix products  30.9 us (19%)
  other arithmetic  25.7 us (16%)
  local copies, waits for them, and re-layouts  25.1 us (15%)
  starting transfers between devices  18.9 us (12%)
    ppermute x6, waiting for transfers between devices, butterfly_gathers(): lax.ppermute(held[which], axis, [(j, j ^ step) for j in range(size)])  37.9 us
    ppermute x2, waiting for transfers between devices, send_to(): return lax.ppermute(arrays, axis, [(source, target)])  15.7 us
    dot_general x7, matrix products, split_product(): jnp.dot(own_part, mine, preferred_element_type=jnp.float32)  12.3 us
    dot_general x7, matrix products, split_product(): jnp.dot(other_part, theirs, preferred_element_type=jnp.float32)  11 us
    ppermute x6, starting transfers between devices, butterfly_gathers(): lax.ppermute(held[which], axis, [(j, j ^ step) for j in range(size)])  9.85 us
    unnamed x86, local copies, waits for them, and re-layouts  8.38 us
    ppermute x4, waiting for transfers between devices, butterfly_sum(): lax.ppermute(value, axis, [(j, j ^ step) for j in range(size)])  7.32 us
    another operation x8, other arithmetic, butterfly_gathers(): jnp.stack([low.reshape(grid), high.reshape(grid)], axis=place)  5.19 us
  transfers between devices with their start and end apart: 14, of which 12 were waited for; matrix products, arithmetic and copies ran while one was open for 27% of the time, Pallas kernels for 0%

profile of v9, /device:TPU:0, one launch (start us, length us, event | category | flops | bytes accessed | tf_op | source)
XLA Modules:
  0.0 163.0 jit_solution(11575959690180375910)
XLA Ops:
  0.7 4.1 %collective-permute-start.4 = (bf16[1,128,1024]{2,1,0:T(8,128)(2,1)}, bf16[1,128,1024]{2,1,0:T(8,128)(2,1)S(1)}, u32[]{:S(2)}, u32[]{:S(2)}) collective-permute-start(bf16[1,128,1024]{2,1,0:T(8,128)(2,1)} %param.12), channel_id=1, source_target_pairs={{0,8},{1,9},{2,10},{3,11},{4,12},{5,13},{6,14},{7,15},{8,0},{9,1},... | collective-permute-start | bytes 786440 | tf_op jit(solution)/shard_map/ppermute | solution.py:37
  4.8 1.2 fusion.29
  6.1 2.2 %bitcast_convert_fusion = f32[4,1,32,2048]{3,2,0,1:T(8,128)} fusion(bf16[4,1,32,2048]{3,2,1,0:T(8,128)(2,1)} %param.8), kind=kLoop, calls=%fused_computation.95 | loop fusion | flops 262144 | bytes 1572864 | tf_op jit(solution)/shard_map/convert_element_type | solution.py:90
  9.8 1.3 copy.143
  11.1 1.7 %copy.88 = f32[128,8,256]{0,2,1:T(8,128)S(1)} copy(f32[128,8,256]{2,1,0:T(8,128)} %bitcast.278) | data formatting | bytes 2097152 | tf_op jit(solution)/shard_map/jvp()/convert_element_type | solution.py:90
  14.1 1.3 copy.141
  15.4 2.6 %copy.94 = f32[128,8,256]{0,2,1:T(8,128)} copy(f32[128,8,256]{2,1,0:T(8,128)} %bitcast.277) | data formatting | bytes 2097152 | tf_op jit(solution)/shard_map/convert_element_type | solution.py:90
  19.1 4.2 %collective-permute-done.4 = bf16[1,128,1024]{2,1,0:T(8,128)(2,1)S(1)} collective-permute-done((bf16[1,128,1024]{2,1,0:T(8,128)(2,1)}, bf16[1,128,1024]{2,1,0:T(8,128)(2,1)S(1)}, u32[]{:S(2)}, u32[]{:S(2)}) %collective-permute-start.4) | collective-permute-done | bytes 262176 | tf_op jit(solution)/shard_map/ppermute | solution.py:37
  23.6 4.6 %collective-permute-done = bf16[1,64,2048]{2,1,0:T(8,128)(2,1)S(1)} collective-permute-done((bf16[1,64,2048]{2,1,0:T(8,128)(2,1)}, bf16[1,64,2048]{2,1,0:T(8,128)(2,1)S(1)}, u32[]{:S(2)}, u32[]{:S(2)}) %collective-permute-start) | collective-permute-done | bytes 262176 | tf_op jit(solution)/shard_map/ppermute | solution.py:37
  29.2 1.6 collective-permute-start.1
  30.7 8.6 %collective-permute-done.5 = bf16[2,128,1024]{2,1,0:T(8,128)(2,1)S(1)} collective-permute-done((bf16[2,128,1024]{2,1,0:T(8,128)(2,1)S(1)}, bf16[2,128,1024]{2,1,0:T(8,128)(2,1)S(1)}, u32[]{:S(2)}, u32[]{:S(2)}) %collective-permute-start.5) | collective-permute-done | bytes 524320 | tf_op jit(solution)/shard_map/ppermute | solution.py:37
  39.6 1.6 %collective-permute-start.6 = (bf16[4,128,1024]{2,1,0:T(8,128)(2,1)S(1)}, bf16[4,128,1024]{2,1,0:T(8,128)(2,1)}, u32[]{:S(2)}, u32[]{:S(2)}) collective-permute-start(bf16[4,128,1024]{2,1,0:T(8,128)(2,1)S(1)} %bitcast.270), channel_id=1, source_target_pairs={{0,2},{1,3},{2,0},{3,1},{4,6},{5,7},{6,4},{7,5},{8,10},{9,11},{10,... | collective-permute-start | bytes 3145736 | tf_op jit(solution)/shard_map/ppermute | solution.py:37
  41.2 1.2 multiply_convert_fusion.1
  42.6 1.3 select_bitcast_fusion.3
  45.0 2.3 %collective-permute-start.2 = (bf16[4,64,2048]{2,1,0:T(8,128)(2,1)}, bf16[4,64,2048]{2,1,0:T(8,128)(2,1)}, u32[]{:S(2)}, u32[]{:S(2)}) collective-permute-start(bf16[4,64,2048]{2,1,0:T(8,128)(2,1)} %bitcast.3), channel_id=1, source_target_pairs={{0,4},{1,5},{2,6},{3,7},{4,0},{5,1},{6,2},{7,3},{8,12},{9,13},{10,... | collective-permute-start | bytes 3145736 | tf_op jit(solution)/shard_map/ppermute | solution.py:37
  47.3 17.7 %collective-permute-done.6 = bf16[4,128,1024]{2,1,0:T(8,128)(2,1)} collective-permute-done((bf16[4,128,1024]{2,1,0:T(8,128)(2,1)S(1)}, bf16[4,128,1024]{2,1,0:T(8,128)(2,1)}, u32[]{:S(2)}, u32[]{:S(2)}) %collective-permute-start.6) | collective-permute-done | bytes 1048608 | tf_op jit(solution)/shard_map/ppermute | solution.py:37
  65.0 1.4 broadcast_select_fusion.1
  67.5 2.6 %collective-permute-done.2 = bf16[4,64,2048]{2,1,0:T(8,128)(2,1)} collective-permute-done((bf16[4,64,2048]{2,1,0:T(8,128)(2,1)}, bf16[4,64,2048]{2,1,0:T(8,128)(2,1)}, u32[]{:S(2)}, u32[]{:S(2)}) %collective-permute-start.2) | collective-permute-done | bytes 1048608 | tf_op jit(solution)/shard_map/ppermute | solution.py:37
  70.0 1.7 %broadcast_select_fusion.3 = (bf16[4,64,2048]{2,1,0:T(8,128)(2,1)S(1)}, bf16[4,64,2048]{2,1,0:T(8,128)(2,1)S(1)}) fusion(bf16[4,64,2048]{2,1,0:T(8,128)(2,1)} %collective-permute-done.2, pred[]{:T(512)S(6)} %eq.60, bf16[2,2,64,2048]{3,2,1,0:T(8,128)(2,1)} %pad_maximum_fusion.3), kind=kLoop, calls=%fused_computation.86 | loop fusion | flops 1048576 | bytes 4194305 | tf_op jit(solution)/shard_map/jit(_where)/select_n | solution.py:39
  71.7 1.5 pad_maximum_fusion.1
  73.2 3.0 %convolution_convert_fusion.16 = bf16[512,128]{1,0:T(8,128)(2,1)} fusion(bf16[512,2048]{1,0:T(8,128)(2,1)} %bitcast.11, bf16[128,2048]{1,0:T(8,128)(2,1)S(1)} %bitcast.286), kind=kOutput, calls=%fused_computation.46 | convolution fusion | flops 268500992 | bytes 2752512 | tf_op jit(solution)/shard_map/transpose(jvp())/dot_general | solution.py:62
  76.7 1.3 fusion.93
  80.3 2.1 %fusion.95 = f32[128,2048]{1,0:T(8,128)S(1)} fusion(bf16[128,512]{0,1:T(8,128)(2,1)S(1)} %bitcast.302, bf16[512,2048]{1,0:T(8,128)(2,1)} %bitcast.11), kind=kOutput, calls=%fused_computation.200 | convolution fusion | flops 268435456 | bytes 3276800 | tf_op jit(solution)/shard_map/dot_general | solution.py:62
  82.4 2.2 %fusion = f32[128,2048]{1,0:T(8,128)S(1)} fusion(f32[128,2048]{1,0:T(8,128)S(1)} %fusion.95, bf16[8,64,2048]{2,1,0:T(8,128)(2,1)} %collective-permute-done.3, bf16[128,8,64]{2,1,0:T(8,128)(2,1)S(1)} %get-tuple-element.42), kind=kOutput, calls=%fused_computation.1 | convolution fusion | flops 268697600 | bytes 4325376 | tf_op jit(solution)/shard_map/dot_general | solution.py:62
  85.5 3.7 %collective-permute-start.8 = (bf16[4,32,2048]{2,1,0:T(8,128)(2,1)}, bf16[4,32,2048]{2,1,0:T(8,128)(2,1)S(1)}, u32[]{:S(2)}, u32[]{:S(2)}) collective-permute-start(bf16[4,32,2048]{2,1,0:T(8,128)(2,1)} %fusion.30), channel_id=1, source_target_pairs={{0,16},{1,17},{2,18},{3,19},{4,20},{5,21},{6,22},{7,23},{8,24},{9,... | collective-permute-start | bytes 1572872 | tf_op jit(solution)/shard_map/ppermute | solution.py:15
  90.6 3.0 %select_add_fusion.3 = (bf16[512,128]{1,0:T(8,128)(2,1)}, bf16[512,128]{1,0:T(8,128)(2,1)}) fusion(bf16[512,128]{1,0:T(8,128)(2,1)S(1)} %copy-done.34, pred[]{:T(512)S(6)} %eq.59, bf16[512,2048]{1,0:T(8,128)(2,1)} %bitcast.9, bf16[128,2048]{1,0:T(8,128)(2,1)S(1)} %bitcast.287), kind=kOutput, calls=%fused_computation.180 | convolution fusion | flops 268894208 | bytes 3014657 | tf_op jit(solution)/shard_map/transpose(jvp())/dot_general | solution.py:62
  94.7 1.8 %copy.84 = bf16[128,8,64]{2,1,0:T(8,128)(2,1)} copy(bf16[128,8,64]{0,2,1:T(8,128)(2,1)} %bitcast.315) | data formatting | bytes 262144 | tf_op jit(solution)/shard_map/transpose(jvp())/reshape | solution.py:59
  96.5 1.1 pad_add_fusion.1
  97.7 3.6 %collective-permute-done.8 = bf16[4,32,2048]{2,1,0:T(8,128)(2,1)S(1)} collective-permute-done((bf16[4,32,2048]{2,1,0:T(8,128)(2,1)}, bf16[4,32,2048]{2,1,0:T(8,128)(2,1)S(1)}, u32[]{:S(2)}, u32[]{:S(2)}) %collective-permute-start.8) | collective-permute-done | bytes 524320 | tf_op jit(solution)/shard_map/ppermute | solution.py:15
  103.8 1.3 collective-permute-start.9
  105.6 1.5 convolution_convert_fusion.3
  107.2 12.2 %collective-permute-done.9 = bf16[4,32,2048]{2,1,0:T(8,128)(2,1)S(1)} collective-permute-done((bf16[4,32,2048]{2,1,0:T(8,128)(2,1)S(1)}, bf16[4,32,2048]{2,1,0:T(8,128)(2,1)S(1)}, u32[]{:S(2)}, u32[]{:S(2)}) %collective-permute-start.9) | collective-permute-done | bytes 524320 | tf_op jit(solution)/shard_map/ppermute | solution.py:15
  119.3 2.4 %convolution_convert_fusion.15 = bf16[128,512]{1,0:T(8,128)(2,1)S(1)} fusion(bf16[128,2048]{1,0:T(8,128)(2,1)S(1)} %bitcast.288, bf16[512,2048]{1,0:T(8,128)(2,1)} %bitcast.9), kind=kOutput, calls=%fused_computation.45 | convolution fusion | flops 268500992 | bytes 2752512 | tf_op jit(solution)/shard_map/transpose(jvp())/dot_general | solution.py:62
  121.7 3.2 %select_add_fusion.1 = (bf16[128,512]{1,0:T(8,128)(2,1)}, bf16[128,512]{1,0:T(8,128)(2,1)}) fusion(bf16[128,512]{1,0:T(8,128)(2,1)S(1)} %convolution_convert_fusion.15, pred[]{:T(512)S(6)} %eq.59, bf16[128,2048]{1,0:T(8,128)(2,1)S(1)} %bitcast.289, bf16[512,2048]{1,0:T(8,128)(2,1)} %bitcast.11), kind=kOutput, calls=%fused_computation.178 | convolution fusion | flops 268894208 | bytes 3014657 | tf_op jit(solution)/shard_map/transpose(jvp())/dot_general | solution.py:62
  124.9 1.7 %copy.112 = bf16[128,512]{0,1:T(8,128)(2,1)} copy(bf16[128,512]{1,0:T(8,128)(2,1)} %get-tuple-element.39) | data formatting | bytes 262144 | tf_op jit(solution)/shard_map/transpose(jvp())/add_any | solution.py:60
  126.6 1.7 %copy.111 = bf16[128,512]{0,1:T(8,128)(2,1)} copy(bf16[128,512]{1,0:T(8,128)(2,1)} %get-tuple-element.38) | data formatting | bytes 262144 | tf_op jit(solution)/shard_map/transpose(jvp())/add_any | solution.py:60
  128.2 1.7 %pad_add_fusion = bf16[128,8,128]{0,2,1:T(8,128)(2,1)} fusion(bf16[128,8,64]{0,2,1:T(8,128)(2,1)} %bitcast.303, bf16[128,8,64]{0,2,1:T(8,128)(2,1)} %bitcast.304), kind=kLoop, calls=%fused_computation.139 | loop fusion | flops 524288 | bytes 524288 | tf_op jit(solution)/shard_map/transpose(jvp())/add_any | solution.py:58
  129.9 1.9 %copy.113 = bf16[128,8,128]{2,1,0:T(8,128)(2,1)} copy(bf16[128,8,128]{0,2,1:T(8,128)(2,1)} %pad_add_fusion) | data formatting | bytes 524288 | tf_op jit(solution)/shard_map/transpose(jvp())/add_any | solution.py:58
  131.8 1.5 multiply_reduce_fusion.3
  133.4 1.5 fusion.11
  139.3 1.6 %add_bitcast_fusion.1 = (bf16[16,8,8,128]{3,1,2,0:T(8,128)(2,1)S(1)}, bf16[16,8,8,128]{3,1,2,0:T(8,128)(2,1)S(1)}, bf16[16,8,8,128]{3,1,2,0:T(8,128)(2,1)}, bf16[16,8,8,128]{3,1,2,0:T(8,128)(2,1)}) fusion(bf16[128,1024]{1,0:T(8,128)(2,1)S(1)} %copy-done.25, pred[]{:T(512)S(6)} %eq.59, bf16[128,1024]{1,0:T(8,128)(2,1)S(1)} %convolution_convert_fusion.6, ...), kind=kOutput, calls=%fused_computation.136 | convolution fusion | flops 270139392 | bytes 4194305 | tf_op jit(solution)/shard_map/transpose(jvp())/dot_general | solution.py:62
  143.4 2.4 %reshape.292 = f32[4,32,2048]{2,1,0:T(8,128)} reshape(f32[128,8,256]{2,1,0:T(8,128)} %add_convert_fusion.1) | data formatting | bytes 2097152 | tf_op jit(solution)/shard_map/transpose(jvp())/convert_element_type | solution.py:93
  146.9 2.4 %fusion.27 = (f32[2048]{0:T(1024)S(1)}, f32[4,32]{1,0:T(4,128)S(1)}, f32[4,32]{1,0:T(4,128)S(1)}, f32[2048]{0:T(1024)S(1)}, f32[4,32]{1,0:T(4,128)S(1)}, /*index=5*/f32[2048]{0:T(1024)S(1)}) fusion(bf16[4,32,1024]{2,1,0:T(8,128)(2,1)S(1)} %get-tuple-element.62, bf16[4,32,1024]{2,1,0:T(8,128)(2,1)S(1)} %get-tuple-element.63, ...), kind=kLoop, calls=%fused_computation.70 | loop fusion | flops 5498496 | bytes 4229632 | tf_op jit(solution)/shard_map/transpose(jvp())/reduce_sum | solution.py:79
  149.4 1.2 collective-permute-done.10
  151.2 3.0 %collective-permute-done.11 = f32[2048]{0:T(1024)S(1)} collective-permute-done((f32[2048]{0:T(1024)S(1)}, f32[2048]{0:T(1024)S(1)}, u32[]{:S(2)}, u32[]{:S(2)}) %collective-permute-start.11) | collective-permute-done | bytes 8224 | tf_op jit(solution)/shard_map/ppermute | solution.py:72
  155.0 2.8 %collective-permute-done.12 = f32[2048]{0:T(1024)S(1)} collective-permute-done((f32[2048]{0:T(1024)S(1)}, f32[2048]{0:T(1024)S(1)}, u32[]{:S(2)}, u32[]{:S(2)}) %collective-permute-start.12) | collective-permute-done | bytes 8224 | tf_op jit(solution)/shard_map/ppermute | solution.py:72
  157.8 2.4 %collective-permute-start.13 = (f32[2048]{0:T(1024)S(1)}, f32[2048]{0:T(1024)S(1)}, u32[]{:S(2)}, u32[]{:S(2)}) collective-permute-start(f32[2048]{0:T(1024)S(1)} %add.124), channel_id=1, source_target_pairs={{0,8},{1,9},{2,10},{3,11},{4,12},{5,13},{6,14},{7,15},{8,0},{9,1},... | collective-permute-start | bytes 24584 | tf_op jit(solution)/shard_map/ppermute | solution.py:72
  160.3 1.8 %fusion.37 = bf16[1,4,1,32,2048]{4,3,2,1,0:T(8,128)(2,1)} fusion(f32[4,32,2048]{2,1,0:T(8,128)S(1)} %copy-done.6, f32[4,32,2048]{2,1,0:T(8,128)S(1)} %reshape.294, f32[4,32,2048]{2,1,0:T(8,128)S(1)} %copy-done.7, bf16[4,32,2048]{2,1,0:T(8,128)(2,1)S(1)} %collective-permute-done.9, bf16[4,32,1024]{2,1,0:T(8,128)(2,1)S(1)} %get-tuple-element.62, ...), kind=kLoop, calls=%fused_computation.91 | loop fusion | flops 8388608 | bytes 5777922
  (159 shorter events, 27.0 us)
Async XLA Ops:
  0.6 7.8 %copy-start = (bf16[16,2048]{1,0:T(8,128)(2,1)S(1)}, bf16[16,2048]{1,0:T(8,128)(2,1)}, u32[]{:S(2)}) copy-start(bf16[16,2048]{1,0:T(8,128)(2,1)} %param.11) | copy-start | bytes 196612
  0.6 7.6 %copy-start.35 = (s32[4,1,16,2]{2,3,1,0:T(2,128)S(1)}, s32[4,1,16,2]{2,3,1,0:T(2,128)}, u32[]{:S(2)}) copy-start(s32[4,1,16,2]{2,3,1,0:T(2,128)} %param.10) | copy-start | bytes 1540
  0.7 22.7 %collective-permute-start.4 = (bf16[1,128,1024]{2,1,0:T(8,128)(2,1)}, bf16[1,128,1024]{2,1,0:T(8,128)(2,1)S(1)}, u32[]{:S(2)}, u32[]{:S(2)}) collective-permute-start(bf16[1,128,1024]{2,1,0:T(8,128)(2,1)} %param.12), channel_id=1, source_target_pairs={{0,8},{1,9},{2,10},{3,11},{4,12},{5,13},{6,14},{7,15},{8,0},{9,1},... | collective-permute-start | bytes 786440 | tf_op jit(solution)/shard_map/ppermute | solution.py:37
  4.8 23.5 %collective-permute-start = (bf16[1,64,2048]{2,1,0:T(8,128)(2,1)}, bf16[1,64,2048]{2,1,0:T(8,128)(2,1)S(1)}, u32[]{:S(2)}, u32[]{:S(2)}) collective-permute-start(bf16[1,64,2048]{2,1,0:T(8,128)(2,1)} %param.13), channel_id=1, source_target_pairs={{0,8},{1,9},{2,10},{3,11},{4,12},{5,13},{6,14},{7,15},{8,0},{9,1},... | collective-permute-start | bytes 786440 | tf_op jit(solution)/shard_map/ppermute | solution.py:37
  9.8 3.5 %copy-start.24 = (f32[1,2048]{1,0:T(1,128)S(1)}, f32[1,2048]{1,0:T(1,128)}, u32[]{:S(2)}) copy-start(f32[1,2048]{1,0:T(1,128)} %param.14) | copy-start | bytes 24580
  11.1 3.0 %copy-start.9 = (f32[4,1,32,2048]{3,2,0,1:T(8,128)S(1)}, f32[4,1,32,2048]{3,2,0,1:T(8,128)}, u32[]{:S(2)}) copy-start(f32[4,1,32,2048]{3,2,0,1:T(8,128)} %bitcast_convert_fusion) | copy-start | bytes 3145732
  14.1 4.0 %copy-start.4 = (bf16[4,1,32,2048]{3,2,1,0:T(8,128)(2,1)S(1)}, bf16[4,1,32,2048]{3,2,1,0:T(8,128)(2,1)}, u32[]{:S(2)}) copy-start(bf16[4,1,32,2048]{3,2,1,0:T(8,128)(2,1)} %param.8) | copy-start | bytes 1572868
  15.4 7.9 %copy-start.30 = (bf16[1,128,1024]{2,1,0:T(8,128)(2,1)S(1)}, bf16[1,128,1024]{2,1,0:T(8,128)(2,1)}, u32[]{:S(2)}) copy-start(bf16[1,128,1024]{2,1,0:T(8,128)(2,1)} %param.12) | copy-start | bytes 786436
  18.0 10.2 %copy-start.31 = (bf16[1,64,2048]{2,1,0:T(8,128)(2,1)S(1)}, bf16[1,64,2048]{2,1,0:T(8,128)(2,1)}, u32[]{:S(2)}) copy-start(bf16[1,64,2048]{2,1,0:T(8,128)(2,1)} %param.13) | copy-start | bytes 786436
  23.4 15.9 %collective-permute-start.5 = (bf16[2,128,1024]{2,1,0:T(8,128)(2,1)S(1)}, bf16[2,128,1024]{2,1,0:T(8,128)(2,1)S(1)}, u32[]{:S(2)}, u32[]{:S(2)}) collective-permute-start(bf16[2,128,1024]{2,1,0:T(8,128)(2,1)S(1)} %pad_maximum_fusion.4), channel_id=1, source_target_pairs={{0,4},{1,5},{2,6},{3,7},{4,0},{5,1},{6,2},{7,3},{8,12},{9,13},{10,... | collective-permute-start | bytes 1572872 | tf_op jit(solution)/shard_map/ppermute | solution.py:37
  28.3 11.2 %copy-start.14 = (bf16[1,64,2048]{2,1,0:T(8,128)(2,1)}, bf16[1,64,2048]{2,1,0:T(8,128)(2,1)S(1)}, u32[]{:S(2)}) copy-start(bf16[1,64,2048]{2,1,0:T(8,128)(2,1)S(1)} %get-tuple-element.33) | copy-start | bytes 786436
  29.2 12.0 %copy-start.8 = (f32[128,8,256]{0,2,1:T(8,128)S(1)}, f32[128,8,256]{0,2,1:T(8,128)}, u32[]{:S(2)}) copy-start(f32[128,8,256]{0,2,1:T(8,128)} %copy.94) | copy-start | bytes 3145732
  29.2 13.4 %collective-permute-start.1 = (bf16[2,64,2048]{2,1,0:T(8,128)(2,1)}, bf16[2,64,2048]{2,1,0:T(8,128)(2,1)}, u32[]{:S(2)}, u32[]{:S(2)}) collective-permute-start(bf16[2,64,2048]{2,1,0:T(8,128)(2,1)} %pad_maximum_fusion.5), channel_id=1, source_target_pairs={{0,2},{1,3},{2,0},{3,1},{4,6},{5,7},{6,4},{7,5},{8,10},{9,11},{10,... | collective-permute-start | bytes 1572872 | tf_op jit(solution)/shard_map/ppermute | solution.py:37
  39.6 25.4 %collective-permute-start.6 = (bf16[4,128,1024]{2,1,0:T(8,128)(2,1)S(1)}, bf16[4,128,1024]{2,1,0:T(8,128)(2,1)}, u32[]{:S(2)}, u32[]{:S(2)}) collective-permute-start(bf16[4,128,1024]{2,1,0:T(8,128)(2,1)S(1)} %bitcast.270), channel_id=1, source_target_pairs={{0,2},{1,3},{2,0},{3,1},{4,6},{5,7},{6,4},{7,5},{8,10},{9,11},{10,... | collective-permute-start | bytes 3145736 | tf_op jit(solution)/shard_map/ppermute | solution.py:37
  42.4 24.3 %copy-start.10 = (bf16[128,8,256]{0,2,1:T(8,128)(2,1)}, bf16[128,8,256]{0,2,1:T(8,128)(2,1)S(1)}, u32[]{:S(2)}) copy-start(bf16[128,8,256]{0,2,1:T(8,128)(2,1)S(1)} %get-tuple-element.46) | copy-start | bytes 1572868
  42.4 4.9 %copy-start.12 = (bf16[128,8,256]{0,2,1:T(8,128)(2,1)S(1)}, bf16[128,8,256]{0,2,1:T(8,128)(2,1)}, u32[]{:S(2)}) copy-start(bf16[128,8,256]{0,2,1:T(8,128)(2,1)} %get-tuple-element.47) | copy-start | bytes 1572868
  42.4 5.0 %copy-start.36 = (s32[4,1,32]{2,1,0:T(1,128)S(1)}, s32[4,1,32]{2,1,0:T(1,128)}, u32[]{:S(2)}) copy-start(s32[4,1,32]{2,1,0:T(1,128)} %param.9) | copy-start | bytes 1540
  45.0 25.1 %collective-permute-start.2 = (bf16[4,64,2048]{2,1,0:T(8,128)(2,1)}, bf16[4,64,2048]{2,1,0:T(8,128)(2,1)}, u32[]{:S(2)}, u32[]{:S(2)}) collective-permute-start(bf16[4,64,2048]{2,1,0:T(8,128)(2,1)} %bitcast.3), channel_id=1, source_target_pairs={{0,4},{1,5},{2,6},{3,7},{4,0},{5,1},{6,2},{7,3},{8,12},{9,13},{10,... | collective-permute-start | bytes 3145736 | tf_op jit(solution)/shard_map/ppermute | solution.py:37
  66.6 11.4 %collective-permute-start.7 = (bf16[8,128,1024]{2,1,0:T(8,128)(2,1)S(1)}, bf16[8,128,1024]{2,1,0:T(8,128)(2,1)S(1)}, u32[]{:S(2)}, u32[]{:S(2)}) collective-permute-start(bf16[8,128,1024]{2,1,0:T(8,128)(2,1)S(1)} %bitcast.262), channel_id=1, source_target_pairs={{0,1},{1,0},{2,3},{3,2},{4,5},{5,4},{6,7},{7,6},{8,9},{9,8},{10,11... | collective-permute-start | bytes 6291464 | tf_op jit(solution)/shard_map/ppermute | solution.py:49
  67.5 11.1 %copy-start.32 = (bf16[4,4,8,8,128]{4,3,2,1,0:T(8,128)(2,1)}, bf16[4,4,8,8,128]{4,3,2,1,0:T(8,128)(2,1)S(1)}, u32[]{:S(2)}) copy-start(bf16[4,4,8,8,128]{4,3,2,1,0:T(8,128)(2,1)S(1)} %get-tuple-element.34) | copy-start | bytes 786436
  67.5 11.9 %copy-start.21 = (bf16[4,4,8,8,128]{4,3,2,1,0:T(8,128)(2,1)}, bf16[4,4,8,8,128]{4,3,2,1,0:T(8,128)(2,1)S(1)}, u32[]{:S(2)}) copy-start(bf16[4,4,8,8,128]{4,3,2,1,0:T(8,128)(2,1)S(1)} %get-tuple-element.35) | copy-start | bytes 786436
  71.7 1.5 copy-start.15
  73.2 9.2 %collective-permute-start.3 = (bf16[8,64,2048]{2,1,0:T(8,128)(2,1)}, bf16[8,64,2048]{2,1,0:T(8,128)(2,1)}, u32[]{:S(2)}, u32[]{:S(2)}) collective-permute-start(bf16[8,64,2048]{2,1,0:T(8,128)(2,1)} %bitcast.8), channel_id=1, source_target_pairs={{0,1},{1,0},{2,3},{3,2},{4,5},{5,4},{6,7},{7,6},{8,9},{9,8},{10,11... | collective-permute-start | bytes 6291464 | tf_op jit(solution)/shard_map/ppermute | solution.py:49
  76.7 1.4 copy-start.13
  78.0 1.3 copy-start.1
  78.6 1.4 copy-start.26
  82.4 6.9 %copy-start.11 = (bf16[128,8,256]{0,2,1:T(8,128)(2,1)S(1)}, bf16[128,8,256]{0,2,1:T(8,128)(2,1)}, u32[]{:S(2)}) copy-start(bf16[128,8,256]{0,2,1:T(8,128)(2,1)} %copy-done.10) | copy-start | bytes 1572868
  82.4 6.9 %copy-start.19 = (f32[128,1024]{1,0:T(8,128)S(1)}, f32[128,1024]{1,0:T(8,128)}, u32[]{:S(2)}) copy-start(f32[128,1024]{1,0:T(8,128)} %fusion.93) | copy-start | bytes 1572868
  84.6 4.7 %copy-start.2 = (bf16[8,128,1024]{2,1,0:T(8,128)(2,1)S(1)}, bf16[8,128,1024]{2,1,0:T(8,128)(2,1)}, u32[]{:S(2)}) copy-start(bf16[8,128,1024]{2,1,0:T(8,128)(2,1)} %copy-done.1) | copy-start | bytes 6291460
  85.5 5.1 %copy-start.16 = (bf16[4,1,32,2048]{3,2,1,0:T(8,128)(2,1)S(1)}, bf16[4,1,32,2048]{3,2,1,0:T(8,128)(2,1)}, u32[]{:S(2)}) copy-start(bf16[4,1,32,2048]{3,2,1,0:T(8,128)(2,1)} %param.15) | copy-start | bytes 1572868
  85.5 5.1 %copy-start.34 = (bf16[512,128]{1,0:T(8,128)(2,1)S(1)}, bf16[512,128]{1,0:T(8,128)(2,1)}, u32[]{:S(2)}) copy-start(bf16[512,128]{1,0:T(8,128)(2,1)} %convolution_convert_fusion.16) | copy-start | bytes 393220
  85.5 15.7 %collective-permute-start.8 = (bf16[4,32,2048]{2,1,0:T(8,128)(2,1)}, bf16[4,32,2048]{2,1,0:T(8,128)(2,1)S(1)}, u32[]{:S(2)}, u32[]{:S(2)}) collective-permute-start(bf16[4,32,2048]{2,1,0:T(8,128)(2,1)} %fusion.30), channel_id=1, source_target_pairs={{0,16},{1,17},{2,18},{3,19},{4,20},{5,21},{6,22},{7,23},{8,24},{9,... | collective-permute-start | bytes 1572872 | tf_op jit(solution)/shard_map/ppermute | solution.py:15
  96.5 5.2 %copy-start.28 = (bf16[16,8,8,128]{3,2,1,0:T(8,128)(2,1)S(1)}, bf16[16,8,8,128]{3,2,1,0:T(8,128)(2,1)}, u32[]{:S(2)}) copy-start(bf16[16,8,8,128]{3,2,1,0:T(8,128)(2,1)} %copy.144) | copy-start | bytes 786436
  103.8 15.5 %collective-permute-start.9 = (bf16[4,32,2048]{2,1,0:T(8,128)(2,1)S(1)}, bf16[4,32,2048]{2,1,0:T(8,128)(2,1)S(1)}, u32[]{:S(2)}, u32[]{:S(2)}) collective-permute-start(bf16[4,32,2048]{2,1,0:T(8,128)(2,1)S(1)} %fusion.17), channel_id=1, source_target_pairs={{16,0},{17,1},{18,2},{19,3},{20,4},{21,5},{22,6},{23,7},{24,8},{25... | collective-permute-start | bytes 1572872 | tf_op jit(solution)/shard_map/ppermute | solution.py:15
  131.8 3.1 %copy-start.23 = (f32[4,8,32,32]{2,3,1,0:T(8,128)S(1)}, f32[4,8,32,32]{2,3,1,0:T(8,128)}, u32[]{:S(2)}) copy-start(f32[4,8,32,32]{2,3,1,0:T(8,128)} %copy-done.22) | copy-start | bytes 393220
  131.8 3.1 %copy-start.27 = (bf16[16,8,8,128]{3,2,1,0:T(8,128)(2,1)S(1)}, bf16[16,8,8,128]{3,2,1,0:T(8,128)(2,1)}, u32[]{:S(2)}) copy-start(bf16[16,8,8,128]{3,2,1,0:T(8,128)(2,1)} %copy-done.26) | copy-start | bytes 786436
  133.4 2.5 %copy-start.20 = (bf16[128,8,128]{2,1,0:T(8,128)(2,1)S(1)}, bf16[128,8,128]{2,1,0:T(8,128)(2,1)}, u32[]{:S(2)}) copy-start(bf16[128,8,128]{2,1,0:T(8,128)(2,1)} %copy.113) | copy-start | bytes 786436
  136.9 1.6 copy-start.3
  137.0 2.3 %copy-start.25 = (bf16[128,1024]{1,0:T(8,128)(2,1)S(1)}, bf16[128,1024]{1,0:T(8,128)(2,1)}, u32[]{:S(2)}) copy-start(bf16[128,1024]{1,0:T(8,128)(2,1)} %convolution_convert_fusion.3) | copy-start | bytes 786436
  141.1 1.3 copy-start.29
  142.4 3.4 %copy-start.33 = (bf16[4,8,4,8,128]{4,3,2,1,0:T(8,128)(2,1)S(1)}, bf16[4,8,4,8,128]{4,3,2,1,0:T(8,128)(2,1)}, u32[]{:S(2)}) copy-start(bf16[4,8,4,8,128]{4,3,2,1,0:T(8,128)(2,1)} %fusion.10) | copy-start | bytes 786436
  142.4 4.5 %copy-start.6 = (f32[4,32,2048]{2,1,0:T(8,128)S(1)}, f32[4,32,2048]{2,1,0:T(8,128)}, u32[]{:S(2)}) copy-start(f32[4,32,2048]{2,1,0:T(8,128)} %copy-done.5) | copy-start | bytes 3145732
  146.8 13.4 %copy-start.7 = (f32[4,32,2048]{2,1,0:T(8,128)S(1)}, f32[4,32,2048]{2,1,0:T(8,128)}, u32[]{:S(2)}) copy-start(f32[4,32,2048]{2,1,0:T(8,128)} %reshape.292) | copy-start | bytes 3145732
  146.9 13.4 %copy-start.17 = (bf16[4,1,32,2048]{3,2,1,0:T(8,128)(2,1)S(1)}, bf16[4,1,32,2048]{3,2,1,0:T(8,128)(2,1)}, u32[]{:S(2)}) copy-start(bf16[4,1,32,2048]{3,2,1,0:T(8,128)(2,1)} %param.15) | copy-start | bytes 1572868
  149.3 1.2 collective-permute-start.10
  150.5 3.7 %collective-permute-start.11 = (f32[2048]{0:T(1024)S(1)}, f32[2048]{0:T(1024)S(1)}, u32[]{:S(2)}, u32[]{:S(2)}) collective-permute-start(f32[2048]{0:T(1024)S(1)} %add.122), channel_id=1, source_target_pairs={{0,2},{1,3},{2,0},{3,1},{4,6},{5,7},{6,4},{7,5},{8,10},{9,11},{10,... | collective-permute-start | bytes 24584 | tf_op jit(solution)/shard_map/ppermute | solution.py:72
  154.2 3.7 %collective-permute-start.12 = (f32[2048]{0:T(1024)S(1)}, f32[2048]{0:T(1024)S(1)}, u32[]{:S(2)}, u32[]{:S(2)}) collective-permute-start(f32[2048]{0:T(1024)S(1)} %add.123), channel_id=1, source_target_pairs={{0,4},{1,5},{2,6},{3,7},{4,0},{5,1},{6,2},{7,3},{8,12},{9,13},{10,... | collective-permute-start | bytes 24584 | tf_op jit(solution)/shard_map/ppermute | solution.py:72
  157.8 4.5 %collective-permute-start.13 = (f32[2048]{0:T(1024)S(1)}, f32[2048]{0:T(1024)S(1)}, u32[]{:S(2)}, u32[]{:S(2)}) collective-permute-start(f32[2048]{0:T(1024)S(1)} %add.124), channel_id=1, source_target_pairs={{0,8},{1,9},{2,10},{3,11},{4,12},{5,13},{6,14},{7,15},{8,0},{9,1},... | collective-permute-start | bytes 24584 | tf_op jit(solution)/shard_map/ppermute | solution.py:72
  (3 other events, 2.8 us)

commit v10 on v3

--- a/solution.py
+++ b/solution.py
@@ -35,10 +35,13 @@
             step = order[level]
             other = lax.ppermute(held[which], axis, [(j, j ^ step) for j in range(size)])
             upper = ((index // step) % 2) == 1
-            low = jnp.where(upper, other, held[which])
-            high = jnp.where(upper, held[which], other)
-            held[which] = jnp.stack([low, high], axis=1).reshape(
-                (-1,) + held[which].shape[1:]
+            mine = held[which]
+            held[which] = lax.cond(
+                upper,
+                lambda a, b: jnp.stack([b, a], axis=1).reshape((-1,) + a.shape[1:]),
+                lambda a, b: jnp.stack([a, b], axis=1).reshape((-1,) + a.shape[1:]),
+                mine,
+                other,
             )
     results = []
     for which, order in enumerate(orders):

time: 137 us -> 148 us (1.080)
  local copies, waits for them, and re-layouts: 5.99 us -> 11.6 us
  matrix products: 13.3 us -> 15.8 us
  starting transfers between devices: 20.2 us -> 21.9 us
    another operation x3 -> x5, local copies, waits for them, and re-layouts: 2.23 us -> 5.19 us  [butterfly_gathers(): jnp.stack([a, b], axis=1).reshape((-1,) + a.shape[1:])]
    ppermute x2, waiting for transfers between devices: 20.2 us -> 22.6 us  [send_to(): return lax.ppermute(arrays, axis, [(source, target)])]
    dot_general x4, matrix products: 4.51 us -> 6.82 us  [attend_layer(): jnp.dot(normed_rows, query_weight, preferred_element_type=jnp.float32)]
    ppermute x4, starting transfers between devices: 4.36 us -> 6.58 us  [butterfly_sum(): lax.ppermute(value, axis, [(j, j ^ step) for j in range(size)])]
    transpose x1, local copies, waits for them, and re-layouts: 0.58 us -> 2.55 us  [butterfly_gathers(): held[which] = jnp.transpose(split, axes)]
    reshape x2, other arithmetic: 0.1 us -> 2 us  [butterfly_gathers(): jnp.stack([a, b], axis=1).reshape((-1,) + a.shape[1:])]
    ppermute x4, waiting for transfers between devices: 6.84 us -> 5.15 us  [butterfly_sum(): lax.ppermute(value, axis, [(j, j ^ step) for j in range(size)])]
    unnamed x37 -> x41, local copies, waits for them, and re-layouts: 1.62 us -> 3.22 us
  transfers between devices with their start and end apart: 14 -> 14, of which waited for: 12 -> 11; matrix products, arithmetic and copies ran while one was open for 15% -> 16% of each run, Pallas kernels for 0% -> 0%
where the time goes in v10:
time: 148 us
  waiting for transfers between devices  80.4 us (54%)
  starting transfers between devices  21.9 us (15%)
  other arithmetic  16.8 us (11%)
  matrix products  15.8 us (11%)
  local copies, waits for them, and re-layouts  11.6 us (8%)
    ppermute x8, waiting for transfers between devices, butterfly_gathers(): lax.ppermute(held[which], axis, [(j, j ^ step) for j in range(size)])  52.6 us
    ppermute x2, waiting for transfers between devices, send_to(): return lax.ppermute(arrays, axis, [(source, target)])  22.6 us
    ppermute x8, starting transfers between devices, butterfly_gathers(): lax.ppermute(held[which], axis, [(j, j ^ step) for j in range(size)])  10.2 us
    another operation x6, other arithmetic, butterfly_gathers(): jnp.stack([a, b], axis=1).reshape((-1,) + a.shape[1:])  9.08 us
    dot_general x4, matrix products, attend_layer(): jnp.dot(normed_rows, query_weight, preferred_element_type=jnp.float32)  6.82 us
    ppermute x4, starting transfers between devices, butterfly_sum(): lax.ppermute(value, axis, [(j, j ^ step) for j in range(size)])  6.58 us
    another operation x5, local copies, waits for them, and re-layouts, butterfly_gathers(): jnp.stack([a, b], axis=1).reshape((-1,) + a.shape[1:])  5.19 us
    ppermute x2, starting transfers between devices, send_to(): return lax.ppermute(arrays, axis, [(source, target)])  5.17 us
  transfers between devices with their start and end apart: 14, of which 11 were waited for; matrix products, arithmetic and copies ran while one was open for 16% of the time, Pallas kernels for 0%

profile of v10, /device:TPU:0, one launch (start us, length us, event | category | flops | bytes accessed | tf_op | source)
XLA Modules:
  0.0 147.8 jit_solution(10839718972740061630)
XLA Ops:
  0.6 4.1 %collective-permute-start.4 = (bf16[1,128,1024]{2,1,0:T(8,128)(2,1)}, bf16[1,128,1024]{2,1,0:T(8,128)(2,1)S(1)}, u32[]{:S(2)}, u32[]{:S(2)}) collective-permute-start(bf16[1,128,1024]{2,1,0:T(8,128)(2,1)} %param.28), channel_id=1, source_target_pairs={{0,8},{1,9},{2,10},{3,11},{4,12},{5,13},{6,14},{7,15},{8,0},{9,1},... | collective-permute-start | bytes 786440 | tf_op jit(solution)/shard_map/ppermute | solution.py:36
  4.8 18.5 %collective-permute-done.4 = bf16[1,128,1024]{2,1,0:T(8,128)(2,1)S(1)} collective-permute-done((bf16[1,128,1024]{2,1,0:T(8,128)(2,1)}, bf16[1,128,1024]{2,1,0:T(8,128)(2,1)S(1)}, u32[]{:S(2)}, u32[]{:S(2)}) %collective-permute-start.4) | collective-permute-done | bytes 262176 | tf_op jit(solution)/shard_map/ppermute | solution.py:36
  23.3 1.0 conditional.12
  23.3 1.0 maximum_bitcast_fusion.2
  24.5 3.7 %collective-permute-done = bf16[1,64,2048]{2,1,0:T(8,128)(2,1)S(1)} collective-permute-done((bf16[1,64,2048]{2,1,0:T(8,128)(2,1)}, bf16[1,64,2048]{2,1,0:T(8,128)(2,1)S(1)}, u32[]{:S(2)}, u32[]{:S(2)}) %collective-permute-start) | collective-permute-done | bytes 262176 | tf_op jit(solution)/shard_map/ppermute | solution.py:36
  28.2 1.0 conditional.8
  28.2 1.0 maximum_bitcast_fusion
  29.2 1.6 %collective-permute-start.1 = (bf16[2,64,2048]{2,1,0:T(8,128)(2,1)S(1)}, bf16[2,64,2048]{2,1,0:T(8,128)(2,1)}, u32[]{:S(2)}, u32[]{:S(2)}) collective-permute-start(bf16[2,64,2048]{2,1,0:T(8,128)(2,1)S(1)} %get-tuple-element.170), channel_id=1, source_target_pairs={{0,2},{1,3},{2,0},{3,1},{4,6},{5,7},{6,4},{7,5},{8,10},{9,11},{10,... | collective-permute-start | bytes 1572872 | tf_op jit(solution)/shard_map/ppermute | solution.py:36
  30.9 8.5 %collective-permute-done.5 = bf16[2,128,1024]{2,1,0:T(8,128)(2,1)S(1)} collective-permute-done((bf16[2,128,1024]{2,1,0:T(8,128)(2,1)S(1)}, bf16[2,128,1024]{2,1,0:T(8,128)(2,1)S(1)}, u32[]{:S(2)}, u32[]{:S(2)}) %collective-permute-start.5) | collective-permute-done | bytes 524320 | tf_op jit(solution)/shard_map/ppermute | solution.py:36
  39.5 1.6 %collective-permute-start.6 = (bf16[4,128,1024]{2,1,0:T(8,128)(2,1)S(1)}, bf16[4,128,1024]{2,1,0:T(8,128)(2,1)S(1)}, u32[]{:S(2)}, u32[]{:S(2)}) collective-permute-start(bf16[4,128,1024]{2,1,0:T(8,128)(2,1)S(1)} %get-tuple-element.175), channel_id=1, source_target_pairs={{0,2},{1,3},{2,0},{3,1},{4,6},{5,7},{6,4},{7,5},{8,10},{9,11},{10,... | collective-permute-start | bytes 3145736 | tf_op jit(solution)/shard_map/ppermute | solution.py:36
  41.2 1.3 collective-permute-done.1
  42.4 2.2 %conditional.9 = (bf16[4,64,2048]{2,1,0:T(8,128)(2,1)}) conditional(s32[]{:T(128)} %convert_element_type.222, (bf16[2,64,2048]{2,1,0:T(8,128)(2,1)S(1)}, bf16[2,64,2048]{2,1,0:T(8,128)(2,1)}) %tuple.93, (bf16[2,64,2048]{2,1,0:T(8,128)(2,1)}, bf16[2,64,2048]{2,1,0:T(8,128)(2,1)S(1)}) %tuple.94), branch_computations={%region_2.3_spmd, %region_3.4_spmd} | conditional | flops 524288 | bytes 4194312 | solution.py:39
  42.4 1.1 pad_maximum_fusion
  43.6 1.1 copy.46
  44.7 2.5 %collective-permute-start.2 = (bf16[4,64,2048]{2,1,0:T(8,128)(2,1)}, bf16[4,64,2048]{2,1,0:T(8,128)(2,1)}, u32[]{:S(2)}, u32[]{:S(2)}) collective-permute-start(bf16[4,64,2048]{2,1,0:T(8,128)(2,1)} %get-tuple-element.171), channel_id=1, source_target_pairs={{0,4},{1,5},{2,6},{3,7},{4,0},{5,1},{6,2},{7,3},{8,12},{9,13},{10,... | collective-permute-start | bytes 3145736 | tf_op jit(solution)/shard_map/ppermute | solution.py:36
  47.2 17.6 %collective-permute-done.6 = bf16[4,128,1024]{2,1,0:T(8,128)(2,1)S(1)} collective-permute-done((bf16[4,128,1024]{2,1,0:T(8,128)(2,1)S(1)}, bf16[4,128,1024]{2,1,0:T(8,128)(2,1)S(1)}, u32[]{:S(2)}, u32[]{:S(2)}) %collective-permute-start.6) | collective-permute-done | bytes 1048608 | tf_op jit(solution)/shard_map/ppermute | solution.py:36
  66.0 3.0 %collective-permute-done.2 = bf16[4,64,2048]{2,1,0:T(8,128)(2,1)} collective-permute-done((bf16[4,64,2048]{2,1,0:T(8,128)(2,1)}, bf16[4,64,2048]{2,1,0:T(8,128)(2,1)}, u32[]{:S(2)}, u32[]{:S(2)}) %collective-permute-start.2) | collective-permute-done | bytes 1048608 | tf_op jit(solution)/shard_map/ppermute | solution.py:36
  69.0 3.2 %conditional.10 = (bf16[8,64,2048]{2,1,0:T(8,128)(2,1)}) conditional(s32[]{:T(128)} %convert_element_type.221, (bf16[4,64,2048]{2,1,0:T(8,128)(2,1)}, bf16[4,64,2048]{2,1,0:T(8,128)(2,1)}) %tuple.95, (bf16[4,64,2048]{2,1,0:T(8,128)(2,1)}, bf16[4,64,2048]{2,1,0:T(8,128)(2,1)}) %tuple.96), branch_computations={%region_4.5_spmd, %region_5.6_spmd} | conditional | flops 1048576 | bytes 8388616 | solution.py:39
  69.0 1.8 %pad_maximum_fusion.2 = bf16[4,2,64,2048]{3,2,0,1:T(8,128)(2,1)S(1)} fusion(bf16[4,1,64,2048]{3,2,0,1:T(8,128)(2,1)} %bitcast.13, bf16[4,1,64,2048]{3,2,0,1:T(8,128)(2,1)} %bitcast.12), kind=kLoop, calls=%fused_computation.4 | loop fusion | flops 1048576 | bytes 4194304 | tf_op jit(solution)/shard_map/cond/branch_0_fun/stack | solution.py:42
  70.8 1.4 copy.48
  72.4 1.3 multiply_reduce_fusion
  74.9 4.4 %conditional.15 = (bf16[2048,1024]{1,0:T(8,128)(2,1)}) conditional(s32[]{:T(128)} %convert_element_type.220, (bf16[8,128,1024]{2,1,0:T(8,128)(2,1)S(1)}, bf16[8,128,1024]{2,1,0:T(8,128)(2,1)}) %tuple.105, (bf16[8,128,1024]{2,1,0:T(8,128)(2,1)}, bf16[8,128,1024]{2,1,0:T(8,128)(2,1)S(1)}) %tuple.106), branch_computations={%region_15.16_spmd, %region_16.17_spmd} | conditional | flops 2097152 | bytes 16777224 | solution.py:39
  74.9 2.0 %pad_maximum_fusion.10 = bf16[8,2,128,1024]{3,2,0,1:T(8,128)(2,1)S(1)} fusion(bf16[8,1,128,1024]{3,2,0,1:T(8,128)(2,1)} %bitcast.41, bf16[8,1,128,1024]{3,2,0,1:T(8,128)(2,1)S(1)} %bitcast.266), kind=kLoop, calls=%fused_computation.14 | loop fusion | flops 2097152 | bytes 8388608 | tf_op jit(solution)/shard_map/cond/branch_0_fun/stack | solution.py:42
  76.9 2.4 %copy.54 = bf16[8,2,128,1024]{3,2,1,0:T(8,128)(2,1)} copy(bf16[8,2,128,1024]{3,2,0,1:T(8,128)(2,1)S(1)} %pad_maximum_fusion.10) | data formatting | bytes 8388608 | tf_op jit(solution)/shard_map/cond/branch_0_fun/stack | solution.py:42
  79.3 3.1 %fusion.21 = bf16[16,8,8,128]{3,1,2,0:T(8,128)(2,1)S(1)} fusion(bf16[128,2048]{1,0:T(8,128)(2,1)S(1)} %bitcast.291, bf16[2048,1024]{1,0:T(8,128)(2,1)} %get-tuple-element.177), kind=kOutput, calls=%fused_computation.70 | convolution fusion | flops 537001984 | bytes 4980736 | tf_op jit(solution)/shard_map/dot_general | solution.py:85
  82.4 0.7 copy.99
  83.1 3.9 %conditional.11 = (bf16[8,2,64,2048]{3,2,0,1:T(8,128)(2,1)}) conditional(s32[]{:T(128)} %convert_element_type.220, (bf16[8,64,2048]{2,1,0:T(8,128)(2,1)S(1)}, bf16[8,64,2048]{2,1,0:T(8,128)(2,1)}) %tuple.143, (bf16[8,64,2048]{2,1,0:T(8,128)(2,1)}, bf16[8,64,2048]{2,1,0:T(8,128)(2,1)S(1)}) %tuple.144), branch_computations={%region_6.7_spmd, %region_7.8_spmd} | conditional | flops 2097152 | bytes 8388616 | solution.py:39
  83.1 3.9 %pad_maximum_fusion.4 = bf16[8,2,64,2048]{3,2,0,1:T(8,128)(2,1)} fusion(bf16[8,1,64,2048]{3,2,0,1:T(8,128)(2,1)} %bitcast.19, bf16[8,1,64,2048]{3,2,0,1:T(8,128)(2,1)S(1)} %bitcast.270), kind=kLoop, calls=%fused_computation.6 | loop fusion | flops 2097152 | bytes 8388608 | tf_op jit(solution)/shard_map/cond/branch_0_fun/stack | solution.py:42
  87.0 2.6 %copy.56 = bf16[2,2,2,2,64,2048]{5,4,3,2,1,0:T(8,128)(2,1)S(1)} copy(bf16[2,2,2,2,64,2048]{5,4,1,2,0,3:T(8,128)(2,1)} %bitcast.272) | data formatting | bytes 8388608 | tf_op jit(solution)/shard_map/transpose | solution.py:53
  89.9 0.8 copy-done.8
  91.1 1.6 %fusion = bf16[4,32,2048]{2,1,0:T(8,128)(2,1)} fusion(bf16[1024,2048,1]{1,0,2:T(8,128)(2,1)S(1)} %bitcast.261, bf16[4,1,32,2048]{3,2,1,0:T(8,128)(2,1)S(1)} %copy-done.5, bf16[4,8,4,8,128]{4,3,2,1,0:T(8,128)(2,1)S(1)} %fusion.23), kind=kOutput, calls=%fused_computation.17 | convolution fusion | flops 537657344 | bytes 5505024 | tf_op jit(solution)/shard_map/dot_general | solution.py:96
  92.7 3.6 %collective-permute-start.8 = (bf16[4,32,2048]{2,1,0:T(8,128)(2,1)}, bf16[4,32,2048]{2,1,0:T(8,128)(2,1)S(1)}, u32[]{:S(2)}, u32[]{:S(2)}) collective-permute-start(bf16[4,32,2048]{2,1,0:T(8,128)(2,1)} %fusion), channel_id=1, source_target_pairs={{0,16},{1,17},{2,18},{3,19},{4,20},{5,21},{6,22},{7,23},{8,24},{9,... | collective-permute-start | bytes 1572872 | tf_op jit(solution)/shard_map/ppermute | solution.py:15
  96.4 1.3 fusion.19
  97.9 10.4 %collective-permute-done.8 = bf16[4,32,2048]{2,1,0:T(8,128)(2,1)S(1)} collective-permute-done((bf16[4,32,2048]{2,1,0:T(8,128)(2,1)}, bf16[4,32,2048]{2,1,0:T(8,128)(2,1)S(1)}, u32[]{:S(2)}, u32[]{:S(2)}) %collective-permute-start.8) | collective-permute-done | bytes 524320 | tf_op jit(solution)/shard_map/ppermute | solution.py:15
  108.8 0.8 fusion.20
  111.8 1.6 %collective-permute-start.9 = (bf16[4,32,2048]{2,1,0:T(8,128)(2,1)S(1)}, bf16[4,32,2048]{2,1,0:T(8,128)(2,1)S(1)}, u32[]{:S(2)}, u32[]{:S(2)}) collective-permute-start(bf16[4,32,2048]{2,1,0:T(8,128)(2,1)S(1)} %fusion.44), channel_id=1, source_target_pairs={{16,0},{17,1},{18,2},{19,3},{20,4},{21,5},{22,6},{23,7},{24,8},{25... | collective-permute-start | bytes 1572872 | tf_op jit(solution)/shard_map/ppermute | solution.py:15
  113.8 1.5 %convolution_convert_fusion = bf16[128,2048]{1,0:T(8,128)(2,1)S(1)} fusion(bf16[2048,1024]{1,0:T(8,128)(2,1)S(1)} %copy-done.1, bf16[16,8,8,128]{3,2,1,0:T(8,128)(2,1)S(1)} %bitcast.297), kind=kOutput, calls=%fused_computation.18 | convolution fusion | flops 537133056 | bytes 4980736 | tf_op jit(solution)/shard_map/transpose(jvp())/dot_general | solution.py:85
  115.3 12.3 %collective-permute-done.9 = bf16[4,32,2048]{2,1,0:T(8,128)(2,1)S(1)} collective-permute-done((bf16[4,32,2048]{2,1,0:T(8,128)(2,1)S(1)}, bf16[4,32,2048]{2,1,0:T(8,128)(2,1)S(1)}, u32[]{:S(2)}, u32[]{:S(2)}) %collective-permute-start.9) | collective-permute-done | bytes 524320 | tf_op jit(solution)/shard_map/ppermute | solution.py:15
  127.6 1.5 %fusion.22 = bf16[16,8,8,128]{3,1,2,0:T(8,128)(2,1)S(1)} fusion(bf16[128,2048]{1,0:T(8,128)(2,1)S(1)} %bitcast.289, bf16[1024,2048]{1,0:T(8,128)(2,1)S(1)} %bitcast.263), kind=kOutput, calls=%fused_computation.71 | convolution fusion | flops 537001984 | bytes 4980736 | tf_op jit(solution)/shard_map/transpose(jvp())/dot_general | solution.py:96
  130.6 1.5 %convolution_convert_fusion.1 = bf16[128,2048]{1,0:T(8,128)(2,1)S(1)} fusion(bf16[2048,1024]{1,0:T(8,128)(2,1)S(1)} %copy-done.1, bf16[16,8,8,128]{3,2,1,0:T(8,128)(2,1)S(1)} %bitcast.296), kind=kOutput, calls=%fused_computation.19 | convolution fusion | flops 537133056 | bytes 4980736 | tf_op jit(solution)/shard_map/transpose(jvp())/dot_general | solution.py:85
  132.2 1.3 fusion.36
  133.6 1.2 collective-permute-done.10
  134.8 1.5 %collective-permute-start.11 = (f32[2048]{0:T(1024)S(1)}, f32[2048]{0:T(1024)S(1)}, u32[]{:S(2)}, u32[]{:S(2)}) collective-permute-start(f32[2048]{0:T(1024)S(1)} %add.91), channel_id=1, source_target_pairs={{0,2},{1,3},{2,0},{3,1},{4,6},{5,7},{6,4},{7,5},{8,10},{9,11},{10,... | collective-permute-start | bytes 24584 | tf_op jit(solution)/shard_map/ppermute | solution.py:63
  136.3 2.1 %collective-permute-done.11 = f32[2048]{0:T(1024)S(1)} collective-permute-done((f32[2048]{0:T(1024)S(1)}, f32[2048]{0:T(1024)S(1)}, u32[]{:S(2)}, u32[]{:S(2)}) %collective-permute-start.11) | collective-permute-done | bytes 8224 | tf_op jit(solution)/shard_map/ppermute | solution.py:63
  138.4 1.8 %collective-permute-start.12 = (f32[2048]{0:T(1024)S(1)}, f32[2048]{0:T(1024)S(1)}, u32[]{:S(2)}, u32[]{:S(2)}) collective-permute-start(f32[2048]{0:T(1024)S(1)} %add.92), channel_id=1, source_target_pairs={{0,4},{1,5},{2,6},{3,7},{4,0},{5,1},{6,2},{7,3},{8,12},{9,13},{10,... | collective-permute-start | bytes 24584 | tf_op jit(solution)/shard_map/ppermute | solution.py:63
  140.2 1.9 %collective-permute-done.12 = f32[2048]{0:T(1024)S(1)} collective-permute-done((f32[2048]{0:T(1024)S(1)}, f32[2048]{0:T(1024)S(1)}, u32[]{:S(2)}, u32[]{:S(2)}) %collective-permute-start.12) | collective-permute-done | bytes 8224 | tf_op jit(solution)/shard_map/ppermute | solution.py:63
  142.1 3.2 %collective-permute-start.13 = (f32[2048]{0:T(1024)S(1)}, f32[2048]{0:T(1024)S(1)}, u32[]{:S(2)}, u32[]{:S(2)}) collective-permute-start(f32[2048]{0:T(1024)S(1)} %add.93), channel_id=1, source_target_pairs={{0,8},{1,9},{2,10},{3,11},{4,12},{5,13},{6,14},{7,15},{8,0},{9,1},... | collective-permute-start | bytes 24584 | tf_op jit(solution)/shard_map/ppermute | solution.py:63
  145.3 1.9 %fusion.54 = bf16[1,4,1,32,2048]{4,3,2,1,0:T(8,128)(2,1)} fusion(f32[4,32,2048]{2,1,0:T(8,128)S(1)} %copy-done.6, bf16[4,32,2048]{2,1,0:T(8,128)(2,1)S(1)} %collective-permute-done.9, bf16[4,32,1024]{2,1,0:T(8,128)(2,1)S(1)} %bitcast.288, bf16[4,32,1024]{2,1,0:T(8,128)(2,1)S(1)} %bitcast.286, bf16[4,1,32,2048]{3,2,1,0:T(8,128)(2,1)S(1)} %copy-done.7, ...), kind=kLoop, calls=%fused_computation.107 | loop fusion | flops 8912896 | bytes 4729346
  (95 shorter events, 9.6 us)
Async XLA Ops:
  0.6 71.8 %copy-start = (bf16[16,2048]{1,0:T(8,128)(2,1)S(1)}, bf16[16,2048]{1,0:T(8,128)(2,1)}, u32[]{:S(2)}) copy-start(bf16[16,2048]{1,0:T(8,128)(2,1)} %param.27) | copy-start | bytes 196612
  0.6 22.7 %collective-permute-start.4 = (bf16[1,128,1024]{2,1,0:T(8,128)(2,1)}, bf16[1,128,1024]{2,1,0:T(8,128)(2,1)S(1)}, u32[]{:S(2)}, u32[]{:S(2)}) collective-permute-start(bf16[1,128,1024]{2,1,0:T(8,128)(2,1)} %param.28), channel_id=1, source_target_pairs={{0,8},{1,9},{2,10},{3,11},{4,12},{5,13},{6,14},{7,15},{8,0},{9,1},... | collective-permute-start | bytes 786440 | tf_op jit(solution)/shard_map/ppermute | solution.py:36
  4.7 23.5 %collective-permute-start = (bf16[1,64,2048]{2,1,0:T(8,128)(2,1)}, bf16[1,64,2048]{2,1,0:T(8,128)(2,1)S(1)}, u32[]{:S(2)}, u32[]{:S(2)}) collective-permute-start(bf16[1,64,2048]{2,1,0:T(8,128)(2,1)} %param.29), channel_id=1, source_target_pairs={{0,8},{1,9},{2,10},{3,11},{4,12},{5,13},{6,14},{7,15},{8,0},{9,1},... | collective-permute-start | bytes 786440 | tf_op jit(solution)/shard_map/ppermute | solution.py:36
  24.3 15.0 %collective-permute-start.5 = (bf16[2,128,1024]{2,1,0:T(8,128)(2,1)S(1)}, bf16[2,128,1024]{2,1,0:T(8,128)(2,1)S(1)}, u32[]{:S(2)}, u32[]{:S(2)}) collective-permute-start(bf16[2,128,1024]{2,1,0:T(8,128)(2,1)S(1)} %get-tuple-element.174), channel_id=1, source_target_pairs={{0,4},{1,5},{2,6},{3,7},{4,0},{5,1},{6,2},{7,3},{8,12},{9,13},{10,... | collective-permute-start | bytes 1572872 | tf_op jit(solution)/shard_map/ppermute | solution.py:36
  29.2 13.2 %collective-permute-start.1 = (bf16[2,64,2048]{2,1,0:T(8,128)(2,1)S(1)}, bf16[2,64,2048]{2,1,0:T(8,128)(2,1)}, u32[]{:S(2)}, u32[]{:S(2)}) collective-permute-start(bf16[2,64,2048]{2,1,0:T(8,128)(2,1)S(1)} %get-tuple-element.170), channel_id=1, source_target_pairs={{0,2},{1,3},{2,0},{3,1},{4,6},{5,7},{6,4},{7,5},{8,10},{9,11},{10,... | collective-permute-start | bytes 1572872 | tf_op jit(solution)/shard_map/ppermute | solution.py:36
  39.5 25.3 %collective-permute-start.6 = (bf16[4,128,1024]{2,1,0:T(8,128)(2,1)S(1)}, bf16[4,128,1024]{2,1,0:T(8,128)(2,1)S(1)}, u32[]{:S(2)}, u32[]{:S(2)}) collective-permute-start(bf16[4,128,1024]{2,1,0:T(8,128)(2,1)S(1)} %get-tuple-element.175), channel_id=1, source_target_pairs={{0,2},{1,3},{2,0},{3,1},{4,6},{5,7},{6,4},{7,5},{8,10},{9,11},{10,... | collective-permute-start | bytes 3145736 | tf_op jit(solution)/shard_map/ppermute | solution.py:36
  44.7 24.3 %collective-permute-start.2 = (bf16[4,64,2048]{2,1,0:T(8,128)(2,1)}, bf16[4,64,2048]{2,1,0:T(8,128)(2,1)}, u32[]{:S(2)}, u32[]{:S(2)}) collective-permute-start(bf16[4,64,2048]{2,1,0:T(8,128)(2,1)} %get-tuple-element.171), channel_id=1, source_target_pairs={{0,4},{1,5},{2,6},{3,7},{4,0},{5,1},{6,2},{7,3},{8,12},{9,13},{10,... | collective-permute-start | bytes 3145736 | tf_op jit(solution)/shard_map/ppermute | solution.py:36
  64.8 1.0 copy-start.5
  65.2 9.7 %collective-permute-start.7 = (bf16[8,128,1024]{2,1,0:T(8,128)(2,1)S(1)}, bf16[8,128,1024]{2,1,0:T(8,128)(2,1)}, u32[]{:S(2)}, u32[]{:S(2)}) collective-permute-start(bf16[8,128,1024]{2,1,0:T(8,128)(2,1)S(1)} %get-tuple-element.176), channel_id=1, source_target_pairs={{0,1},{1,0},{2,3},{3,2},{4,5},{5,4},{6,7},{7,6},{8,9},{9,8},{10,11... | collective-permute-start | bytes 6291464 | tf_op jit(solution)/shard_map/ppermute | solution.py:36
  69.0 3.2 %copy-start.16 = (s32[4,1,32]{2,1,0:T(1,128)S(1)}, s32[4,1,32]{2,1,0:T(1,128)}, u32[]{:S(2)}) copy-start(s32[4,1,32]{2,1,0:T(1,128)} %param.25) | copy-start | bytes 1540
  69.0 3.2 %copy-start.15 = (s32[4,1,16,2]{2,3,1,0:T(2,128)S(1)}, s32[4,1,16,2]{2,3,1,0:T(2,128)}, u32[]{:S(2)}) copy-start(s32[4,1,16,2]{2,3,1,0:T(2,128)} %param.26) | copy-start | bytes 1540
  69.0 4.7 %copy-start.10 = (f32[1,2048]{1,0:T(1,128)S(1)}, f32[1,2048]{1,0:T(1,128)}, u32[]{:S(2)}) copy-start(f32[1,2048]{1,0:T(1,128)} %param.30) | copy-start | bytes 24580
  72.2 10.9 %collective-permute-start.3 = (bf16[8,64,2048]{2,1,0:T(8,128)(2,1)}, bf16[8,64,2048]{2,1,0:T(8,128)(2,1)}, u32[]{:S(2)}, u32[]{:S(2)}) collective-permute-start(bf16[8,64,2048]{2,1,0:T(8,128)(2,1)} %get-tuple-element.172), channel_id=1, source_target_pairs={{0,1},{1,0},{2,3},{3,2},{4,5},{5,4},{6,7},{7,6},{8,9},{9,8},{10,11... | collective-permute-start | bytes 6291464 | tf_op jit(solution)/shard_map/ppermute | solution.py:36
  79.3 3.8 %copy-start.4 = (bf16[8,64,2048]{2,1,0:T(8,128)(2,1)S(1)}, bf16[8,64,2048]{2,1,0:T(8,128)(2,1)}, u32[]{:S(2)}) copy-start(bf16[8,64,2048]{2,1,0:T(8,128)(2,1)} %get-tuple-element.172) | copy-start | bytes 6291460
  87.0 2.6 %copy-start.11 = (bf16[16,8,8,128]{3,2,1,0:T(8,128)(2,1)S(1)}, bf16[16,8,8,128]{3,2,1,0:T(8,128)(2,1)}, u32[]{:S(2)}) copy-start(bf16[16,8,8,128]{3,2,1,0:T(8,128)(2,1)} %copy.99) | copy-start | bytes 786436
  87.0 2.6 %copy-start.13 = (bf16[4,4,8,8,128]{4,3,2,1,0:T(8,128)(2,1)S(1)}, bf16[4,4,8,8,128]{4,3,2,1,0:T(8,128)(2,1)}, u32[]{:S(2)}) copy-start(bf16[4,4,8,8,128]{4,3,2,1,0:T(8,128)(2,1)} %get-tuple-element.150) | copy-start | bytes 786436
  89.6 6.8 %copy-start.2 = (bf16[2,2,2,2,64,2048]{5,4,3,2,1,0:T(8,128)(2,1)}, bf16[2,2,2,2,64,2048]{5,4,3,2,1,0:T(8,128)(2,1)S(1)}, u32[]{:S(2)}) copy-start(bf16[2,2,2,2,64,2048]{5,4,3,2,1,0:T(8,128)(2,1)S(1)} %copy.56) | copy-start | bytes 12582916
  89.6 6.8 %copy-start.7 = (bf16[4,1,32,2048]{3,2,1,0:T(8,128)(2,1)S(1)}, bf16[4,1,32,2048]{3,2,1,0:T(8,128)(2,1)}, u32[]{:S(2)}) copy-start(bf16[4,1,32,2048]{3,2,1,0:T(8,128)(2,1)} %param.31) | copy-start | bytes 1572868
  89.9 0.9 copy-start.8
  92.7 15.5 %collective-permute-start.8 = (bf16[4,32,2048]{2,1,0:T(8,128)(2,1)}, bf16[4,32,2048]{2,1,0:T(8,128)(2,1)S(1)}, u32[]{:S(2)}, u32[]{:S(2)}) collective-permute-start(bf16[4,32,2048]{2,1,0:T(8,128)(2,1)} %fusion), channel_id=1, source_target_pairs={{0,16},{1,17},{2,18},{3,19},{4,20},{5,21},{6,22},{7,23},{8,24},{9,... | collective-permute-start | bytes 1572872 | tf_op jit(solution)/shard_map/ppermute | solution.py:15
  96.4 12.1 %copy-start.6 = (f32[4,32,2048]{2,1,0:T(8,128)S(1)}, f32[4,32,2048]{2,1,0:T(8,128)}, u32[]{:S(2)}) copy-start(f32[4,32,2048]{2,1,0:T(8,128)} %get-tuple-element.161) | copy-start | bytes 3145732
  97.8 11.0 %copy-start.1 = (bf16[2048,1024]{1,0:T(8,128)(2,1)S(1)}, bf16[2048,1024]{1,0:T(8,128)(2,1)}, u32[]{:S(2)}) copy-start(bf16[2048,1024]{1,0:T(8,128)(2,1)} %get-tuple-element.177) | copy-start | bytes 12582916
  111.8 15.8 %copy-start.3 = (bf16[2,2,2,2,64,2048]{5,4,3,2,1,0:T(8,128)(2,1)S(1)}, bf16[2,2,2,2,64,2048]{5,4,3,2,1,0:T(8,128)(2,1)}, u32[]{:S(2)}) copy-start(bf16[2,2,2,2,64,2048]{5,4,3,2,1,0:T(8,128)(2,1)} %copy-done.2) | copy-start | bytes 12582916
  111.8 15.8 %collective-permute-start.9 = (bf16[4,32,2048]{2,1,0:T(8,128)(2,1)S(1)}, bf16[4,32,2048]{2,1,0:T(8,128)(2,1)S(1)}, u32[]{:S(2)}, u32[]{:S(2)}) collective-permute-start(bf16[4,32,2048]{2,1,0:T(8,128)(2,1)S(1)} %fusion.44), channel_id=1, source_target_pairs={{16,0},{17,1},{18,2},{19,3},{20,4},{21,5},{22,6},{23,7},{24,8},{25... | collective-permute-start | bytes 1572872 | tf_op jit(solution)/shard_map/ppermute | solution.py:15
  113.8 15.4 %copy-start.9 = (f32[4,8,32,32]{2,3,1,0:T(8,128)S(1)}, f32[4,8,32,32]{2,3,1,0:T(8,128)}, u32[]{:S(2)}) copy-start(f32[4,8,32,32]{2,3,1,0:T(8,128)} %copy-done.8) | copy-start | bytes 393220
  127.6 2.2 %copy-start.14 = (bf16[4,4,8,8,128]{4,3,2,1,0:T(8,128)(2,1)S(1)}, bf16[4,4,8,8,128]{4,3,2,1,0:T(8,128)(2,1)}, u32[]{:S(2)}) copy-start(bf16[4,4,8,8,128]{4,3,2,1,0:T(8,128)(2,1)} %get-tuple-element.150) | copy-start | bytes 786436
  129.1 1.0 copy-start.12
  133.5 1.2 collective-permute-start.10
  134.8 3.7 %collective-permute-start.11 = (f32[2048]{0:T(1024)S(1)}, f32[2048]{0:T(1024)S(1)}, u32[]{:S(2)}, u32[]{:S(2)}) collective-permute-start(f32[2048]{0:T(1024)S(1)} %add.91), channel_id=1, source_target_pairs={{0,2},{1,3},{2,0},{3,1},{4,6},{5,7},{6,4},{7,5},{8,10},{9,11},{10,... | collective-permute-start | bytes 24584 | tf_op jit(solution)/shard_map/ppermute | solution.py:63
  138.4 3.7 %collective-permute-start.12 = (f32[2048]{0:T(1024)S(1)}, f32[2048]{0:T(1024)S(1)}, u32[]{:S(2)}, u32[]{:S(2)}) collective-permute-start(f32[2048]{0:T(1024)S(1)} %add.92), channel_id=1, source_target_pairs={{0,4},{1,5},{2,6},{3,7},{4,0},{5,1},{6,2},{7,3},{8,12},{9,13},{10,... | collective-permute-start | bytes 24584 | tf_op jit(solution)/shard_map/ppermute | solution.py:63
  142.1 5.1 %collective-permute-start.13 = (f32[2048]{0:T(1024)S(1)}, f32[2048]{0:T(1024)S(1)}, u32[]{:S(2)}, u32[]{:S(2)}) collective-permute-start(f32[2048]{0:T(1024)S(1)} %add.93), channel_id=1, source_target_pairs={{0,8},{1,9},{2,10},{3,11},{4,12},{5,13},{6,14},{7,15},{8,0},{9,1},... | collective-permute-start | bytes 24584 | tf_op jit(solution)/shard_map/ppermute | solution.py:63

commit v11 on v3

--- a/solution.py
+++ b/solution.py
@@ -30,6 +30,7 @@
 def butterfly_gathers(shards, orders, axis, size):
     index = lax.axis_index(axis)
     held = [shard for shard in shards]
+    done = [[] for _ in shards]
     for level in range(len(orders[0])):
         for which, order in enumerate(orders):
             step = order[level]
@@ -37,19 +38,13 @@
             upper = ((index // step) % 2) == 1
             low = jnp.where(upper, other, held[which])
             high = jnp.where(upper, held[which], other)
-            held[which] = jnp.stack([low, high], axis=1).reshape(
-                (-1,) + held[which].shape[1:]
-            )
-    results = []
-    for which, order in enumerate(orders):
-        block_rows, width = held[which].shape[1:]
-        wanted = sorted(order, reverse=True)
-        if order != wanted:
-            split = held[which].reshape(tuple(2 for _ in order) + (block_rows, width))
-            axes = tuple(order.index(value) for value in wanted) + (len(order), len(order) + 1)
-            held[which] = jnp.transpose(split, axes)
-        results.append(held[which].reshape(size * block_rows, width))
-    return results
+            grid = (2,) * len(done[which]) + held[which].shape[1:]
+            place = sum(1 for value in done[which] if value > step)
+            held[which] = jnp.stack(
+                [low.reshape(grid), high.reshape(grid)], axis=place
+            ).reshape((-1,) + held[which].shape[1:])
+            done[which].append(step)
+    return [array.reshape(-1, array.shape[-1]) for array in held]
 
 
 def butterfly_sum(value, axis, size):

time: 137 us -> 136 us (level)
  local copies, waits for them, and re-layouts: 5.99 us -> 3.16 us
    select_n x1 -> x6, other arithmetic: 0.41 us -> 7.93 us  [butterfly_gathers(): low = jnp.where(upper, other, held[which])]
    another operation x14 -> x12, other arithmetic: 10.1 us -> 4.37 us  [the longest x10 3.89 us: butterfly_gathers(): jnp.stack([low.reshape(grid), high.reshape(grid)], axis=place)]
    another operation x3 -> x0, local copies, waits for them, and re-layouts: 2.23 us -> none  [butterfly_gathers(): jnp.stack([low, high], axis=1).reshape((-1,) + held[which].shape[1:])]
where the time goes in v11:
time: 136 us; the launch traced here: 135 us
  waiting for transfers between devices  79.8 us (59%)
  starting transfers between devices  20.2 us (15%)
  other arithmetic  17.6 us (13%)
  matrix products  13.4 us (10%)
  local copies, waits for them, and re-layouts  3.16 us (2%)
    ppermute x8, waiting for transfers between devices, butterfly_gathers(): lax.ppermute(held[which], axis, [(j, j ^ step) for j in range(size)])  52.7 us
    ppermute x2, waiting for transfers between devices, send_to(): return lax.ppermute(arrays, axis, [(source, target)])  20.2 us
    ppermute x8, starting transfers between devices, butterfly_gathers(): lax.ppermute(held[which], axis, [(j, j ^ step) for j in range(size)])  10.7 us
    select_n x6, other arithmetic, butterfly_gathers(): low = jnp.where(upper, other, held[which])  7.93 us
    ppermute x4, waiting for transfers between devices, butterfly_sum(): lax.ppermute(value, axis, [(j, j ^ step) for j in range(size)])  6.83 us
    ppermute x2, starting transfers between devices, send_to(): return lax.ppermute(arrays, axis, [(source, target)])  5.11 us
    dot_general x3, matrix products, attend_layer(): update = jnp.dot(mixed, output_weight, preferred_element_type=jnp.float32)  5.11 us
    dot_general x4, matrix products, attend_layer(): jnp.dot(normed_rows, query_weight, preferred_element_type=jnp.float32)  4.51 us
  transfers between devices with their start and end apart: 14, of which 12 were waited for; matrix products, arithmetic and copies ran while one was open for 15% of the time, Pallas kernels for 0%

profile of v11, /device:TPU:0, one launch (start us, length us, event | category | flops | bytes accessed | tf_op | source)
XLA Modules:
  0.0 135.3 jit_solution(16542085131779760431)
XLA Ops:
  0.7 4.1 %collective-permute-start.4 = (bf16[1,128,1024]{2,1,0:T(8,128)(2,1)}, bf16[1,128,1024]{2,1,0:T(8,128)(2,1)S(1)}, u32[]{:S(2)}, u32[]{:S(2)}) collective-permute-start(bf16[1,128,1024]{2,1,0:T(8,128)(2,1)} %param.12), channel_id=1, source_target_pairs={{0,8},{1,9},{2,10},{3,11},{4,12},{5,13},{6,14},{7,15},{8,0},{9,1},... | collective-permute-start | bytes 786440 | tf_op jit(solution)/shard_map/ppermute | solution.py:37
  4.8 18.5 %collective-permute-done.4 = bf16[1,128,1024]{2,1,0:T(8,128)(2,1)S(1)} collective-permute-done((bf16[1,128,1024]{2,1,0:T(8,128)(2,1)}, bf16[1,128,1024]{2,1,0:T(8,128)(2,1)S(1)}, u32[]{:S(2)}, u32[]{:S(2)}) %collective-permute-start.4) | collective-permute-done | bytes 262176 | tf_op jit(solution)/shard_map/ppermute | solution.py:37
  23.3 1.0 broadcast_select_fusion.9
  24.5 3.7 %collective-permute-done = bf16[1,64,2048]{2,1,0:T(8,128)(2,1)S(1)} collective-permute-done((bf16[1,64,2048]{2,1,0:T(8,128)(2,1)}, bf16[1,64,2048]{2,1,0:T(8,128)(2,1)S(1)}, u32[]{:S(2)}, u32[]{:S(2)}) %collective-permute-start) | collective-permute-done | bytes 262176 | tf_op jit(solution)/shard_map/ppermute | solution.py:37
  28.2 1.0 broadcast_select_fusion.11
  29.3 1.6 %collective-permute-start.1 = (bf16[2,64,2048]{2,1,0:T(8,128)(2,1)S(1)}, bf16[2,64,2048]{2,1,0:T(8,128)(2,1)S(1)}, u32[]{:S(2)}, u32[]{:S(2)}) collective-permute-start(bf16[2,64,2048]{2,1,0:T(8,128)(2,1)S(1)} %pad_maximum_fusion.7), channel_id=1, source_target_pairs={{0,2},{1,3},{2,0},{3,1},{4,6},{5,7},{6,4},{7,5},{8,10},{9,11},{10,... | collective-permute-start | bytes 1572872 | tf_op jit(solution)/shard_map/ppermute | solution.py:37
  31.1 8.3 %collective-permute-done.5 = bf16[2,128,1024]{2,1,0:T(8,128)(2,1)S(1)} collective-permute-done((bf16[2,128,1024]{2,1,0:T(8,128)(2,1)S(1)}, bf16[2,128,1024]{2,1,0:T(8,128)(2,1)S(1)}, u32[]{:S(2)}, u32[]{:S(2)}) %collective-permute-start.5) | collective-permute-done | bytes 524320 | tf_op jit(solution)/shard_map/ppermute | solution.py:37
  39.4 1.1 pad_maximum_fusion.4
  40.5 1.6 %collective-permute-start.6 = (bf16[4,128,1024]{2,1,0:T(8,128)(2,1)}, bf16[4,128,1024]{2,1,0:T(8,128)(2,1)}, u32[]{:S(2)}, u32[]{:S(2)}) collective-permute-start(bf16[4,128,1024]{2,1,0:T(8,128)(2,1)} %bitcast.24), channel_id=1, source_target_pairs={{0,2},{1,3},{2,0},{3,1},{4,6},{5,7},{6,4},{7,5},{8,10},{9,11},{10,... | collective-permute-start | bytes 3145736 | tf_op jit(solution)/shard_map/ppermute | solution.py:37
  42.6 2.6 %collective-permute-start.2 = (bf16[4,64,2048]{2,1,0:T(8,128)(2,1)S(1)}, bf16[4,64,2048]{2,1,0:T(8,128)(2,1)}, u32[]{:S(2)}, u32[]{:S(2)}) collective-permute-start(bf16[4,64,2048]{2,1,0:T(8,128)(2,1)S(1)} %bitcast.269), channel_id=1, source_target_pairs={{0,4},{1,5},{2,6},{3,7},{4,0},{5,1},{6,2},{7,3},{8,12},{9,13},{10,... | collective-permute-start | bytes 3145736 | tf_op jit(solution)/shard_map/ppermute | solution.py:37
  45.3 0.4 multiply_reduce_fusion
  45.8 20.1 %collective-permute-done.6 = bf16[4,128,1024]{2,1,0:T(8,128)(2,1)} collective-permute-done((bf16[4,128,1024]{2,1,0:T(8,128)(2,1)}, bf16[4,128,1024]{2,1,0:T(8,128)(2,1)}, u32[]{:S(2)}, u32[]{:S(2)}) %collective-permute-start.6) | collective-permute-done | bytes 1048608 | tf_op jit(solution)/shard_map/ppermute | solution.py:37
  65.9 1.7 %broadcast_select_fusion.5 = (bf16[4,128,1024]{2,1,0:T(8,128)(2,1)S(1)}, bf16[4,128,1024]{2,1,0:T(8,128)(2,1)S(1)}) fusion(bf16[4,128,1024]{2,1,0:T(8,128)(2,1)} %collective-permute-done.6, pred[]{:T(512)S(6)} %eq.52, bf16[2,2,128,1024]{3,2,1,0:T(8,128)(2,1)} %pad_maximum_fusion.4), kind=kLoop, calls=%fused_computation.98 | loop fusion | flops 1048576 | bytes 4194305 | tf_op jit(solution)/shard_map/jit(_where)/select_n | solution.py:39
  67.6 1.5 %pad_maximum_fusion.2 = bf16[2,2,2,128,1024]{4,3,2,1,0:T(8,128)(2,1)} fusion(bf16[2,2,1,128,1024]{4,3,2,1,0:T(8,128)(2,1)S(1)} %bitcast.271, bf16[2,2,1,128,1024]{4,3,2,1,0:T(8,128)(2,1)S(1)} %bitcast.270), kind=kLoop, calls=%fused_computation.8 | loop fusion | flops 1048576 | bytes 4194304 | tf_op jit(solution)/shard_map/stack | solution.py:43
  69.1 1.4 %broadcast_select_fusion.7 = (bf16[4,64,2048]{2,1,0:T(8,128)(2,1)S(1)}, bf16[4,64,2048]{2,1,0:T(8,128)(2,1)S(1)}) fusion(bf16[4,64,2048]{2,1,0:T(8,128)(2,1)} %collective-permute-done.2, pred[]{:T(512)S(6)} %eq.51, bf16[2,2,64,2048]{3,2,1,0:T(8,128)(2,1)S(1)} %pad_maximum_fusion.5), kind=kLoop, calls=%fused_computation.100 | loop fusion | flops 1048576 | bytes 4194305 | tf_op jit(solution)/shard_map/jit(_where)/select_n | solution.py:39
  70.7 0.6 collective-permute-start.3
  71.7 1.9 %collective-permute-done.7 = bf16[8,128,1024]{2,1,0:T(8,128)(2,1)} collective-permute-done((bf16[8,128,1024]{2,1,0:T(8,128)(2,1)}, bf16[8,128,1024]{2,1,0:T(8,128)(2,1)}, u32[]{:S(2)}, u32[]{:S(2)}) %collective-permute-start.7) | collective-permute-done | bytes 2097184 | tf_op jit(solution)/shard_map/ppermute | solution.py:37
  73.6 2.5 %broadcast_select_fusion.1 = (bf16[8,128,1024]{2,1,0:T(8,128)(2,1)S(1)}, bf16[8,128,1024]{2,1,0:T(8,128)(2,1)S(1)}) fusion(bf16[8,128,1024]{2,1,0:T(8,128)(2,1)} %collective-permute-done.7, pred[]{:T(512)S(6)} %eq.50, bf16[2,2,2,128,1024]{4,3,2,1,0:T(8,128)(2,1)} %pad_maximum_fusion.2), kind=kLoop, calls=%fused_computation.11 | loop fusion | flops 2097152 | bytes 8388609 | tf_op jit(solution)/shard_map/jit(_where)/select_n | solution.py:39
  76.1 0.4 pad_maximum_fusion
  76.5 0.7 fusion.21
  77.3 0.4 broadcast_select_fusion.3
  77.7 0.7 copy-done.1
  78.4 0.4 pad_maximum_fusion.1
  79.5 0.5 copy-done.7
  80.0 1.6 %fusion = bf16[4,32,2048]{2,1,0:T(8,128)(2,1)} fusion(bf16[1024,2048,1]{1,0,2:T(8,128)(2,1)S(1)} %bitcast.259, bf16[4,1,32,2048]{3,2,1,0:T(8,128)(2,1)S(1)} %copy-done.5, bf16[4,8,4,8,128]{4,3,2,1,0:T(8,128)(2,1)S(1)} %fusion.23), kind=kOutput, calls=%fused_computation.3 | convolution fusion | flops 537657344 | bytes 5505024 | tf_op jit(solution)/shard_map/dot_general | solution.py:88
  81.6 3.4 %collective-permute-start.8 = (bf16[4,32,2048]{2,1,0:T(8,128)(2,1)}, bf16[4,32,2048]{2,1,0:T(8,128)(2,1)S(1)}, u32[]{:S(2)}, u32[]{:S(2)}) collective-permute-start(bf16[4,32,2048]{2,1,0:T(8,128)(2,1)} %fusion), channel_id=1, source_target_pairs={{0,16},{1,17},{2,18},{3,19},{4,20},{5,21},{6,22},{7,23},{8,24},{9,... | collective-permute-start | bytes 1572872 | tf_op jit(solution)/shard_map/ppermute | solution.py:15
  85.0 2.0 %fusion.19 = bf16[128,1024]{0,1:T(8,128)(2,1)} fusion(bf16[1024,2048]{1,0:T(8,128)(2,1)S(1)} %bitcast.260, bf16[128,2048]{1,0:T(8,128)(2,1)S(1)} %bitcast.287), kind=kOutput, calls=%fused_computation.60 | convolution fusion | flops 537001984 | bytes 4980736 | tf_op jit(solution)/shard_map/transpose(jvp())/dot_general | solution.py:88
  87.0 1.1 copy.72
  88.2 8.5 %collective-permute-done.8 = bf16[4,32,2048]{2,1,0:T(8,128)(2,1)S(1)} collective-permute-done((bf16[4,32,2048]{2,1,0:T(8,128)(2,1)}, bf16[4,32,2048]{2,1,0:T(8,128)(2,1)S(1)}, u32[]{:S(2)}, u32[]{:S(2)}) %collective-permute-start.8) | collective-permute-done | bytes 524320 | tf_op jit(solution)/shard_map/ppermute | solution.py:15
  97.3 0.8 fusion.20
  99.3 0.6 fusion.31
  100.2 1.7 %collective-permute-start.9 = (bf16[4,32,2048]{2,1,0:T(8,128)(2,1)S(1)}, bf16[4,32,2048]{2,1,0:T(8,128)(2,1)S(1)}, u32[]{:S(2)}, u32[]{:S(2)}) collective-permute-start(bf16[4,32,2048]{2,1,0:T(8,128)(2,1)S(1)} %fusion.44), channel_id=1, source_target_pairs={{16,0},{17,1},{18,2},{19,3},{20,4},{21,5},{22,6},{23,7},{24,8},{25... | collective-permute-start | bytes 1572872 | tf_op jit(solution)/shard_map/ppermute | solution.py:15
  102.0 0.4 fusion.27
  102.4 1.5 %convolution_convert_fusion = bf16[128,2048]{1,0:T(8,128)(2,1)S(1)} fusion(bf16[2048,1024]{1,0:T(8,128)(2,1)S(1)} %bitcast.257, bf16[16,8,8,128]{3,2,1,0:T(8,128)(2,1)S(1)} %bitcast.284), kind=kOutput, calls=%fused_computation.4 | convolution fusion | flops 537133056 | bytes 4980736 | tf_op jit(solution)/shard_map/transpose(jvp())/dot_general | solution.py:77
  103.9 11.7 %collective-permute-done.9 = bf16[4,32,2048]{2,1,0:T(8,128)(2,1)S(1)} collective-permute-done((bf16[4,32,2048]{2,1,0:T(8,128)(2,1)S(1)}, bf16[4,32,2048]{2,1,0:T(8,128)(2,1)S(1)}, u32[]{:S(2)}, u32[]{:S(2)}) %collective-permute-start.9) | collective-permute-done | bytes 524320 | tf_op jit(solution)/shard_map/ppermute | solution.py:15
  115.6 1.5 %fusion.22 = bf16[16,8,8,128]{3,1,2,0:T(8,128)(2,1)S(1)} fusion(bf16[128,2048]{1,0:T(8,128)(2,1)S(1)} %bitcast.278, bf16[1024,2048]{1,0:T(8,128)(2,1)S(1)} %bitcast.261), kind=kOutput, calls=%fused_computation.63 | convolution fusion | flops 537001984 | bytes 4980736 | tf_op jit(solution)/shard_map/transpose(jvp())/dot_general | solution.py:88
  117.8 0.4 fusion.26
  118.6 1.5 %convolution_convert_fusion.1 = bf16[128,2048]{1,0:T(8,128)(2,1)S(1)} fusion(bf16[2048,1024]{1,0:T(8,128)(2,1)S(1)} %bitcast.258, bf16[16,8,8,128]{3,2,1,0:T(8,128)(2,1)S(1)} %bitcast.283), kind=kOutput, calls=%fused_computation.5 | convolution fusion | flops 537133056 | bytes 4980736 | tf_op jit(solution)/shard_map/transpose(jvp())/dot_general | solution.py:77
  120.2 1.3 fusion.36
  121.7 1.2 collective-permute-done.10
  122.8 1.5 %collective-permute-start.11 = (f32[2048]{0:T(1024)S(1)}, f32[2048]{0:T(1024)S(1)}, u32[]{:S(2)}, u32[]{:S(2)}) collective-permute-start(f32[2048]{0:T(1024)S(1)} %add.91), channel_id=1, source_target_pairs={{0,2},{1,3},{2,0},{3,1},{4,6},{5,7},{6,4},{7,5},{8,10},{9,11},{10,... | collective-permute-start | bytes 24584 | tf_op jit(solution)/shard_map/ppermute | solution.py:55
  124.3 2.1 %collective-permute-done.11 = f32[2048]{0:T(1024)S(1)} collective-permute-done((f32[2048]{0:T(1024)S(1)}, f32[2048]{0:T(1024)S(1)}, u32[]{:S(2)}, u32[]{:S(2)}) %collective-permute-start.11) | collective-permute-done | bytes 8224 | tf_op jit(solution)/shard_map/ppermute | solution.py:55
  126.5 0.7 collective-permute-start.12
  127.1 3.0 %collective-permute-done.12 = f32[2048]{0:T(1024)S(1)} collective-permute-done((f32[2048]{0:T(1024)S(1)}, f32[2048]{0:T(1024)S(1)}, u32[]{:S(2)}, u32[]{:S(2)}) %collective-permute-start.12) | collective-permute-done | bytes 8224 | tf_op jit(solution)/shard_map/ppermute | solution.py:55
  130.1 2.1 %collective-permute-start.13 = (f32[2048]{0:T(1024)S(1)}, f32[2048]{0:T(1024)S(1)}, u32[]{:S(2)}, u32[]{:S(2)}) collective-permute-start(f32[2048]{0:T(1024)S(1)} %add.93), channel_id=1, source_target_pairs={{0,8},{1,9},{2,10},{3,11},{4,12},{5,13},{6,14},{7,15},{8,0},{9,1},... | collective-permute-start | bytes 24584 | tf_op jit(solution)/shard_map/ppermute | solution.py:55
  132.2 1.9 %fusion.54 = bf16[1,4,1,32,2048]{4,3,2,1,0:T(8,128)(2,1)} fusion(f32[4,32,2048]{2,1,0:T(8,128)S(1)} %get-tuple-element.45, bf16[4,32,2048]{2,1,0:T(8,128)(2,1)S(1)} %collective-permute-done.9, bf16[4,32,1024]{2,1,0:T(8,128)(2,1)S(1)} %bitcast.277, bf16[4,32,1024]{2,1,0:T(8,128)(2,1)S(1)} %bitcast.275, bf16[4,1,32,2048]{3,2,1,0:T(8,128)(2,1)S(1)} %copy-done.6, ...), kind=kLoop, calls=%fused_computation.105 | loop fusion | flops 8912896 | bytes 4729346
  134.1 0.6 collective-permute-done.13
  134.7 0.6 add.94
  (83 shorter events, 6.1 us)
Async XLA Ops:
  0.6 44.7 %copy-start = (bf16[16,2048]{1,0:T(8,128)(2,1)S(1)}, bf16[16,2048]{1,0:T(8,128)(2,1)}, u32[]{:S(2)}) copy-start(bf16[16,2048]{1,0:T(8,128)(2,1)} %param.11) | copy-start | bytes 196612
  0.6 30.3 %copy-start.5 = (bf16[4,1,32,2048]{3,2,1,0:T(8,128)(2,1)S(1)}, bf16[4,1,32,2048]{3,2,1,0:T(8,128)(2,1)}, u32[]{:S(2)}) copy-start(bf16[4,1,32,2048]{3,2,1,0:T(8,128)(2,1)} %param.8) | copy-start | bytes 1572868
  0.7 22.7 %collective-permute-start.4 = (bf16[1,128,1024]{2,1,0:T(8,128)(2,1)}, bf16[1,128,1024]{2,1,0:T(8,128)(2,1)S(1)}, u32[]{:S(2)}, u32[]{:S(2)}) collective-permute-start(bf16[1,128,1024]{2,1,0:T(8,128)(2,1)} %param.12), channel_id=1, source_target_pairs={{0,8},{1,9},{2,10},{3,11},{4,12},{5,13},{6,14},{7,15},{8,0},{9,1},... | collective-permute-start | bytes 786440 | tf_op jit(solution)/shard_map/ppermute | solution.py:37
  4.8 23.5 %collective-permute-start = (bf16[1,64,2048]{2,1,0:T(8,128)(2,1)}, bf16[1,64,2048]{2,1,0:T(8,128)(2,1)S(1)}, u32[]{:S(2)}, u32[]{:S(2)}) collective-permute-start(bf16[1,64,2048]{2,1,0:T(8,128)(2,1)} %param.13), channel_id=1, source_target_pairs={{0,8},{1,9},{2,10},{3,11},{4,12},{5,13},{6,14},{7,15},{8,0},{9,1},... | collective-permute-start | bytes 786440 | tf_op jit(solution)/shard_map/ppermute | solution.py:37
  24.4 15.0 %collective-permute-start.5 = (bf16[2,128,1024]{2,1,0:T(8,128)(2,1)S(1)}, bf16[2,128,1024]{2,1,0:T(8,128)(2,1)S(1)}, u32[]{:S(2)}, u32[]{:S(2)}) collective-permute-start(bf16[2,128,1024]{2,1,0:T(8,128)(2,1)S(1)} %pad_maximum_fusion.6), channel_id=1, source_target_pairs={{0,4},{1,5},{2,6},{3,7},{4,0},{5,1},{6,2},{7,3},{8,12},{9,13},{10,... | collective-permute-start | bytes 1572872 | tf_op jit(solution)/shard_map/ppermute | solution.py:37
  29.3 13.1 %collective-permute-start.1 = (bf16[2,64,2048]{2,1,0:T(8,128)(2,1)S(1)}, bf16[2,64,2048]{2,1,0:T(8,128)(2,1)S(1)}, u32[]{:S(2)}, u32[]{:S(2)}) collective-permute-start(bf16[2,64,2048]{2,1,0:T(8,128)(2,1)S(1)} %pad_maximum_fusion.7), channel_id=1, source_target_pairs={{0,2},{1,3},{2,0},{3,1},{4,6},{5,7},{6,4},{7,5},{8,10},{9,11},{10,... | collective-permute-start | bytes 1572872 | tf_op jit(solution)/shard_map/ppermute | solution.py:37
  31.1 14.1 %copy-start.12 = (s32[4,1,16,2]{2,3,1,0:T(2,128)S(1)}, s32[4,1,16,2]{2,3,1,0:T(2,128)}, u32[]{:S(2)}) copy-start(s32[4,1,16,2]{2,3,1,0:T(2,128)} %param.10) | copy-start | bytes 1540
  40.5 25.4 %collective-permute-start.6 = (bf16[4,128,1024]{2,1,0:T(8,128)(2,1)}, bf16[4,128,1024]{2,1,0:T(8,128)(2,1)}, u32[]{:S(2)}, u32[]{:S(2)}) collective-permute-start(bf16[4,128,1024]{2,1,0:T(8,128)(2,1)} %bitcast.24), channel_id=1, source_target_pairs={{0,2},{1,3},{2,0},{3,1},{4,6},{5,7},{6,4},{7,5},{8,10},{9,11},{10,... | collective-permute-start | bytes 3145736 | tf_op jit(solution)/shard_map/ppermute | solution.py:37
  42.6 26.6 %collective-permute-start.2 = (bf16[4,64,2048]{2,1,0:T(8,128)(2,1)S(1)}, bf16[4,64,2048]{2,1,0:T(8,128)(2,1)}, u32[]{:S(2)}, u32[]{:S(2)}) collective-permute-start(bf16[4,64,2048]{2,1,0:T(8,128)(2,1)S(1)} %bitcast.269), channel_id=1, source_target_pairs={{0,4},{1,5},{2,6},{3,7},{4,0},{5,1},{6,2},{7,3},{8,12},{9,13},{10,... | collective-permute-start | bytes 3145736 | tf_op jit(solution)/shard_map/ppermute | solution.py:37
  45.8 23.3 %copy-start.13 = (s32[4,1,32]{2,1,0:T(1,128)S(1)}, s32[4,1,32]{2,1,0:T(1,128)}, u32[]{:S(2)}) copy-start(s32[4,1,32]{2,1,0:T(1,128)} %param.9) | copy-start | bytes 1540
  69.1 4.5 %collective-permute-start.7 = (bf16[8,128,1024]{2,1,0:T(8,128)(2,1)}, bf16[8,128,1024]{2,1,0:T(8,128)(2,1)}, u32[]{:S(2)}, u32[]{:S(2)}) collective-permute-start(bf16[8,128,1024]{2,1,0:T(8,128)(2,1)} %bitcast.29), channel_id=1, source_target_pairs={{0,1},{1,0},{2,3},{3,2},{4,5},{5,4},{6,7},{7,6},{8,9},{9,8},{10,11... | collective-permute-start | bytes 6291464 | tf_op jit(solution)/shard_map/ppermute | solution.py:37
  69.1 2.2 %copy-start.9 = (f32[1,2048]{1,0:T(1,128)S(1)}, f32[1,2048]{1,0:T(1,128)}, u32[]{:S(2)}) copy-start(f32[1,2048]{1,0:T(1,128)} %param.14) | copy-start | bytes 24580
  70.7 6.6 %collective-permute-start.3 = (bf16[8,64,2048]{2,1,0:T(8,128)(2,1)S(1)}, bf16[8,64,2048]{2,1,0:T(8,128)(2,1)S(1)}, u32[]{:S(2)}, u32[]{:S(2)}) collective-permute-start(bf16[8,64,2048]{2,1,0:T(8,128)(2,1)S(1)} %bitcast.262), channel_id=1, source_target_pairs={{0,1},{1,0},{2,3},{3,2},{4,5},{5,4},{6,7},{7,6},{8,9},{9,8},{10,11... | collective-permute-start | bytes 6291464 | tf_op jit(solution)/shard_map/ppermute | solution.py:37
  71.5 7.3 %copy-start.10 = (bf16[4,4,8,8,128]{4,3,2,1,0:T(8,128)(2,1)}, bf16[4,4,8,8,128]{4,3,2,1,0:T(8,128)(2,1)S(1)}, u32[]{:S(2)}) copy-start(bf16[4,4,8,8,128]{4,3,2,1,0:T(8,128)(2,1)S(1)} %get-tuple-element.32) | copy-start | bytes 786436
  76.5 1.9 %copy-start.1 = (bf16[2,2,2,2,128,1024]{5,4,3,2,1,0:T(8,128)(2,1)}, bf16[2,2,2,2,128,1024]{5,4,3,2,1,0:T(8,128)(2,1)S(1)}, u32[]{:S(2)}) copy-start(bf16[2,2,2,2,128,1024]{5,4,3,2,1,0:T(8,128)(2,1)S(1)} %pad_maximum_fusion) | copy-start | bytes 12582916
  78.8 6.2 %copy-start.3 = (bf16[2,2,2,2,64,2048]{5,4,3,2,1,0:T(8,128)(2,1)}, bf16[2,2,2,2,64,2048]{5,4,3,2,1,0:T(8,128)(2,1)S(1)}, u32[]{:S(2)}) copy-start(bf16[2,2,2,2,64,2048]{5,4,3,2,1,0:T(8,128)(2,1)S(1)} %pad_maximum_fusion.1) | copy-start | bytes 12582916
  78.8 6.1 %copy-start.6 = (bf16[4,1,32,2048]{3,2,1,0:T(8,128)(2,1)S(1)}, bf16[4,1,32,2048]{3,2,1,0:T(8,128)(2,1)}, u32[]{:S(2)}) copy-start(bf16[4,1,32,2048]{3,2,1,0:T(8,128)(2,1)} %param.15) | copy-start | bytes 1572868
  79.1 0.8 copy-start.7
  81.6 15.1 %collective-permute-start.8 = (bf16[4,32,2048]{2,1,0:T(8,128)(2,1)}, bf16[4,32,2048]{2,1,0:T(8,128)(2,1)S(1)}, u32[]{:S(2)}, u32[]{:S(2)}) collective-permute-start(bf16[4,32,2048]{2,1,0:T(8,128)(2,1)} %fusion), channel_id=1, source_target_pairs={{0,16},{1,17},{2,18},{3,19},{4,20},{5,21},{6,22},{7,23},{8,24},{9,... | collective-permute-start | bytes 1572872 | tf_op jit(solution)/shard_map/ppermute | solution.py:15
  88.1 9.2 %copy-start.2 = (bf16[2,2,2,2,128,1024]{5,4,3,2,1,0:T(8,128)(2,1)S(1)}, bf16[2,2,2,2,128,1024]{5,4,3,2,1,0:T(8,128)(2,1)}, u32[]{:S(2)}) copy-start(bf16[2,2,2,2,128,1024]{5,4,3,2,1,0:T(8,128)(2,1)} %copy-done.1) | copy-start | bytes 12582916
  100.2 15.4 %copy-start.4 = (bf16[2,2,2,2,64,2048]{5,4,3,2,1,0:T(8,128)(2,1)S(1)}, bf16[2,2,2,2,64,2048]{5,4,3,2,1,0:T(8,128)(2,1)}, u32[]{:S(2)}) copy-start(bf16[2,2,2,2,64,2048]{5,4,3,2,1,0:T(8,128)(2,1)} %copy-done.3) | copy-start | bytes 12582916
  100.2 15.4 %collective-permute-start.9 = (bf16[4,32,2048]{2,1,0:T(8,128)(2,1)S(1)}, bf16[4,32,2048]{2,1,0:T(8,128)(2,1)S(1)}, u32[]{:S(2)}, u32[]{:S(2)}) collective-permute-start(bf16[4,32,2048]{2,1,0:T(8,128)(2,1)S(1)} %fusion.44), channel_id=1, source_target_pairs={{16,0},{17,1},{18,2},{19,3},{20,4},{21,5},{22,6},{23,7},{24,8},{25... | collective-permute-start | bytes 1572872 | tf_op jit(solution)/shard_map/ppermute | solution.py:15
  102.4 14.8 %copy-start.8 = (f32[4,8,32,32]{2,3,1,0:T(8,128)S(1)}, f32[4,8,32,32]{2,3,1,0:T(8,128)}, u32[]{:S(2)}) copy-start(f32[4,8,32,32]{2,3,1,0:T(8,128)} %copy-done.7) | copy-start | bytes 393220
  115.6 2.2 %copy-start.11 = (bf16[4,4,8,8,128]{4,3,2,1,0:T(8,128)(2,1)S(1)}, bf16[4,4,8,8,128]{4,3,2,1,0:T(8,128)(2,1)}, u32[]{:S(2)}) copy-start(bf16[4,4,8,8,128]{4,3,2,1,0:T(8,128)(2,1)} %copy-done.10) | copy-start | bytes 786436
  121.6 1.2 collective-permute-start.10
  122.8 3.7 %collective-permute-start.11 = (f32[2048]{0:T(1024)S(1)}, f32[2048]{0:T(1024)S(1)}, u32[]{:S(2)}, u32[]{:S(2)}) collective-permute-start(f32[2048]{0:T(1024)S(1)} %add.91), channel_id=1, source_target_pairs={{0,2},{1,3},{2,0},{3,1},{4,6},{5,7},{6,4},{7,5},{8,10},{9,11},{10,... | collective-permute-start | bytes 24584 | tf_op jit(solution)/shard_map/ppermute | solution.py:55
  126.5 3.7 %collective-permute-start.12 = (f32[2048]{0:T(1024)S(1)}, f32[2048]{0:T(1024)S(1)}, u32[]{:S(2)}, u32[]{:S(2)}) collective-permute-start(f32[2048]{0:T(1024)S(1)} %add.92), channel_id=1, source_target_pairs={{0,4},{1,5},{2,6},{3,7},{4,0},{5,1},{6,2},{7,3},{8,12},{9,13},{10,... | collective-permute-start | bytes 24584 | tf_op jit(solution)/shard_map/ppermute | solution.py:55
  130.1 4.5 %collective-permute-start.13 = (f32[2048]{0:T(1024)S(1)}, f32[2048]{0:T(1024)S(1)}, u32[]{:S(2)}, u32[]{:S(2)}) collective-permute-start(f32[2048]{0:T(1024)S(1)} %add.93), channel_id=1, source_target_pairs={{0,8},{1,9},{2,10},{3,11},{4,12},{5,13},{6,14},{7,15},{8,0},{9,1},... | collective-permute-start | bytes 24584 | tf_op jit(solution)/shard_map/ppermute | solution.py:55

commit v12 on v11

--- a/solution.py
+++ b/solution.py
@@ -24,7 +24,7 @@
     other = list(steps)
     if len(other) >= 3:
         other[1], other[2] = other[2], other[1]
-    return steps, other
+    return other, steps
 
 
 def butterfly_gathers(shards, orders, axis, size):

time: 136 us -> 135 us (level)
  waiting for transfers between devices: 79.8 us -> 77.1 us
  starting transfers between devices: 20.2 us -> 22.4 us
    ppermute x4, starting transfers between devices: 4.37 us -> 6.64 us  [butterfly_sum(): lax.ppermute(value, axis, [(j, j ^ step) for j in range(size)])]
    ppermute x4, waiting for transfers between devices: 6.83 us -> 5.16 us  [butterfly_sum(): lax.ppermute(value, axis, [(j, j ^ step) for j in range(size)])]
  transfers between devices with their start and end apart: 14 -> 14, of which waited for: 12 -> 11; matrix products, arithmetic and copies ran while one was open for 15% -> 15% of each run, Pallas kernels for 0% -> 0%
where the time goes in v12:
time: 135 us
  waiting for transfers between devices  77.1 us (57%)
  starting transfers between devices  22.4 us (17%)
  other arithmetic  17.6 us (13%)
  matrix products  13.3 us (10%)
  local copies, waits for them, and re-layouts  3.16 us (2%)
    ppermute x8, waiting for transfers between devices, butterfly_gathers(): lax.ppermute(held[which], axis, [(j, j ^ step) for j in range(size)])  51.7 us
    ppermute x2, waiting for transfers between devices, send_to(): return lax.ppermute(arrays, axis, [(source, target)])  20.2 us
    ppermute x8, starting transfers between devices, butterfly_gathers(): lax.ppermute(held[which], axis, [(j, j ^ step) for j in range(size)])  10.8 us
    select_n x6, other arithmetic, butterfly_gathers(): low = jnp.where(upper, other, held[which])  7.93 us
    ppermute x4, starting transfers between devices, butterfly_sum(): lax.ppermute(value, axis, [(j, j ^ step) for j in range(size)])  6.64 us
    ppermute x4, waiting for transfers between devices, butterfly_sum(): lax.ppermute(value, axis, [(j, j ^ step) for j in range(size)])  5.16 us
    dot_general x3, matrix products, attend_layer(): update = jnp.dot(mixed, output_weight, preferred_element_type=jnp.float32)  5.1 us
    ppermute x2, starting transfers between devices, send_to(): return lax.ppermute(arrays, axis, [(source, target)])  4.97 us
  transfers between devices with their start and end apart: 14, of which 11 were waited for; matrix products, arithmetic and copies ran while one was open for 15% of the time, Pallas kernels for 0%

profile of v12, /device:TPU:0, one launch (start us, length us, event | category | flops | bytes accessed | tf_op | source)
XLA Modules:
  0.0 134.8 jit_solution(12172896925434492826)
XLA Ops:
  0.7 4.1 %collective-permute-start.4 = (bf16[1,128,1024]{2,1,0:T(8,128)(2,1)}, bf16[1,128,1024]{2,1,0:T(8,128)(2,1)S(1)}, u32[]{:S(2)}, u32[]{:S(2)}) collective-permute-start(bf16[1,128,1024]{2,1,0:T(8,128)(2,1)} %param.12), channel_id=1, source_target_pairs={{0,8},{1,9},{2,10},{3,11},{4,12},{5,13},{6,14},{7,15},{8,0},{9,1},... | collective-permute-start | bytes 786440 | tf_op jit(solution)/shard_map/ppermute | solution.py:37
  4.8 18.5 %collective-permute-done.4 = bf16[1,128,1024]{2,1,0:T(8,128)(2,1)S(1)} collective-permute-done((bf16[1,128,1024]{2,1,0:T(8,128)(2,1)}, bf16[1,128,1024]{2,1,0:T(8,128)(2,1)S(1)}, u32[]{:S(2)}, u32[]{:S(2)}) %collective-permute-start.4) | collective-permute-done | bytes 262176 | tf_op jit(solution)/shard_map/ppermute | solution.py:37
  23.3 1.0 broadcast_select_fusion.9
  24.4 1.9 %collective-permute-start.5 = (bf16[2,128,1024]{2,1,0:T(8,128)(2,1)S(1)}, bf16[2,128,1024]{2,1,0:T(8,128)(2,1)S(1)}, u32[]{:S(2)}, u32[]{:S(2)}) collective-permute-start(bf16[2,128,1024]{2,1,0:T(8,128)(2,1)S(1)} %pad_maximum_fusion.6), channel_id=1, source_target_pairs={{0,2},{1,3},{2,0},{3,1},{4,6},{5,7},{6,4},{7,5},{8,10},{9,11},{10,... | collective-permute-start | bytes 1572872 | tf_op jit(solution)/shard_map/ppermute | solution.py:37
  26.3 1.8 %collective-permute-done = bf16[1,64,2048]{2,1,0:T(8,128)(2,1)S(1)} collective-permute-done((bf16[1,64,2048]{2,1,0:T(8,128)(2,1)}, bf16[1,64,2048]{2,1,0:T(8,128)(2,1)S(1)}, u32[]{:S(2)}, u32[]{:S(2)}) %collective-permute-start) | collective-permute-done | bytes 262176 | tf_op jit(solution)/shard_map/ppermute | solution.py:37
  28.1 1.0 broadcast_select_fusion.11
  29.2 0.9 collective-permute-start.1
  30.3 6.5 %collective-permute-done.5 = bf16[2,128,1024]{2,1,0:T(8,128)(2,1)S(1)} collective-permute-done((bf16[2,128,1024]{2,1,0:T(8,128)(2,1)S(1)}, bf16[2,128,1024]{2,1,0:T(8,128)(2,1)S(1)}, u32[]{:S(2)}, u32[]{:S(2)}) %collective-permute-start.5) | collective-permute-done | bytes 524320 | tf_op jit(solution)/shard_map/ppermute | solution.py:37
  36.8 1.1 pad_maximum_fusion.4
  37.9 1.6 %collective-permute-start.6 = (bf16[4,128,1024]{2,1,0:T(8,128)(2,1)}, bf16[4,128,1024]{2,1,0:T(8,128)(2,1)}, u32[]{:S(2)}, u32[]{:S(2)}) collective-permute-start(bf16[4,128,1024]{2,1,0:T(8,128)(2,1)} %bitcast.24), channel_id=1, source_target_pairs={{0,4},{1,5},{2,6},{3,7},{4,0},{5,1},{6,2},{7,3},{8,12},{9,13},{10,... | collective-permute-start | bytes 3145736 | tf_op jit(solution)/shard_map/ppermute | solution.py:37
  39.4 4.7 %collective-permute-done.1 = bf16[2,64,2048]{2,1,0:T(8,128)(2,1)S(1)} collective-permute-done((bf16[2,64,2048]{2,1,0:T(8,128)(2,1)S(1)}, bf16[2,64,2048]{2,1,0:T(8,128)(2,1)S(1)}, u32[]{:S(2)}, u32[]{:S(2)}) %collective-permute-start.1) | collective-permute-done | bytes 524320 | tf_op jit(solution)/shard_map/ppermute | solution.py:37
  44.3 1.6 %collective-permute-start.2 = (bf16[4,64,2048]{2,1,0:T(8,128)(2,1)S(1)}, bf16[4,64,2048]{2,1,0:T(8,128)(2,1)}, u32[]{:S(2)}, u32[]{:S(2)}) collective-permute-start(bf16[4,64,2048]{2,1,0:T(8,128)(2,1)S(1)} %bitcast.269), channel_id=1, source_target_pairs={{0,2},{1,3},{2,0},{3,1},{4,6},{5,7},{6,4},{7,5},{8,10},{9,11},{10,... | collective-permute-start | bytes 3145736 | tf_op jit(solution)/shard_map/ppermute | solution.py:37
  46.1 0.4 multiply_reduce_fusion
  46.5 18.4 %collective-permute-done.6 = bf16[4,128,1024]{2,1,0:T(8,128)(2,1)} collective-permute-done((bf16[4,128,1024]{2,1,0:T(8,128)(2,1)}, bf16[4,128,1024]{2,1,0:T(8,128)(2,1)}, u32[]{:S(2)}, u32[]{:S(2)}) %collective-permute-start.6) | collective-permute-done | bytes 1048608 | tf_op jit(solution)/shard_map/ppermute | solution.py:37
  64.9 1.7 %broadcast_select_fusion.5 = (bf16[4,128,1024]{2,1,0:T(8,128)(2,1)S(1)}, bf16[4,128,1024]{2,1,0:T(8,128)(2,1)S(1)}) fusion(bf16[4,128,1024]{2,1,0:T(8,128)(2,1)} %collective-permute-done.6, pred[]{:T(512)S(6)} %eq.52, bf16[2,2,128,1024]{3,2,1,0:T(8,128)(2,1)} %pad_maximum_fusion.4), kind=kLoop, calls=%fused_computation.98 | loop fusion | flops 1048576 | bytes 4194305 | tf_op jit(solution)/shard_map/jit(_where)/select_n | solution.py:39
  66.6 1.5 %pad_maximum_fusion.2 = bf16[2,2,2,128,1024]{4,3,2,1,0:T(8,128)(2,1)} fusion(bf16[2,1,2,128,1024]{4,3,2,1,0:T(8,128)(2,1)S(1)} %bitcast.271, bf16[2,1,2,128,1024]{4,3,2,1,0:T(8,128)(2,1)S(1)} %bitcast.270), kind=kLoop, calls=%fused_computation.8 | loop fusion | flops 1048576 | bytes 4194304 | tf_op jit(solution)/shard_map/stack | solution.py:43
  68.2 1.4 %broadcast_select_fusion.7 = (bf16[4,64,2048]{2,1,0:T(8,128)(2,1)S(1)}, bf16[4,64,2048]{2,1,0:T(8,128)(2,1)S(1)}) fusion(bf16[4,64,2048]{2,1,0:T(8,128)(2,1)} %collective-permute-done.2, pred[]{:T(512)S(6)} %eq.51, bf16[2,2,64,2048]{3,2,1,0:T(8,128)(2,1)S(1)} %pad_maximum_fusion.5), kind=kLoop, calls=%fused_computation.100 | loop fusion | flops 1048576 | bytes 4194305 | tf_op jit(solution)/shard_map/jit(_where)/select_n | solution.py:39
  69.7 0.6 collective-permute-start.3
  70.8 1.9 %collective-permute-done.7 = bf16[8,128,1024]{2,1,0:T(8,128)(2,1)} collective-permute-done((bf16[8,128,1024]{2,1,0:T(8,128)(2,1)}, bf16[8,128,1024]{2,1,0:T(8,128)(2,1)}, u32[]{:S(2)}, u32[]{:S(2)}) %collective-permute-start.7) | collective-permute-done | bytes 2097184 | tf_op jit(solution)/shard_map/ppermute | solution.py:37
  72.6 2.5 %broadcast_select_fusion.1 = (bf16[8,128,1024]{2,1,0:T(8,128)(2,1)S(1)}, bf16[8,128,1024]{2,1,0:T(8,128)(2,1)S(1)}) fusion(bf16[8,128,1024]{2,1,0:T(8,128)(2,1)} %collective-permute-done.7, pred[]{:T(512)S(6)} %eq.50, bf16[2,2,2,128,1024]{4,3,2,1,0:T(8,128)(2,1)} %pad_maximum_fusion.2), kind=kLoop, calls=%fused_computation.11 | loop fusion | flops 2097152 | bytes 8388609 | tf_op jit(solution)/shard_map/jit(_where)/select_n | solution.py:39
  75.1 0.4 pad_maximum_fusion
  75.5 0.7 fusion.21
  76.3 0.4 broadcast_select_fusion.3
  76.8 0.7 copy-done.1
  77.5 0.4 pad_maximum_fusion.1
  78.5 0.5 copy-done.7
  79.0 1.6 %fusion = bf16[4,32,2048]{2,1,0:T(8,128)(2,1)} fusion(bf16[1024,2048,1]{1,0,2:T(8,128)(2,1)S(1)} %bitcast.259, bf16[4,1,32,2048]{3,2,1,0:T(8,128)(2,1)S(1)} %copy-done.5, bf16[4,8,4,8,128]{4,3,2,1,0:T(8,128)(2,1)S(1)} %fusion.23), kind=kOutput, calls=%fused_computation.3 | convolution fusion | flops 537657344 | bytes 5505024 | tf_op jit(solution)/shard_map/dot_general | solution.py:88
  80.6 3.2 %collective-permute-start.8 = (bf16[4,32,2048]{2,1,0:T(8,128)(2,1)}, bf16[4,32,2048]{2,1,0:T(8,128)(2,1)S(1)}, u32[]{:S(2)}, u32[]{:S(2)}) collective-permute-start(bf16[4,32,2048]{2,1,0:T(8,128)(2,1)} %fusion), channel_id=1, source_target_pairs={{0,16},{1,17},{2,18},{3,19},{4,20},{5,21},{6,22},{7,23},{8,24},{9,... | collective-permute-start | bytes 1572872 | tf_op jit(solution)/shard_map/ppermute | solution.py:15
  83.9 2.0 %fusion.19 = bf16[128,1024]{0,1:T(8,128)(2,1)} fusion(bf16[1024,2048]{1,0:T(8,128)(2,1)S(1)} %bitcast.260, bf16[128,2048]{1,0:T(8,128)(2,1)S(1)} %bitcast.287), kind=kOutput, calls=%fused_computation.60 | convolution fusion | flops 537001984 | bytes 4980736 | tf_op jit(solution)/shard_map/transpose(jvp())/dot_general | solution.py:88
  85.9 1.1 copy.72
  87.1 8.5 %collective-permute-done.8 = bf16[4,32,2048]{2,1,0:T(8,128)(2,1)S(1)} collective-permute-done((bf16[4,32,2048]{2,1,0:T(8,128)(2,1)}, bf16[4,32,2048]{2,1,0:T(8,128)(2,1)S(1)}, u32[]{:S(2)}, u32[]{:S(2)}) %collective-permute-start.8) | collective-permute-done | bytes 524320 | tf_op jit(solution)/shard_map/ppermute | solution.py:15
  96.2 0.8 fusion.20
  98.2 0.6 fusion.31
  99.1 1.7 %collective-permute-start.9 = (bf16[4,32,2048]{2,1,0:T(8,128)(2,1)S(1)}, bf16[4,32,2048]{2,1,0:T(8,128)(2,1)S(1)}, u32[]{:S(2)}, u32[]{:S(2)}) collective-permute-start(bf16[4,32,2048]{2,1,0:T(8,128)(2,1)S(1)} %fusion.44), channel_id=1, source_target_pairs={{16,0},{17,1},{18,2},{19,3},{20,4},{21,5},{22,6},{23,7},{24,8},{25... | collective-permute-start | bytes 1572872 | tf_op jit(solution)/shard_map/ppermute | solution.py:15
  101.3 1.5 %convolution_convert_fusion = bf16[128,2048]{1,0:T(8,128)(2,1)S(1)} fusion(bf16[2048,1024]{1,0:T(8,128)(2,1)S(1)} %bitcast.257, bf16[16,8,8,128]{3,2,1,0:T(8,128)(2,1)S(1)} %bitcast.284), kind=kOutput, calls=%fused_computation.4 | convolution fusion | flops 537133056 | bytes 4980736 | tf_op jit(solution)/shard_map/transpose(jvp())/dot_general | solution.py:77
  102.8 11.7 %collective-permute-done.9 = bf16[4,32,2048]{2,1,0:T(8,128)(2,1)S(1)} collective-permute-done((bf16[4,32,2048]{2,1,0:T(8,128)(2,1)S(1)}, bf16[4,32,2048]{2,1,0:T(8,128)(2,1)S(1)}, u32[]{:S(2)}, u32[]{:S(2)}) %collective-permute-start.9) | collective-permute-done | bytes 524320 | tf_op jit(solution)/shard_map/ppermute | solution.py:15
  114.5 1.5 %fusion.22 = bf16[16,8,8,128]{3,1,2,0:T(8,128)(2,1)S(1)} fusion(bf16[128,2048]{1,0:T(8,128)(2,1)S(1)} %bitcast.278, bf16[1024,2048]{1,0:T(8,128)(2,1)S(1)} %bitcast.261), kind=kOutput, calls=%fused_computation.63 | convolution fusion | flops 537001984 | bytes 4980736 | tf_op jit(solution)/shard_map/transpose(jvp())/dot_general | solution.py:88
  116.7 0.4 fusion.26
  117.5 1.5 %convolution_convert_fusion.1 = bf16[128,2048]{1,0:T(8,128)(2,1)S(1)} fusion(bf16[2048,1024]{1,0:T(8,128)(2,1)S(1)} %bitcast.258, bf16[16,8,8,128]{3,2,1,0:T(8,128)(2,1)S(1)} %bitcast.283), kind=kOutput, calls=%fused_computation.5 | convolution fusion | flops 537133056 | bytes 4980736 | tf_op jit(solution)/shard_map/transpose(jvp())/dot_general | solution.py:77
  119.1 1.3 fusion.36
  120.5 1.2 collective-permute-done.10
  121.7 1.5 %collective-permute-start.11 = (f32[2048]{0:T(1024)S(1)}, f32[2048]{0:T(1024)S(1)}, u32[]{:S(2)}, u32[]{:S(2)}) collective-permute-start(f32[2048]{0:T(1024)S(1)} %add.91), channel_id=1, source_target_pairs={{0,2},{1,3},{2,0},{3,1},{4,6},{5,7},{6,4},{7,5},{8,10},{9,11},{10,... | collective-permute-start | bytes 24584 | tf_op jit(solution)/shard_map/ppermute | solution.py:55
  123.2 2.1 %collective-permute-done.11 = f32[2048]{0:T(1024)S(1)} collective-permute-done((f32[2048]{0:T(1024)S(1)}, f32[2048]{0:T(1024)S(1)}, u32[]{:S(2)}, u32[]{:S(2)}) %collective-permute-start.11) | collective-permute-done | bytes 8224 | tf_op jit(solution)/shard_map/ppermute | solution.py:55
  125.4 1.8 %collective-permute-start.12 = (f32[2048]{0:T(1024)S(1)}, f32[2048]{0:T(1024)S(1)}, u32[]{:S(2)}, u32[]{:S(2)}) collective-permute-start(f32[2048]{0:T(1024)S(1)} %add.92), channel_id=1, source_target_pairs={{0,4},{1,5},{2,6},{3,7},{4,0},{5,1},{6,2},{7,3},{8,12},{9,13},{10,... | collective-permute-start | bytes 24584 | tf_op jit(solution)/shard_map/ppermute | solution.py:55
  127.1 1.9 %collective-permute-done.12 = f32[2048]{0:T(1024)S(1)} collective-permute-done((f32[2048]{0:T(1024)S(1)}, f32[2048]{0:T(1024)S(1)}, u32[]{:S(2)}, u32[]{:S(2)}) %collective-permute-start.12) | collective-permute-done | bytes 8224 | tf_op jit(solution)/shard_map/ppermute | solution.py:55
  129.0 3.3 %collective-permute-start.13 = (f32[2048]{0:T(1024)S(1)}, f32[2048]{0:T(1024)S(1)}, u32[]{:S(2)}, u32[]{:S(2)}) collective-permute-start(f32[2048]{0:T(1024)S(1)} %add.93), channel_id=1, source_target_pairs={{0,8},{1,9},{2,10},{3,11},{4,12},{5,13},{6,14},{7,15},{8,0},{9,1},... | collective-permute-start | bytes 24584 | tf_op jit(solution)/shard_map/ppermute | solution.py:55
  132.3 1.9 %fusion.54 = bf16[1,4,1,32,2048]{4,3,2,1,0:T(8,128)(2,1)} fusion(f32[4,32,2048]{2,1,0:T(8,128)S(1)} %get-tuple-element.45, bf16[4,32,2048]{2,1,0:T(8,128)(2,1)S(1)} %collective-permute-done.9, bf16[4,32,1024]{2,1,0:T(8,128)(2,1)S(1)} %bitcast.277, bf16[4,32,1024]{2,1,0:T(8,128)(2,1)S(1)} %bitcast.275, bf16[4,1,32,2048]{3,2,1,0:T(8,128)(2,1)S(1)} %copy-done.6, ...), kind=kLoop, calls=%fused_computation.105 | loop fusion | flops 8912896 | bytes 4729346
  134.2 0.6 add.94
  (83 shorter events, 6.0 us)
Async XLA Ops:
  0.6 45.5 %copy-start = (bf16[16,2048]{1,0:T(8,128)(2,1)S(1)}, bf16[16,2048]{1,0:T(8,128)(2,1)}, u32[]{:S(2)}) copy-start(bf16[16,2048]{1,0:T(8,128)(2,1)} %param.11) | copy-start | bytes 196612
  0.6 29.4 %copy-start.5 = (bf16[4,1,32,2048]{3,2,1,0:T(8,128)(2,1)S(1)}, bf16[4,1,32,2048]{3,2,1,0:T(8,128)(2,1)}, u32[]{:S(2)}) copy-start(bf16[4,1,32,2048]{3,2,1,0:T(8,128)(2,1)} %param.8) | copy-start | bytes 1572868
  0.7 22.7 %collective-permute-start.4 = (bf16[1,128,1024]{2,1,0:T(8,128)(2,1)}, bf16[1,128,1024]{2,1,0:T(8,128)(2,1)S(1)}, u32[]{:S(2)}, u32[]{:S(2)}) collective-permute-start(bf16[1,128,1024]{2,1,0:T(8,128)(2,1)} %param.12), channel_id=1, source_target_pairs={{0,8},{1,9},{2,10},{3,11},{4,12},{5,13},{6,14},{7,15},{8,0},{9,1},... | collective-permute-start | bytes 786440 | tf_op jit(solution)/shard_map/ppermute | solution.py:37
  4.8 23.4 %collective-permute-start = (bf16[1,64,2048]{2,1,0:T(8,128)(2,1)}, bf16[1,64,2048]{2,1,0:T(8,128)(2,1)S(1)}, u32[]{:S(2)}, u32[]{:S(2)}) collective-permute-start(bf16[1,64,2048]{2,1,0:T(8,128)(2,1)} %param.13), channel_id=1, source_target_pairs={{0,8},{1,9},{2,10},{3,11},{4,12},{5,13},{6,14},{7,15},{8,0},{9,1},... | collective-permute-start | bytes 786440 | tf_op jit(solution)/shard_map/ppermute | solution.py:37
  24.4 12.3 %collective-permute-start.5 = (bf16[2,128,1024]{2,1,0:T(8,128)(2,1)S(1)}, bf16[2,128,1024]{2,1,0:T(8,128)(2,1)S(1)}, u32[]{:S(2)}, u32[]{:S(2)}) collective-permute-start(bf16[2,128,1024]{2,1,0:T(8,128)(2,1)S(1)} %pad_maximum_fusion.6), channel_id=1, source_target_pairs={{0,2},{1,3},{2,0},{3,1},{4,6},{5,7},{6,4},{7,5},{8,10},{9,11},{10,... | collective-permute-start | bytes 1572872 | tf_op jit(solution)/shard_map/ppermute | solution.py:37
  29.2 14.9 %collective-permute-start.1 = (bf16[2,64,2048]{2,1,0:T(8,128)(2,1)S(1)}, bf16[2,64,2048]{2,1,0:T(8,128)(2,1)S(1)}, u32[]{:S(2)}, u32[]{:S(2)}) collective-permute-start(bf16[2,64,2048]{2,1,0:T(8,128)(2,1)S(1)} %pad_maximum_fusion.7), channel_id=1, source_target_pairs={{0,4},{1,5},{2,6},{3,7},{4,0},{5,1},{6,2},{7,3},{8,12},{9,13},{10,... | collective-permute-start | bytes 1572872 | tf_op jit(solution)/shard_map/ppermute | solution.py:37
  30.3 15.7 %copy-start.12 = (s32[4,1,16,2]{2,3,1,0:T(2,128)S(1)}, s32[4,1,16,2]{2,3,1,0:T(2,128)}, u32[]{:S(2)}) copy-start(s32[4,1,16,2]{2,3,1,0:T(2,128)} %param.10) | copy-start | bytes 1540
  37.9 27.1 %collective-permute-start.6 = (bf16[4,128,1024]{2,1,0:T(8,128)(2,1)}, bf16[4,128,1024]{2,1,0:T(8,128)(2,1)}, u32[]{:S(2)}, u32[]{:S(2)}) collective-permute-start(bf16[4,128,1024]{2,1,0:T(8,128)(2,1)} %bitcast.24), channel_id=1, source_target_pairs={{0,4},{1,5},{2,6},{3,7},{4,0},{5,1},{6,2},{7,3},{8,12},{9,13},{10,... | collective-permute-start | bytes 3145736 | tf_op jit(solution)/shard_map/ppermute | solution.py:37
  44.3 23.9 %collective-permute-start.2 = (bf16[4,64,2048]{2,1,0:T(8,128)(2,1)S(1)}, bf16[4,64,2048]{2,1,0:T(8,128)(2,1)}, u32[]{:S(2)}, u32[]{:S(2)}) collective-permute-start(bf16[4,64,2048]{2,1,0:T(8,128)(2,1)S(1)} %bitcast.269), channel_id=1, source_target_pairs={{0,2},{1,3},{2,0},{3,1},{4,6},{5,7},{6,4},{7,5},{8,10},{9,11},{10,... | collective-permute-start | bytes 3145736 | tf_op jit(solution)/shard_map/ppermute | solution.py:37
  46.5 21.6 %copy-start.13 = (s32[4,1,32]{2,1,0:T(1,128)S(1)}, s32[4,1,32]{2,1,0:T(1,128)}, u32[]{:S(2)}) copy-start(s32[4,1,32]{2,1,0:T(1,128)} %param.9) | copy-start | bytes 1540
  68.1 4.5 %collective-permute-start.7 = (bf16[8,128,1024]{2,1,0:T(8,128)(2,1)}, bf16[8,128,1024]{2,1,0:T(8,128)(2,1)}, u32[]{:S(2)}, u32[]{:S(2)}) collective-permute-start(bf16[8,128,1024]{2,1,0:T(8,128)(2,1)} %bitcast.29), channel_id=1, source_target_pairs={{0,1},{1,0},{2,3},{3,2},{4,5},{5,4},{6,7},{7,6},{8,9},{9,8},{10,11... | collective-permute-start | bytes 6291464 | tf_op jit(solution)/shard_map/ppermute | solution.py:37
  68.2 2.2 %copy-start.9 = (f32[1,2048]{1,0:T(1,128)S(1)}, f32[1,2048]{1,0:T(1,128)}, u32[]{:S(2)}) copy-start(f32[1,2048]{1,0:T(1,128)} %param.14) | copy-start | bytes 24580
  69.7 6.6 %collective-permute-start.3 = (bf16[8,64,2048]{2,1,0:T(8,128)(2,1)S(1)}, bf16[8,64,2048]{2,1,0:T(8,128)(2,1)S(1)}, u32[]{:S(2)}, u32[]{:S(2)}) collective-permute-start(bf16[8,64,2048]{2,1,0:T(8,128)(2,1)S(1)} %bitcast.262), channel_id=1, source_target_pairs={{0,1},{1,0},{2,3},{3,2},{4,5},{5,4},{6,7},{7,6},{8,9},{9,8},{10,11... | collective-permute-start | bytes 6291464 | tf_op jit(solution)/shard_map/ppermute | solution.py:37
  70.6 7.3 %copy-start.10 = (bf16[4,4,8,8,128]{4,3,2,1,0:T(8,128)(2,1)}, bf16[4,4,8,8,128]{4,3,2,1,0:T(8,128)(2,1)S(1)}, u32[]{:S(2)}) copy-start(bf16[4,4,8,8,128]{4,3,2,1,0:T(8,128)(2,1)S(1)} %get-tuple-element.32) | copy-start | bytes 786436
  75.5 1.9 %copy-start.1 = (bf16[2,2,2,2,128,1024]{5,4,3,2,1,0:T(8,128)(2,1)}, bf16[2,2,2,2,128,1024]{5,4,3,2,1,0:T(8,128)(2,1)S(1)}, u32[]{:S(2)}) copy-start(bf16[2,2,2,2,128,1024]{5,4,3,2,1,0:T(8,128)(2,1)S(1)} %pad_maximum_fusion) | copy-start | bytes 12582916
  77.9 6.0 %copy-start.3 = (bf16[2,2,2,2,64,2048]{5,4,3,2,1,0:T(8,128)(2,1)}, bf16[2,2,2,2,64,2048]{5,4,3,2,1,0:T(8,128)(2,1)S(1)}, u32[]{:S(2)}) copy-start(bf16[2,2,2,2,64,2048]{5,4,3,2,1,0:T(8,128)(2,1)S(1)} %pad_maximum_fusion.1) | copy-start | bytes 12582916
  77.9 6.0 %copy-start.6 = (bf16[4,1,32,2048]{3,2,1,0:T(8,128)(2,1)S(1)}, bf16[4,1,32,2048]{3,2,1,0:T(8,128)(2,1)}, u32[]{:S(2)}) copy-start(bf16[4,1,32,2048]{3,2,1,0:T(8,128)(2,1)} %param.15) | copy-start | bytes 1572868
  78.2 0.8 copy-start.7
  80.6 15.0 %collective-permute-start.8 = (bf16[4,32,2048]{2,1,0:T(8,128)(2,1)}, bf16[4,32,2048]{2,1,0:T(8,128)(2,1)S(1)}, u32[]{:S(2)}, u32[]{:S(2)}) collective-permute-start(bf16[4,32,2048]{2,1,0:T(8,128)(2,1)} %fusion), channel_id=1, source_target_pairs={{0,16},{1,17},{2,18},{3,19},{4,20},{5,21},{6,22},{7,23},{8,24},{9,... | collective-permute-start | bytes 1572872 | tf_op jit(solution)/shard_map/ppermute | solution.py:15
  87.0 9.2 %copy-start.2 = (bf16[2,2,2,2,128,1024]{5,4,3,2,1,0:T(8,128)(2,1)S(1)}, bf16[2,2,2,2,128,1024]{5,4,3,2,1,0:T(8,128)(2,1)}, u32[]{:S(2)}) copy-start(bf16[2,2,2,2,128,1024]{5,4,3,2,1,0:T(8,128)(2,1)} %copy-done.1) | copy-start | bytes 12582916
  99.1 15.4 %copy-start.4 = (bf16[2,2,2,2,64,2048]{5,4,3,2,1,0:T(8,128)(2,1)S(1)}, bf16[2,2,2,2,64,2048]{5,4,3,2,1,0:T(8,128)(2,1)}, u32[]{:S(2)}) copy-start(bf16[2,2,2,2,64,2048]{5,4,3,2,1,0:T(8,128)(2,1)} %copy-done.3) | copy-start | bytes 12582916
  99.1 15.4 %collective-permute-start.9 = (bf16[4,32,2048]{2,1,0:T(8,128)(2,1)S(1)}, bf16[4,32,2048]{2,1,0:T(8,128)(2,1)S(1)}, u32[]{:S(2)}, u32[]{:S(2)}) collective-permute-start(bf16[4,32,2048]{2,1,0:T(8,128)(2,1)S(1)} %fusion.44), channel_id=1, source_target_pairs={{16,0},{17,1},{18,2},{19,3},{20,4},{21,5},{22,6},{23,7},{24,8},{25... | collective-permute-start | bytes 1572872 | tf_op jit(solution)/shard_map/ppermute | solution.py:15
  101.3 14.8 %copy-start.8 = (f32[4,8,32,32]{2,3,1,0:T(8,128)S(1)}, f32[4,8,32,32]{2,3,1,0:T(8,128)}, u32[]{:S(2)}) copy-start(f32[4,8,32,32]{2,3,1,0:T(8,128)} %copy-done.7) | copy-start | bytes 393220
  114.5 2.2 %copy-start.11 = (bf16[4,4,8,8,128]{4,3,2,1,0:T(8,128)(2,1)S(1)}, bf16[4,4,8,8,128]{4,3,2,1,0:T(8,128)(2,1)}, u32[]{:S(2)}) copy-start(bf16[4,4,8,8,128]{4,3,2,1,0:T(8,128)(2,1)} %copy-done.10) | copy-start | bytes 786436
  120.5 1.2 collective-permute-start.10
  121.7 3.7 %collective-permute-start.11 = (f32[2048]{0:T(1024)S(1)}, f32[2048]{0:T(1024)S(1)}, u32[]{:S(2)}, u32[]{:S(2)}) collective-permute-start(f32[2048]{0:T(1024)S(1)} %add.91), channel_id=1, source_target_pairs={{0,2},{1,3},{2,0},{3,1},{4,6},{5,7},{6,4},{7,5},{8,10},{9,11},{10,... | collective-permute-start | bytes 24584 | tf_op jit(solution)/shard_map/ppermute | solution.py:55
  125.4 3.7 %collective-permute-start.12 = (f32[2048]{0:T(1024)S(1)}, f32[2048]{0:T(1024)S(1)}, u32[]{:S(2)}, u32[]{:S(2)}) collective-permute-start(f32[2048]{0:T(1024)S(1)} %add.92), channel_id=1, source_target_pairs={{0,4},{1,5},{2,6},{3,7},{4,0},{5,1},{6,2},{7,3},{8,12},{9,13},{10,... | collective-permute-start | bytes 24584 | tf_op jit(solution)/shard_map/ppermute | solution.py:55
  129.0 5.2 %collective-permute-start.13 = (f32[2048]{0:T(1024)S(1)}, f32[2048]{0:T(1024)S(1)}, u32[]{:S(2)}, u32[]{:S(2)}) collective-permute-start(f32[2048]{0:T(1024)S(1)} %add.93), channel_id=1, source_target_pairs={{0,8},{1,9},{2,10},{3,11},{4,12},{5,13},{6,14},{7,15},{8,0},{9,1},... | collective-permute-start | bytes 24584 | tf_op jit(solution)/shard_map/ppermute | solution.py:55

commit v13 on v12

--- a/solution.py
+++ b/solution.py
@@ -12,7 +12,21 @@
 
 
 def send_to(arrays, axis, source, target):
-    return lax.ppermute(arrays, axis, [(source, target)])
+    def halves(array):
+        half = array.shape[0] // 2
+        if half == 0:
+            return (array,)
+        return (array[:half], array[half:])
+
+    leaves, tree = jax.tree.flatten(arrays)
+    parts = [halves(leaf) for leaf in leaves]
+    moved = lax.ppermute(tuple(piece for pieces in parts for piece in pieces), axis, [(source, target)])
+    joined = []
+    at = 0
+    for pieces in parts:
+        joined.append(jnp.concatenate(moved[at:at + len(pieces)], axis=0))
+        at += len(pieces)
+    return jax.tree.unflatten(tree, joined)
 
 
 def exchange_orders(size):

time: 135 us -> 135 us (level)
  starting transfers between devices: 22.4 us -> 24.9 us
  waiting for transfers between devices: 77.1 us -> 75 us
    ppermute x2 -> x4, starting transfers between devices: 4.97 us -> 7.56 us  [send_to(): lax.ppermute(tuple((piece for pieces in parts for piece in pieces)), axis...]
    ppermute x2 -> x4, waiting for transfers between devices: 20.2 us -> 18.1 us  [send_to(): lax.ppermute(tuple((piece for pieces in parts for piece in pieces)), axis...]
  transfers between devices with their start and end apart: 14 -> 16, of which waited for: 11 -> 13; matrix products, arithmetic and copies ran while one was open for 15% -> 15% of each run, Pallas kernels for 0% -> 0%
where the time goes in v13:
time: 135 us
  waiting for transfers between devices  75 us (56%)
  starting transfers between devices  24.9 us (18%)
  other arithmetic  17.6 us (13%)
  matrix products  12.5 us (9%)
  local copies, waits for them, and re-layouts  3.66 us (3%)
    ppermute x8, waiting for transfers between devices, butterfly_gathers(): lax.ppermute(held[which], axis, [(j, j ^ step) for j in range(size)])  51.7 us
    ppermute x4, waiting for transfers between devices, send_to(): lax.ppermute(tuple((piece for pieces in parts for piece in pieces)), axis...  18.1 us
    ppermute x8, starting transfers between devices, butterfly_gathers(): lax.ppermute(held[which], axis, [(j, j ^ step) for j in range(size)])  10.8 us
    select_n x6, other arithmetic, butterfly_gathers(): low = jnp.where(upper, other, held[which])  7.93 us
    ppermute x4, starting transfers between devices, send_to(): lax.ppermute(tuple((piece for pieces in parts for piece in pieces)), axis...  7.56 us
    ppermute x4, starting transfers between devices, butterfly_sum(): lax.ppermute(value, axis, [(j, j ^ step) for j in range(size)])  6.61 us
    ppermute x4, waiting for transfers between devices, butterfly_sum(): lax.ppermute(value, axis, [(j, j ^ step) for j in range(size)])  5.17 us
    dot_general x4, matrix products, attend_layer(): jnp.dot(normed_rows, query_weight, preferred_element_type=jnp.float32)  4.51 us
  transfers between devices with their start and end apart: 16, of which 13 were waited for; matrix products, arithmetic and copies ran while one was open for 15% of the time, Pallas kernels for 0%

profile of v13, /device:TPU:0, one launch (start us, length us, event | category | flops | bytes accessed | tf_op | source)
XLA Modules:
  0.0 135.0 jit_solution(12315224176354639698)
XLA Ops:
  0.7 4.1 %collective-permute-start.4 = (bf16[1,128,1024]{2,1,0:T(8,128)(2,1)}, bf16[1,128,1024]{2,1,0:T(8,128)(2,1)S(1)}, u32[]{:S(2)}, u32[]{:S(2)}) collective-permute-start(bf16[1,128,1024]{2,1,0:T(8,128)(2,1)} %param.12), channel_id=1, source_target_pairs={{0,8},{1,9},{2,10},{3,11},{4,12},{5,13},{6,14},{7,15},{8,0},{9,1},... | collective-permute-start | bytes 786440 | tf_op jit(solution)/shard_map/ppermute | solution.py:51
  4.8 18.5 %collective-permute-done.4 = bf16[1,128,1024]{2,1,0:T(8,128)(2,1)S(1)} collective-permute-done((bf16[1,128,1024]{2,1,0:T(8,128)(2,1)}, bf16[1,128,1024]{2,1,0:T(8,128)(2,1)S(1)}, u32[]{:S(2)}, u32[]{:S(2)}) %collective-permute-start.4) | collective-permute-done | bytes 262176 | tf_op jit(solution)/shard_map/ppermute | solution.py:51
  23.3 1.0 broadcast_select_fusion.9
  24.4 1.9 %collective-permute-start.5 = (bf16[2,128,1024]{2,1,0:T(8,128)(2,1)S(1)}, bf16[2,128,1024]{2,1,0:T(8,128)(2,1)S(1)}, u32[]{:S(2)}, u32[]{:S(2)}) collective-permute-start(bf16[2,128,1024]{2,1,0:T(8,128)(2,1)S(1)} %pad_maximum_fusion.6), channel_id=1, source_target_pairs={{0,2},{1,3},{2,0},{3,1},{4,6},{5,7},{6,4},{7,5},{8,10},{9,11},{10,... | collective-permute-start | bytes 1572872 | tf_op jit(solution)/shard_map/ppermute | solution.py:51
  26.3 1.8 %collective-permute-done = bf16[1,64,2048]{2,1,0:T(8,128)(2,1)S(1)} collective-permute-done((bf16[1,64,2048]{2,1,0:T(8,128)(2,1)}, bf16[1,64,2048]{2,1,0:T(8,128)(2,1)S(1)}, u32[]{:S(2)}, u32[]{:S(2)}) %collective-permute-start) | collective-permute-done | bytes 262176 | tf_op jit(solution)/shard_map/ppermute | solution.py:51
  28.1 1.0 broadcast_select_fusion.11
  29.2 0.9 collective-permute-start.1
  30.3 6.5 %collective-permute-done.5 = bf16[2,128,1024]{2,1,0:T(8,128)(2,1)S(1)} collective-permute-done((bf16[2,128,1024]{2,1,0:T(8,128)(2,1)S(1)}, bf16[2,128,1024]{2,1,0:T(8,128)(2,1)S(1)}, u32[]{:S(2)}, u32[]{:S(2)}) %collective-permute-start.5) | collective-permute-done | bytes 524320 | tf_op jit(solution)/shard_map/ppermute | solution.py:51
  36.8 1.1 pad_maximum_fusion.4
  37.9 1.6 %collective-permute-start.6 = (bf16[4,128,1024]{2,1,0:T(8,128)(2,1)}, bf16[4,128,1024]{2,1,0:T(8,128)(2,1)}, u32[]{:S(2)}, u32[]{:S(2)}) collective-permute-start(bf16[4,128,1024]{2,1,0:T(8,128)(2,1)} %bitcast.24), channel_id=1, source_target_pairs={{0,4},{1,5},{2,6},{3,7},{4,0},{5,1},{6,2},{7,3},{8,12},{9,13},{10,... | collective-permute-start | bytes 3145736 | tf_op jit(solution)/shard_map/ppermute | solution.py:51
  39.4 4.7 %collective-permute-done.1 = bf16[2,64,2048]{2,1,0:T(8,128)(2,1)S(1)} collective-permute-done((bf16[2,64,2048]{2,1,0:T(8,128)(2,1)S(1)}, bf16[2,64,2048]{2,1,0:T(8,128)(2,1)S(1)}, u32[]{:S(2)}, u32[]{:S(2)}) %collective-permute-start.1) | collective-permute-done | bytes 524320 | tf_op jit(solution)/shard_map/ppermute | solution.py:51
  44.3 1.6 %collective-permute-start.2 = (bf16[4,64,2048]{2,1,0:T(8,128)(2,1)S(1)}, bf16[4,64,2048]{2,1,0:T(8,128)(2,1)}, u32[]{:S(2)}, u32[]{:S(2)}) collective-permute-start(bf16[4,64,2048]{2,1,0:T(8,128)(2,1)S(1)} %bitcast.269), channel_id=1, source_target_pairs={{0,2},{1,3},{2,0},{3,1},{4,6},{5,7},{6,4},{7,5},{8,10},{9,11},{10,... | collective-permute-start | bytes 3145736 | tf_op jit(solution)/shard_map/ppermute | solution.py:51
  46.1 0.4 multiply_reduce_fusion
  46.5 18.4 %collective-permute-done.6 = bf16[4,128,1024]{2,1,0:T(8,128)(2,1)} collective-permute-done((bf16[4,128,1024]{2,1,0:T(8,128)(2,1)}, bf16[4,128,1024]{2,1,0:T(8,128)(2,1)}, u32[]{:S(2)}, u32[]{:S(2)}) %collective-permute-start.6) | collective-permute-done | bytes 1048608 | tf_op jit(solution)/shard_map/ppermute | solution.py:51
  64.9 1.7 %broadcast_select_fusion.5 = (bf16[4,128,1024]{2,1,0:T(8,128)(2,1)S(1)}, bf16[4,128,1024]{2,1,0:T(8,128)(2,1)S(1)}) fusion(bf16[4,128,1024]{2,1,0:T(8,128)(2,1)} %collective-permute-done.6, pred[]{:T(512)S(6)} %eq.52, bf16[2,2,128,1024]{3,2,1,0:T(8,128)(2,1)} %pad_maximum_fusion.4), kind=kLoop, calls=%fused_computation.98 | loop fusion | flops 1048576 | bytes 4194305 | tf_op jit(solution)/shard_map/jit(_where)/select_n | solution.py:53
  66.6 1.5 %pad_maximum_fusion.2 = bf16[2,2,2,128,1024]{4,3,2,1,0:T(8,128)(2,1)} fusion(bf16[2,1,2,128,1024]{4,3,2,1,0:T(8,128)(2,1)S(1)} %bitcast.271, bf16[2,1,2,128,1024]{4,3,2,1,0:T(8,128)(2,1)S(1)} %bitcast.270), kind=kLoop, calls=%fused_computation.8 | loop fusion | flops 1048576 | bytes 4194304 | tf_op jit(solution)/shard_map/stack | solution.py:57
  68.2 1.4 %broadcast_select_fusion.7 = (bf16[4,64,2048]{2,1,0:T(8,128)(2,1)S(1)}, bf16[4,64,2048]{2,1,0:T(8,128)(2,1)S(1)}) fusion(bf16[4,64,2048]{2,1,0:T(8,128)(2,1)} %collective-permute-done.2, pred[]{:T(512)S(6)} %eq.51, bf16[2,2,64,2048]{3,2,1,0:T(8,128)(2,1)S(1)} %pad_maximum_fusion.5), kind=kLoop, calls=%fused_computation.100 | loop fusion | flops 1048576 | bytes 4194305 | tf_op jit(solution)/shard_map/jit(_where)/select_n | solution.py:53
  69.8 0.6 collective-permute-start.3
  70.8 1.9 %collective-permute-done.7 = bf16[8,128,1024]{2,1,0:T(8,128)(2,1)} collective-permute-done((bf16[8,128,1024]{2,1,0:T(8,128)(2,1)}, bf16[8,128,1024]{2,1,0:T(8,128)(2,1)}, u32[]{:S(2)}, u32[]{:S(2)}) %collective-permute-start.7) | collective-permute-done | bytes 2097184 | tf_op jit(solution)/shard_map/ppermute | solution.py:51
  72.6 2.5 %broadcast_select_fusion.1 = (bf16[8,128,1024]{2,1,0:T(8,128)(2,1)S(1)}, bf16[8,128,1024]{2,1,0:T(8,128)(2,1)S(1)}) fusion(bf16[8,128,1024]{2,1,0:T(8,128)(2,1)} %collective-permute-done.7, pred[]{:T(512)S(6)} %eq.50, bf16[2,2,2,128,1024]{4,3,2,1,0:T(8,128)(2,1)} %pad_maximum_fusion.2), kind=kLoop, calls=%fused_computation.11 | loop fusion | flops 2097152 | bytes 8388609 | tf_op jit(solution)/shard_map/jit(_where)/select_n | solution.py:53
  75.5 0.7 fusion.21
  76.8 0.7 copy-done.1
  78.6 0.8 fusion
  79.4 0.9 fusion.94
  80.3 3.2 %collective-permute-start.8 = (bf16[2,32,2048]{2,1,0:T(8,128)(2,1)}, bf16[2,32,2048]{2,1,0:T(8,128)(2,1)S(1)}, u32[]{:S(2)}, u32[]{:S(2)}) collective-permute-start(bf16[2,32,2048]{2,1,0:T(8,128)(2,1)} %get-tuple-element.32), channel_id=1, source_target_pairs={{0,16},{1,17},{2,18},{3,19},{4,20},{5,21},{6,22},{7,23},{8,24},{9,... | collective-permute-start | bytes 786440 | tf_op jit(solution)/shard_map/ppermute | solution.py:23
  83.5 1.3 collective-permute-start.9
  84.8 2.0 %fusion.19 = bf16[128,1024]{0,1:T(8,128)(2,1)} fusion(bf16[1024,2048]{1,0:T(8,128)(2,1)S(1)} %bitcast.260, bf16[128,2048]{1,0:T(8,128)(2,1)S(1)} %bitcast.287), kind=kOutput, calls=%fused_computation.60 | convolution fusion | flops 537001984 | bytes 4980736 | tf_op jit(solution)/shard_map/transpose(jvp())/dot_general | solution.py:102
  86.8 1.1 copy.72
  88.0 2.4 %collective-permute-done.8 = bf16[2,32,2048]{2,1,0:T(8,128)(2,1)S(1)} collective-permute-done((bf16[2,32,2048]{2,1,0:T(8,128)(2,1)}, bf16[2,32,2048]{2,1,0:T(8,128)(2,1)S(1)}, u32[]{:S(2)}, u32[]{:S(2)}) %collective-permute-start.8) | collective-permute-done | bytes 262176 | tf_op jit(solution)/shard_map/ppermute | solution.py:23
  90.4 4.8 %collective-permute-done.9 = bf16[2,32,2048]{2,1,0:T(8,128)(2,1)S(1)} collective-permute-done((bf16[2,32,2048]{2,1,0:T(8,128)(2,1)}, bf16[2,32,2048]{2,1,0:T(8,128)(2,1)S(1)}, u32[]{:S(2)}, u32[]{:S(2)}) %collective-permute-start.9) | collective-permute-done | bytes 262176 | tf_op jit(solution)/shard_map/ppermute | solution.py:23
  95.8 0.8 fusion.20
  98.3 0.6 fusion.31
  99.3 1.6 %collective-permute-start.10 = (bf16[2,32,2048]{2,1,0:T(8,128)(2,1)S(1)}, bf16[2,32,2048]{2,1,0:T(8,128)(2,1)S(1)}, u32[]{:S(2)}, u32[]{:S(2)}) collective-permute-start(bf16[2,32,2048]{2,1,0:T(8,128)(2,1)S(1)} %get-tuple-element.29), channel_id=1, source_target_pairs={{16,0},{17,1},{18,2},{19,3},{20,4},{21,5},{22,6},{23,7},{24,8},{25... | collective-permute-start | bytes 786440 | tf_op jit(solution)/shard_map/ppermute | solution.py:23
  100.8 1.5 %collective-permute-start.11 = (bf16[2,32,2048]{2,1,0:T(8,128)(2,1)S(1)}, bf16[2,32,2048]{2,1,0:T(8,128)(2,1)S(1)}, u32[]{:S(2)}, u32[]{:S(2)}) collective-permute-start(bf16[2,32,2048]{2,1,0:T(8,128)(2,1)S(1)} %get-tuple-element.28), channel_id=1, source_target_pairs={{16,0},{17,1},{18,2},{19,3},{20,4},{21,5},{22,6},{23,7},{24,8},{25... | collective-permute-start | bytes 786440 | tf_op jit(solution)/shard_map/ppermute | solution.py:23
  102.3 1.5 %convolution_convert_fusion = bf16[128,2048]{1,0:T(8,128)(2,1)S(1)} fusion(bf16[2048,1024]{1,0:T(8,128)(2,1)S(1)} %bitcast.257, bf16[16,8,8,128]{3,2,1,0:T(8,128)(2,1)S(1)} %bitcast.281), kind=kOutput, calls=%fused_computation.4 | convolution fusion | flops 537133056 | bytes 4980736 | tf_op jit(solution)/shard_map/transpose(jvp())/dot_general | solution.py:91
  103.8 6.8 %collective-permute-done.10 = bf16[2,32,2048]{2,1,0:T(8,128)(2,1)S(1)} collective-permute-done((bf16[2,32,2048]{2,1,0:T(8,128)(2,1)S(1)}, bf16[2,32,2048]{2,1,0:T(8,128)(2,1)S(1)}, u32[]{:S(2)}, u32[]{:S(2)}) %collective-permute-start.10) | collective-permute-done | bytes 262176 | tf_op jit(solution)/shard_map/ppermute | solution.py:23
  110.7 4.0 %collective-permute-done.11 = bf16[2,32,2048]{2,1,0:T(8,128)(2,1)S(1)} collective-permute-done((bf16[2,32,2048]{2,1,0:T(8,128)(2,1)S(1)}, bf16[2,32,2048]{2,1,0:T(8,128)(2,1)S(1)}, u32[]{:S(2)}, u32[]{:S(2)}) %collective-permute-start.11) | collective-permute-done | bytes 262176 | tf_op jit(solution)/shard_map/ppermute | solution.py:23
  114.7 1.5 %fusion.22 = bf16[16,8,8,128]{3,1,2,0:T(8,128)(2,1)S(1)} fusion(bf16[128,2048]{1,0:T(8,128)(2,1)S(1)} %bitcast.274, bf16[1024,2048]{1,0:T(8,128)(2,1)S(1)} %bitcast.261), kind=kOutput, calls=%fused_computation.63 | convolution fusion | flops 537001984 | bytes 4980736 | tf_op jit(solution)/shard_map/transpose(jvp())/dot_general | solution.py:102
  117.7 1.5 %convolution_convert_fusion.1 = bf16[128,2048]{1,0:T(8,128)(2,1)S(1)} fusion(bf16[2048,1024]{1,0:T(8,128)(2,1)S(1)} %bitcast.258, bf16[16,8,8,128]{3,2,1,0:T(8,128)(2,1)S(1)} %bitcast.284), kind=kOutput, calls=%fused_computation.5 | convolution fusion | flops 537133056 | bytes 4980736 | tf_op jit(solution)/shard_map/transpose(jvp())/dot_general | solution.py:91
  119.3 1.3 fusion.36
  120.7 1.2 collective-permute-done.12
  121.9 1.5 %collective-permute-start.13 = (f32[2048]{0:T(1024)S(1)}, f32[2048]{0:T(1024)S(1)}, u32[]{:S(2)}, u32[]{:S(2)}) collective-permute-start(f32[2048]{0:T(1024)S(1)} %add.91), channel_id=1, source_target_pairs={{0,2},{1,3},{2,0},{3,1},{4,6},{5,7},{6,4},{7,5},{8,10},{9,11},{10,... | collective-permute-start | bytes 24584 | tf_op jit(solution)/shard_map/ppermute | solution.py:69
  123.4 2.1 %collective-permute-done.13 = f32[2048]{0:T(1024)S(1)} collective-permute-done((f32[2048]{0:T(1024)S(1)}, f32[2048]{0:T(1024)S(1)}, u32[]{:S(2)}, u32[]{:S(2)}) %collective-permute-start.13) | collective-permute-done | bytes 8224 | tf_op jit(solution)/shard_map/ppermute | solution.py:69
  125.6 1.8 %collective-permute-start.14 = (f32[2048]{0:T(1024)S(1)}, f32[2048]{0:T(1024)S(1)}, u32[]{:S(2)}, u32[]{:S(2)}) collective-permute-start(f32[2048]{0:T(1024)S(1)} %add.92), channel_id=1, source_target_pairs={{0,4},{1,5},{2,6},{3,7},{4,0},{5,1},{6,2},{7,3},{8,12},{9,13},{10,... | collective-permute-start | bytes 24584 | tf_op jit(solution)/shard_map/ppermute | solution.py:69
  127.3 1.9 %collective-permute-done.14 = f32[2048]{0:T(1024)S(1)} collective-permute-done((f32[2048]{0:T(1024)S(1)}, f32[2048]{0:T(1024)S(1)}, u32[]{:S(2)}, u32[]{:S(2)}) %collective-permute-start.14) | collective-permute-done | bytes 8224 | tf_op jit(solution)/shard_map/ppermute | solution.py:69
  129.2 3.3 %collective-permute-start.15 = (f32[2048]{0:T(1024)S(1)}, f32[2048]{0:T(1024)S(1)}, u32[]{:S(2)}, u32[]{:S(2)}) collective-permute-start(f32[2048]{0:T(1024)S(1)} %add.93), channel_id=1, source_target_pairs={{0,8},{1,9},{2,10},{3,11},{4,12},{5,13},{6,14},{7,15},{8,0},{9,1},... | collective-permute-start | bytes 24584 | tf_op jit(solution)/shard_map/ppermute | solution.py:69
  132.5 1.9 %fusion.54 = bf16[1,4,1,32,2048]{4,3,2,1,0:T(8,128)(2,1)} fusion(f32[4,32,2048]{2,1,0:T(8,128)S(1)} %get-tuple-element.49, bf16[4,32,2048]{2,1,0:T(8,128)(2,1)S(1)} %constant_dynamic-update-slice_fusion, bf16[4,32,1024]{2,1,0:T(8,128)(2,1)S(1)} %bitcast.278, bf16[4,32,1024]{2,1,0:T(8,128)(2,1)S(1)} %bitcast.276, bf16[4,1,32,2048]{3,2,1,0:T(8,128)(2,1)S(1)} %copy-done.6, ...), kind=kLoop, calls=%fused_computation.105 | loop fusion | flops 8912896 | bytes 4729346
  134.3 0.6 add.94
  (91 shorter events, 7.6 us)
Async XLA Ops:
  0.6 45.5 %copy-start = (bf16[16,2048]{1,0:T(8,128)(2,1)S(1)}, bf16[16,2048]{1,0:T(8,128)(2,1)}, u32[]{:S(2)}) copy-start(bf16[16,2048]{1,0:T(8,128)(2,1)} %param.11) | copy-start | bytes 196612
  0.6 29.4 %copy-start.5 = (bf16[4,1,32,2048]{3,2,1,0:T(8,128)(2,1)S(1)}, bf16[4,1,32,2048]{3,2,1,0:T(8,128)(2,1)}, u32[]{:S(2)}) copy-start(bf16[4,1,32,2048]{3,2,1,0:T(8,128)(2,1)} %param.8) | copy-start | bytes 1572868
  0.7 22.7 %collective-permute-start.4 = (bf16[1,128,1024]{2,1,0:T(8,128)(2,1)}, bf16[1,128,1024]{2,1,0:T(8,128)(2,1)S(1)}, u32[]{:S(2)}, u32[]{:S(2)}) collective-permute-start(bf16[1,128,1024]{2,1,0:T(8,128)(2,1)} %param.12), channel_id=1, source_target_pairs={{0,8},{1,9},{2,10},{3,11},{4,12},{5,13},{6,14},{7,15},{8,0},{9,1},... | collective-permute-start | bytes 786440 | tf_op jit(solution)/shard_map/ppermute | solution.py:51
  4.8 23.4 %collective-permute-start = (bf16[1,64,2048]{2,1,0:T(8,128)(2,1)}, bf16[1,64,2048]{2,1,0:T(8,128)(2,1)S(1)}, u32[]{:S(2)}, u32[]{:S(2)}) collective-permute-start(bf16[1,64,2048]{2,1,0:T(8,128)(2,1)} %param.13), channel_id=1, source_target_pairs={{0,8},{1,9},{2,10},{3,11},{4,12},{5,13},{6,14},{7,15},{8,0},{9,1},... | collective-permute-start | bytes 786440 | tf_op jit(solution)/shard_map/ppermute | solution.py:51
  24.4 12.3 %collective-permute-start.5 = (bf16[2,128,1024]{2,1,0:T(8,128)(2,1)S(1)}, bf16[2,128,1024]{2,1,0:T(8,128)(2,1)S(1)}, u32[]{:S(2)}, u32[]{:S(2)}) collective-permute-start(bf16[2,128,1024]{2,1,0:T(8,128)(2,1)S(1)} %pad_maximum_fusion.6), channel_id=1, source_target_pairs={{0,2},{1,3},{2,0},{3,1},{4,6},{5,7},{6,4},{7,5},{8,10},{9,11},{10,... | collective-permute-start | bytes 1572872 | tf_op jit(solution)/shard_map/ppermute | solution.py:51
  29.2 14.9 %collective-permute-start.1 = (bf16[2,64,2048]{2,1,0:T(8,128)(2,1)S(1)}, bf16[2,64,2048]{2,1,0:T(8,128)(2,1)S(1)}, u32[]{:S(2)}, u32[]{:S(2)}) collective-permute-start(bf16[2,64,2048]{2,1,0:T(8,128)(2,1)S(1)} %pad_maximum_fusion.7), channel_id=1, source_target_pairs={{0,4},{1,5},{2,6},{3,7},{4,0},{5,1},{6,2},{7,3},{8,12},{9,13},{10,... | collective-permute-start | bytes 1572872 | tf_op jit(solution)/shard_map/ppermute | solution.py:51
  30.3 15.7 %copy-start.12 = (s32[4,1,16,2]{2,3,1,0:T(2,128)S(1)}, s32[4,1,16,2]{2,3,1,0:T(2,128)}, u32[]{:S(2)}) copy-start(s32[4,1,16,2]{2,3,1,0:T(2,128)} %param.10) | copy-start | bytes 1540
  37.9 27.1 %collective-permute-start.6 = (bf16[4,128,1024]{2,1,0:T(8,128)(2,1)}, bf16[4,128,1024]{2,1,0:T(8,128)(2,1)}, u32[]{:S(2)}, u32[]{:S(2)}) collective-permute-start(bf16[4,128,1024]{2,1,0:T(8,128)(2,1)} %bitcast.24), channel_id=1, source_target_pairs={{0,4},{1,5},{2,6},{3,7},{4,0},{5,1},{6,2},{7,3},{8,12},{9,13},{10,... | collective-permute-start | bytes 3145736 | tf_op jit(solution)/shard_map/ppermute | solution.py:51
  44.3 23.9 %collective-permute-start.2 = (bf16[4,64,2048]{2,1,0:T(8,128)(2,1)S(1)}, bf16[4,64,2048]{2,1,0:T(8,128)(2,1)}, u32[]{:S(2)}, u32[]{:S(2)}) collective-permute-start(bf16[4,64,2048]{2,1,0:T(8,128)(2,1)S(1)} %bitcast.269), channel_id=1, source_target_pairs={{0,2},{1,3},{2,0},{3,1},{4,6},{5,7},{6,4},{7,5},{8,10},{9,11},{10,... | collective-permute-start | bytes 3145736 | tf_op jit(solution)/shard_map/ppermute | solution.py:51
  46.5 21.6 %copy-start.13 = (s32[4,1,32]{2,1,0:T(1,128)S(1)}, s32[4,1,32]{2,1,0:T(1,128)}, u32[]{:S(2)}) copy-start(s32[4,1,32]{2,1,0:T(1,128)} %param.9) | copy-start | bytes 1540
  68.1 4.5 %collective-permute-start.7 = (bf16[8,128,1024]{2,1,0:T(8,128)(2,1)}, bf16[8,128,1024]{2,1,0:T(8,128)(2,1)}, u32[]{:S(2)}, u32[]{:S(2)}) collective-permute-start(bf16[8,128,1024]{2,1,0:T(8,128)(2,1)} %bitcast.29), channel_id=1, source_target_pairs={{0,1},{1,0},{2,3},{3,2},{4,5},{5,4},{6,7},{7,6},{8,9},{9,8},{10,11... | collective-permute-start | bytes 6291464 | tf_op jit(solution)/shard_map/ppermute | solution.py:51
  68.2 2.2 %copy-start.9 = (f32[1,2048]{1,0:T(1,128)S(1)}, f32[1,2048]{1,0:T(1,128)}, u32[]{:S(2)}) copy-start(f32[1,2048]{1,0:T(1,128)} %param.14) | copy-start | bytes 24580
  69.8 6.6 %collective-permute-start.3 = (bf16[8,64,2048]{2,1,0:T(8,128)(2,1)S(1)}, bf16[8,64,2048]{2,1,0:T(8,128)(2,1)S(1)}, u32[]{:S(2)}, u32[]{:S(2)}) collective-permute-start(bf16[8,64,2048]{2,1,0:T(8,128)(2,1)S(1)} %bitcast.262), channel_id=1, source_target_pairs={{0,1},{1,0},{2,3},{3,2},{4,5},{5,4},{6,7},{7,6},{8,9},{9,8},{10,11... | collective-permute-start | bytes 6291464 | tf_op jit(solution)/shard_map/ppermute | solution.py:51
  70.6 7.3 %copy-start.10 = (bf16[4,4,8,8,128]{4,3,2,1,0:T(8,128)(2,1)}, bf16[4,4,8,8,128]{4,3,2,1,0:T(8,128)(2,1)S(1)}, u32[]{:S(2)}) copy-start(bf16[4,4,8,8,128]{4,3,2,1,0:T(8,128)(2,1)S(1)} %get-tuple-element.34) | copy-start | bytes 786436
  75.5 1.9 %copy-start.1 = (bf16[2,2,2,2,128,1024]{5,4,3,2,1,0:T(8,128)(2,1)}, bf16[2,2,2,2,128,1024]{5,4,3,2,1,0:T(8,128)(2,1)S(1)}, u32[]{:S(2)}) copy-start(bf16[2,2,2,2,128,1024]{5,4,3,2,1,0:T(8,128)(2,1)S(1)} %pad_maximum_fusion) | copy-start | bytes 12582916
  77.9 6.9 %copy-start.3 = (bf16[2,2,2,2,64,2048]{5,4,3,2,1,0:T(8,128)(2,1)}, bf16[2,2,2,2,64,2048]{5,4,3,2,1,0:T(8,128)(2,1)S(1)}, u32[]{:S(2)}) copy-start(bf16[2,2,2,2,64,2048]{5,4,3,2,1,0:T(8,128)(2,1)S(1)} %pad_maximum_fusion.1) | copy-start | bytes 12582916
  78.2 2.1 %copy-start.7 = (f32[4,8,32,32]{2,3,1,0:T(8,128)}, f32[4,8,32,32]{2,3,1,0:T(8,128)S(1)}, u32[]{:S(2)}) copy-start(f32[4,8,32,32]{2,3,1,0:T(8,128)S(1)} %get-tuple-element.47) | copy-start | bytes 393220
  78.2 6.6 %copy-start.6 = (bf16[4,1,32,2048]{3,2,1,0:T(8,128)(2,1)S(1)}, bf16[4,1,32,2048]{3,2,1,0:T(8,128)(2,1)}, u32[]{:S(2)}) copy-start(bf16[4,1,32,2048]{3,2,1,0:T(8,128)(2,1)} %param.15) | copy-start | bytes 1572868
  80.3 10.2 %collective-permute-start.8 = (bf16[2,32,2048]{2,1,0:T(8,128)(2,1)}, bf16[2,32,2048]{2,1,0:T(8,128)(2,1)S(1)}, u32[]{:S(2)}, u32[]{:S(2)}) collective-permute-start(bf16[2,32,2048]{2,1,0:T(8,128)(2,1)} %get-tuple-element.32), channel_id=1, source_target_pairs={{0,16},{1,17},{2,18},{3,19},{4,20},{5,21},{6,22},{7,23},{8,24},{9,... | collective-permute-start | bytes 786440 | tf_op jit(solution)/shard_map/ppermute | solution.py:23
  83.5 11.8 %collective-permute-start.9 = (bf16[2,32,2048]{2,1,0:T(8,128)(2,1)}, bf16[2,32,2048]{2,1,0:T(8,128)(2,1)S(1)}, u32[]{:S(2)}, u32[]{:S(2)}) collective-permute-start(bf16[2,32,2048]{2,1,0:T(8,128)(2,1)} %get-tuple-element.33), channel_id=1, source_target_pairs={{0,16},{1,17},{2,18},{3,19},{4,20},{5,21},{6,22},{7,23},{8,24},{9,... | collective-permute-start | bytes 786440 | tf_op jit(solution)/shard_map/ppermute | solution.py:23
  87.9 7.9 %copy-start.2 = (bf16[2,2,2,2,128,1024]{5,4,3,2,1,0:T(8,128)(2,1)S(1)}, bf16[2,2,2,2,128,1024]{5,4,3,2,1,0:T(8,128)(2,1)}, u32[]{:S(2)}) copy-start(bf16[2,2,2,2,128,1024]{5,4,3,2,1,0:T(8,128)(2,1)} %copy-done.1) | copy-start | bytes 12582916
  98.9 15.8 %copy-start.4 = (bf16[2,2,2,2,64,2048]{5,4,3,2,1,0:T(8,128)(2,1)S(1)}, bf16[2,2,2,2,64,2048]{5,4,3,2,1,0:T(8,128)(2,1)}, u32[]{:S(2)}) copy-start(bf16[2,2,2,2,64,2048]{5,4,3,2,1,0:T(8,128)(2,1)} %copy-done.3) | copy-start | bytes 12582916
  99.3 11.4 %collective-permute-start.10 = (bf16[2,32,2048]{2,1,0:T(8,128)(2,1)S(1)}, bf16[2,32,2048]{2,1,0:T(8,128)(2,1)S(1)}, u32[]{:S(2)}, u32[]{:S(2)}) collective-permute-start(bf16[2,32,2048]{2,1,0:T(8,128)(2,1)S(1)} %get-tuple-element.29), channel_id=1, source_target_pairs={{16,0},{17,1},{18,2},{19,3},{20,4},{21,5},{22,6},{23,7},{24,8},{25... | collective-permute-start | bytes 786440 | tf_op jit(solution)/shard_map/ppermute | solution.py:23
  100.8 13.9 %collective-permute-start.11 = (bf16[2,32,2048]{2,1,0:T(8,128)(2,1)S(1)}, bf16[2,32,2048]{2,1,0:T(8,128)(2,1)S(1)}, u32[]{:S(2)}, u32[]{:S(2)}) collective-permute-start(bf16[2,32,2048]{2,1,0:T(8,128)(2,1)S(1)} %get-tuple-element.28), channel_id=1, source_target_pairs={{16,0},{17,1},{18,2},{19,3},{20,4},{21,5},{22,6},{23,7},{24,8},{25... | collective-permute-start | bytes 786440 | tf_op jit(solution)/shard_map/ppermute | solution.py:23
  103.8 12.5 %copy-start.8 = (f32[4,8,32,32]{2,3,1,0:T(8,128)S(1)}, f32[4,8,32,32]{2,3,1,0:T(8,128)}, u32[]{:S(2)}) copy-start(f32[4,8,32,32]{2,3,1,0:T(8,128)} %copy-done.7) | copy-start | bytes 393220
  114.7 2.2 %copy-start.11 = (bf16[4,4,8,8,128]{4,3,2,1,0:T(8,128)(2,1)S(1)}, bf16[4,4,8,8,128]{4,3,2,1,0:T(8,128)(2,1)}, u32[]{:S(2)}) copy-start(bf16[4,4,8,8,128]{4,3,2,1,0:T(8,128)(2,1)} %copy-done.10) | copy-start | bytes 786436
  120.7 1.2 collective-permute-start.12
  121.9 3.7 %collective-permute-start.13 = (f32[2048]{0:T(1024)S(1)}, f32[2048]{0:T(1024)S(1)}, u32[]{:S(2)}, u32[]{:S(2)}) collective-permute-start(f32[2048]{0:T(1024)S(1)} %add.91), channel_id=1, source_target_pairs={{0,2},{1,3},{2,0},{3,1},{4,6},{5,7},{6,4},{7,5},{8,10},{9,11},{10,... | collective-permute-start | bytes 24584 | tf_op jit(solution)/shard_map/ppermute | solution.py:69
  125.6 3.7 %collective-permute-start.14 = (f32[2048]{0:T(1024)S(1)}, f32[2048]{0:T(1024)S(1)}, u32[]{:S(2)}, u32[]{:S(2)}) collective-permute-start(f32[2048]{0:T(1024)S(1)} %add.92), channel_id=1, source_target_pairs={{0,4},{1,5},{2,6},{3,7},{4,0},{5,1},{6,2},{7,3},{8,12},{9,13},{10,... | collective-permute-start | bytes 24584 | tf_op jit(solution)/shard_map/ppermute | solution.py:69
  129.2 5.1 %collective-permute-start.15 = (f32[2048]{0:T(1024)S(1)}, f32[2048]{0:T(1024)S(1)}, u32[]{:S(2)}, u32[]{:S(2)}) collective-permute-start(f32[2048]{0:T(1024)S(1)} %add.93), channel_id=1, source_target_pairs={{0,8},{1,9},{2,10},{3,11},{4,12},{5,13},{6,14},{7,15},{8,0},{9,1},... | collective-permute-start | bytes 24584 | tf_op jit(solution)/shard_map/ppermute | solution.py:69

commit v14 on v12

--- a/solution.py
+++ b/solution.py
@@ -135,8 +135,8 @@
         else:
             layer_input = got_input
         if tick < half_sections:
-            output = encoder_map(layer_input, gain_vector)
-            saved_inputs[tick] = (layer_input, None)
+            output, pull = jax.vjp(encoder_map, layer_input, gain_vector)
+            saved_inputs[tick] = pull
             if tick == half_sections - 1:
                 got_memory = send_to(output, "section", tick, tick + 1)
             else:
@@ -159,9 +159,9 @@
     for tick in range(section_count):
         run = section_count - 1 - tick
         out_grad = cotangent.reshape(act_shape) if run == section_count - 1 else got_grad
-        layer_input, layer_memory = saved_inputs[run]
         mine = section_index == run
         if run >= half_sections:
+            layer_input, layer_memory = saved_inputs[run]
             _, pull = jax.vjp(decoder_map, layer_input, layer_memory, gain_vector)
             input_grad, memory_grad, gain_grad = pull(out_grad)
             if got_memory_grad is not None:
@@ -173,8 +173,7 @@
                     (input_grad, memory_grad), "section", run, run - 1
                 )
         else:
-            _, pull = jax.vjp(encoder_map, layer_input, gain_vector)
-            input_grad, gain_grad = pull(out_grad)
+            input_grad, gain_grad = saved_inputs[run](out_grad)
             if run > 0:
                 got_grad = send_to(input_grad, "section", run, run - 1)
         grads_out = jnp.where(mine, input_grad, grads_out)

time: 135 us -> 135 us (level)
  no operation moved by 1% of the time
where the time goes in v14:
time: 135 us
  waiting for transfers between devices  77.1 us (57%)
  starting transfers between devices  22.4 us (17%)
  other arithmetic  17.6 us (13%)
  matrix products  13.3 us (10%)
  local copies, waits for them, and re-layouts  3.16 us (2%)
    ppermute x8, waiting for transfers between devices, butterfly_gathers(): lax.ppermute(held[which], axis, [(j, j ^ step) for j in range(size)])  51.7 us
    ppermute x2, waiting for transfers between devices, send_to(): return lax.ppermute(arrays, axis, [(source, target)])  20.2 us
    ppermute x8, starting transfers between devices, butterfly_gathers(): lax.ppermute(held[which], axis, [(j, j ^ step) for j in range(size)])  10.8 us
    select_n x6, other arithmetic, butterfly_gathers(): low = jnp.where(upper, other, held[which])  7.93 us
    ppermute x4, starting transfers between devices, butterfly_sum(): lax.ppermute(value, axis, [(j, j ^ step) for j in range(size)])  6.64 us
    ppermute x4, waiting for transfers between devices, butterfly_sum(): lax.ppermute(value, axis, [(j, j ^ step) for j in range(size)])  5.16 us
    dot_general x3, matrix products, attend_layer(): update = jnp.dot(mixed, output_weight, preferred_element_type=jnp.float32)  5.1 us
    ppermute x2, starting transfers between devices, send_to(): return lax.ppermute(arrays, axis, [(source, target)])  4.97 us
  transfers between devices with their start and end apart: 14, of which 11 were waited for; matrix products, arithmetic and copies ran while one was open for 15% of the time, Pallas kernels for 0%

profile of v14, /device:TPU:0, one launch (start us, length us, event | category | flops | bytes accessed | tf_op | source)
XLA Modules:
  0.0 134.8 jit_solution(12172896925434492826)
XLA Ops:
  0.7 4.1 %collective-permute-start.4 = (bf16[1,128,1024]{2,1,0:T(8,128)(2,1)}, bf16[1,128,1024]{2,1,0:T(8,128)(2,1)S(1)}, u32[]{:S(2)}, u32[]{:S(2)}) collective-permute-start(bf16[1,128,1024]{2,1,0:T(8,128)(2,1)} %param.12), channel_id=1, source_target_pairs={{0,8},{1,9},{2,10},{3,11},{4,12},{5,13},{6,14},{7,15},{8,0},{9,1},... | collective-permute-start | bytes 786440 | tf_op jit(solution)/shard_map/ppermute | solution.py:37
  4.8 18.5 %collective-permute-done.4 = bf16[1,128,1024]{2,1,0:T(8,128)(2,1)S(1)} collective-permute-done((bf16[1,128,1024]{2,1,0:T(8,128)(2,1)}, bf16[1,128,1024]{2,1,0:T(8,128)(2,1)S(1)}, u32[]{:S(2)}, u32[]{:S(2)}) %collective-permute-start.4) | collective-permute-done | bytes 262176 | tf_op jit(solution)/shard_map/ppermute | solution.py:37
  23.3 1.0 broadcast_select_fusion.9
  24.4 1.9 %collective-permute-start.5 = (bf16[2,128,1024]{2,1,0:T(8,128)(2,1)S(1)}, bf16[2,128,1024]{2,1,0:T(8,128)(2,1)S(1)}, u32[]{:S(2)}, u32[]{:S(2)}) collective-permute-start(bf16[2,128,1024]{2,1,0:T(8,128)(2,1)S(1)} %pad_maximum_fusion.6), channel_id=1, source_target_pairs={{0,2},{1,3},{2,0},{3,1},{4,6},{5,7},{6,4},{7,5},{8,10},{9,11},{10,... | collective-permute-start | bytes 1572872 | tf_op jit(solution)/shard_map/ppermute | solution.py:37
  26.3 1.8 %collective-permute-done = bf16[1,64,2048]{2,1,0:T(8,128)(2,1)S(1)} collective-permute-done((bf16[1,64,2048]{2,1,0:T(8,128)(2,1)}, bf16[1,64,2048]{2,1,0:T(8,128)(2,1)S(1)}, u32[]{:S(2)}, u32[]{:S(2)}) %collective-permute-start) | collective-permute-done | bytes 262176 | tf_op jit(solution)/shard_map/ppermute | solution.py:37
  28.1 1.0 broadcast_select_fusion.11
  29.2 0.9 collective-permute-start.1
  30.3 6.5 %collective-permute-done.5 = bf16[2,128,1024]{2,1,0:T(8,128)(2,1)S(1)} collective-permute-done((bf16[2,128,1024]{2,1,0:T(8,128)(2,1)S(1)}, bf16[2,128,1024]{2,1,0:T(8,128)(2,1)S(1)}, u32[]{:S(2)}, u32[]{:S(2)}) %collective-permute-start.5) | collective-permute-done | bytes 524320 | tf_op jit(solution)/shard_map/ppermute | solution.py:37
  36.8 1.1 pad_maximum_fusion.4
  37.9 1.6 %collective-permute-start.6 = (bf16[4,128,1024]{2,1,0:T(8,128)(2,1)}, bf16[4,128,1024]{2,1,0:T(8,128)(2,1)}, u32[]{:S(2)}, u32[]{:S(2)}) collective-permute-start(bf16[4,128,1024]{2,1,0:T(8,128)(2,1)} %bitcast.24), channel_id=1, source_target_pairs={{0,4},{1,5},{2,6},{3,7},{4,0},{5,1},{6,2},{7,3},{8,12},{9,13},{10,... | collective-permute-start | bytes 3145736 | tf_op jit(solution)/shard_map/ppermute | solution.py:37
  39.4 4.7 %collective-permute-done.1 = bf16[2,64,2048]{2,1,0:T(8,128)(2,1)S(1)} collective-permute-done((bf16[2,64,2048]{2,1,0:T(8,128)(2,1)S(1)}, bf16[2,64,2048]{2,1,0:T(8,128)(2,1)S(1)}, u32[]{:S(2)}, u32[]{:S(2)}) %collective-permute-start.1) | collective-permute-done | bytes 524320 | tf_op jit(solution)/shard_map/ppermute | solution.py:37
  44.3 1.6 %collective-permute-start.2 = (bf16[4,64,2048]{2,1,0:T(8,128)(2,1)S(1)}, bf16[4,64,2048]{2,1,0:T(8,128)(2,1)}, u32[]{:S(2)}, u32[]{:S(2)}) collective-permute-start(bf16[4,64,2048]{2,1,0:T(8,128)(2,1)S(1)} %bitcast.269), channel_id=1, source_target_pairs={{0,2},{1,3},{2,0},{3,1},{4,6},{5,7},{6,4},{7,5},{8,10},{9,11},{10,... | collective-permute-start | bytes 3145736 | tf_op jit(solution)/shard_map/ppermute | solution.py:37
  46.1 0.4 multiply_reduce_fusion
  46.5 18.4 %collective-permute-done.6 = bf16[4,128,1024]{2,1,0:T(8,128)(2,1)} collective-permute-done((bf16[4,128,1024]{2,1,0:T(8,128)(2,1)}, bf16[4,128,1024]{2,1,0:T(8,128)(2,1)}, u32[]{:S(2)}, u32[]{:S(2)}) %collective-permute-start.6) | collective-permute-done | bytes 1048608 | tf_op jit(solution)/shard_map/ppermute | solution.py:37
  64.9 1.7 %broadcast_select_fusion.5 = (bf16[4,128,1024]{2,1,0:T(8,128)(2,1)S(1)}, bf16[4,128,1024]{2,1,0:T(8,128)(2,1)S(1)}) fusion(bf16[4,128,1024]{2,1,0:T(8,128)(2,1)} %collective-permute-done.6, pred[]{:T(512)S(6)} %eq.52, bf16[2,2,128,1024]{3,2,1,0:T(8,128)(2,1)} %pad_maximum_fusion.4), kind=kLoop, calls=%fused_computation.98 | loop fusion | flops 1048576 | bytes 4194305 | tf_op jit(solution)/shard_map/jit(_where)/select_n | solution.py:39
  66.6 1.5 %pad_maximum_fusion.2 = bf16[2,2,2,128,1024]{4,3,2,1,0:T(8,128)(2,1)} fusion(bf16[2,1,2,128,1024]{4,3,2,1,0:T(8,128)(2,1)S(1)} %bitcast.271, bf16[2,1,2,128,1024]{4,3,2,1,0:T(8,128)(2,1)S(1)} %bitcast.270), kind=kLoop, calls=%fused_computation.8 | loop fusion | flops 1048576 | bytes 4194304 | tf_op jit(solution)/shard_map/stack | solution.py:43
  68.2 1.4 %broadcast_select_fusion.7 = (bf16[4,64,2048]{2,1,0:T(8,128)(2,1)S(1)}, bf16[4,64,2048]{2,1,0:T(8,128)(2,1)S(1)}) fusion(bf16[4,64,2048]{2,1,0:T(8,128)(2,1)} %collective-permute-done.2, pred[]{:T(512)S(6)} %eq.51, bf16[2,2,64,2048]{3,2,1,0:T(8,128)(2,1)S(1)} %pad_maximum_fusion.5), kind=kLoop, calls=%fused_computation.100 | loop fusion | flops 1048576 | bytes 4194305 | tf_op jit(solution)/shard_map/jit(_where)/select_n | solution.py:39
  69.7 0.6 collective-permute-start.3
  70.8 1.9 %collective-permute-done.7 = bf16[8,128,1024]{2,1,0:T(8,128)(2,1)} collective-permute-done((bf16[8,128,1024]{2,1,0:T(8,128)(2,1)}, bf16[8,128,1024]{2,1,0:T(8,128)(2,1)}, u32[]{:S(2)}, u32[]{:S(2)}) %collective-permute-start.7) | collective-permute-done | bytes 2097184 | tf_op jit(solution)/shard_map/ppermute | solution.py:37
  72.6 2.5 %broadcast_select_fusion.1 = (bf16[8,128,1024]{2,1,0:T(8,128)(2,1)S(1)}, bf16[8,128,1024]{2,1,0:T(8,128)(2,1)S(1)}) fusion(bf16[8,128,1024]{2,1,0:T(8,128)(2,1)} %collective-permute-done.7, pred[]{:T(512)S(6)} %eq.50, bf16[2,2,2,128,1024]{4,3,2,1,0:T(8,128)(2,1)} %pad_maximum_fusion.2), kind=kLoop, calls=%fused_computation.11 | loop fusion | flops 2097152 | bytes 8388609 | tf_op jit(solution)/shard_map/jit(_where)/select_n | solution.py:39
  75.1 0.4 pad_maximum_fusion
  75.5 0.7 fusion.21
  76.3 0.4 broadcast_select_fusion.3
  76.8 0.7 copy-done.1
  77.5 0.4 pad_maximum_fusion.1
  78.5 0.5 copy-done.7
  79.0 1.6 %fusion = bf16[4,32,2048]{2,1,0:T(8,128)(2,1)} fusion(bf16[1024,2048,1]{1,0,2:T(8,128)(2,1)S(1)} %bitcast.259, bf16[4,1,32,2048]{3,2,1,0:T(8,128)(2,1)S(1)} %copy-done.5, bf16[4,8,4,8,128]{4,3,2,1,0:T(8,128)(2,1)S(1)} %fusion.23), kind=kOutput, calls=%fused_computation.3 | convolution fusion | flops 537657344 | bytes 5505024 | tf_op jit(solution)/shard_map/jvp()/dot_general | solution.py:88
  80.6 3.2 %collective-permute-start.8 = (bf16[4,32,2048]{2,1,0:T(8,128)(2,1)}, bf16[4,32,2048]{2,1,0:T(8,128)(2,1)S(1)}, u32[]{:S(2)}, u32[]{:S(2)}) collective-permute-start(bf16[4,32,2048]{2,1,0:T(8,128)(2,1)} %fusion), channel_id=1, source_target_pairs={{0,16},{1,17},{2,18},{3,19},{4,20},{5,21},{6,22},{7,23},{8,24},{9,... | collective-permute-start | bytes 1572872 | tf_op jit(solution)/shard_map/ppermute | solution.py:15
  83.9 2.0 %fusion.19 = bf16[128,1024]{0,1:T(8,128)(2,1)} fusion(bf16[1024,2048]{1,0:T(8,128)(2,1)S(1)} %bitcast.260, bf16[128,2048]{1,0:T(8,128)(2,1)S(1)} %bitcast.287), kind=kOutput, calls=%fused_computation.60 | convolution fusion | flops 537001984 | bytes 4980736 | tf_op jit(solution)/shard_map/transpose(jvp())/dot_general | solution.py:88
  85.9 1.1 copy.72
  87.1 8.5 %collective-permute-done.8 = bf16[4,32,2048]{2,1,0:T(8,128)(2,1)S(1)} collective-permute-done((bf16[4,32,2048]{2,1,0:T(8,128)(2,1)}, bf16[4,32,2048]{2,1,0:T(8,128)(2,1)S(1)}, u32[]{:S(2)}, u32[]{:S(2)}) %collective-permute-start.8) | collective-permute-done | bytes 524320 | tf_op jit(solution)/shard_map/ppermute | solution.py:15
  96.2 0.8 fusion.20
  98.2 0.6 fusion.31
  99.1 1.7 %collective-permute-start.9 = (bf16[4,32,2048]{2,1,0:T(8,128)(2,1)S(1)}, bf16[4,32,2048]{2,1,0:T(8,128)(2,1)S(1)}, u32[]{:S(2)}, u32[]{:S(2)}) collective-permute-start(bf16[4,32,2048]{2,1,0:T(8,128)(2,1)S(1)} %fusion.44), channel_id=1, source_target_pairs={{16,0},{17,1},{18,2},{19,3},{20,4},{21,5},{22,6},{23,7},{24,8},{25... | collective-permute-start | bytes 1572872 | tf_op jit(solution)/shard_map/ppermute | solution.py:15
  101.3 1.5 %convolution_convert_fusion = bf16[128,2048]{1,0:T(8,128)(2,1)S(1)} fusion(bf16[2048,1024]{1,0:T(8,128)(2,1)S(1)} %bitcast.257, bf16[16,8,8,128]{3,2,1,0:T(8,128)(2,1)S(1)} %bitcast.284), kind=kOutput, calls=%fused_computation.4 | convolution fusion | flops 537133056 | bytes 4980736 | tf_op jit(solution)/shard_map/transpose(jvp())/dot_general | solution.py:77
  102.8 11.7 %collective-permute-done.9 = bf16[4,32,2048]{2,1,0:T(8,128)(2,1)S(1)} collective-permute-done((bf16[4,32,2048]{2,1,0:T(8,128)(2,1)S(1)}, bf16[4,32,2048]{2,1,0:T(8,128)(2,1)S(1)}, u32[]{:S(2)}, u32[]{:S(2)}) %collective-permute-start.9) | collective-permute-done | bytes 524320 | tf_op jit(solution)/shard_map/ppermute | solution.py:15
  114.5 1.5 %fusion.22 = bf16[16,8,8,128]{3,1,2,0:T(8,128)(2,1)S(1)} fusion(bf16[128,2048]{1,0:T(8,128)(2,1)S(1)} %bitcast.278, bf16[1024,2048]{1,0:T(8,128)(2,1)S(1)} %bitcast.261), kind=kOutput, calls=%fused_computation.63 | convolution fusion | flops 537001984 | bytes 4980736 | tf_op jit(solution)/shard_map/transpose(jvp())/dot_general | solution.py:88
  116.7 0.4 fusion.26
  117.5 1.5 %convolution_convert_fusion.1 = bf16[128,2048]{1,0:T(8,128)(2,1)S(1)} fusion(bf16[2048,1024]{1,0:T(8,128)(2,1)S(1)} %bitcast.258, bf16[16,8,8,128]{3,2,1,0:T(8,128)(2,1)S(1)} %bitcast.283), kind=kOutput, calls=%fused_computation.5 | convolution fusion | flops 537133056 | bytes 4980736 | tf_op jit(solution)/shard_map/transpose(jvp())/dot_general | solution.py:77
  119.1 1.3 fusion.36
  120.5 1.2 collective-permute-done.10
  121.7 1.5 %collective-permute-start.11 = (f32[2048]{0:T(1024)S(1)}, f32[2048]{0:T(1024)S(1)}, u32[]{:S(2)}, u32[]{:S(2)}) collective-permute-start(f32[2048]{0:T(1024)S(1)} %add.89), channel_id=1, source_target_pairs={{0,2},{1,3},{2,0},{3,1},{4,6},{5,7},{6,4},{7,5},{8,10},{9,11},{10,... | collective-permute-start | bytes 24584 | tf_op jit(solution)/shard_map/ppermute | solution.py:55
  123.2 2.1 %collective-permute-done.11 = f32[2048]{0:T(1024)S(1)} collective-permute-done((f32[2048]{0:T(1024)S(1)}, f32[2048]{0:T(1024)S(1)}, u32[]{:S(2)}, u32[]{:S(2)}) %collective-permute-start.11) | collective-permute-done | bytes 8224 | tf_op jit(solution)/shard_map/ppermute | solution.py:55
  125.4 1.8 %collective-permute-start.12 = (f32[2048]{0:T(1024)S(1)}, f32[2048]{0:T(1024)S(1)}, u32[]{:S(2)}, u32[]{:S(2)}) collective-permute-start(f32[2048]{0:T(1024)S(1)} %add.90), channel_id=1, source_target_pairs={{0,4},{1,5},{2,6},{3,7},{4,0},{5,1},{6,2},{7,3},{8,12},{9,13},{10,... | collective-permute-start | bytes 24584 | tf_op jit(solution)/shard_map/ppermute | solution.py:55
  127.1 1.9 %collective-permute-done.12 = f32[2048]{0:T(1024)S(1)} collective-permute-done((f32[2048]{0:T(1024)S(1)}, f32[2048]{0:T(1024)S(1)}, u32[]{:S(2)}, u32[]{:S(2)}) %collective-permute-start.12) | collective-permute-done | bytes 8224 | tf_op jit(solution)/shard_map/ppermute | solution.py:55
  129.0 3.3 %collective-permute-start.13 = (f32[2048]{0:T(1024)S(1)}, f32[2048]{0:T(1024)S(1)}, u32[]{:S(2)}, u32[]{:S(2)}) collective-permute-start(f32[2048]{0:T(1024)S(1)} %add.91), channel_id=1, source_target_pairs={{0,8},{1,9},{2,10},{3,11},{4,12},{5,13},{6,14},{7,15},{8,0},{9,1},... | collective-permute-start | bytes 24584 | tf_op jit(solution)/shard_map/ppermute | solution.py:55
  132.3 1.9 %fusion.54 = bf16[1,4,1,32,2048]{4,3,2,1,0:T(8,128)(2,1)} fusion(f32[4,32,2048]{2,1,0:T(8,128)S(1)} %get-tuple-element.45, bf16[4,32,2048]{2,1,0:T(8,128)(2,1)S(1)} %collective-permute-done.9, bf16[4,32,1024]{2,1,0:T(8,128)(2,1)S(1)} %bitcast.277, bf16[4,32,1024]{2,1,0:T(8,128)(2,1)S(1)} %bitcast.275, bf16[4,1,32,2048]{3,2,1,0:T(8,128)(2,1)S(1)} %copy-done.6, ...), kind=kLoop, calls=%fused_computation.105 | loop fusion | flops 8912896 | bytes 4729346
  134.2 0.6 add.92
  (83 shorter events, 6.0 us)
Async XLA Ops:
  0.6 45.5 %copy-start = (bf16[16,2048]{1,0:T(8,128)(2,1)S(1)}, bf16[16,2048]{1,0:T(8,128)(2,1)}, u32[]{:S(2)}) copy-start(bf16[16,2048]{1,0:T(8,128)(2,1)} %param.11) | copy-start | bytes 196612
  0.6 29.4 %copy-start.5 = (bf16[4,1,32,2048]{3,2,1,0:T(8,128)(2,1)S(1)}, bf16[4,1,32,2048]{3,2,1,0:T(8,128)(2,1)}, u32[]{:S(2)}) copy-start(bf16[4,1,32,2048]{3,2,1,0:T(8,128)(2,1)} %param.8) | copy-start | bytes 1572868
  0.7 22.7 %collective-permute-start.4 = (bf16[1,128,1024]{2,1,0:T(8,128)(2,1)}, bf16[1,128,1024]{2,1,0:T(8,128)(2,1)S(1)}, u32[]{:S(2)}, u32[]{:S(2)}) collective-permute-start(bf16[1,128,1024]{2,1,0:T(8,128)(2,1)} %param.12), channel_id=1, source_target_pairs={{0,8},{1,9},{2,10},{3,11},{4,12},{5,13},{6,14},{7,15},{8,0},{9,1},... | collective-permute-start | bytes 786440 | tf_op jit(solution)/shard_map/ppermute | solution.py:37
  4.8 23.4 %collective-permute-start = (bf16[1,64,2048]{2,1,0:T(8,128)(2,1)}, bf16[1,64,2048]{2,1,0:T(8,128)(2,1)S(1)}, u32[]{:S(2)}, u32[]{:S(2)}) collective-permute-start(bf16[1,64,2048]{2,1,0:T(8,128)(2,1)} %param.13), channel_id=1, source_target_pairs={{0,8},{1,9},{2,10},{3,11},{4,12},{5,13},{6,14},{7,15},{8,0},{9,1},... | collective-permute-start | bytes 786440 | tf_op jit(solution)/shard_map/ppermute | solution.py:37
  24.4 12.3 %collective-permute-start.5 = (bf16[2,128,1024]{2,1,0:T(8,128)(2,1)S(1)}, bf16[2,128,1024]{2,1,0:T(8,128)(2,1)S(1)}, u32[]{:S(2)}, u32[]{:S(2)}) collective-permute-start(bf16[2,128,1024]{2,1,0:T(8,128)(2,1)S(1)} %pad_maximum_fusion.6), channel_id=1, source_target_pairs={{0,2},{1,3},{2,0},{3,1},{4,6},{5,7},{6,4},{7,5},{8,10},{9,11},{10,... | collective-permute-start | bytes 1572872 | tf_op jit(solution)/shard_map/ppermute | solution.py:37
  29.2 14.9 %collective-permute-start.1 = (bf16[2,64,2048]{2,1,0:T(8,128)(2,1)S(1)}, bf16[2,64,2048]{2,1,0:T(8,128)(2,1)S(1)}, u32[]{:S(2)}, u32[]{:S(2)}) collective-permute-start(bf16[2,64,2048]{2,1,0:T(8,128)(2,1)S(1)} %pad_maximum_fusion.7), channel_id=1, source_target_pairs={{0,4},{1,5},{2,6},{3,7},{4,0},{5,1},{6,2},{7,3},{8,12},{9,13},{10,... | collective-permute-start | bytes 1572872 | tf_op jit(solution)/shard_map/ppermute | solution.py:37
  30.3 15.7 %copy-start.12 = (s32[4,1,16,2]{2,3,1,0:T(2,128)S(1)}, s32[4,1,16,2]{2,3,1,0:T(2,128)}, u32[]{:S(2)}) copy-start(s32[4,1,16,2]{2,3,1,0:T(2,128)} %param.10) | copy-start | bytes 1540
  37.9 27.1 %collective-permute-start.6 = (bf16[4,128,1024]{2,1,0:T(8,128)(2,1)}, bf16[4,128,1024]{2,1,0:T(8,128)(2,1)}, u32[]{:S(2)}, u32[]{:S(2)}) collective-permute-start(bf16[4,128,1024]{2,1,0:T(8,128)(2,1)} %bitcast.24), channel_id=1, source_target_pairs={{0,4},{1,5},{2,6},{3,7},{4,0},{5,1},{6,2},{7,3},{8,12},{9,13},{10,... | collective-permute-start | bytes 3145736 | tf_op jit(solution)/shard_map/ppermute | solution.py:37
  44.3 23.9 %collective-permute-start.2 = (bf16[4,64,2048]{2,1,0:T(8,128)(2,1)S(1)}, bf16[4,64,2048]{2,1,0:T(8,128)(2,1)}, u32[]{:S(2)}, u32[]{:S(2)}) collective-permute-start(bf16[4,64,2048]{2,1,0:T(8,128)(2,1)S(1)} %bitcast.269), channel_id=1, source_target_pairs={{0,2},{1,3},{2,0},{3,1},{4,6},{5,7},{6,4},{7,5},{8,10},{9,11},{10,... | collective-permute-start | bytes 3145736 | tf_op jit(solution)/shard_map/ppermute | solution.py:37
  46.5 21.6 %copy-start.13 = (s32[4,1,32]{2,1,0:T(1,128)S(1)}, s32[4,1,32]{2,1,0:T(1,128)}, u32[]{:S(2)}) copy-start(s32[4,1,32]{2,1,0:T(1,128)} %param.9) | copy-start | bytes 1540
  68.1 4.5 %collective-permute-start.7 = (bf16[8,128,1024]{2,1,0:T(8,128)(2,1)}, bf16[8,128,1024]{2,1,0:T(8,128)(2,1)}, u32[]{:S(2)}, u32[]{:S(2)}) collective-permute-start(bf16[8,128,1024]{2,1,0:T(8,128)(2,1)} %bitcast.29), channel_id=1, source_target_pairs={{0,1},{1,0},{2,3},{3,2},{4,5},{5,4},{6,7},{7,6},{8,9},{9,8},{10,11... | collective-permute-start | bytes 6291464 | tf_op jit(solution)/shard_map/ppermute | solution.py:37
  68.2 2.2 %copy-start.9 = (f32[1,2048]{1,0:T(1,128)S(1)}, f32[1,2048]{1,0:T(1,128)}, u32[]{:S(2)}) copy-start(f32[1,2048]{1,0:T(1,128)} %param.14) | copy-start | bytes 24580
  69.7 6.6 %collective-permute-start.3 = (bf16[8,64,2048]{2,1,0:T(8,128)(2,1)S(1)}, bf16[8,64,2048]{2,1,0:T(8,128)(2,1)S(1)}, u32[]{:S(2)}, u32[]{:S(2)}) collective-permute-start(bf16[8,64,2048]{2,1,0:T(8,128)(2,1)S(1)} %bitcast.262), channel_id=1, source_target_pairs={{0,1},{1,0},{2,3},{3,2},{4,5},{5,4},{6,7},{7,6},{8,9},{9,8},{10,11... | collective-permute-start | bytes 6291464 | tf_op jit(solution)/shard_map/ppermute | solution.py:37
  70.6 7.3 %copy-start.10 = (bf16[4,4,8,8,128]{4,3,2,1,0:T(8,128)(2,1)}, bf16[4,4,8,8,128]{4,3,2,1,0:T(8,128)(2,1)S(1)}, u32[]{:S(2)}) copy-start(bf16[4,4,8,8,128]{4,3,2,1,0:T(8,128)(2,1)S(1)} %get-tuple-element.32) | copy-start | bytes 786436
  75.5 1.9 %copy-start.1 = (bf16[2,2,2,2,128,1024]{5,4,3,2,1,0:T(8,128)(2,1)}, bf16[2,2,2,2,128,1024]{5,4,3,2,1,0:T(8,128)(2,1)S(1)}, u32[]{:S(2)}) copy-start(bf16[2,2,2,2,128,1024]{5,4,3,2,1,0:T(8,128)(2,1)S(1)} %pad_maximum_fusion) | copy-start | bytes 12582916
  77.9 6.0 %copy-start.3 = (bf16[2,2,2,2,64,2048]{5,4,3,2,1,0:T(8,128)(2,1)}, bf16[2,2,2,2,64,2048]{5,4,3,2,1,0:T(8,128)(2,1)S(1)}, u32[]{:S(2)}) copy-start(bf16[2,2,2,2,64,2048]{5,4,3,2,1,0:T(8,128)(2,1)S(1)} %pad_maximum_fusion.1) | copy-start | bytes 12582916
  77.9 6.0 %copy-start.6 = (bf16[4,1,32,2048]{3,2,1,0:T(8,128)(2,1)S(1)}, bf16[4,1,32,2048]{3,2,1,0:T(8,128)(2,1)}, u32[]{:S(2)}) copy-start(bf16[4,1,32,2048]{3,2,1,0:T(8,128)(2,1)} %param.15) | copy-start | bytes 1572868
  78.2 0.8 copy-start.7
  80.6 15.0 %collective-permute-start.8 = (bf16[4,32,2048]{2,1,0:T(8,128)(2,1)}, bf16[4,32,2048]{2,1,0:T(8,128)(2,1)S(1)}, u32[]{:S(2)}, u32[]{:S(2)}) collective-permute-start(bf16[4,32,2048]{2,1,0:T(8,128)(2,1)} %fusion), channel_id=1, source_target_pairs={{0,16},{1,17},{2,18},{3,19},{4,20},{5,21},{6,22},{7,23},{8,24},{9,... | collective-permute-start | bytes 1572872 | tf_op jit(solution)/shard_map/ppermute | solution.py:15
  87.0 9.2 %copy-start.2 = (bf16[2,2,2,2,128,1024]{5,4,3,2,1,0:T(8,128)(2,1)S(1)}, bf16[2,2,2,2,128,1024]{5,4,3,2,1,0:T(8,128)(2,1)}, u32[]{:S(2)}) copy-start(bf16[2,2,2,2,128,1024]{5,4,3,2,1,0:T(8,128)(2,1)} %copy-done.1) | copy-start | bytes 12582916
  99.1 15.4 %copy-start.4 = (bf16[2,2,2,2,64,2048]{5,4,3,2,1,0:T(8,128)(2,1)S(1)}, bf16[2,2,2,2,64,2048]{5,4,3,2,1,0:T(8,128)(2,1)}, u32[]{:S(2)}) copy-start(bf16[2,2,2,2,64,2048]{5,4,3,2,1,0:T(8,128)(2,1)} %copy-done.3) | copy-start | bytes 12582916
  99.1 15.4 %collective-permute-start.9 = (bf16[4,32,2048]{2,1,0:T(8,128)(2,1)S(1)}, bf16[4,32,2048]{2,1,0:T(8,128)(2,1)S(1)}, u32[]{:S(2)}, u32[]{:S(2)}) collective-permute-start(bf16[4,32,2048]{2,1,0:T(8,128)(2,1)S(1)} %fusion.44), channel_id=1, source_target_pairs={{16,0},{17,1},{18,2},{19,3},{20,4},{21,5},{22,6},{23,7},{24,8},{25... | collective-permute-start | bytes 1572872 | tf_op jit(solution)/shard_map/ppermute | solution.py:15
  101.3 14.8 %copy-start.8 = (f32[4,8,32,32]{2,3,1,0:T(8,128)S(1)}, f32[4,8,32,32]{2,3,1,0:T(8,128)}, u32[]{:S(2)}) copy-start(f32[4,8,32,32]{2,3,1,0:T(8,128)} %copy-done.7) | copy-start | bytes 393220
  114.5 2.2 %copy-start.11 = (bf16[4,4,8,8,128]{4,3,2,1,0:T(8,128)(2,1)S(1)}, bf16[4,4,8,8,128]{4,3,2,1,0:T(8,128)(2,1)}, u32[]{:S(2)}) copy-start(bf16[4,4,8,8,128]{4,3,2,1,0:T(8,128)(2,1)} %copy-done.10) | copy-start | bytes 786436
  120.5 1.2 collective-permute-start.10
  121.7 3.7 %collective-permute-start.11 = (f32[2048]{0:T(1024)S(1)}, f32[2048]{0:T(1024)S(1)}, u32[]{:S(2)}, u32[]{:S(2)}) collective-permute-start(f32[2048]{0:T(1024)S(1)} %add.89), channel_id=1, source_target_pairs={{0,2},{1,3},{2,0},{3,1},{4,6},{5,7},{6,4},{7,5},{8,10},{9,11},{10,... | collective-permute-start | bytes 24584 | tf_op jit(solution)/shard_map/ppermute | solution.py:55
  125.4 3.7 %collective-permute-start.12 = (f32[2048]{0:T(1024)S(1)}, f32[2048]{0:T(1024)S(1)}, u32[]{:S(2)}, u32[]{:S(2)}) collective-permute-start(f32[2048]{0:T(1024)S(1)} %add.90), channel_id=1, source_target_pairs={{0,4},{1,5},{2,6},{3,7},{4,0},{5,1},{6,2},{7,3},{8,12},{9,13},{10,... | collective-permute-start | bytes 24584 | tf_op jit(solution)/shard_map/ppermute | solution.py:55
  129.0 5.2 %collective-permute-start.13 = (f32[2048]{0:T(1024)S(1)}, f32[2048]{0:T(1024)S(1)}, u32[]{:S(2)}, u32[]{:S(2)}) collective-permute-start(f32[2048]{0:T(1024)S(1)} %add.91), channel_id=1, source_target_pairs={{0,8},{1,9},{2,10},{3,11},{4,12},{5,13},{6,14},{7,15},{8,0},{9,1},... | collective-permute-start | bytes 24584 | tf_op jit(solution)/shard_map/ppermute | solution.py:55

commit v15 on v6

--- a/solution.py
+++ b/solution.py
@@ -24,12 +24,13 @@
     other = list(steps)
     if len(other) >= 3:
         other[1], other[2] = other[2], other[1]
-    return steps, other
+    return other, steps
 
 
 def butterfly_gathers(shards, orders, axis, size):
     index = lax.axis_index(axis)
     held = [shard for shard in shards]
+    done = [[] for _ in shards]
     for level in range(len(orders[0])):
         for which, order in enumerate(orders):
             step = order[level]
@@ -37,19 +38,13 @@
             upper = ((index // step) % 2) == 1
             low = jnp.where(upper, other, held[which])
             high = jnp.where(upper, held[which], other)
-            held[which] = jnp.stack([low, high], axis=1).reshape(
-                (-1,) + held[which].shape[1:]
-            )
-    results = []
-    for which, order in enumerate(orders):
-        block_rows, width = held[which].shape[1:]
-        wanted = sorted(order, reverse=True)
-        if order != wanted:
-            split = held[which].reshape(tuple(2 for _ in order) + (block_rows, width))
-            axes = tuple(order.index(value) for value in wanted) + (len(order), len(order) + 1)
-            held[which] = jnp.transpose(split, axes)
-        results.append(held[which].reshape(size * block_rows, width))
-    return results
+            grid = (2,) * len(done[which]) + held[which].shape[1:]
+            place = sum(1 for value in done[which] if value > step)
+            held[which] = jnp.stack(
+                [low.reshape(grid), high.reshape(grid)], axis=place
+            ).reshape((-1,) + held[which].shape[1:])
+            done[which].append(step)
+    return [array.reshape(-1, array.shape[-1]) for array in held]
 
 
 def butterfly_sum(value, axis, size):

time: 139 us -> 140 us (level)
  other arithmetic: 15.4 us -> 19.6 us
  local copies, waits for them, and re-layouts: 7.56 us -> 3.51 us
  waiting for transfers between devices: 67.5 us -> 70.3 us
  matrix products: 22.4 us -> 20.6 us
    select_n x1 -> x6, other arithmetic: 0.41 us -> 5.19 us  [butterfly_gathers(): low = jnp.where(upper, other, held[which])]
    transpose x1 -> x0, local copies, waits for them, and re-layouts: 2.23 us -> none  [butterfly_gathers(): held[which] = jnp.transpose(split, axes)]
    another operation x14 -> x12, other arithmetic: 6.4 us -> 4.81 us  [the longest x10 4.53 us: butterfly_gathers(): jnp.stack([low.reshape(grid), high.reshape(grid)], axis=place)]
    reduce_sum x4, other arithmetic: 1.96 us -> 3.52 us  [rms_scale(): jnp.mean(inputs * inputs, axis=-1, keepdims=True) + EPSILON]
    unnamed x30 -> x50, local copies, waits for them, and re-layouts: 3.91 us -> 3.11 us
  transfers between devices with their start and end apart: 15 -> 15, of which waited for: 13 -> 11; matrix products, arithmetic and copies ran while one was open for 15% -> 16% of each run, Pallas kernels for 0% -> 0%
where the time goes in v15:
time: 140 us; the launch traced here: 139 us
  waiting for transfers between devices  70.3 us (50%)
  starting transfers between devices  23.7 us (17%)
  matrix products  20.6 us (15%)
  other arithmetic  19.6 us (14%)
  local copies, waits for them, and re-layouts  3.51 us (3%)
  between operations  1.45 us (1%)
    ppermute x8, waiting for transfers between devices, butterfly_gathers(): lax.ppermute(held[which], axis, [(j, j ^ step) for j in range(size)])  50.2 us
    ppermute x8, starting transfers between devices, butterfly_gathers(): lax.ppermute(held[which], axis, [(j, j ^ step) for j in range(size)])  9.95 us
    ppermute x2, waiting for transfers between devices, send_to(): return lax.ppermute(arrays, axis, [(source, target)])  9.28 us
    dot_general x5, matrix products, attend_layer(): update = jnp.dot(mixed, output_weight, preferred_element_type=jnp.float32)  8.39 us
    dot_general x7, matrix products, attend_layer(): jnp.dot(normed_rows, query_weight, preferred_element_type=jnp.float32)  7.6 us
    ppermute x4, waiting for transfers between devices, butterfly_sum(): lax.ppermute(value, axis, [(j, j ^ step) for j in range(size)])  6.05 us
    ppermute x4, starting transfers between devices, butterfly_sum(): lax.ppermute(value, axis, [(j, j ^ step) for j in range(size)])  6.01 us
    ppermute x2, starting transfers between devices, send_to(): return lax.ppermute(arrays, axis, [(source, target)])  5.24 us
  transfers between devices with their start and end apart: 15, of which 11 were waited for; matrix products, arithmetic and copies ran while one was open for 16% of the time, Pallas kernels for 0%

profile of v15, /device:TPU:0, one launch (start us, length us, event | category | flops | bytes accessed | tf_op | source)
XLA Modules:
  0.0 139.2 jit_solution(14964532595208478875)
XLA Ops:
  0.7 4.1 %collective-permute-start.4 = (bf16[1,64,2048]{2,1,0:T(8,128)(2,1)}, bf16[1,64,2048]{2,1,0:T(8,128)(2,1)S(1)}, u32[]{:S(2)}, u32[]{:S(2)}) collective-permute-start(bf16[1,64,2048]{2,1,0:T(8,128)(2,1)} %param.13), channel_id=1, source_target_pairs={{0,8},{1,9},{2,10},{3,11},{4,12},{5,13},{6,14},{7,15},{8,0},{9,1},... | collective-permute-start | bytes 786440 | tf_op jit(solution)/shard_map/ppermute | solution.py:37
  4.8 1.2 fusion.51
  6.0 0.8 copy.98
  7.3 2.0 %fusion.64 = (f32[2,32]{1,0:T(2,128)S(1)}, bf16[2,32,2048]{2,1,0:T(8,128)(2,1)S(1)}, f32[2,32]{1,0:T(2,128)S(1)}, bf16[2,32,2048]{2,1,0:T(8,128)(2,1)}, bf16[2,3...) fusion(bf16[4,32,2048]{2,1,0:T(8,128)(2,1)S(1)} %convolution_convert_fusion, ...), kind=kLoop, calls=%fused_computation.144 | loop fusion | flops 2097024 | bytes 2106369 | tf_op jit(solution)/shard_map/jvp()/reduce_sum | solution.py:63
  9.2 18.9 %collective-permute-done = bf16[1,128,1024]{2,1,0:T(8,128)(2,1)S(1)} collective-permute-done((bf16[1,128,1024]{2,1,0:T(8,128)(2,1)}, bf16[1,128,1024]{2,1,0:T(8,128)(2,1)S(1)}, u32[]{:S(2)}, u32[]{:S(2)}) %collective-permute-start) | collective-permute-done | bytes 262176 | tf_op jit(solution)/shard_map/ppermute | solution.py:37
  28.1 1.0 broadcast_select_fusion.11
  29.2 1.6 %collective-permute-start.1 = (bf16[2,128,1024]{2,1,0:T(8,128)(2,1)S(1)}, bf16[2,128,1024]{2,1,0:T(8,128)(2,1)S(1)}, u32[]{:S(2)}, u32[]{:S(2)}) collective-permute-start(bf16[2,128,1024]{2,1,0:T(8,128)(2,1)S(1)} %pad_maximum_fusion.6), channel_id=1, source_target_pairs={{0,2},{1,3},{2,0},{3,1},{4,6},{5,7},{6,4},{7,5},{8,10},{9,11},{10,... | collective-permute-start | bytes 1572872 | tf_op jit(solution)/shard_map/ppermute | solution.py:37
  30.9 0.8 collective-permute-start.5
  31.8 0.7 slice_bitcast_fusion.8
  32.5 9.9 %collective-permute-done.1 = bf16[2,128,1024]{2,1,0:T(8,128)(2,1)S(1)} collective-permute-done((bf16[2,128,1024]{2,1,0:T(8,128)(2,1)S(1)}, bf16[2,128,1024]{2,1,0:T(8,128)(2,1)S(1)}, u32[]{:S(2)}, u32[]{:S(2)}) %collective-permute-start.1) | collective-permute-done | bytes 524320 | tf_op jit(solution)/shard_map/ppermute | solution.py:37
  42.5 1.6 %collective-permute-start.2 = (bf16[4,128,1024]{2,1,0:T(8,128)(2,1)S(1)}, bf16[4,128,1024]{2,1,0:T(8,128)(2,1)S(1)}, u32[]{:S(2)}, u32[]{:S(2)}) collective-permute-start(bf16[4,128,1024]{2,1,0:T(8,128)(2,1)S(1)} %bitcast.356), channel_id=1, source_target_pairs={{0,4},{1,5},{2,6},{3,7},{4,0},{5,1},{6,2},{7,3},{8,12},{9,13},{10,... | collective-permute-start | bytes 3145736 | tf_op jit(solution)/shard_map/ppermute | solution.py:37
  44.2 1.1 pad_maximum_fusion.5
  45.3 1.5 %collective-permute-start.6 = (bf16[4,64,2048]{2,1,0:T(8,128)(2,1)}, bf16[4,64,2048]{2,1,0:T(8,128)(2,1)}, u32[]{:S(2)}, u32[]{:S(2)}) collective-permute-start(bf16[4,64,2048]{2,1,0:T(8,128)(2,1)} %bitcast.27), channel_id=1, source_target_pairs={{0,2},{1,3},{2,0},{3,1},{4,6},{5,7},{6,4},{7,5},{8,10},{9,11},{10,... | collective-permute-start | bytes 3145736 | tf_op jit(solution)/shard_map/ppermute | solution.py:37
  46.9 0.7 slice_bitcast_fusion.2
  47.6 19.1 %collective-permute-done.2 = bf16[4,128,1024]{2,1,0:T(8,128)(2,1)S(1)} collective-permute-done((bf16[4,128,1024]{2,1,0:T(8,128)(2,1)S(1)}, bf16[4,128,1024]{2,1,0:T(8,128)(2,1)S(1)}, u32[]{:S(2)}, u32[]{:S(2)}) %collective-permute-start.2) | collective-permute-done | bytes 1048608 | tf_op jit(solution)/shard_map/ppermute | solution.py:37
  67.2 2.4 %collective-permute-done.6 = bf16[4,64,2048]{2,1,0:T(8,128)(2,1)} collective-permute-done((bf16[4,64,2048]{2,1,0:T(8,128)(2,1)}, bf16[4,64,2048]{2,1,0:T(8,128)(2,1)}, u32[]{:S(2)}, u32[]{:S(2)}) %collective-permute-start.6) | collective-permute-done | bytes 1048608 | tf_op jit(solution)/shard_map/ppermute | solution.py:37
  69.6 1.7 %broadcast_select_fusion.5 = (bf16[4,64,2048]{2,1,0:T(8,128)(2,1)S(1)}, bf16[4,64,2048]{2,1,0:T(8,128)(2,1)S(1)}) fusion(bf16[4,64,2048]{2,1,0:T(8,128)(2,1)} %collective-permute-done.6, pred[]{:T(512)S(6)} %eq.53, bf16[2,2,64,2048]{3,2,1,0:T(8,128)(2,1)} %pad_maximum_fusion.5), kind=kLoop, calls=%fused_computation.81 | loop fusion | flops 1048576 | bytes 4194305 | tf_op jit(solution)/shard_map/jit(_where)/select_n | solution.py:39
  71.6 0.7 slice_select_fusion
  72.3 1.1 multiply_convert_fusion.1
  73.4 1.9 %broadcast_select_fusion.3 = (bf16[8,128,1024]{2,1,0:T(8,128)(2,1)S(1)}, bf16[8,128,1024]{2,1,0:T(8,128)(2,1)S(1)}) fusion(bf16[8,128,1024]{2,1,0:T(8,128)(2,1)} %collective-permute-done.3, pred[]{:T(512)S(6)} %eq.51, bf16[2,2,2,128,1024]{4,3,2,1,0:T(8,128)(2,1)S(1)} %pad_maximum_fusion.2), kind=kLoop, calls=%fused_computation.16 | loop fusion | flops 2097152 | bytes 8388609 | tf_op jit(solution)/shard_map/jit(_where)/select_n | solution.py:39
  75.7 0.8 fusion.11
  77.6 2.3 %pad_maximum_fusion.1 = bf16[2,2,2,2,64,2048]{5,4,3,2,1,0:T(8,128)(2,1)} fusion(bf16[2,2,2,1,64,2048]{5,4,3,2,1,0:T(8,128)(2,1)S(1)} %bitcast.351, bf16[2,2,2,1,64,2048]{5,4,3,2,1,0:T(8,128)(2,1)S(1)} %bitcast.350), kind=kLoop, calls=%fused_computation.1 | loop fusion | flops 2097152 | bytes 8388608 | tf_op jit(solution)/shard_map/stack | solution.py:43
  80.5 3.2 %fusion = bf16[2,32,2048]{2,1,0:T(8,128)(2,1)S(1)} fusion(bf16[1024,2048,1]{1,0,2:T(8,128)(2,1)} %bitcast.335, bf16[2,8,4,8,128]{4,3,2,1,0:T(8,128)(2,1)S(1)} %fusion.24, bf16[4,1,32,2048]{3,2,0,1:T(8,128)(2,1)S(1)} %bitcast.343), kind=kOutput, calls=%fused_computation.5 | convolution fusion | flops 268828672 | bytes 4849664 | tf_op jit(solution)/shard_map/dot_general | solution.py:88
  83.7 3.7 %collective-permute-start.8 = (bf16[2,32,2048]{2,1,0:T(8,128)(2,1)S(1)}, bf16[2,32,2048]{2,1,0:T(8,128)(2,1)S(1)}, u32[]{:S(2)}, u32[]{:S(2)}) collective-permute-start(bf16[2,32,2048]{2,1,0:T(8,128)(2,1)S(1)} %fusion), channel_id=1, source_target_pairs={{0,16},{1,17},{2,18},{3,19},{4,20},{5,21},{6,22},{7,23},{8,24},{9,... | collective-permute-start | bytes 786440 | tf_op jit(solution)/shard_map/ppermute | solution.py:15
  87.4 0.9 fusion.12
  88.3 1.4 %fusion.13 = bf16[8,8,8,128]{3,1,2,0:T(8,128)(2,1)S(1)} fusion(bf16[64,2048]{1,0:T(8,128)(2,1)S(1)} %bitcast.383, bf16[1024,2048]{1,0:T(8,128)(2,1)S(1)} %bitcast.336), kind=kOutput, calls=%fused_computation.58 | convolution fusion | flops 268500992 | bytes 4587520 | tf_op jit(solution)/shard_map/transpose(jvp())/dot_general | solution.py:88
  89.8 0.9 fusion.16
  90.7 0.9 fusion.21
  91.6 1.8 %collective-permute-done.8 = bf16[2,32,2048]{2,1,0:T(8,128)(2,1)S(1)} collective-permute-done((bf16[2,32,2048]{2,1,0:T(8,128)(2,1)S(1)}, bf16[2,32,2048]{2,1,0:T(8,128)(2,1)S(1)}, u32[]{:S(2)}, u32[]{:S(2)}) %collective-permute-start.8) | collective-permute-done | bytes 262176 | tf_op jit(solution)/shard_map/ppermute | solution.py:15
  95.7 1.0 fusion.2
  96.7 2.5 %collective-permute-start.9 = (bf16[2,32,2048]{2,1,0:T(8,128)(2,1)S(1)}, bf16[2,32,2048]{2,1,0:T(8,128)(2,1)S(1)}, u32[]{:S(2)}, u32[]{:S(2)}) collective-permute-start(bf16[2,32,2048]{2,1,0:T(8,128)(2,1)S(1)} %fusion.2), channel_id=1, source_target_pairs={{0,16},{16,0},{1,17},{17,1},{2,18},{18,2},{3,19},{19,3},{4,20},{20... | collective-permute-start | bytes 786440 | tf_op jit(solution)/shard_map/ppermute | solution.py:125
  99.3 1.4 convolution_convert_fusion.2
  100.7 4.7 %collective-permute-done.9 = bf16[2,32,2048]{2,1,0:T(8,128)(2,1)S(1)} collective-permute-done((bf16[2,32,2048]{2,1,0:T(8,128)(2,1)S(1)}, bf16[2,32,2048]{2,1,0:T(8,128)(2,1)S(1)}, u32[]{:S(2)}, u32[]{:S(2)}) %collective-permute-start.9) | collective-permute-done | bytes 262176 | tf_op jit(solution)/shard_map/ppermute | solution.py:125
  105.4 1.4 fusion.15
  108.5 1.4 convolution_convert_fusion.3
  110.0 0.8 fusion.40
  111.4 1.5 %collective-permute-start.10 = (bf16[2,32,2048]{2,1,0:T(8,128)(2,1)S(1)}, bf16[2,32,2048]{2,1,0:T(8,128)(2,1)S(1)}, u32[]{:S(2)}, u32[]{:S(2)}) collective-permute-start(bf16[2,32,2048]{2,1,0:T(8,128)(2,1)S(1)} %get-tuple-element.23), channel_id=1, source_target_pairs={{16,0},{17,1},{18,2},{19,3},{20,4},{21,5},{22,6},{23,7},{24,8},{25... | collective-permute-start | bytes 786440 | tf_op jit(solution)/shard_map/ppermute | solution.py:15
  113.2 7.5 %collective-permute-done.10 = bf16[2,32,2048]{2,1,0:T(8,128)(2,1)S(1)} collective-permute-done((bf16[2,32,2048]{2,1,0:T(8,128)(2,1)S(1)}, bf16[2,32,2048]{2,1,0:T(8,128)(2,1)S(1)}, u32[]{:S(2)}, u32[]{:S(2)}) %collective-permute-start.10) | collective-permute-done | bytes 262176 | tf_op jit(solution)/shard_map/ppermute | solution.py:15
  120.6 1.4 fusion.20
  123.1 1.4 convolution_convert_fusion.1
  125.2 1.1 collective-permute-done.11
  126.4 1.5 %collective-permute-start.12 = (f32[2048]{0:T(1024)S(1)}, f32[2048]{0:T(1024)S(1)}, u32[]{:S(2)}, u32[]{:S(2)}) collective-permute-start(f32[2048]{0:T(1024)S(1)} %add.141), channel_id=1, source_target_pairs={{0,2},{1,3},{2,0},{3,1},{4,6},{5,7},{6,4},{7,5},{8,10},{9,11},{10,... | collective-permute-start | bytes 24584 | tf_op jit(solution)/shard_map/ppermute | solution.py:55
  127.9 2.1 %collective-permute-done.12 = f32[2048]{0:T(1024)S(1)} collective-permute-done((f32[2048]{0:T(1024)S(1)}, f32[2048]{0:T(1024)S(1)}, u32[]{:S(2)}, u32[]{:S(2)}) %collective-permute-start.12) | collective-permute-done | bytes 8224 | tf_op jit(solution)/shard_map/ppermute | solution.py:55
  130.0 1.1 collective-permute-start.13
  131.7 2.0 %collective-permute-done.13 = f32[2048]{0:T(1024)S(1)} collective-permute-done((f32[2048]{0:T(1024)S(1)}, f32[2048]{0:T(1024)S(1)}, u32[]{:S(2)}, u32[]{:S(2)}) %collective-permute-start.13) | collective-permute-done | bytes 8224 | tf_op jit(solution)/shard_map/ppermute | solution.py:55
  133.7 3.3 %collective-permute-start.14 = (f32[2048]{0:T(1024)S(1)}, f32[2048]{0:T(1024)S(1)}, u32[]{:S(2)}, u32[]{:S(2)}) collective-permute-start(f32[2048]{0:T(1024)S(1)} %add.143), channel_id=1, source_target_pairs={{0,8},{1,9},{2,10},{3,11},{4,12},{5,13},{6,14},{7,15},{8,0},{9,1},... | collective-permute-start | bytes 24584 | tf_op jit(solution)/shard_map/ppermute | solution.py:55
  137.0 0.8 maximum_bitcast_fusion
  137.8 0.8 collective-permute-done.14
  (127 shorter events, 11.3 us)
Async XLA Ops:
  0.6 6.3 %copy-start = (bf16[16,2048]{1,0:T(8,128)(2,1)S(1)}, bf16[16,2048]{1,0:T(8,128)(2,1)}, u32[]{:S(2)}) copy-start(bf16[16,2048]{1,0:T(8,128)(2,1)} %param.11) | copy-start | bytes 196612
  0.6 30.2 %copy-start.14 = (bf16[1,64,2048]{2,1,0:T(8,128)(2,1)S(1)}, bf16[1,64,2048]{2,1,0:T(8,128)(2,1)}, u32[]{:S(2)}) copy-start(bf16[1,64,2048]{2,1,0:T(8,128)(2,1)} %param.13) | copy-start | bytes 786436
  0.7 30.2 %collective-permute-start.4 = (bf16[1,64,2048]{2,1,0:T(8,128)(2,1)}, bf16[1,64,2048]{2,1,0:T(8,128)(2,1)S(1)}, u32[]{:S(2)}, u32[]{:S(2)}) collective-permute-start(bf16[1,64,2048]{2,1,0:T(8,128)(2,1)} %param.13), channel_id=1, source_target_pairs={{0,8},{1,9},{2,10},{3,11},{4,12},{5,13},{6,14},{7,15},{8,0},{9,1},... | collective-permute-start | bytes 786440 | tf_op jit(solution)/shard_map/ppermute | solution.py:37
  4.8 23.4 %collective-permute-start = (bf16[1,128,1024]{2,1,0:T(8,128)(2,1)}, bf16[1,128,1024]{2,1,0:T(8,128)(2,1)S(1)}, u32[]{:S(2)}, u32[]{:S(2)}) collective-permute-start(bf16[1,128,1024]{2,1,0:T(8,128)(2,1)} %param.12), channel_id=1, source_target_pairs={{0,8},{1,9},{2,10},{3,11},{4,12},{5,13},{6,14},{7,15},{8,0},{9,1},... | collective-permute-start | bytes 786440 | tf_op jit(solution)/shard_map/ppermute | solution.py:37
  29.2 13.2 %collective-permute-start.1 = (bf16[2,128,1024]{2,1,0:T(8,128)(2,1)S(1)}, bf16[2,128,1024]{2,1,0:T(8,128)(2,1)S(1)}, u32[]{:S(2)}, u32[]{:S(2)}) collective-permute-start(bf16[2,128,1024]{2,1,0:T(8,128)(2,1)S(1)} %pad_maximum_fusion.6), channel_id=1, source_target_pairs={{0,2},{1,3},{2,0},{3,1},{4,6},{5,7},{6,4},{7,5},{8,10},{9,11},{10,... | collective-permute-start | bytes 1572872 | tf_op jit(solution)/shard_map/ppermute | solution.py:37
  30.9 13.2 %collective-permute-start.5 = (bf16[2,64,2048]{2,1,0:T(8,128)(2,1)S(1)}, bf16[2,64,2048]{2,1,0:T(8,128)(2,1)S(1)}, u32[]{:S(2)}, u32[]{:S(2)}) collective-permute-start(bf16[2,64,2048]{2,1,0:T(8,128)(2,1)S(1)} %pad_maximum_fusion.7), channel_id=1, source_target_pairs={{0,4},{1,5},{2,6},{3,7},{4,0},{5,1},{6,2},{7,3},{8,12},{9,13},{10,... | collective-permute-start | bytes 1572872 | tf_op jit(solution)/shard_map/ppermute | solution.py:37
  32.5 14.3 %copy-start.18 = (s32[4,1,32]{2,1,0:T(1,128)S(1)}, s32[4,1,32]{2,1,0:T(1,128)}, u32[]{:S(2)}) copy-start(s32[4,1,32]{2,1,0:T(1,128)} %param.9) | copy-start | bytes 1540
  42.5 24.1 %collective-permute-start.2 = (bf16[4,128,1024]{2,1,0:T(8,128)(2,1)S(1)}, bf16[4,128,1024]{2,1,0:T(8,128)(2,1)S(1)}, u32[]{:S(2)}, u32[]{:S(2)}) collective-permute-start(bf16[4,128,1024]{2,1,0:T(8,128)(2,1)S(1)} %bitcast.356), channel_id=1, source_target_pairs={{0,4},{1,5},{2,6},{3,7},{4,0},{5,1},{6,2},{7,3},{8,12},{9,13},{10,... | collective-permute-start | bytes 3145736 | tf_op jit(solution)/shard_map/ppermute | solution.py:37
  45.3 24.3 %collective-permute-start.6 = (bf16[4,64,2048]{2,1,0:T(8,128)(2,1)}, bf16[4,64,2048]{2,1,0:T(8,128)(2,1)}, u32[]{:S(2)}, u32[]{:S(2)}) collective-permute-start(bf16[4,64,2048]{2,1,0:T(8,128)(2,1)} %bitcast.27), channel_id=1, source_target_pairs={{0,2},{1,3},{2,0},{3,1},{4,6},{5,7},{6,4},{7,5},{8,10},{9,11},{10,... | collective-permute-start | bytes 3145736 | tf_op jit(solution)/shard_map/ppermute | solution.py:37
  67.1 6.4 %collective-permute-start.3 = (bf16[8,128,1024]{2,1,0:T(8,128)(2,1)S(1)}, bf16[8,128,1024]{2,1,0:T(8,128)(2,1)}, u32[]{:S(2)}, u32[]{:S(2)}) collective-permute-start(bf16[8,128,1024]{2,1,0:T(8,128)(2,1)S(1)} %bitcast.348), channel_id=1, source_target_pairs={{0,1},{1,0},{2,3},{3,2},{4,5},{5,4},{6,7},{7,6},{8,9},{9,8},{10,11... | collective-permute-start | bytes 6291464 | tf_op jit(solution)/shard_map/ppermute | solution.py:37
  67.2 4.4 %copy-start.6 = (bf16[4,1,32,2048]{3,2,1,0:T(8,128)(2,1)S(1)}, bf16[4,1,32,2048]{3,2,1,0:T(8,128)(2,1)}, u32[]{:S(2)}) copy-start(bf16[4,1,32,2048]{3,2,1,0:T(8,128)(2,1)} %param.15) | copy-start | bytes 1572868
  67.2 5.1 %copy-start.4 = (bf16[4,1,32,2048]{3,2,1,0:T(8,128)(2,1)S(1)}, bf16[4,1,32,2048]{3,2,1,0:T(8,128)(2,1)}, u32[]{:S(2)}) copy-start(bf16[4,1,32,2048]{3,2,1,0:T(8,128)(2,1)} %param.8) | copy-start | bytes 1572868
  67.2 5.1 %copy-start.12 = (f32[1,2048]{1,0:T(1,128)S(1)}, f32[1,2048]{1,0:T(1,128)}, u32[]{:S(2)}) copy-start(f32[1,2048]{1,0:T(1,128)} %param.14) | copy-start | bytes 24580
  71.5 5.1 %collective-permute-start.7 = (bf16[8,64,2048]{2,1,0:T(8,128)(2,1)S(1)}, bf16[8,64,2048]{2,1,0:T(8,128)(2,1)S(1)}, u32[]{:S(2)}, u32[]{:S(2)}) collective-permute-start(bf16[8,64,2048]{2,1,0:T(8,128)(2,1)S(1)} %bitcast.349), channel_id=1, source_target_pairs={{0,1},{1,0},{2,3},{3,2},{4,5},{5,4},{6,7},{7,6},{8,9},{9,8},{10,11... | collective-permute-start | bytes 6291464 | tf_op jit(solution)/shard_map/ppermute | solution.py:37
  75.7 1.9 %copy-start.1 = (bf16[2,2,2,2,128,1024]{5,4,3,2,1,0:T(8,128)(2,1)}, bf16[2,2,2,2,128,1024]{5,4,3,2,1,0:T(8,128)(2,1)S(1)}, u32[]{:S(2)}) copy-start(bf16[2,2,2,2,128,1024]{5,4,3,2,1,0:T(8,128)(2,1)S(1)} %pad_maximum_fusion) | copy-start | bytes 12582916
  77.6 2.3 %copy-start.17 = (bf16[2,4,8,8,128]{4,3,2,1,0:T(8,128)(2,1)S(1)}, bf16[2,4,8,8,128]{4,3,2,1,0:T(8,128)(2,1)}, u32[]{:S(2)}) copy-start(bf16[2,4,8,8,128]{4,3,2,1,0:T(8,128)(2,1)} %get-tuple-element.65) | copy-start | bytes 393220
  77.6 2.5 %copy-start.16 = (bf16[2,4,8,8,128]{4,3,2,1,0:T(8,128)(2,1)S(1)}, bf16[2,4,8,8,128]{4,3,2,1,0:T(8,128)(2,1)}, u32[]{:S(2)}) copy-start(bf16[2,4,8,8,128]{4,3,2,1,0:T(8,128)(2,1)} %get-tuple-element.64) | copy-start | bytes 393220
  80.0 7.4 %copy-start.10 = (bf16[2,1,32,2048]{3,2,0,1:T(8,128)(2,1)S(1)}, bf16[2,1,32,2048]{3,2,0,1:T(8,128)(2,1)}, u32[]{:S(2)}) copy-start(bf16[2,1,32,2048]{3,2,0,1:T(8,128)(2,1)} %get-tuple-element.43) | copy-start | bytes 786436
  80.4 7.0 %copy-start.2 = (bf16[2,2,2,2,128,1024]{5,4,3,2,1,0:T(8,128)(2,1)S(1)}, bf16[2,2,2,2,128,1024]{5,4,3,2,1,0:T(8,128)(2,1)}, u32[]{:S(2)}) copy-start(bf16[2,2,2,2,128,1024]{5,4,3,2,1,0:T(8,128)(2,1)} %copy-done.1) | copy-start | bytes 12582916
  80.5 7.9 %copy-start.3 = (bf16[2,2,2,2,64,2048]{5,4,3,2,1,0:T(8,128)(2,1)S(1)}, bf16[2,2,2,2,64,2048]{5,4,3,2,1,0:T(8,128)(2,1)}, u32[]{:S(2)}) copy-start(bf16[2,2,2,2,64,2048]{5,4,3,2,1,0:T(8,128)(2,1)} %pad_maximum_fusion.1) | copy-start | bytes 12582916
  80.5 7.9 %copy-start.11 = (bf16[2,1,32,2048]{3,2,0,1:T(8,128)(2,1)S(1)}, bf16[2,1,32,2048]{3,2,0,1:T(8,128)(2,1)}, u32[]{:S(2)}) copy-start(bf16[2,1,32,2048]{3,2,0,1:T(8,128)(2,1)} %slice_select_fusion) | copy-start | bytes 786436
  83.7 9.7 %collective-permute-start.8 = (bf16[2,32,2048]{2,1,0:T(8,128)(2,1)S(1)}, bf16[2,32,2048]{2,1,0:T(8,128)(2,1)S(1)}, u32[]{:S(2)}, u32[]{:S(2)}) collective-permute-start(bf16[2,32,2048]{2,1,0:T(8,128)(2,1)S(1)} %fusion), channel_id=1, source_target_pairs={{0,16},{1,17},{2,18},{3,19},{4,20},{5,21},{6,22},{7,23},{8,24},{9,... | collective-permute-start | bytes 786440 | tf_op jit(solution)/shard_map/ppermute | solution.py:15
  87.4 2.4 %copy-start.9 = (bf16[2,1,32,2048]{3,2,0,1:T(8,128)(2,1)S(1)}, bf16[2,1,32,2048]{3,2,0,1:T(8,128)(2,1)}, u32[]{:S(2)}) copy-start(bf16[2,1,32,2048]{3,2,0,1:T(8,128)(2,1)} %get-tuple-element.42) | copy-start | bytes 786436
  88.3 2.3 %copy-start.8 = (bf16[2,1,32,2048]{3,2,0,1:T(8,128)(2,1)S(1)}, bf16[2,1,32,2048]{3,2,0,1:T(8,128)(2,1)}, u32[]{:S(2)}) copy-start(bf16[2,1,32,2048]{3,2,0,1:T(8,128)(2,1)} %get-tuple-element.50) | copy-start | bytes 786436
  93.6 2.1 %copy-start.5 = (bf16[2,32,2048]{2,1,0:T(8,128)(2,1)S(1)}, bf16[2,32,2048]{2,1,0:T(8,128)(2,1)}, u32[]{:S(2)}) copy-start(bf16[2,32,2048]{2,1,0:T(8,128)(2,1)} %get-tuple-element.45) | copy-start | bytes 786436
  95.6 9.8 %copy-start.7 = (bf16[4,1,32,2048]{3,2,1,0:T(8,128)(2,1)S(1)}, bf16[4,1,32,2048]{3,2,1,0:T(8,128)(2,1)}, u32[]{:S(2)}) copy-start(bf16[4,1,32,2048]{3,2,1,0:T(8,128)(2,1)} %param.15) | copy-start | bytes 1572868
  96.7 8.7 %collective-permute-start.9 = (bf16[2,32,2048]{2,1,0:T(8,128)(2,1)S(1)}, bf16[2,32,2048]{2,1,0:T(8,128)(2,1)S(1)}, u32[]{:S(2)}, u32[]{:S(2)}) collective-permute-start(bf16[2,32,2048]{2,1,0:T(8,128)(2,1)S(1)} %fusion.2), channel_id=1, source_target_pairs={{0,16},{16,0},{1,17},{17,1},{2,18},{18,2},{3,19},{19,3},{4,20},{20... | collective-permute-start | bytes 786440 | tf_op jit(solution)/shard_map/ppermute | solution.py:125
  108.5 4.4 %copy-start.15 = (bf16[2,4,8,8,128]{4,3,2,1,0:T(8,128)(2,1)S(1)}, bf16[2,4,8,8,128]{4,3,2,1,0:T(8,128)(2,1)}, u32[]{:S(2)}) copy-start(bf16[2,4,8,8,128]{4,3,2,1,0:T(8,128)(2,1)} %get-tuple-element.67) | copy-start | bytes 393220
  110.8 11.5 %copy-start.13 = (bf16[2,4,8,8,128]{4,3,2,1,0:T(8,128)(2,1)S(1)}, bf16[2,4,8,8,128]{4,3,2,1,0:T(8,128)(2,1)}, u32[]{:S(2)}) copy-start(bf16[2,4,8,8,128]{4,3,2,1,0:T(8,128)(2,1)} %get-tuple-element.66) | copy-start | bytes 393220
  111.4 9.2 %collective-permute-start.10 = (bf16[2,32,2048]{2,1,0:T(8,128)(2,1)S(1)}, bf16[2,32,2048]{2,1,0:T(8,128)(2,1)S(1)}, u32[]{:S(2)}, u32[]{:S(2)}) collective-permute-start(bf16[2,32,2048]{2,1,0:T(8,128)(2,1)S(1)} %get-tuple-element.23), channel_id=1, source_target_pairs={{16,0},{17,1},{18,2},{19,3},{20,4},{21,5},{22,6},{23,7},{24,8},{25... | collective-permute-start | bytes 786440 | tf_op jit(solution)/shard_map/ppermute | solution.py:15
  125.1 1.2 collective-permute-start.11
  126.4 3.7 %collective-permute-start.12 = (f32[2048]{0:T(1024)S(1)}, f32[2048]{0:T(1024)S(1)}, u32[]{:S(2)}, u32[]{:S(2)}) collective-permute-start(f32[2048]{0:T(1024)S(1)} %add.141), channel_id=1, source_target_pairs={{0,2},{1,3},{2,0},{3,1},{4,6},{5,7},{6,4},{7,5},{8,10},{9,11},{10,... | collective-permute-start | bytes 24584 | tf_op jit(solution)/shard_map/ppermute | solution.py:55
  130.0 3.7 %collective-permute-start.13 = (f32[2048]{0:T(1024)S(1)}, f32[2048]{0:T(1024)S(1)}, u32[]{:S(2)}, u32[]{:S(2)}) collective-permute-start(f32[2048]{0:T(1024)S(1)} %add.142), channel_id=1, source_target_pairs={{0,4},{1,5},{2,6},{3,7},{4,0},{5,1},{6,2},{7,3},{8,12},{9,13},{10,... | collective-permute-start | bytes 24584 | tf_op jit(solution)/shard_map/ppermute | solution.py:55
  133.7 4.9 %collective-permute-start.14 = (f32[2048]{0:T(1024)S(1)}, f32[2048]{0:T(1024)S(1)}, u32[]{:S(2)}, u32[]{:S(2)}) collective-permute-start(f32[2048]{0:T(1024)S(1)} %add.143), channel_id=1, source_target_pairs={{0,8},{1,9},{2,10},{3,11},{4,12},{5,13},{6,14},{7,15},{8,0},{9,1},... | collective-permute-start | bytes 24584 | tf_op jit(solution)/shard_map/ppermute | solution.py:55

commit v16 on v12

--- a/solution.py
+++ b/solution.py
@@ -50,10 +50,26 @@
 def butterfly_sum(value, axis, size):
     if size & (size - 1):
         return lax.psum(value, axis)
+    index = lax.axis_index(axis)
     step = 1
     while step < size:
-        value = value + lax.ppermute(value, axis, [(j, j ^ step) for j in range(size)])
-        step *= 2
+        width = 4 if step * 4 <= size else 2
+        offsets = [step * k for k in range(1, width)]
+        received = [value] + [
+            lax.ppermute(value, axis, [(j, j ^ offset) for j in range(size)]) for offset in offsets
+        ]
+        own = (index // step) % width
+        ordered = []
+        for member in range(width):
+            pick = received[0]
+            for k in range(1, width):
+                pick = jnp.where((own ^ member) == k, received[k], pick)
+            ordered.append(pick)
+        if width == 4:
+            value = (ordered[0] + ordered[1]) + (ordered[2] + ordered[3])
+        else:
+            value = ordered[0] + ordered[1]
+        step *= width
     return value
 
 

time: 135 us -> 134 us (level)
    ppermute x4 -> x6, waiting for transfers between devices: 5.16 us -> 3.89 us  [butterfly_sum(): lax.ppermute(value, axis, [(j, j ^ offset) for j in range(size)])]
    ppermute x4 -> x6, starting transfers between devices: 6.64 us -> 7.06 us  [butterfly_sum(): lax.ppermute(value, axis, [(j, j ^ offset) for j in range(size)])]
  transfers between devices with their start and end apart: 14 -> 16, of which waited for: 11 -> 11; matrix products, arithmetic and copies ran while one was open for 15% -> 15% of each run, Pallas kernels for 0% -> 0%
where the time goes in v16:
time: 134 us
  waiting for transfers between devices  75.8 us (57%)
  starting transfers between devices  22.8 us (17%)
  other arithmetic  17.6 us (13%)
  matrix products  13.3 us (10%)
  local copies, waits for them, and re-layouts  3.15 us (2%)
    ppermute x8, waiting for transfers between devices, butterfly_gathers(): lax.ppermute(held[which], axis, [(j, j ^ step) for j in range(size)])  51.7 us
    ppermute x2, waiting for transfers between devices, send_to(): return lax.ppermute(arrays, axis, [(source, target)])  20.2 us
    ppermute x8, starting transfers between devices, butterfly_gathers(): lax.ppermute(held[which], axis, [(j, j ^ step) for j in range(size)])  10.8 us
    select_n x6, other arithmetic, butterfly_gathers(): low = jnp.where(upper, other, held[which])  7.93 us
    ppermute x6, starting transfers between devices, butterfly_sum(): lax.ppermute(value, axis, [(j, j ^ offset) for j in range(size)])  7.06 us
    dot_general x3, matrix products, attend_layer(): update = jnp.dot(mixed, output_weight, preferred_element_type=jnp.float32)  5.11 us
    ppermute x2, starting transfers between devices, send_to(): return lax.ppermute(arrays, axis, [(source, target)])  4.97 us
    dot_general x4, matrix products, attend_layer(): jnp.dot(normed_rows, query_weight, preferred_element_type=jnp.float32)  4.51 us
  transfers between devices with their start and end apart: 16, of which 11 were waited for; matrix products, arithmetic and copies ran while one was open for 15% of the time, Pallas kernels for 0%

profile of v16, /device:TPU:0, one launch (start us, length us, event | category | flops | bytes accessed | tf_op | source)
XLA Modules:
  0.0 134.0 jit_solution(17631140000049416275)
XLA Ops:
  0.7 4.1 %collective-permute-start.4 = (bf16[1,128,1024]{2,1,0:T(8,128)(2,1)}, bf16[1,128,1024]{2,1,0:T(8,128)(2,1)S(1)}, u32[]{:S(2)}, u32[]{:S(2)}) collective-permute-start(bf16[1,128,1024]{2,1,0:T(8,128)(2,1)} %param.12), channel_id=1, source_target_pairs={{0,8},{1,9},{2,10},{3,11},{4,12},{5,13},{6,14},{7,15},{8,0},{9,1},... | collective-permute-start | bytes 786440 | tf_op jit(solution)/shard_map/ppermute | solution.py:37
  4.8 18.5 %collective-permute-done.4 = bf16[1,128,1024]{2,1,0:T(8,128)(2,1)S(1)} collective-permute-done((bf16[1,128,1024]{2,1,0:T(8,128)(2,1)}, bf16[1,128,1024]{2,1,0:T(8,128)(2,1)S(1)}, u32[]{:S(2)}, u32[]{:S(2)}) %collective-permute-start.4) | collective-permute-done | bytes 262176 | tf_op jit(solution)/shard_map/ppermute | solution.py:37
  23.3 1.0 broadcast_select_fusion.9
  24.4 1.9 %collective-permute-start.5 = (bf16[2,128,1024]{2,1,0:T(8,128)(2,1)S(1)}, bf16[2,128,1024]{2,1,0:T(8,128)(2,1)S(1)}, u32[]{:S(2)}, u32[]{:S(2)}) collective-permute-start(bf16[2,128,1024]{2,1,0:T(8,128)(2,1)S(1)} %pad_maximum_fusion.6), channel_id=1, source_target_pairs={{0,2},{1,3},{2,0},{3,1},{4,6},{5,7},{6,4},{7,5},{8,10},{9,11},{10,... | collective-permute-start | bytes 1572872 | tf_op jit(solution)/shard_map/ppermute | solution.py:37
  26.3 1.8 %collective-permute-done = bf16[1,64,2048]{2,1,0:T(8,128)(2,1)S(1)} collective-permute-done((bf16[1,64,2048]{2,1,0:T(8,128)(2,1)}, bf16[1,64,2048]{2,1,0:T(8,128)(2,1)S(1)}, u32[]{:S(2)}, u32[]{:S(2)}) %collective-permute-start) | collective-permute-done | bytes 262176 | tf_op jit(solution)/shard_map/ppermute | solution.py:37
  28.1 1.0 broadcast_select_fusion.11
  29.2 0.9 collective-permute-start.1
  30.3 6.5 %collective-permute-done.5 = bf16[2,128,1024]{2,1,0:T(8,128)(2,1)S(1)} collective-permute-done((bf16[2,128,1024]{2,1,0:T(8,128)(2,1)S(1)}, bf16[2,128,1024]{2,1,0:T(8,128)(2,1)S(1)}, u32[]{:S(2)}, u32[]{:S(2)}) %collective-permute-start.5) | collective-permute-done | bytes 524320 | tf_op jit(solution)/shard_map/ppermute | solution.py:37
  36.8 1.1 pad_maximum_fusion.4
  37.9 1.6 %collective-permute-start.6 = (bf16[4,128,1024]{2,1,0:T(8,128)(2,1)}, bf16[4,128,1024]{2,1,0:T(8,128)(2,1)}, u32[]{:S(2)}, u32[]{:S(2)}) collective-permute-start(bf16[4,128,1024]{2,1,0:T(8,128)(2,1)} %bitcast.24), channel_id=1, source_target_pairs={{0,4},{1,5},{2,6},{3,7},{4,0},{5,1},{6,2},{7,3},{8,12},{9,13},{10,... | collective-permute-start | bytes 3145736 | tf_op jit(solution)/shard_map/ppermute | solution.py:37
  39.4 4.7 %collective-permute-done.1 = bf16[2,64,2048]{2,1,0:T(8,128)(2,1)S(1)} collective-permute-done((bf16[2,64,2048]{2,1,0:T(8,128)(2,1)S(1)}, bf16[2,64,2048]{2,1,0:T(8,128)(2,1)S(1)}, u32[]{:S(2)}, u32[]{:S(2)}) %collective-permute-start.1) | collective-permute-done | bytes 524320 | tf_op jit(solution)/shard_map/ppermute | solution.py:37
  44.3 1.6 %collective-permute-start.2 = (bf16[4,64,2048]{2,1,0:T(8,128)(2,1)S(1)}, bf16[4,64,2048]{2,1,0:T(8,128)(2,1)}, u32[]{:S(2)}, u32[]{:S(2)}) collective-permute-start(bf16[4,64,2048]{2,1,0:T(8,128)(2,1)S(1)} %bitcast.269), channel_id=1, source_target_pairs={{0,2},{1,3},{2,0},{3,1},{4,6},{5,7},{6,4},{7,5},{8,10},{9,11},{10,... | collective-permute-start | bytes 3145736 | tf_op jit(solution)/shard_map/ppermute | solution.py:37
  46.1 0.4 multiply_reduce_fusion
  46.5 18.4 %collective-permute-done.6 = bf16[4,128,1024]{2,1,0:T(8,128)(2,1)} collective-permute-done((bf16[4,128,1024]{2,1,0:T(8,128)(2,1)}, bf16[4,128,1024]{2,1,0:T(8,128)(2,1)}, u32[]{:S(2)}, u32[]{:S(2)}) %collective-permute-start.6) | collective-permute-done | bytes 1048608 | tf_op jit(solution)/shard_map/ppermute | solution.py:37
  64.9 1.7 %broadcast_select_fusion.5 = (bf16[4,128,1024]{2,1,0:T(8,128)(2,1)S(1)}, bf16[4,128,1024]{2,1,0:T(8,128)(2,1)S(1)}) fusion(bf16[4,128,1024]{2,1,0:T(8,128)(2,1)} %collective-permute-done.6, pred[]{:T(512)S(6)} %eq.126, bf16[2,2,128,1024]{3,2,1,0:T(8,128)(2,1)} %pad_maximum_fusion.4), kind=kLoop, calls=%fused_computation.98 | loop fusion | flops 1048576 | bytes 4194305 | tf_op jit(solution)/shard_map/jit(_where)/select_n | solution.py:39
  66.6 1.5 %pad_maximum_fusion.2 = bf16[2,2,2,128,1024]{4,3,2,1,0:T(8,128)(2,1)} fusion(bf16[2,1,2,128,1024]{4,3,2,1,0:T(8,128)(2,1)S(1)} %bitcast.271, bf16[2,1,2,128,1024]{4,3,2,1,0:T(8,128)(2,1)S(1)} %bitcast.270), kind=kLoop, calls=%fused_computation.8 | loop fusion | flops 1048576 | bytes 4194304 | tf_op jit(solution)/shard_map/stack | solution.py:43
  68.2 1.4 %broadcast_select_fusion.7 = (bf16[4,64,2048]{2,1,0:T(8,128)(2,1)S(1)}, bf16[4,64,2048]{2,1,0:T(8,128)(2,1)S(1)}) fusion(bf16[4,64,2048]{2,1,0:T(8,128)(2,1)} %collective-permute-done.2, pred[]{:T(512)S(6)} %eq.125, bf16[2,2,64,2048]{3,2,1,0:T(8,128)(2,1)S(1)} %pad_maximum_fusion.5), kind=kLoop, calls=%fused_computation.100 | loop fusion | flops 1048576 | bytes 4194305 | tf_op jit(solution)/shard_map/jit(_where)/select_n | solution.py:39
  69.8 0.6 collective-permute-start.3
  70.8 1.9 %collective-permute-done.7 = bf16[8,128,1024]{2,1,0:T(8,128)(2,1)} collective-permute-done((bf16[8,128,1024]{2,1,0:T(8,128)(2,1)}, bf16[8,128,1024]{2,1,0:T(8,128)(2,1)}, u32[]{:S(2)}, u32[]{:S(2)}) %collective-permute-start.7) | collective-permute-done | bytes 2097184 | tf_op jit(solution)/shard_map/ppermute | solution.py:37
  72.6 2.5 %broadcast_select_fusion.1 = (bf16[8,128,1024]{2,1,0:T(8,128)(2,1)S(1)}, bf16[8,128,1024]{2,1,0:T(8,128)(2,1)S(1)}) fusion(bf16[8,128,1024]{2,1,0:T(8,128)(2,1)} %collective-permute-done.7, pred[]{:T(512)S(6)} %eq.124, bf16[2,2,2,128,1024]{4,3,2,1,0:T(8,128)(2,1)} %pad_maximum_fusion.2), kind=kLoop, calls=%fused_computation.11 | loop fusion | flops 2097152 | bytes 8388609 | tf_op jit(solution)/shard_map/jit(_where)/select_n | solution.py:39
  75.1 0.4 pad_maximum_fusion
  75.5 0.7 fusion.21
  76.3 0.4 broadcast_select_fusion.3
  76.8 0.7 copy-done.1
  77.5 0.4 pad_maximum_fusion.1
  78.5 0.5 copy-done.7
  79.0 1.6 %fusion = bf16[4,32,2048]{2,1,0:T(8,128)(2,1)} fusion(bf16[1024,2048,1]{1,0,2:T(8,128)(2,1)S(1)} %bitcast.259, bf16[4,1,32,2048]{3,2,1,0:T(8,128)(2,1)S(1)} %copy-done.5, bf16[4,8,4,8,128]{4,3,2,1,0:T(8,128)(2,1)S(1)} %fusion.23), kind=kOutput, calls=%fused_computation.3 | convolution fusion | flops 537657344 | bytes 5505024 | tf_op jit(solution)/shard_map/dot_general | solution.py:104
  80.6 3.2 %collective-permute-start.8 = (bf16[4,32,2048]{2,1,0:T(8,128)(2,1)}, bf16[4,32,2048]{2,1,0:T(8,128)(2,1)S(1)}, u32[]{:S(2)}, u32[]{:S(2)}) collective-permute-start(bf16[4,32,2048]{2,1,0:T(8,128)(2,1)} %fusion), channel_id=1, source_target_pairs={{0,16},{1,17},{2,18},{3,19},{4,20},{5,21},{6,22},{7,23},{8,24},{9,... | collective-permute-start | bytes 1572872 | tf_op jit(solution)/shard_map/ppermute | solution.py:15
  83.9 2.0 %fusion.19 = bf16[128,1024]{0,1:T(8,128)(2,1)} fusion(bf16[1024,2048]{1,0:T(8,128)(2,1)S(1)} %bitcast.260, bf16[128,2048]{1,0:T(8,128)(2,1)S(1)} %bitcast.287), kind=kOutput, calls=%fused_computation.60 | convolution fusion | flops 537001984 | bytes 4980736 | tf_op jit(solution)/shard_map/transpose(jvp())/dot_general | solution.py:104
  85.9 1.1 copy.72
  87.1 8.5 %collective-permute-done.8 = bf16[4,32,2048]{2,1,0:T(8,128)(2,1)S(1)} collective-permute-done((bf16[4,32,2048]{2,1,0:T(8,128)(2,1)}, bf16[4,32,2048]{2,1,0:T(8,128)(2,1)S(1)}, u32[]{:S(2)}, u32[]{:S(2)}) %collective-permute-start.8) | collective-permute-done | bytes 524320 | tf_op jit(solution)/shard_map/ppermute | solution.py:15
  96.2 0.8 fusion.20
  98.2 0.6 fusion.31
  99.1 1.7 %collective-permute-start.9 = (bf16[4,32,2048]{2,1,0:T(8,128)(2,1)S(1)}, bf16[4,32,2048]{2,1,0:T(8,128)(2,1)S(1)}, u32[]{:S(2)}, u32[]{:S(2)}) collective-permute-start(bf16[4,32,2048]{2,1,0:T(8,128)(2,1)S(1)} %fusion.44), channel_id=1, source_target_pairs={{16,0},{17,1},{18,2},{19,3},{20,4},{21,5},{22,6},{23,7},{24,8},{25... | collective-permute-start | bytes 1572872 | tf_op jit(solution)/shard_map/ppermute | solution.py:15
  101.3 1.5 %convolution_convert_fusion = bf16[128,2048]{1,0:T(8,128)(2,1)S(1)} fusion(bf16[2048,1024]{1,0:T(8,128)(2,1)S(1)} %bitcast.257, bf16[16,8,8,128]{3,2,1,0:T(8,128)(2,1)S(1)} %bitcast.284), kind=kOutput, calls=%fused_computation.4 | convolution fusion | flops 537133056 | bytes 4980736 | tf_op jit(solution)/shard_map/transpose(jvp())/dot_general | solution.py:93
  102.8 11.7 %collective-permute-done.9 = bf16[4,32,2048]{2,1,0:T(8,128)(2,1)S(1)} collective-permute-done((bf16[4,32,2048]{2,1,0:T(8,128)(2,1)S(1)}, bf16[4,32,2048]{2,1,0:T(8,128)(2,1)S(1)}, u32[]{:S(2)}, u32[]{:S(2)}) %collective-permute-start.9) | collective-permute-done | bytes 524320 | tf_op jit(solution)/shard_map/ppermute | solution.py:15
  114.5 1.5 %fusion.22 = bf16[16,8,8,128]{3,1,2,0:T(8,128)(2,1)S(1)} fusion(bf16[128,2048]{1,0:T(8,128)(2,1)S(1)} %bitcast.278, bf16[1024,2048]{1,0:T(8,128)(2,1)S(1)} %bitcast.261), kind=kOutput, calls=%fused_computation.63 | convolution fusion | flops 537001984 | bytes 4980736 | tf_op jit(solution)/shard_map/transpose(jvp())/dot_general | solution.py:104
  116.7 0.4 fusion.26
  117.5 1.5 %convolution_convert_fusion.1 = bf16[128,2048]{1,0:T(8,128)(2,1)S(1)} fusion(bf16[2048,1024]{1,0:T(8,128)(2,1)S(1)} %bitcast.258, bf16[16,8,8,128]{3,2,1,0:T(8,128)(2,1)S(1)} %bitcast.283), kind=kOutput, calls=%fused_computation.5 | convolution fusion | flops 537133056 | bytes 4980736 | tf_op jit(solution)/shard_map/transpose(jvp())/dot_general | solution.py:93
  119.1 1.3 fusion.36
  120.6 1.6 %collective-permute-start.11 = (f32[2048]{0:T(1024)S(1)}, f32[2048]{0:T(1024)S(1)}, u32[]{:S(2)}, u32[]{:S(2)}) collective-permute-start(f32[2048]{0:T(1024)S(1)} %select_add_fusion), channel_id=1, source_target_pairs={{0,2},{1,3},{2,0},{3,1},{4,6},{5,7},{6,4},{7,5},{8,10},{9,11},{10,... | collective-permute-start | bytes 24584 | tf_op jit(solution)/shard_map/ppermute | solution.py:59
  122.4 1.2 collective-permute-done.10
  123.6 0.6 collective-permute-done.11
  124.3 4.5 %collective-permute-start.13 = (f32[2048]{0:T(1024)S(1)}, f32[2048]{0:T(1024)S(1)}, u32[]{:S(2)}, u32[]{:S(2)}) collective-permute-start(f32[2048]{0:T(1024)S(1)} %add_add_fusion.5), channel_id=1, source_target_pairs={{0,12},{1,13},{2,14},{3,15},{4,8},{5,9},{6,10},{7,11},{8,4},{9,5},... | collective-permute-start | bytes 24584 | tf_op jit(solution)/shard_map/ppermute | solution.py:59
  128.8 0.6 collective-permute-start.15
  129.4 1.9 %fusion.54 = bf16[1,4,1,32,2048]{4,3,2,1,0:T(8,128)(2,1)} fusion(f32[4,32,2048]{2,1,0:T(8,128)S(1)} %get-tuple-element.45, bf16[4,32,2048]{2,1,0:T(8,128)(2,1)S(1)} %collective-permute-done.9, bf16[4,32,1024]{2,1,0:T(8,128)(2,1)S(1)} %bitcast.277, bf16[4,32,1024]{2,1,0:T(8,128)(2,1)S(1)} %bitcast.275, bf16[4,1,32,2048]{3,2,1,0:T(8,128)(2,1)S(1)} %copy-done.6, ...), kind=kLoop, calls=%fused_computation.105 | loop fusion | flops 8912896 | bytes 4729346
  131.3 2.0 %collective-permute-done.14 = f32[2048]{0:T(1024)S(1)} collective-permute-done((f32[2048]{0:T(1024)S(1)}, f32[2048]{0:T(1024)S(1)}, u32[]{:S(2)}, u32[]{:S(2)}) %collective-permute-start.14) | collective-permute-done | bytes 8224 | tf_op jit(solution)/shard_map/ppermute | solution.py:59
  133.3 0.6 add_add_fusion.4
  (85 shorter events, 6.2 us)
Async XLA Ops:
  0.6 45.5 %copy-start = (bf16[16,2048]{1,0:T(8,128)(2,1)S(1)}, bf16[16,2048]{1,0:T(8,128)(2,1)}, u32[]{:S(2)}) copy-start(bf16[16,2048]{1,0:T(8,128)(2,1)} %param.11) | copy-start | bytes 196612
  0.6 29.4 %copy-start.5 = (bf16[4,1,32,2048]{3,2,1,0:T(8,128)(2,1)S(1)}, bf16[4,1,32,2048]{3,2,1,0:T(8,128)(2,1)}, u32[]{:S(2)}) copy-start(bf16[4,1,32,2048]{3,2,1,0:T(8,128)(2,1)} %param.8) | copy-start | bytes 1572868
  0.7 22.7 %collective-permute-start.4 = (bf16[1,128,1024]{2,1,0:T(8,128)(2,1)}, bf16[1,128,1024]{2,1,0:T(8,128)(2,1)S(1)}, u32[]{:S(2)}, u32[]{:S(2)}) collective-permute-start(bf16[1,128,1024]{2,1,0:T(8,128)(2,1)} %param.12), channel_id=1, source_target_pairs={{0,8},{1,9},{2,10},{3,11},{4,12},{5,13},{6,14},{7,15},{8,0},{9,1},... | collective-permute-start | bytes 786440 | tf_op jit(solution)/shard_map/ppermute | solution.py:37
  4.8 23.4 %collective-permute-start = (bf16[1,64,2048]{2,1,0:T(8,128)(2,1)}, bf16[1,64,2048]{2,1,0:T(8,128)(2,1)S(1)}, u32[]{:S(2)}, u32[]{:S(2)}) collective-permute-start(bf16[1,64,2048]{2,1,0:T(8,128)(2,1)} %param.13), channel_id=1, source_target_pairs={{0,8},{1,9},{2,10},{3,11},{4,12},{5,13},{6,14},{7,15},{8,0},{9,1},... | collective-permute-start | bytes 786440 | tf_op jit(solution)/shard_map/ppermute | solution.py:37
  24.4 12.3 %collective-permute-start.5 = (bf16[2,128,1024]{2,1,0:T(8,128)(2,1)S(1)}, bf16[2,128,1024]{2,1,0:T(8,128)(2,1)S(1)}, u32[]{:S(2)}, u32[]{:S(2)}) collective-permute-start(bf16[2,128,1024]{2,1,0:T(8,128)(2,1)S(1)} %pad_maximum_fusion.6), channel_id=1, source_target_pairs={{0,2},{1,3},{2,0},{3,1},{4,6},{5,7},{6,4},{7,5},{8,10},{9,11},{10,... | collective-permute-start | bytes 1572872 | tf_op jit(solution)/shard_map/ppermute | solution.py:37
  29.2 14.9 %collective-permute-start.1 = (bf16[2,64,2048]{2,1,0:T(8,128)(2,1)S(1)}, bf16[2,64,2048]{2,1,0:T(8,128)(2,1)S(1)}, u32[]{:S(2)}, u32[]{:S(2)}) collective-permute-start(bf16[2,64,2048]{2,1,0:T(8,128)(2,1)S(1)} %pad_maximum_fusion.7), channel_id=1, source_target_pairs={{0,4},{1,5},{2,6},{3,7},{4,0},{5,1},{6,2},{7,3},{8,12},{9,13},{10,... | collective-permute-start | bytes 1572872 | tf_op jit(solution)/shard_map/ppermute | solution.py:37
  30.3 15.7 %copy-start.12 = (s32[4,1,16,2]{2,3,1,0:T(2,128)S(1)}, s32[4,1,16,2]{2,3,1,0:T(2,128)}, u32[]{:S(2)}) copy-start(s32[4,1,16,2]{2,3,1,0:T(2,128)} %param.10) | copy-start | bytes 1540
  37.9 27.0 %collective-permute-start.6 = (bf16[4,128,1024]{2,1,0:T(8,128)(2,1)}, bf16[4,128,1024]{2,1,0:T(8,128)(2,1)}, u32[]{:S(2)}, u32[]{:S(2)}) collective-permute-start(bf16[4,128,1024]{2,1,0:T(8,128)(2,1)} %bitcast.24), channel_id=1, source_target_pairs={{0,4},{1,5},{2,6},{3,7},{4,0},{5,1},{6,2},{7,3},{8,12},{9,13},{10,... | collective-permute-start | bytes 3145736 | tf_op jit(solution)/shard_map/ppermute | solution.py:37
  44.3 23.9 %collective-permute-start.2 = (bf16[4,64,2048]{2,1,0:T(8,128)(2,1)S(1)}, bf16[4,64,2048]{2,1,0:T(8,128)(2,1)}, u32[]{:S(2)}, u32[]{:S(2)}) collective-permute-start(bf16[4,64,2048]{2,1,0:T(8,128)(2,1)S(1)} %bitcast.269), channel_id=1, source_target_pairs={{0,2},{1,3},{2,0},{3,1},{4,6},{5,7},{6,4},{7,5},{8,10},{9,11},{10,... | collective-permute-start | bytes 3145736 | tf_op jit(solution)/shard_map/ppermute | solution.py:37
  46.5 21.6 %copy-start.13 = (s32[4,1,32]{2,1,0:T(1,128)S(1)}, s32[4,1,32]{2,1,0:T(1,128)}, u32[]{:S(2)}) copy-start(s32[4,1,32]{2,1,0:T(1,128)} %param.9) | copy-start | bytes 1540
  68.1 4.5 %collective-permute-start.7 = (bf16[8,128,1024]{2,1,0:T(8,128)(2,1)}, bf16[8,128,1024]{2,1,0:T(8,128)(2,1)}, u32[]{:S(2)}, u32[]{:S(2)}) collective-permute-start(bf16[8,128,1024]{2,1,0:T(8,128)(2,1)} %bitcast.29), channel_id=1, source_target_pairs={{0,1},{1,0},{2,3},{3,2},{4,5},{5,4},{6,7},{7,6},{8,9},{9,8},{10,11... | collective-permute-start | bytes 6291464 | tf_op jit(solution)/shard_map/ppermute | solution.py:37
  68.2 2.2 %copy-start.9 = (f32[1,2048]{1,0:T(1,128)S(1)}, f32[1,2048]{1,0:T(1,128)}, u32[]{:S(2)}) copy-start(f32[1,2048]{1,0:T(1,128)} %param.14) | copy-start | bytes 24580
  69.8 6.6 %collective-permute-start.3 = (bf16[8,64,2048]{2,1,0:T(8,128)(2,1)S(1)}, bf16[8,64,2048]{2,1,0:T(8,128)(2,1)S(1)}, u32[]{:S(2)}, u32[]{:S(2)}) collective-permute-start(bf16[8,64,2048]{2,1,0:T(8,128)(2,1)S(1)} %bitcast.262), channel_id=1, source_target_pairs={{0,1},{1,0},{2,3},{3,2},{4,5},{5,4},{6,7},{7,6},{8,9},{9,8},{10,11... | collective-permute-start | bytes 6291464 | tf_op jit(solution)/shard_map/ppermute | solution.py:37
  70.6 7.3 %copy-start.10 = (bf16[4,4,8,8,128]{4,3,2,1,0:T(8,128)(2,1)}, bf16[4,4,8,8,128]{4,3,2,1,0:T(8,128)(2,1)S(1)}, u32[]{:S(2)}) copy-start(bf16[4,4,8,8,128]{4,3,2,1,0:T(8,128)(2,1)S(1)} %get-tuple-element.32) | copy-start | bytes 786436
  75.5 1.9 %copy-start.1 = (bf16[2,2,2,2,128,1024]{5,4,3,2,1,0:T(8,128)(2,1)}, bf16[2,2,2,2,128,1024]{5,4,3,2,1,0:T(8,128)(2,1)S(1)}, u32[]{:S(2)}) copy-start(bf16[2,2,2,2,128,1024]{5,4,3,2,1,0:T(8,128)(2,1)S(1)} %pad_maximum_fusion) | copy-start | bytes 12582916
  77.9 6.0 %copy-start.3 = (bf16[2,2,2,2,64,2048]{5,4,3,2,1,0:T(8,128)(2,1)}, bf16[2,2,2,2,64,2048]{5,4,3,2,1,0:T(8,128)(2,1)S(1)}, u32[]{:S(2)}) copy-start(bf16[2,2,2,2,64,2048]{5,4,3,2,1,0:T(8,128)(2,1)S(1)} %pad_maximum_fusion.1) | copy-start | bytes 12582916
  77.9 6.0 %copy-start.6 = (bf16[4,1,32,2048]{3,2,1,0:T(8,128)(2,1)S(1)}, bf16[4,1,32,2048]{3,2,1,0:T(8,128)(2,1)}, u32[]{:S(2)}) copy-start(bf16[4,1,32,2048]{3,2,1,0:T(8,128)(2,1)} %param.15) | copy-start | bytes 1572868
  78.2 0.8 copy-start.7
  80.6 15.0 %collective-permute-start.8 = (bf16[4,32,2048]{2,1,0:T(8,128)(2,1)}, bf16[4,32,2048]{2,1,0:T(8,128)(2,1)S(1)}, u32[]{:S(2)}, u32[]{:S(2)}) collective-permute-start(bf16[4,32,2048]{2,1,0:T(8,128)(2,1)} %fusion), channel_id=1, source_target_pairs={{0,16},{1,17},{2,18},{3,19},{4,20},{5,21},{6,22},{7,23},{8,24},{9,... | collective-permute-start | bytes 1572872 | tf_op jit(solution)/shard_map/ppermute | solution.py:15
  87.0 9.2 %copy-start.2 = (bf16[2,2,2,2,128,1024]{5,4,3,2,1,0:T(8,128)(2,1)S(1)}, bf16[2,2,2,2,128,1024]{5,4,3,2,1,0:T(8,128)(2,1)}, u32[]{:S(2)}) copy-start(bf16[2,2,2,2,128,1024]{5,4,3,2,1,0:T(8,128)(2,1)} %copy-done.1) | copy-start | bytes 12582916
  99.1 15.4 %copy-start.4 = (bf16[2,2,2,2,64,2048]{5,4,3,2,1,0:T(8,128)(2,1)S(1)}, bf16[2,2,2,2,64,2048]{5,4,3,2,1,0:T(8,128)(2,1)}, u32[]{:S(2)}) copy-start(bf16[2,2,2,2,64,2048]{5,4,3,2,1,0:T(8,128)(2,1)} %copy-done.3) | copy-start | bytes 12582916
  99.1 15.4 %collective-permute-start.9 = (bf16[4,32,2048]{2,1,0:T(8,128)(2,1)S(1)}, bf16[4,32,2048]{2,1,0:T(8,128)(2,1)S(1)}, u32[]{:S(2)}, u32[]{:S(2)}) collective-permute-start(bf16[4,32,2048]{2,1,0:T(8,128)(2,1)S(1)} %fusion.44), channel_id=1, source_target_pairs={{16,0},{17,1},{18,2},{19,3},{20,4},{21,5},{22,6},{23,7},{24,8},{25... | collective-permute-start | bytes 1572872 | tf_op jit(solution)/shard_map/ppermute | solution.py:15
  101.3 14.8 %copy-start.8 = (f32[4,8,32,32]{2,3,1,0:T(8,128)S(1)}, f32[4,8,32,32]{2,3,1,0:T(8,128)}, u32[]{:S(2)}) copy-start(f32[4,8,32,32]{2,3,1,0:T(8,128)} %copy-done.7) | copy-start | bytes 393220
  114.5 2.2 %copy-start.11 = (bf16[4,4,8,8,128]{4,3,2,1,0:T(8,128)(2,1)S(1)}, bf16[4,4,8,8,128]{4,3,2,1,0:T(8,128)(2,1)}, u32[]{:S(2)}) copy-start(bf16[4,4,8,8,128]{4,3,2,1,0:T(8,128)(2,1)} %copy-done.10) | copy-start | bytes 786436
  120.5 3.2 %collective-permute-start.10 = (f32[2048]{0:T(1024)S(1)}, f32[2048]{0:T(1024)S(1)}, u32[]{:S(2)}, u32[]{:S(2)}) collective-permute-start(f32[2048]{0:T(1024)S(1)} %select_add_fusion), channel_id=1, source_target_pairs={{0,3},{1,2},{2,1},{3,0},{4,7},{5,6},{6,5},{7,4},{8,11},{9,10},{10,... | collective-permute-start | bytes 24584 | tf_op jit(solution)/shard_map/ppermute | solution.py:59
  120.6 3.7 %collective-permute-start.11 = (f32[2048]{0:T(1024)S(1)}, f32[2048]{0:T(1024)S(1)}, u32[]{:S(2)}, u32[]{:S(2)}) collective-permute-start(f32[2048]{0:T(1024)S(1)} %select_add_fusion), channel_id=1, source_target_pairs={{0,2},{1,3},{2,0},{3,1},{4,6},{5,7},{6,4},{7,5},{8,10},{9,11},{10,... | collective-permute-start | bytes 24584 | tf_op jit(solution)/shard_map/ppermute | solution.py:59
  122.1 2.1 %collective-permute-start.12 = (f32[2048]{0:T(1024)S(1)}, f32[2048]{0:T(1024)S(1)}, u32[]{:S(2)}, u32[]{:S(2)}) collective-permute-start(f32[2048]{0:T(1024)S(1)} %select_add_fusion), channel_id=1, source_target_pairs={{0,1},{1,0},{2,3},{3,2},{4,5},{5,4},{6,7},{7,6},{8,9},{9,8},{10,11... | collective-permute-start | bytes 24584 | tf_op jit(solution)/shard_map/ppermute | solution.py:59
  124.3 7.0 %collective-permute-start.13 = (f32[2048]{0:T(1024)S(1)}, f32[2048]{0:T(1024)S(1)}, u32[]{:S(2)}, u32[]{:S(2)}) collective-permute-start(f32[2048]{0:T(1024)S(1)} %add_add_fusion.5), channel_id=1, source_target_pairs={{0,12},{1,13},{2,14},{3,15},{4,8},{5,9},{6,10},{7,11},{8,4},{9,5},... | collective-permute-start | bytes 24584 | tf_op jit(solution)/shard_map/ppermute | solution.py:59
  128.8 4.5 %collective-permute-start.14 = (f32[2048]{0:T(1024)S(1)}, f32[2048]{0:T(1024)S(1)}, u32[]{:S(2)}, u32[]{:S(2)}) collective-permute-start(f32[2048]{0:T(1024)S(1)} %add_add_fusion.5), channel_id=1, source_target_pairs={{0,8},{1,9},{2,10},{3,11},{4,12},{5,13},{6,14},{7,15},{8,0},{9,1},... | collective-permute-start | bytes 24584 | tf_op jit(solution)/shard_map/ppermute | solution.py:59
  128.8 4.5 %collective-permute-start.15 = (f32[2048]{0:T(1024)S(1)}, f32[2048]{0:T(1024)S(1)}, u32[]{:S(2)}, u32[]{:S(2)}) collective-permute-start(f32[2048]{0:T(1024)S(1)} %add_add_fusion.5), channel_id=1, source_target_pairs={{0,4},{1,5},{2,6},{3,7},{4,0},{5,1},{6,2},{7,3},{8,12},{9,13},{10,... | collective-permute-start | bytes 24584 | tf_op jit(solution)/shard_map/ppermute | solution.py:59
